TPU v7x, 512 devices: a whole 4x8x8 slice. The times are simulated.
512 devices in a mesh: ctx: 64 (over y, x, core), head: 8 (over z).
Axes of the slice: x: 4, y: 8, z: 8, core: 2. Of those that a mesh axis runs over, the one named last changes fastest.
Arguments:
- queries: bfloat16 [65536, 4096], P('ctx', 'head')
- keys: bfloat16 [65536, 4096], P('ctx', 'head'), may hold values from -5 to 5
- values: bfloat16 [65536, 4096], P('ctx', 'head')
- log_decay: float32 [65536, 32], P('ctx', 'head'), as said below
- gate: bfloat16 [65536, 4096], P('ctx', 'head'), may hold values from -6 to 6
- norm_gain: float32 [4096], replicated, may hold values from 0.1 to 1.9
Outputs:
- output: bfloat16 [65536, 4096], P(('ctx', 'head'))
Inputs may be any that keep to these rules, and one draw needn't show every extreme that they name: `log_decay`: every entry is at most 0.
All inputs are finite; a program needn't handle non-finite values.
Results may differ from a plain program's by a relative error of at most 0.0085.
Values may be sent and summed in bfloat16 or wider, within the bound.
No kernel may reach another device: no remote copies, remote signals or barrier semaphores. Data moves between devices by JAX's collectives and lax.ppermute only.
A program may use at most 128 MiB of HBM per device.

v0:
```python
import jax
import jax.numpy as jnp
from jax import lax
from jax.sharding import PartitionSpec as P

eps_norm = 1e-05


def carried_in(value, axis, join, neutral):
    count, mine = (lax.axis_size(axis), lax.axis_index(axis))
    pieces = jax.tree.map(lambda part: lax.all_gather(part, axis), value)
    subtotal = jax.tree.map(
        lambda part, zero: jnp.full_like(part, 0) + jnp.asarray(zero, part.dtype), value, neutral
    )

    def step(position, subtotal):
        longer = join(subtotal, jax.tree.map(lambda part: part[position], pieces))
        return jax.tree.map(lambda new, old: jnp.where(position < mine, new, old), longer, subtotal)

    return lax.fori_loop(0, count - 1, step, subtotal)


def head_block(qh, kh, vh, ch):
    count = qh.shape[0]
    target_index = jnp.arange(count)
    causal = target_index[:, None] >= target_index[None, :]
    scores = jnp.dot(qh, kh.T, preferred_element_type=jnp.float32)
    spread = jnp.where(causal, ch[:, None] - ch[None, :], 0.0)
    weights = (scores * jnp.where(causal, jnp.exp(spread), 0.0)).astype(jnp.bfloat16)
    inner = jnp.dot(weights, vh, preferred_element_type=jnp.float32)
    keyed = kh.astype(jnp.float32) * jnp.exp(ch[-1] - ch)[:, None]
    state = jnp.dot(keyed.T, vh.astype(jnp.float32), precision=lax.Precision.HIGHEST)
    return (inner, state)


def split_heads(block, heads):
    count = block.shape[0]
    return block.reshape(count, heads, block.shape[1] // heads).transpose(1, 0, 2)


def local_block(queries, keys, values, log_decay):
    heads = log_decay.shape[1]
    cum = jnp.cumsum(log_decay, axis=0)
    inner, state = lax.map(
        lambda parts: head_block(parts[0], parts[1], parts[2], parts[3]),
        (split_heads(queries, heads), split_heads(keys, heads), split_heads(values, heads), cum.T),
    )
    return (cum, inner, state)


def join_block(queries, cum, inner, carried):
    heads = cum.shape[1]
    count = queries.shape[0]
    qfloat = split_heads(queries, heads).astype(jnp.float32)
    across = jnp.einsum("hcd,hde->hce", qfloat, carried, precision=lax.Precision.HIGHEST)
    total = inner + jnp.exp(cum).T[:, :, None] * across
    return total.transpose(1, 0, 2).reshape(count, queries.shape[1]).astype(jnp.bfloat16)


def chain(earlier, later):
    return (earlier[0] * later[0], later[0][:, None, None] * earlier[1] + later[1])


def body(queries, keys, values, log_decay, gate, norm_gain):
    cum, inner, state = local_block(queries, keys, values, log_decay)
    heads = log_decay.shape[1]
    size = state.shape[1]
    totals = cum[-1]
    identity_pair = (jnp.ones((heads,), jnp.float32), jnp.zeros((heads, size, size), jnp.float32))
    passed = carried_in((jnp.exp(totals), state), "ctx", chain, identity_pair)
    carried = passed[1]
    attended = join_block(queries, cum, inner, carried)
    width = queries.shape[1]
    shade = attended.astype(jnp.float32)
    sums = lax.psum(jnp.sum(shade * shade, axis=1), "head")
    columns = width * lax.axis_size("head")
    scale = lax.rsqrt(sums / columns + eps_norm)[:, None]
    gain = lax.dynamic_slice_in_dim(norm_gain, lax.axis_index("head") * width, width, 0)
    shaped = (shade * scale * gain * jax.nn.sigmoid(gate.astype(jnp.float32))).astype(jnp.bfloat16)
    return lax.all_to_all(shaped, "head", split_axis=0, concat_axis=1, tiled=True)


def solution(mesh):
    in_specs = (
        P("ctx", "head"),
        P("ctx", "head"),
        P("ctx", "head"),
        P("ctx", "head"),
        P("ctx", "head"),
        P(),
    )
    out_specs = P(("ctx", "head"), None)
    return jax.shard_map(body, mesh=mesh, in_specs=in_specs, out_specs=out_specs, check_vma=False)
```

profile of v0, /device:TPU:24, one launch (start us, length us, event | category | flops | bytes accessed | tf_op | source)
XLA Modules:
  0.0 277.9 jit_solution(2023523587393030911)
XLA Ops:
  7.3 1.1 reduce-window.6
  8.9 2.4 copy.32
  12.4 24.4 %while.26 = (s32[]{:T(128)}, f32[4,1024,128]{1,2,0:T(8,128)}, f32[4,128,128]{2,1,0:T(8,128)}, bf16[4,1024,128]{1,2,0:T(8,128)(2,1)}, bf16[4,1024,128]{1,2,0:T(8,...) while((s32[]{:T(128)}, f32[4,1024,128]{1,2,0:T(8,128)}, ...), condition=%wide.region_3.4_spmd, body=%wide.region_2.3_spmd.sunk | while | flops 744752128 | bytes 2981001 | solution.py:44
  14.0 1.4 fusion.44
  15.3 3.1 %fusion.43 = f32[4,1024,128]{1,2,0:T(8,128)} fusion(f32[4,1024,128]{1,2,0:T(8,128)} %get-tuple-element.292, s32[]{:T(128)} %get-tuple-element.291, f32[1024]{0:T(1024)S(1)} %bitcast.111, bf16[4,1024,128]{1,2,0:T(8,128)(2,1)} %get-tuple-element.304, bf16[4,1024,128]{1,2,0:T(8,128)(2,1)S(1)} %get-tuple-element.307, ...), kind=kOutput, calls=%fused_computation.4.clone.1 | convolution fusion | flops 543162368 | bytes 1320960 | tf_op jit(solution)/shard_map/while/body/eval_jaxpr/dot_general | solution.py:30
  20.1 1.4 fusion.44
  21.4 3.1 %fusion.43 = f32[4,1024,128]{1,2,0:T(8,128)} fusion(f32[4,1024,128]{1,2,0:T(8,128)} %get-tuple-element.292, s32[]{:T(128)} %get-tuple-element.291, f32[1024]{0:T(1024)S(1)} %bitcast.111, bf16[4,1024,128]{1,2,0:T(8,128)(2,1)} %get-tuple-element.304, bf16[4,1024,128]{1,2,0:T(8,128)(2,1)S(1)} %get-tuple-element.307, ...), kind=kOutput, calls=%fused_computation.4.clone.1 | convolution fusion | flops 543162368 | bytes 1320960 | tf_op jit(solution)/shard_map/while/body/eval_jaxpr/dot_general | solution.py:30
  26.1 1.4 fusion.44
  27.5 3.2 %fusion.43 = f32[4,1024,128]{1,2,0:T(8,128)} fusion(f32[4,1024,128]{1,2,0:T(8,128)} %get-tuple-element.292, s32[]{:T(128)} %get-tuple-element.291, f32[1024]{0:T(1024)S(1)} %bitcast.111, bf16[4,1024,128]{1,2,0:T(8,128)(2,1)} %get-tuple-element.304, bf16[4,1024,128]{1,2,0:T(8,128)(2,1)S(1)} %get-tuple-element.307, ...), kind=kOutput, calls=%fused_computation.4.clone.1 | convolution fusion | flops 543162368 | bytes 1320960 | tf_op jit(solution)/shard_map/while/body/eval_jaxpr/dot_general | solution.py:30
  32.3 1.4 fusion.44
  33.6 3.2 %fusion.43 = f32[4,1024,128]{1,2,0:T(8,128)} fusion(f32[4,1024,128]{1,2,0:T(8,128)} %get-tuple-element.292, s32[]{:T(128)} %get-tuple-element.291, f32[1024]{0:T(1024)S(1)} %bitcast.111, bf16[4,1024,128]{1,2,0:T(8,128)(2,1)} %get-tuple-element.304, bf16[4,1024,128]{1,2,0:T(8,128)(2,1)S(1)} %get-tuple-element.307, ...), kind=kOutput, calls=%fused_computation.4.clone.1 | convolution fusion | flops 543162368 | bytes 1320960 | tf_op jit(solution)/shard_map/while/body/eval_jaxpr/dot_general | solution.py:30
  37.9 37.0 %all-gather.1 = f32[64,1,4]{2,1,0:T(1,128)S(1)} all-gather(f32[1,1,4]{2,1,0:T(1,128)S(1)} %bitcast.119), channel_id=1, replica_groups=mesh['ctx'=64,'head'=8] {'ctx'}, dimensions={0}, use_global_device_ids=true | all-gather | bytes 1040 | tf_op jit(solution)/shard_map/all_gather | solution.py:11
  74.8 71.1 %all-gather.4.cloned.1.call-done = f32[256,128,128]{2,1,0:T(8,128)} async-done(((f32[4,128,128]{2,1,0:T(8,128)}), f32[256,128,128]{2,1,0:T(8,128)}) %all-gather.4.cloned.1.call-update) | async-done | bytes 16777232 | tf_op jit(solution)/shard_map/all_gather | solution.py:11
  146.0 68.9 %while.27 = (s32[]{:T(128)}, f32[4,128,128]{2,1,0:T(8,128)S(1)}, s32[]{:T(128)}, f32[64,4]{1,0:T(8,128)S(1)}, f32[64,4,128,128]{3,2,1,0:T(8,128)}, /*index=5*/s32[]{:T(128)}, s32[]{:T(128)}) while((s32[]{:T(128)}, f32[4,128,128]{2,1,0:T(8,128)S(1)}, s32[]{:T(128)}, f32[64,4]{1,0:T(8,128)S(1)}, f32[64,4,128,128]{3,2,1,0:T(8,128)}, ...), condition=%wide.region_5.6_spmd.clone, body=%wide.region_4.5_spmd.clone.sunk | while | flops 262148 | bytes 786585 | solution.py:20
  147.1 1.1 fusion.45
  150.3 1.1 fusion.45
  151.4 1.1 fusion.45
  152.5 1.1 fusion.45
  155.8 1.1 fusion.45
  156.9 1.1 fusion.45
  158.0 1.1 fusion.45
  161.3 1.1 fusion.45
  162.4 1.1 fusion.45
  165.7 1.1 fusion.45
  166.8 1.1 fusion.45
  167.8 1.1 fusion.45
  171.1 1.1 fusion.45
  214.9 4.1 %multiply_reduce_fusion = (f32[1024]{0:T(1024)S(1)}, f32[4,1024,128]{1,2,0:T(8,128)}) fusion(f32[4,1024,128]{1,2,0:T(8,128)} %get-tuple-element.137, f32[4,128,128]{2,1,0:T(8,128)S(1)} %get-tuple-element.139, bf16[4,1024,128]{1,2,0:T(8,128)(2,1)S(1)} %copy-done, f32[4,1024]{1,0:T(4,128)S(1)} %fusion.27), kind=kOutput, calls=%fused_computation.30 | convolution fusion | flops 808451072 | bytes 5525504 | tf_op jit(solution)/shard_map/hcd,hde->hce/dot_general | solution.py:55
  219.0 2.0 copy.41
  221.0 18.1 %psum.7 = f32[1024]{0:T(1024)S(1)} all-reduce(f32[1024]{0:T(1024)S(1)} %get-tuple-element.205), channel_id=1, replica_groups=mesh['ctx'=64,'head'=8] {'head'}, use_global_device_ids=true, to_apply=%region_7.8 | all-reduce | flops 1024 | bytes 8192 | tf_op jit(solution)/shard_map/psum | solution.py:75
  239.8 29.4 %all_to_all.19 = bf16[8,128,512]{2,1,0:T(8,128)(2,1)S(1)} all-to-all(bf16[8,128,512]{2,1,0:T(8,128)(2,1)S(1)} %bitcast.107), channel_id=1, replica_groups=mesh['ctx'=64,'head'=8] {'head'}, dimensions={0} | all-to-all | bytes 2097152 | tf_op jit(solution)/shard_map/all_to_all | solution.py:80
  269.8 1.3 copy.43
  (159 shorter events, 64.1 us)
Async XLA Ops:
  6.5 4.7 %copy-start.2 = (bf16[1024,512]{1,0:T(8,128)(2,1)S(1)}, bf16[1024,512]{1,0:T(8,128)(2,1)}, u32[]{:S(2)}) copy-start(bf16[1024,512]{1,0:T(8,128)(2,1)} %param.11) | copy-start | bytes 3145732
  6.5 139.4 %all-gather.4.cloned.1.call-start = ((), (), s32[]{:S(2)}) async-start(), calls=%async_computation.1 | async-start | bytes 17039360 | tf_op jit(solution)/shard_map/all_gather | solution.py:11
  8.9 2.9 %copy-start.3 = (bf16[1024,512]{1,0:T(8,128)(2,1)S(1)}, bf16[1024,512]{1,0:T(8,128)(2,1)}, u32[]{:S(2)}) copy-start(bf16[1024,512]{1,0:T(8,128)(2,1)} %param.12) | copy-start | bytes 3145732
  36.8 178.1 %copy-start = (bf16[4,1024,128]{1,2,0:T(8,128)(2,1)S(1)}, bf16[4,1024,128]{1,2,0:T(8,128)(2,1)}, u32[]{:S(2)}) copy-start(bf16[4,1024,128]{1,2,0:T(8,128)(2,1)} %get-tuple-element.333) | copy-start | bytes 3145732
  219.0 20.1 %copy-start.1 = (bf16[1024,512]{1,0:T(8,128)(2,1)S(1)}, bf16[1024,512]{1,0:T(8,128)(2,1)}, u32[]{:S(2)}) copy-start(bf16[1024,512]{1,0:T(8,128)(2,1)} %param.14) | copy-start | bytes 3145732
Sparse Core Ops, SparseCore 0:
  36.9 108.9 all-gather.3
where the time goes:
time: 280 us; the launch traced here: 278 us
  blocking collectives  84.4 us (30%)
  other arithmetic  71.1 us (25%)
  waiting for transfers between devices  71.1 us (25%)
  matrix products  22.2 us (8%)
  local copies, waits for them, and re-layouts  13.5 us (5%)
  between operations  13.5 us (5%)
    all_gather x1, waiting for transfers between devices, carried_in(): pieces = jax.tree.map(lambda part: lax.all_gather(part, axis), value)  71.1 us
    select_n x63, other arithmetic, step(): jnp.where(position < mine, new, old)  66.3 us
    all_gather x1, blocking collectives, carried_in(): pieces = jax.tree.map(lambda part: lax.all_gather(part, axis), value)  37 us
    all_to_all x1, blocking collectives, body(): lax.all_to_all(shaped, 'head', split_axis=0, concat_axis=1, tiled=True)  29.4 us
    psum x1, blocking collectives, body(): sums = lax.psum(jnp.sum(shade * shade, axis=1), 'head')  18.1 us
    dot_general x4, matrix products, head_block(): inner = jnp.dot(weights, vh, preferred_element_type=jnp.float32)  12.6 us
  transfers between devices with their start and end apart: 1, of which 1 were waited for; matrix products, arithmetic and copies ran while one was open for 0% of the time, Pallas kernels for 0%

commit v1 on v0

v1 whole, which is shorter than its diff:
```python
import jax
import jax.numpy as jnp
from jax import lax
from jax.sharding import Mesh, PartitionSpec as P

eps_norm = 1e-05
HI = lax.Precision.HIGHEST
F32 = jnp.float32


def split_ctx(mesh):
    devices = mesh.devices
    ctx_devices = list(devices[:, 0])
    rows = len({d.coords[1] for d in ctx_devices})
    cols = len({d.coords[0] for d in ctx_devices})
    cores = len(ctx_devices) // (rows * cols)
    shape = (rows, cols, cores, devices.shape[1])
    return Mesh(devices.reshape(shape), ("cy", "cx", "cc", "head"))


def shifted(x, axis, n):
    out = [x]
    for s in range(1, n):
        out.append(lax.ppermute(x, axis, [(j, (j + s) % n) for j in range(n)]))
    return out


def scan_pieces(logs, states, i, n):
    log_before = jnp.zeros_like(logs[0])
    before = jnp.zeros_like(states[0])
    log_after = jnp.zeros_like(logs[0])
    after = jnp.zeros_like(states[0])
    for s in range(1, n):
        early = s <= i
        weight_b = jnp.where(early, jnp.exp(log_before), 0.0)
        weight_a = jnp.where(early, 0.0, jnp.exp(log_after))
        before = before + weight_b[:, None, None] * states[s]
        after = after + weight_a[:, None, None] * states[s]
        log_before = log_before + jnp.where(early, logs[s], 0.0)
        log_after = log_after + jnp.where(early, 0.0, logs[s])
    return log_before, before, log_after, after


def carried_state(L, S):
    rows, cols, cores = lax.axis_size("cy"), lax.axis_size("cx"), lax.axis_size("cc")
    y, x, c = lax.axis_index("cy"), lax.axis_index("cx"), lax.axis_index("cc")
    heads, size = S.shape[0], S.shape[1]
    group = heads // cores

    pair = lax.ppermute((L, S), "cc", [(0, 1), (1, 0)])
    L0 = jnp.where(c == 0, L, pair[0])
    S0 = jnp.where(c == 0, S, pair[1])
    L1 = jnp.where(c == 0, pair[0], L)
    S1 = jnp.where(c == 0, pair[1], S)
    chip_log = L0 + L1
    chip_state = jnp.exp(L1)[:, None, None] * S0 + S1
    g_log = lax.dynamic_slice_in_dim(chip_log, c * group, group, 0)
    g_state = lax.dynamic_slice_in_dim(chip_state, c * group, group, 0)

    row_pieces = shifted((g_log, g_state), "cx", cols)
    e_log, e_state, f_log, f_state = scan_pieces(
        [p[0] for p in row_pieces], [p[1] for p in row_pieces], x, cols
    )
    row_log = e_log + g_log + f_log
    row_state = jnp.exp(f_log)[:, None, None] * (jnp.exp(g_log)[:, None, None] * e_state + g_state) + f_state

    part = size // cols
    q_state = lax.dynamic_slice_in_dim(row_state, x * part, part, 1)
    col_pieces = shifted((row_log, q_state), "cy", rows)
    y_log, y_state, _, _ = scan_pieces([p[0] for p in col_pieces], [p[1] for p in col_pieces], y, rows)

    parts = shifted(y_state, "cx", cols)
    ordered = [lax.select_n((x - q) % cols, *parts) for q in range(cols)]
    y_full = jnp.concatenate(ordered, axis=1)

    chip_before = jnp.exp(e_log)[:, None, None] * y_full + e_state

    other = lax.ppermute(chip_before, "cc", [(0, 1), (1, 0)])
    full0 = jnp.concatenate([chip_before, other], axis=0)
    full1 = jnp.concatenate([other, chip_before], axis=0)
    chip_full = jnp.where(c == 0, full0, full1)
    return jnp.where(c == 0, chip_full, jnp.exp(L0)[:, None, None] * chip_full + S0)


def inner_head(qh, kh, vh, ch):
    count = qh.shape[0]
    target_index = jnp.arange(count)
    causal = target_index[:, None] >= target_index[None, :]
    scores = jnp.dot(qh, kh.T, preferred_element_type=F32)
    spread = jnp.where(causal, ch[:, None] - ch[None, :], 0.0)
    weights = (scores * jnp.where(causal, jnp.exp(spread), 0.0)).astype(jnp.bfloat16)
    return jnp.dot(weights, vh, preferred_element_type=F32)


def body(queries, keys, values, log_decay, gate, norm_gain):
    count, width = queries.shape
    heads = log_decay.shape[1]
    size = width // heads
    cum = jnp.cumsum(log_decay, axis=0)
    last = cum[-1]

    k3 = keys.reshape(count, heads, size)
    v3 = values.reshape(count, heads, size)
    q3 = queries.reshape(count, heads, size)
    keyed = k3.astype(F32) * jnp.exp(last[None, :] - cum)[:, :, None]
    state = jnp.einsum("thd,the->hde", keyed, v3.astype(F32), precision=HI)

    carried = carried_state(last, state)

    inner = jnp.stack(
        [inner_head(q3[:, h], k3[:, h], v3[:, h], cum[:, h]) for h in range(heads)], axis=1
    )
    across = jnp.einsum("thd,hde->the", q3.astype(F32), carried, precision=HI)
    attended = (inner + jnp.exp(cum)[:, :, None] * across).reshape(count, width).astype(jnp.bfloat16)

    shade = attended.astype(F32)
    sums = lax.psum(jnp.sum(shade * shade, axis=1), "head")
    columns = width * lax.axis_size("head")
    scale = lax.rsqrt(sums / columns + eps_norm)[:, None]
    gain = lax.dynamic_slice_in_dim(norm_gain, lax.axis_index("head") * width, width, 0)
    shaped = (shade * scale * gain * jax.nn.sigmoid(gate.astype(F32))).astype(jnp.bfloat16)
    return lax.all_to_all(shaped, "head", split_axis=0, concat_axis=1, tiled=True)


def solution(mesh):
    fine = split_ctx(mesh)
    ctx = ("cy", "cx", "cc")
    spec = P(ctx, "head")
    in_specs = (spec, spec, spec, spec, spec, P())
    out_specs = P((*ctx, "head"), None)
    return jax.shard_map(body, mesh=fine, in_specs=in_specs, out_specs=out_specs, check_vma=False)
```

time: 280 us -> 183 us (0.65)
  the two profiles are of different devices: /device:TPU:24 before, /device:TPU:6 now
where the time goes in v1:
time: 183 us; the launch traced here: 182 us
  starting transfers between devices  88.9 us (49%)
  blocking collectives  48.9 us (27%)
  matrix products  16.8 us (9%)
  local copies, waits for them, and re-layouts  10.5 us (6%)
  waiting for transfers between devices  10.1 us (6%)
  other arithmetic  6.55 us (4%)
    ppermute x22, starting transfers between devices, shifted(): out.append(lax.ppermute(x, axis, [(j, (j + s) % n) for j in range(n)]))  82.7 us
    all_to_all x1, blocking collectives, body(): lax.all_to_all(shaped, 'head', split_axis=0, concat_axis=1, tiled=True)  28.5 us
    psum x1, blocking collectives, body(): sums = lax.psum(jnp.sum(shade * shade, axis=1), 'head')  20.4 us
    dot_general x4, matrix products, inner_head(): return jnp.dot(weights, vh, preferred_element_type=F32)  11.3 us
    ppermute x22, waiting for transfers between devices, shifted(): out.append(lax.ppermute(x, axis, [(j, (j + s) % n) for j in range(n)]))  10.1 us
    ppermute x2, starting transfers between devices, carried_state(): pair = lax.ppermute((L, S), 'cc', [(0, 1), (1, 0)])  4.32 us
    dot_general x1, matrix products, body(): across = jnp.einsum('thd,hde->the', q3.astype(F32), carried, precision=HI)  4.25 us
    unnamed x17, local copies, waits for them, and re-layouts  4.17 us
  transfers between devices with their start and end apart: 25, of which 5 were waited for; matrix products, arithmetic and copies ran while one was open for 11% of the time, Pallas kernels for 0%

profile of v1, /device:TPU:6, one launch (start us, length us, event | category | flops | bytes accessed | tf_op | source)
XLA Modules:
  0.0 182.2 jit_solution(12873079977297989048)
XLA Ops:
  7.9 2.4 %collective-permute-start.4 = (f32[4,128,128]{2,1,0:T(8,128)S(1)}, f32[4,128,128]{2,1,0:T(8,128)}, u32[]{:S(2)}, u32[]{:S(2)}) collective-permute-start(f32[4,128,128]{2,1,0:T(8,128)S(1)} %fusion.1), channel_id=1, source_target_pairs={{0,8},{8,0},{1,9},{9,1},{2,10},{10,2},{3,11},{11,3},{4,12},{12,4},... | collective-permute-start | bytes 786440 | tf_op jit(solution)/shard_map/ppermute | solution.py:50
  12.2 3.2 %fusion.10 = f32[1024,1,128]{0,2,1:T(8,128)} fusion(f32[1024]{0:T(1024)S(1)} %bitcast.132, bf16[1024,4,128]{0,2,1:T(8,128)(2,1)S(1)} %bitcast.113, bf16[1024,4,128]{0,2,1:T(8,128)(2,1)S(1)} %bitcast.108, bf16[1024,4,128]{0,2,1:T(8,128)(2,1)} %bitcast.119), kind=kOutput, calls=%fused_computation.19 | convolution fusion | flops 543162368 | bytes 1318912 | tf_op jit(solution)/shard_map/dot_general | solution.py:92
  15.4 2.2 %fusion.11 = f32[1024,1,128]{0,2,1:T(8,128)} fusion(f32[1024]{0:T(1024)S(1)} %bitcast.131, bf16[1024,4,128]{0,2,1:T(8,128)(2,1)S(1)} %bitcast.114, bf16[1024,4,128]{0,2,1:T(8,128)(2,1)S(1)} %bitcast.109, bf16[1024,4,128]{0,2,1:T(8,128)(2,1)S(1)} %bitcast.120), kind=kOutput, calls=%fused_computation.20 | convolution fusion | flops 543162368 | bytes 1318912 | tf_op jit(solution)/shard_map/dot_general | solution.py:92
  18.2 2.7 %collective-permute-start.3 = (f32[2]{0:T(128)S(1)}, f32[2]{0:T(128)S(1)}, u32[]{:S(2)}, u32[]{:S(2)}) collective-permute-start(f32[2]{0:T(128)S(1)} %get-tuple-element.14), channel_id=1, source_target_pairs={{0,48},{16,0},{32,16},{48,32},{1,49},{17,1},{33,17},{49,33},{2,50}... | collective-permute-start | bytes 32 | tf_op jit(solution)/shard_map/ppermute | solution.py:24
  21.0 6.9 %collective-permute-start.1 = (f32[2]{0:T(128)S(1)}, f32[2]{0:T(128)S(1)}, u32[]{:S(2)}, u32[]{:S(2)}) collective-permute-start(f32[2]{0:T(128)S(1)} %get-tuple-element.14), channel_id=1, source_target_pairs={{0,16},{16,32},{32,48},{48,0},{1,17},{17,33},{33,49},{49,1},{2,18}... | collective-permute-start | bytes 32 | tf_op jit(solution)/shard_map/ppermute | solution.py:24
  27.9 3.4 %collective-permute-start.2 = (f32[2]{0:T(128)S(1)}, f32[2]{0:T(128)S(1)}, u32[]{:S(2)}, u32[]{:S(2)}) collective-permute-start(f32[2]{0:T(128)S(1)} %get-tuple-element.14), channel_id=1, source_target_pairs={{0,32},{16,48},{32,0},{48,16},{1,33},{17,49},{33,1},{49,17},{2,34}... | collective-permute-start | bytes 32 | tf_op jit(solution)/shard_map/ppermute | solution.py:24
  31.4 3.5 %collective-permute-done.2 = f32[2]{0:T(128)S(1)} collective-permute-done((f32[2]{0:T(128)S(1)}, f32[2]{0:T(128)S(1)}, u32[]{:S(2)}, u32[]{:S(2)}) %collective-permute-start.2) | collective-permute-done | bytes 40 | tf_op jit(solution)/shard_map/ppermute | solution.py:24
  35.4 1.9 %collective-permute-start.11 = (f32[2]{0:T(128)S(1)}, f32[2]{0:T(128)S(1)}, u32[]{:S(2)}, u32[]{:S(2)}) collective-permute-start(f32[2]{0:T(128)S(1)} %get-tuple-element.11), channel_id=1, source_target_pairs={{0,128},{64,192},{128,256},{192,320},{256,384},{320,448},{384,0},{... | collective-permute-start | bytes 32 | tf_op jit(solution)/shard_map/ppermute | solution.py:24
  37.3 3.4 %collective-permute-start.9 = (f32[2]{0:T(128)S(1)}, f32[2]{0:T(128)S(1)}, u32[]{:S(2)}, u32[]{:S(2)}) collective-permute-start(f32[2]{0:T(128)S(1)} %get-tuple-element.11), channel_id=1, source_target_pairs={{0,64},{64,128},{128,192},{192,256},{256,320},{320,384},{384,448},... | collective-permute-start | bytes 32 | tf_op jit(solution)/shard_map/ppermute | solution.py:24
  40.8 4.9 %collective-permute-start.13 = (f32[2]{0:T(128)S(1)}, f32[2]{0:T(128)S(1)}, u32[]{:S(2)}, u32[]{:S(2)}) collective-permute-start(f32[2]{0:T(128)S(1)} %get-tuple-element.11), channel_id=1, source_target_pairs={{0,192},{64,256},{128,320},{192,384},{256,448},{320,0},{384,64},{4... | collective-permute-start | bytes 32 | tf_op jit(solution)/shard_map/ppermute | solution.py:24
  45.7 3.9 %collective-permute-start.15 = (f32[2]{0:T(128)S(1)}, f32[2]{0:T(128)S(1)}, u32[]{:S(2)}, u32[]{:S(2)}) collective-permute-start(f32[2]{0:T(128)S(1)} %get-tuple-element.11), channel_id=1, source_target_pairs={{0,256},{64,320},{128,384},{192,448},{256,0},{320,64},{384,128},{4... | collective-permute-start | bytes 32 | tf_op jit(solution)/shard_map/ppermute | solution.py:24
  50.7 3.9 %collective-permute-start.5 = (f32[2,128,128]{2,1,0:T(8,128)S(1)}, f32[2,128,128]{2,1,0:T(8,128)S(1)}, u32[]{:S(2)}, u32[]{:S(2)}) collective-permute-start(f32[2,128,128]{2,1,0:T(8,128)S(1)} %fusion.17), channel_id=1, source_target_pairs={{0,16},{16,32},{32,48},{48,0},{1,17},{17,33},{33,49},{49,1},{2,18}... | collective-permute-start | bytes 393224 | tf_op jit(solution)/shard_map/ppermute | solution.py:24
  56.6 2.8 %collective-permute-start.7 = (f32[2,128,128]{2,1,0:T(8,128)S(1)}, f32[2,128,128]{2,1,0:T(8,128)S(1)}, u32[]{:S(2)}, u32[]{:S(2)}) collective-permute-start(f32[2,128,128]{2,1,0:T(8,128)S(1)} %fusion.17), channel_id=1, source_target_pairs={{0,48},{16,0},{32,16},{48,32},{1,49},{17,1},{33,17},{49,33},{2,50}... | collective-permute-start | bytes 393224 | tf_op jit(solution)/shard_map/ppermute | solution.py:24
  59.8 3.9 %collective-permute-start.17 = (f32[2]{0:T(128)S(1)}, f32[2]{0:T(128)S(1)}, u32[]{:S(2)}, u32[]{:S(2)}) collective-permute-start(f32[2]{0:T(128)S(1)} %get-tuple-element.11), channel_id=1, source_target_pairs={{0,320},{64,384},{128,448},{192,0},{256,64},{320,128},{384,192},{4... | collective-permute-start | bytes 32 | tf_op jit(solution)/shard_map/ppermute | solution.py:24
  64.3 5.7 %collective-permute-start.19 = (f32[2]{0:T(128)S(1)}, f32[2]{0:T(128)S(1)}, u32[]{:S(2)}, u32[]{:S(2)}) collective-permute-start(f32[2]{0:T(128)S(1)} %get-tuple-element.11), channel_id=1, source_target_pairs={{0,384},{64,448},{128,0},{192,64},{256,128},{320,192},{384,256},{4... | collective-permute-start | bytes 32 | tf_op jit(solution)/shard_map/ppermute | solution.py:24
  72.2 3.5 %collective-permute-start.12 = (f32[2,32,128]{2,1,0:T(8,128)S(1)}, f32[2,32,128]{2,1,0:T(8,128)S(1)}, u32[]{:S(2)}, u32[]{:S(2)}) collective-permute-start(f32[2,32,128]{2,1,0:T(8,128)S(1)} %fusion.22), channel_id=1, source_target_pairs={{0,192},{64,256},{128,320},{192,384},{256,448},{320,0},{384,64},{4... | collective-permute-start | bytes 98312 | tf_op jit(solution)/shard_map/ppermute | solution.py:24
  75.7 6.5 %collective-permute-start.14 = (f32[2,32,128]{2,1,0:T(8,128)S(1)}, f32[2,32,128]{2,1,0:T(8,128)S(1)}, u32[]{:S(2)}, u32[]{:S(2)}) collective-permute-start(f32[2,32,128]{2,1,0:T(8,128)S(1)} %fusion.22), channel_id=1, source_target_pairs={{0,256},{64,320},{128,384},{192,448},{256,0},{320,64},{384,128},{4... | collective-permute-start | bytes 98312 | tf_op jit(solution)/shard_map/ppermute | solution.py:24
  82.2 3.1 %collective-permute-start.16 = (f32[2,32,128]{2,1,0:T(8,128)S(1)}, f32[2,32,128]{2,1,0:T(8,128)S(1)}, u32[]{:S(2)}, u32[]{:S(2)}) collective-permute-start(f32[2,32,128]{2,1,0:T(8,128)S(1)} %fusion.22), channel_id=1, source_target_pairs={{0,320},{64,384},{128,448},{192,0},{256,64},{320,128},{384,192},{4... | collective-permute-start | bytes 98312 | tf_op jit(solution)/shard_map/ppermute | solution.py:24
  85.4 5.9 %collective-permute-start.18 = (f32[2,32,128]{2,1,0:T(8,128)S(1)}, f32[2,32,128]{2,1,0:T(8,128)S(1)}, u32[]{:S(2)}, u32[]{:S(2)}) collective-permute-start(f32[2,32,128]{2,1,0:T(8,128)S(1)} %fusion.22), channel_id=1, source_target_pairs={{0,384},{64,448},{128,0},{192,64},{256,128},{320,192},{384,256},{4... | collective-permute-start | bytes 98312 | tf_op jit(solution)/shard_map/ppermute | solution.py:24
  91.3 2.3 %collective-permute-start.20 = (f32[2,32,128]{2,1,0:T(8,128)S(1)}, f32[2,32,128]{2,1,0:T(8,128)S(1)}, u32[]{:S(2)}, u32[]{:S(2)}) collective-permute-start(f32[2,32,128]{2,1,0:T(8,128)S(1)} %fusion.22), channel_id=1, source_target_pairs={{0,448},{64,0},{128,64},{192,128},{256,192},{320,256},{384,320},{4... | collective-permute-start | bytes 98312 | tf_op jit(solution)/shard_map/ppermute | solution.py:24
  93.6 3.5 %collective-permute-start.8 = (f32[2,32,128]{2,1,0:T(8,128)S(1)}, f32[2,32,128]{2,1,0:T(8,128)S(1)}, u32[]{:S(2)}, u32[]{:S(2)}) collective-permute-start(f32[2,32,128]{2,1,0:T(8,128)S(1)} %fusion.22), channel_id=1, source_target_pairs={{0,64},{64,128},{128,192},{192,256},{256,320},{320,384},{384,448},... | collective-permute-start | bytes 98312 | tf_op jit(solution)/shard_map/ppermute | solution.py:24
  97.2 3.4 %collective-permute-done.8 = f32[2,32,128]{2,1,0:T(8,128)S(1)} collective-permute-done((f32[2,32,128]{2,1,0:T(8,128)S(1)}, f32[2,32,128]{2,1,0:T(8,128)S(1)}, u32[]{:S(2)}, u32[]{:S(2)}) %collective-permute-start.8) | collective-permute-done | bytes 32800 | tf_op jit(solution)/shard_map/ppermute | solution.py:24
  100.7 5.8 %collective-permute-start.21 = (f32[2,32,128]{2,1,0:T(8,128)S(1)}, f32[2,32,128]{2,1,0:T(8,128)S(1)}, u32[]{:S(2)}, u32[]{:S(2)}) collective-permute-start(f32[2,32,128]{2,1,0:T(8,128)S(1)} %multiply_add_fusion.1), channel_id=1, source_target_pairs={{0,16},{16,32},{32,48},{48,0},{1,17},{17,33},{33,49},{49,1},{2,18}... | collective-permute-start | bytes 98312 | tf_op jit(solution)/shard_map/ppermute | solution.py:24
  106.5 2.7 %collective-permute-start.22 = (f32[2,32,128]{2,1,0:T(8,128)S(1)}, f32[2,32,128]{2,1,0:T(8,128)S(1)}, u32[]{:S(2)}, u32[]{:S(2)}) collective-permute-start(f32[2,32,128]{2,1,0:T(8,128)S(1)} %multiply_add_fusion.1), channel_id=1, source_target_pairs={{0,32},{16,48},{32,0},{48,16},{1,33},{17,49},{33,1},{49,17},{2,34}... | collective-permute-start | bytes 98312 | tf_op jit(solution)/shard_map/ppermute | solution.py:24
  109.3 2.0 %collective-permute-start.23 = (f32[2,32,128]{2,1,0:T(8,128)S(1)}, f32[2,32,128]{2,1,0:T(8,128)S(1)}, u32[]{:S(2)}, u32[]{:S(2)}) collective-permute-start(f32[2,32,128]{2,1,0:T(8,128)S(1)} %multiply_add_fusion.1), channel_id=1, source_target_pairs={{0,48},{16,0},{32,16},{48,32},{1,49},{17,1},{33,17},{49,33},{2,50}... | collective-permute-start | bytes 98312 | tf_op jit(solution)/shard_map/ppermute | solution.py:24
  111.2 2.9 %fusion.12 = f32[1024,1,128]{0,2,1:T(8,128)} fusion(f32[1024]{0:T(1024)} %bitcast.130, bf16[1024,4,128]{0,2,1:T(8,128)(2,1)S(1)} %bitcast.115, bf16[1024,4,128]{0,2,1:T(8,128)(2,1)S(1)} %bitcast.110, bf16[1024,4,128]{0,2,1:T(8,128)(2,1)S(1)} %bitcast.121), kind=kOutput, calls=%fused_computation.21 | convolution fusion | flops 543162368 | bytes 1318912 | tf_op jit(solution)/shard_map/dot_general | solution.py:92
  114.2 2.1 %collective-permute-done.23 = f32[2,32,128]{2,1,0:T(8,128)S(1)} collective-permute-done((f32[2,32,128]{2,1,0:T(8,128)S(1)}, f32[2,32,128]{2,1,0:T(8,128)S(1)}, u32[]{:S(2)}, u32[]{:S(2)}) %collective-permute-start.23) | collective-permute-done | bytes 32800 | tf_op jit(solution)/shard_map/ppermute | solution.py:24
  117.1 1.9 %collective-permute-start.24 = (f32[2,128,128]{2,1,0:T(8,128)S(1)}, f32[2,128,128]{2,1,0:T(8,128)}, u32[]{:S(2)}, u32[]{:S(2)}) collective-permute-start(f32[2,128,128]{2,1,0:T(8,128)S(1)} %fusion.18), channel_id=1, source_target_pairs={{0,8},{8,0},{1,9},{9,1},{2,10},{10,2},{3,11},{11,3},{4,12},{12,4},... | collective-permute-start | bytes 393224 | tf_op jit(solution)/shard_map/ppermute | solution.py:78
  119.0 2.9 %fusion.9 = f32[1024,1,128]{0,2,1:T(8,128)} fusion(f32[1024]{0:T(1024)} %bitcast.129, bf16[1024,4,128]{0,2,1:T(8,128)(2,1)S(1)} %bitcast.116, bf16[1024,4,128]{0,2,1:T(8,128)(2,1)S(1)} %bitcast.111, bf16[1024,4,128]{0,2,1:T(8,128)(2,1)S(1)} %bitcast.122), kind=kOutput, calls=%fused_computation.18 | convolution fusion | flops 543162368 | bytes 1318912 | tf_op jit(solution)/shard_map/dot_general | solution.py:92
  123.3 4.3 %multiply_reduce_fusion = (f32[1024]{0:T(1024)S(1)}, f32[1024,4,128]{0,2,1:T(8,128)}) fusion(bf16[1024,4,128]{0,2,1:T(8,128)(2,1)S(1)} %bitcast.123, f32[4,128,128]{2,1,0:T(8,128)S(1)} %copy-done.4, f32[2,128,128]{2,1,0:T(8,128)S(1)} %fusion.18, f32[2,128,128]{2,1,0:T(8,128)} %collective-permute-done.24, f32[4]{0:T(128)} %get-tuple-element.25, pred[]{:T(512)S(6)} %eq.7, ...), kind=kOutput, calls=%fused_computation.9 | convolution fusion | flops 810417152 | bytes 5787665 | tf_op jit(solution)/shard_map/thd,hde->the/dot_general | solution.py:113
  129.5 20.4 %psum.7 = f32[1024]{0:T(1024)S(1)} all-reduce(f32[1024]{0:T(1024)S(1)} %get-tuple-element.37), channel_id=1, replica_groups=mesh['cy'=8,'cx'=4,'cc'=2,'head'=8] {'head'}, use_global_device_ids=true, to_apply=%region_3.4 | all-reduce | flops 1024 | bytes 8192 | tf_op jit(solution)/shard_map/psum | solution.py:117
  151.7 28.5 %all_to_all.19 = bf16[8,128,512]{2,1,0:T(8,128)(2,1)S(1)} all-to-all(bf16[8,128,512]{2,1,0:T(8,128)(2,1)S(1)} %bitcast.106), channel_id=1, replica_groups=mesh['cy'=8,'cx'=4,'cc'=2,'head'=8] {'head'}, dimensions={0} | all-to-all | bytes 2097152 | tf_op jit(solution)/shard_map/all_to_all | solution.py:122
  (72 shorter events, 25.1 us)
Async XLA Ops:
  0.0 6.1 %copy-start = (bf16[1024,512]{1,0:T(8,128)(2,1)S(1)}, bf16[1024,512]{1,0:T(8,128)(2,1)}, u32[]{:S(2)}) copy-start(bf16[1024,512]{1,0:T(8,128)(2,1)} %param.8) | copy-start | bytes 3145732
  2.6 15.1 %collective-permute-start = (f32[4]{0:T(128)S(1)}, f32[4]{0:T(128)S(1)}, u32[]{:S(2)}, u32[]{:S(2)}) collective-permute-start(f32[4]{0:T(128)S(1)} %slice_reduce_fusion.1), channel_id=1, source_target_pairs={{0,8},{8,0},{1,9},{9,1},{2,10},{10,2},{3,11},{11,3},{4,12},{12,4},... | collective-permute-start | bytes 56 | tf_op jit(solution)/shard_map/ppermute | solution.py:50
  6.6 4.3 %copy-start.1 = (bf16[1024,512]{1,0:T(8,128)(2,1)S(1)}, bf16[1024,512]{1,0:T(8,128)(2,1)}, u32[]{:S(2)}) copy-start(bf16[1024,512]{1,0:T(8,128)(2,1)} %param.6) | copy-start | bytes 3145732
  7.9 41.7 %collective-permute-start.4 = (f32[4,128,128]{2,1,0:T(8,128)S(1)}, f32[4,128,128]{2,1,0:T(8,128)}, u32[]{:S(2)}, u32[]{:S(2)}) collective-permute-start(f32[4,128,128]{2,1,0:T(8,128)S(1)} %fusion.1), channel_id=1, source_target_pairs={{0,8},{8,0},{1,9},{9,1},{2,10},{10,2},{3,11},{11,3},{4,12},{12,4},... | collective-permute-start | bytes 786440 | tf_op jit(solution)/shard_map/ppermute | solution.py:50
  12.2 3.2 %copy-start.2 = (bf16[1024,512]{0,1:T(8,128)(2,1)S(1)}, bf16[1024,512]{0,1:T(8,128)(2,1)}, u32[]{:S(2)}) copy-start(bf16[1024,512]{0,1:T(8,128)(2,1)} %copy.113) | copy-start | bytes 3145732
  18.2 13.2 %collective-permute-start.3 = (f32[2]{0:T(128)S(1)}, f32[2]{0:T(128)S(1)}, u32[]{:S(2)}, u32[]{:S(2)}) collective-permute-start(f32[2]{0:T(128)S(1)} %get-tuple-element.14), channel_id=1, source_target_pairs={{0,48},{16,0},{32,16},{48,32},{1,49},{17,1},{33,17},{49,33},{2,50}... | collective-permute-start | bytes 32 | tf_op jit(solution)/shard_map/ppermute | solution.py:24
  21.0 10.4 %collective-permute-start.1 = (f32[2]{0:T(128)S(1)}, f32[2]{0:T(128)S(1)}, u32[]{:S(2)}, u32[]{:S(2)}) collective-permute-start(f32[2]{0:T(128)S(1)} %get-tuple-element.14), channel_id=1, source_target_pairs={{0,16},{16,32},{32,48},{48,0},{1,17},{17,33},{33,49},{49,1},{2,18}... | collective-permute-start | bytes 32 | tf_op jit(solution)/shard_map/ppermute | solution.py:24
  27.9 6.9 %collective-permute-start.2 = (f32[2]{0:T(128)S(1)}, f32[2]{0:T(128)S(1)}, u32[]{:S(2)}, u32[]{:S(2)}) collective-permute-start(f32[2]{0:T(128)S(1)} %get-tuple-element.14), channel_id=1, source_target_pairs={{0,32},{16,48},{32,0},{48,16},{1,33},{17,49},{33,1},{49,17},{2,34}... | collective-permute-start | bytes 32 | tf_op jit(solution)/shard_map/ppermute | solution.py:24
  35.4 19.3 %collective-permute-start.11 = (f32[2]{0:T(128)S(1)}, f32[2]{0:T(128)S(1)}, u32[]{:S(2)}, u32[]{:S(2)}) collective-permute-start(f32[2]{0:T(128)S(1)} %get-tuple-element.11), channel_id=1, source_target_pairs={{0,128},{64,192},{128,256},{192,320},{256,384},{320,448},{384,0},{... | collective-permute-start | bytes 32 | tf_op jit(solution)/shard_map/ppermute | solution.py:24
  37.3 19.3 %collective-permute-start.9 = (f32[2]{0:T(128)S(1)}, f32[2]{0:T(128)S(1)}, u32[]{:S(2)}, u32[]{:S(2)}) collective-permute-start(f32[2]{0:T(128)S(1)} %get-tuple-element.11), channel_id=1, source_target_pairs={{0,64},{64,128},{128,192},{192,256},{256,320},{320,384},{384,448},... | collective-permute-start | bytes 32 | tf_op jit(solution)/shard_map/ppermute | solution.py:24
  40.8 31.4 %collective-permute-start.13 = (f32[2]{0:T(128)S(1)}, f32[2]{0:T(128)S(1)}, u32[]{:S(2)}, u32[]{:S(2)}) collective-permute-start(f32[2]{0:T(128)S(1)} %get-tuple-element.11), channel_id=1, source_target_pairs={{0,192},{64,256},{128,320},{192,384},{256,448},{320,0},{384,64},{4... | collective-permute-start | bytes 32 | tf_op jit(solution)/shard_map/ppermute | solution.py:24
  45.7 30.0 %collective-permute-start.15 = (f32[2]{0:T(128)S(1)}, f32[2]{0:T(128)S(1)}, u32[]{:S(2)}, u32[]{:S(2)}) collective-permute-start(f32[2]{0:T(128)S(1)} %get-tuple-element.11), channel_id=1, source_target_pairs={{0,256},{64,320},{128,384},{192,448},{256,0},{320,64},{384,128},{4... | collective-permute-start | bytes 32 | tf_op jit(solution)/shard_map/ppermute | solution.py:24
  49.6 20.4 %copy-start.3 = (f32[4,128,128]{2,1,0:T(8,128)}, f32[4,128,128]{2,1,0:T(8,128)S(1)}, u32[]{:S(2)}) copy-start(f32[4,128,128]{2,1,0:T(8,128)S(1)} %broadcast_select_fusion) | copy-start | bytes 786436
  50.7 9.1 %collective-permute-start.5 = (f32[2,128,128]{2,1,0:T(8,128)S(1)}, f32[2,128,128]{2,1,0:T(8,128)S(1)}, u32[]{:S(2)}, u32[]{:S(2)}) collective-permute-start(f32[2,128,128]{2,1,0:T(8,128)S(1)} %fusion.17), channel_id=1, source_target_pairs={{0,16},{16,32},{32,48},{48,0},{1,17},{17,33},{33,49},{49,1},{2,18}... | collective-permute-start | bytes 393224 | tf_op jit(solution)/shard_map/ppermute | solution.py:24
  54.7 9.6 %collective-permute-start.6 = (f32[2,128,128]{2,1,0:T(8,128)S(1)}, f32[2,128,128]{2,1,0:T(8,128)S(1)}, u32[]{:S(2)}, u32[]{:S(2)}) collective-permute-start(f32[2,128,128]{2,1,0:T(8,128)S(1)} %fusion.17), channel_id=1, source_target_pairs={{0,32},{16,48},{32,0},{48,16},{1,33},{17,49},{33,1},{49,17},{2,34}... | collective-permute-start | bytes 393224 | tf_op jit(solution)/shard_map/ppermute | solution.py:24
  56.6 13.4 %collective-permute-start.7 = (f32[2,128,128]{2,1,0:T(8,128)S(1)}, f32[2,128,128]{2,1,0:T(8,128)S(1)}, u32[]{:S(2)}, u32[]{:S(2)}) collective-permute-start(f32[2,128,128]{2,1,0:T(8,128)S(1)} %fusion.17), channel_id=1, source_target_pairs={{0,48},{16,0},{32,16},{48,32},{1,49},{17,1},{33,17},{49,33},{2,50}... | collective-permute-start | bytes 393224 | tf_op jit(solution)/shard_map/ppermute | solution.py:24
  59.8 22.4 %collective-permute-start.17 = (f32[2]{0:T(128)S(1)}, f32[2]{0:T(128)S(1)}, u32[]{:S(2)}, u32[]{:S(2)}) collective-permute-start(f32[2]{0:T(128)S(1)} %get-tuple-element.11), channel_id=1, source_target_pairs={{0,320},{64,384},{128,448},{192,0},{256,64},{320,128},{384,192},{4... | collective-permute-start | bytes 32 | tf_op jit(solution)/shard_map/ppermute | solution.py:24
  64.3 21.1 %collective-permute-start.19 = (f32[2]{0:T(128)S(1)}, f32[2]{0:T(128)S(1)}, u32[]{:S(2)}, u32[]{:S(2)}) collective-permute-start(f32[2]{0:T(128)S(1)} %get-tuple-element.11), channel_id=1, source_target_pairs={{0,384},{64,448},{128,0},{192,64},{256,128},{320,192},{384,256},{4... | collective-permute-start | bytes 32 | tf_op jit(solution)/shard_map/ppermute | solution.py:24
  70.2 21.1 %collective-permute-start.10 = (f32[2,32,128]{2,1,0:T(8,128)S(1)}, f32[2,32,128]{2,1,0:T(8,128)S(1)}, u32[]{:S(2)}, u32[]{:S(2)}) collective-permute-start(f32[2,32,128]{2,1,0:T(8,128)S(1)} %fusion.22), channel_id=1, source_target_pairs={{0,128},{64,192},{128,256},{192,320},{256,384},{320,448},{384,0},{... | collective-permute-start | bytes 98312 | tf_op jit(solution)/shard_map/ppermute | solution.py:24
  72.2 21.5 %collective-permute-start.12 = (f32[2,32,128]{2,1,0:T(8,128)S(1)}, f32[2,32,128]{2,1,0:T(8,128)S(1)}, u32[]{:S(2)}, u32[]{:S(2)}) collective-permute-start(f32[2,32,128]{2,1,0:T(8,128)S(1)} %fusion.22), channel_id=1, source_target_pairs={{0,192},{64,256},{128,320},{192,384},{256,448},{320,0},{384,64},{4... | collective-permute-start | bytes 98312 | tf_op jit(solution)/shard_map/ppermute | solution.py:24
  75.7 21.5 %collective-permute-start.14 = (f32[2,32,128]{2,1,0:T(8,128)S(1)}, f32[2,32,128]{2,1,0:T(8,128)S(1)}, u32[]{:S(2)}, u32[]{:S(2)}) collective-permute-start(f32[2,32,128]{2,1,0:T(8,128)S(1)} %fusion.22), channel_id=1, source_target_pairs={{0,256},{64,320},{128,384},{192,448},{256,0},{320,64},{384,128},{4... | collective-permute-start | bytes 98312 | tf_op jit(solution)/shard_map/ppermute | solution.py:24
  82.2 14.9 %collective-permute-start.16 = (f32[2,32,128]{2,1,0:T(8,128)S(1)}, f32[2,32,128]{2,1,0:T(8,128)S(1)}, u32[]{:S(2)}, u32[]{:S(2)}) collective-permute-start(f32[2,32,128]{2,1,0:T(8,128)S(1)} %fusion.22), channel_id=1, source_target_pairs={{0,320},{64,384},{128,448},{192,0},{256,64},{320,128},{384,192},{4... | collective-permute-start | bytes 98312 | tf_op jit(solution)/shard_map/ppermute | solution.py:24
  85.4 11.8 %collective-permute-start.18 = (f32[2,32,128]{2,1,0:T(8,128)S(1)}, f32[2,32,128]{2,1,0:T(8,128)S(1)}, u32[]{:S(2)}, u32[]{:S(2)}) collective-permute-start(f32[2,32,128]{2,1,0:T(8,128)S(1)} %fusion.22), channel_id=1, source_target_pairs={{0,384},{64,448},{128,0},{192,64},{256,128},{320,192},{384,256},{4... | collective-permute-start | bytes 98312 | tf_op jit(solution)/shard_map/ppermute | solution.py:24
  91.3 5.9 %collective-permute-start.20 = (f32[2,32,128]{2,1,0:T(8,128)S(1)}, f32[2,32,128]{2,1,0:T(8,128)S(1)}, u32[]{:S(2)}, u32[]{:S(2)}) collective-permute-start(f32[2,32,128]{2,1,0:T(8,128)S(1)} %fusion.22), channel_id=1, source_target_pairs={{0,448},{64,0},{128,64},{192,128},{256,192},{320,256},{384,320},{4... | collective-permute-start | bytes 98312 | tf_op jit(solution)/shard_map/ppermute | solution.py:24
  93.6 7.0 %collective-permute-start.8 = (f32[2,32,128]{2,1,0:T(8,128)S(1)}, f32[2,32,128]{2,1,0:T(8,128)S(1)}, u32[]{:S(2)}, u32[]{:S(2)}) collective-permute-start(f32[2,32,128]{2,1,0:T(8,128)S(1)} %fusion.22), channel_id=1, source_target_pairs={{0,64},{64,128},{128,192},{192,256},{256,320},{320,384},{384,448},... | collective-permute-start | bytes 98312 | tf_op jit(solution)/shard_map/ppermute | solution.py:24
  100.7 13.4 %collective-permute-start.21 = (f32[2,32,128]{2,1,0:T(8,128)S(1)}, f32[2,32,128]{2,1,0:T(8,128)S(1)}, u32[]{:S(2)}, u32[]{:S(2)}) collective-permute-start(f32[2,32,128]{2,1,0:T(8,128)S(1)} %multiply_add_fusion.1), channel_id=1, source_target_pairs={{0,16},{16,32},{32,48},{48,0},{1,17},{17,33},{33,49},{49,1},{2,18}... | collective-permute-start | bytes 98312 | tf_op jit(solution)/shard_map/ppermute | solution.py:24
  106.5 7.6 %collective-permute-start.22 = (f32[2,32,128]{2,1,0:T(8,128)S(1)}, f32[2,32,128]{2,1,0:T(8,128)S(1)}, u32[]{:S(2)}, u32[]{:S(2)}) collective-permute-start(f32[2,32,128]{2,1,0:T(8,128)S(1)} %multiply_add_fusion.1), channel_id=1, source_target_pairs={{0,32},{16,48},{32,0},{48,16},{1,33},{17,49},{33,1},{49,17},{2,34}... | collective-permute-start | bytes 98312 | tf_op jit(solution)/shard_map/ppermute | solution.py:24
  109.3 7.0 %collective-permute-start.23 = (f32[2,32,128]{2,1,0:T(8,128)S(1)}, f32[2,32,128]{2,1,0:T(8,128)S(1)}, u32[]{:S(2)}, u32[]{:S(2)}) collective-permute-start(f32[2,32,128]{2,1,0:T(8,128)S(1)} %multiply_add_fusion.1), channel_id=1, source_target_pairs={{0,48},{16,0},{32,16},{48,32},{1,49},{17,1},{33,17},{49,33},{2,50}... | collective-permute-start | bytes 98312 | tf_op jit(solution)/shard_map/ppermute | solution.py:24
  117.1 6.2 %collective-permute-start.24 = (f32[2,128,128]{2,1,0:T(8,128)S(1)}, f32[2,128,128]{2,1,0:T(8,128)}, u32[]{:S(2)}, u32[]{:S(2)}) collective-permute-start(f32[2,128,128]{2,1,0:T(8,128)S(1)} %fusion.18), channel_id=1, source_target_pairs={{0,8},{8,0},{1,9},{9,1},{2,10},{10,2},{3,11},{11,3},{4,12},{12,4},... | collective-permute-start | bytes 393224 | tf_op jit(solution)/shard_map/ppermute | solution.py:78
  119.0 4.3 %copy-start.4 = (f32[4,128,128]{2,1,0:T(8,128)S(1)}, f32[4,128,128]{2,1,0:T(8,128)}, u32[]{:S(2)}) copy-start(f32[4,128,128]{2,1,0:T(8,128)} %copy-done.3) | copy-start | bytes 786436
  127.5 22.3 %copy-start.5 = (f32[512]{0:T(512)S(1)}, f32[512]{0:T(512)}, u32[]{:S(2)}) copy-start(f32[512]{0:T(512)} %dynamic_slice.15) | copy-start | bytes 6148

commit v2 on v1

--- a/solution.py
+++ b/solution.py
@@ -16,6 +16,15 @@
     cores = len(ctx_devices) // (rows * cols)
     shape = (rows, cols, cores, devices.shape[1])
     return Mesh(devices.reshape(shape), ("cy", "cx", "cc", "head"))
+
+
+def pack(log, state):
+    row = jnp.broadcast_to(log[:, None, None], (state.shape[0], 1, state.shape[2]))
+    return jnp.concatenate([state, row], axis=1)
+
+
+def unpack(packed):
+    return packed[:, -1, 0], packed[:, :-1]
 
 
 def shifted(x, axis, n):
@@ -47,7 +56,7 @@
     heads, size = S.shape[0], S.shape[1]
     group = heads // cores
 
-    pair = lax.ppermute((L, S), "cc", [(0, 1), (1, 0)])
+    pair = unpack(lax.ppermute(pack(L, S), "cc", [(0, 1), (1, 0)]))
     L0 = jnp.where(c == 0, L, pair[0])
     S0 = jnp.where(c == 0, S, pair[1])
     L1 = jnp.where(c == 0, pair[0], L)
@@ -57,7 +66,7 @@
     g_log = lax.dynamic_slice_in_dim(chip_log, c * group, group, 0)
     g_state = lax.dynamic_slice_in_dim(chip_state, c * group, group, 0)
 
-    row_pieces = shifted((g_log, g_state), "cx", cols)
+    row_pieces = [unpack(p) for p in shifted(pack(g_log, g_state), "cx", cols)]
     e_log, e_state, f_log, f_state = scan_pieces(
         [p[0] for p in row_pieces], [p[1] for p in row_pieces], x, cols
     )
@@ -66,7 +75,7 @@
 
     part = size // cols
     q_state = lax.dynamic_slice_in_dim(row_state, x * part, part, 1)
-    col_pieces = shifted((row_log, q_state), "cy", rows)
+    col_pieces = [unpack(p) for p in shifted(pack(row_log, q_state), "cy", rows)]
     y_log, y_state, _, _ = scan_pieces([p[0] for p in col_pieces], [p[1] for p in col_pieces], y, rows)
 
     parts = shifted(y_state, "cx", cols)
@@ -113,13 +122,24 @@
     across = jnp.einsum("thd,hde->the", q3.astype(F32), carried, precision=HI)
     attended = (inner + jnp.exp(cum)[:, :, None] * across).reshape(count, width).astype(jnp.bfloat16)
 
+    groups = lax.axis_size("head")
     shade = attended.astype(F32)
-    sums = lax.psum(jnp.sum(shade * shade, axis=1), "head")
-    columns = width * lax.axis_size("head")
-    scale = lax.rsqrt(sums / columns + eps_norm)[:, None]
+    sums = jnp.sum(shade * shade, axis=1)
     gain = lax.dynamic_slice_in_dim(norm_gain, lax.axis_index("head") * width, width, 0)
-    shaped = (shade * scale * gain * jax.nn.sigmoid(gate.astype(F32))).astype(jnp.bfloat16)
-    return lax.all_to_all(shaped, "head", split_axis=0, concat_axis=1, tiled=True)
+    shaped = (shade * gain * jax.nn.sigmoid(gate.astype(F32))).astype(jnp.bfloat16)
+    chunk = count // groups
+    high = sums.astype(jnp.bfloat16)
+    low = (sums - high.astype(F32)).astype(jnp.bfloat16)
+    extra = jnp.zeros((groups, 1, width), jnp.bfloat16)
+    extra = extra.at[:, 0, :chunk].set(high.reshape(groups, chunk))
+    extra = extra.at[:, 0, chunk : 2 * chunk].set(low.reshape(groups, chunk))
+    payload = jnp.concatenate([shaped.reshape(groups, chunk, width), extra], axis=1)
+    got = lax.all_to_all(payload, "head", split_axis=0, concat_axis=0, tiled=True)
+    parts = got[:, -1, :].astype(F32)
+    total = jnp.sum(parts[:, :chunk] + parts[:, chunk : 2 * chunk], axis=0)
+    scale = lax.rsqrt(total / (width * groups) + eps_norm)
+    rows_out = got[:, :chunk, :].astype(F32) * scale[None, :, None]
+    return rows_out.transpose(1, 0, 2).reshape(chunk, width * groups).astype(jnp.bfloat16)
 
 
 def solution(mesh):

time: 183 us -> 146 us (0.80)
  the two profiles are of different devices: /device:TPU:6 before, /device:TPU:1 now
where the time goes in v2:
time: 146 us; the launch traced here: 145 us
  starting transfers between devices  57 us (39%)
  blocking collectives  40.5 us (28%)
  matrix products  16.8 us (12%)
  local copies, waits for them, and re-layouts  13 us (9%)
  other arithmetic  12.1 us (8%)
  waiting for transfers between devices  5.09 us (3%)
    ppermute x13, starting transfers between devices, shifted(): out.append(lax.ppermute(x, axis, [(j, (j + s) % n) for j in range(n)]))  41.6 us
    all_to_all x1, blocking collectives, body(): lax.all_to_all(payload, 'head', split_axis=0, concat_axis=0, tiled=True)  40.5 us
    dot_general x4, matrix products, inner_head(): return jnp.dot(weights, vh, preferred_element_type=F32)  11.3 us
    ppermute x1, starting transfers between devices, carried_state(): pair = unpack(lax.ppermute(pack(L, S), 'cc', [(0, 1), (1, 0)]))  8.77 us
    ppermute x1, starting transfers between devices, carried_state(): other = lax.ppermute(chip_before, 'cc', [(0, 1), (1, 0)])  6.68 us
    unnamed x29, local copies, waits for them, and re-layouts  5.46 us
    ppermute x13, waiting for transfers between devices, shifted(): out.append(lax.ppermute(x, axis, [(j, (j + s) % n) for j in range(n)]))  5.08 us
    dot_general x1, matrix products, body(): across = jnp.einsum('thd,hde->the', q3.astype(F32), carried, precision=HI)  4.23 us
  transfers between devices with their start and end apart: 15, of which 4 were waited for; matrix products, arithmetic and copies ran while one was open for 11% of the time, Pallas kernels for 0%

profile of v2, /device:TPU:1, one launch (start us, length us, event | category | flops | bytes accessed | tf_op | source)
XLA Modules:
  0.0 144.9 jit_solution(3552930513571655208)
XLA Ops:
  0.8 1.1 reduce-window.6
  2.6 1.5 %copy.127 = bf16[1024,512]{0,1:T(8,128)(2,1)S(1)} copy(bf16[1024,512]{1,0:T(8,128)(2,1)} %param.11) | data formatting | bytes 2097152 | tf_op args[1]
  4.7 1.2 fusion.1
  6.7 8.8 %collective-permute-start = (f32[4,129,128]{2,1,0:T(8,128)}, f32[4,129,128]{2,1,0:T(8,128)}, u32[]{:S(2)}, u32[]{:S(2)}) collective-permute-start(f32[4,129,128]{2,1,0:T(8,128)} %pad_maximum_fusion.1), channel_id=1, source_target_pairs={{0,8},{8,0},{1,9},{9,1},{2,10},{10,2},{3,11},{11,3},{4,12},{12,4},... | collective-permute-start | bytes 792584 | tf_op jit(solution)/shard_map/ppermute | solution.py:59
  16.1 1.3 copy.125
  17.4 3.2 %fusion.10 = f32[1024,1,128]{0,2,1:T(8,128)} fusion(f32[1024]{0:T(1024)S(1)} %bitcast.143, bf16[1024,4,128]{0,2,1:T(8,128)(2,1)S(1)} %bitcast.119, bf16[1024,4,128]{0,2,1:T(8,128)(2,1)S(1)} %bitcast.114, bf16[1024,4,128]{0,2,1:T(8,128)(2,1)} %bitcast.126), kind=kOutput, calls=%fused_computation.20 | convolution fusion | flops 543162368 | bytes 1318912 | tf_op jit(solution)/shard_map/dot_general | solution.py:101
  20.7 1.4 fusion.34
  24.5 1.9 %collective-permute-start.1 = (f32[2,129,128]{2,1,0:T(8,128)S(1)}, f32[2,129,128]{2,1,0:T(8,128)}, u32[]{:S(2)}, u32[]{:S(2)}) collective-permute-start(f32[2,129,128]{2,1,0:T(8,128)S(1)} %pad_maximum_fusion.2), channel_id=1, source_target_pairs={{0,16},{16,32},{32,48},{48,0},{1,17},{17,33},{33,49},{49,1},{2,18}... | collective-permute-start | bytes 396296 | tf_op jit(solution)/shard_map/ppermute | solution.py:33
  26.4 1.9 %collective-permute-start.2 = (f32[2,129,128]{2,1,0:T(8,128)S(1)}, f32[2,129,128]{2,1,0:T(8,128)}, u32[]{:S(2)}, u32[]{:S(2)}) collective-permute-start(f32[2,129,128]{2,1,0:T(8,128)S(1)} %pad_maximum_fusion.2), channel_id=1, source_target_pairs={{0,32},{16,48},{32,0},{48,16},{1,33},{17,49},{33,1},{49,17},{2,34}... | collective-permute-start | bytes 396296 | tf_op jit(solution)/shard_map/ppermute | solution.py:33
  28.4 4.6 %collective-permute-start.3 = (f32[2,129,128]{2,1,0:T(8,128)S(1)}, f32[2,129,128]{2,1,0:T(8,128)}, u32[]{:S(2)}, u32[]{:S(2)}) collective-permute-start(f32[2,129,128]{2,1,0:T(8,128)S(1)} %pad_maximum_fusion.2), channel_id=1, source_target_pairs={{0,48},{16,0},{32,16},{48,32},{1,49},{17,1},{33,17},{49,33},{2,50}... | collective-permute-start | bytes 396296 | tf_op jit(solution)/shard_map/ppermute | solution.py:33
  33.0 3.0 %fusion.11 = f32[1024,1,128]{0,2,1:T(8,128)} fusion(f32[1024]{0:T(1024)} %bitcast.142, bf16[1024,4,128]{0,2,1:T(8,128)(2,1)S(1)} %bitcast.120, bf16[1024,4,128]{0,2,1:T(8,128)(2,1)S(1)} %bitcast.115, bf16[1024,4,128]{0,2,1:T(8,128)(2,1)S(1)} %bitcast.127), kind=kOutput, calls=%fused_computation.21 | convolution fusion | flops 543162368 | bytes 1318912 | tf_op jit(solution)/shard_map/dot_general | solution.py:101
  36.0 2.2 %collective-permute-done.3 = f32[2,129,128]{2,1,0:T(8,128)} collective-permute-done((f32[2,129,128]{2,1,0:T(8,128)S(1)}, f32[2,129,128]{2,1,0:T(8,128)}, u32[]{:S(2)}, u32[]{:S(2)}) %collective-permute-start.3) | collective-permute-done | bytes 132128 | tf_op jit(solution)/shard_map/ppermute | solution.py:33
  39.1 1.3 exponential_reduce_fusion
  42.3 1.9 %collective-permute-start.4 = (f32[2,33,128]{2,1,0:T(8,128)S(1)}, f32[2,33,128]{2,1,0:T(8,128)S(1)}, u32[]{:S(2)}, u32[]{:S(2)}) collective-permute-start(f32[2,33,128]{2,1,0:T(8,128)S(1)} %pad_maximum_fusion.3), channel_id=1, source_target_pairs={{0,64},{64,128},{128,192},{192,256},{256,320},{320,384},{384,448},... | collective-permute-start | bytes 101384 | tf_op jit(solution)/shard_map/ppermute | solution.py:33
  44.2 1.9 %collective-permute-start.5 = (f32[2,33,128]{2,1,0:T(8,128)S(1)}, f32[2,33,128]{2,1,0:T(8,128)S(1)}, u32[]{:S(2)}, u32[]{:S(2)}) collective-permute-start(f32[2,33,128]{2,1,0:T(8,128)S(1)} %pad_maximum_fusion.3), channel_id=1, source_target_pairs={{0,128},{64,192},{128,256},{192,320},{256,384},{320,448},{384,0},{... | collective-permute-start | bytes 101384 | tf_op jit(solution)/shard_map/ppermute | solution.py:33
  46.2 3.3 %collective-permute-start.6 = (f32[2,33,128]{2,1,0:T(8,128)S(1)}, f32[2,33,128]{2,1,0:T(8,128)S(1)}, u32[]{:S(2)}, u32[]{:S(2)}) collective-permute-start(f32[2,33,128]{2,1,0:T(8,128)S(1)} %pad_maximum_fusion.3), channel_id=1, source_target_pairs={{0,192},{64,256},{128,320},{192,384},{256,448},{320,0},{384,64},{4... | collective-permute-start | bytes 101384 | tf_op jit(solution)/shard_map/ppermute | solution.py:33
  49.5 2.9 %fusion.12 = f32[1024,1,128]{0,2,1:T(8,128)} fusion(f32[1024]{0:T(1024)} %bitcast.141, bf16[1024,4,128]{0,2,1:T(8,128)(2,1)S(1)} %bitcast.121, bf16[1024,4,128]{0,2,1:T(8,128)(2,1)S(1)} %bitcast.116, bf16[1024,4,128]{0,2,1:T(8,128)(2,1)S(1)} %bitcast.128), kind=kOutput, calls=%fused_computation.22 | convolution fusion | flops 543162368 | bytes 1318912 | tf_op jit(solution)/shard_map/dot_general | solution.py:101
  52.5 6.1 %collective-permute-start.7 = (f32[2,33,128]{2,1,0:T(8,128)S(1)}, f32[2,33,128]{2,1,0:T(8,128)S(1)}, u32[]{:S(2)}, u32[]{:S(2)}) collective-permute-start(f32[2,33,128]{2,1,0:T(8,128)S(1)} %pad_maximum_fusion.3), channel_id=1, source_target_pairs={{0,256},{64,320},{128,384},{192,448},{256,0},{320,64},{384,128},{4... | collective-permute-start | bytes 101384 | tf_op jit(solution)/shard_map/ppermute | solution.py:33
  58.6 2.3 %collective-permute-start.8 = (f32[2,33,128]{2,1,0:T(8,128)S(1)}, f32[2,33,128]{2,1,0:T(8,128)S(1)}, u32[]{:S(2)}, u32[]{:S(2)}) collective-permute-start(f32[2,33,128]{2,1,0:T(8,128)S(1)} %pad_maximum_fusion.3), channel_id=1, source_target_pairs={{0,320},{64,384},{128,448},{192,0},{256,64},{320,128},{384,192},{4... | collective-permute-start | bytes 101384 | tf_op jit(solution)/shard_map/ppermute | solution.py:33
  60.9 5.1 %collective-permute-start.9 = (f32[2,33,128]{2,1,0:T(8,128)S(1)}, f32[2,33,128]{2,1,0:T(8,128)S(1)}, u32[]{:S(2)}, u32[]{:S(2)}) collective-permute-start(f32[2,33,128]{2,1,0:T(8,128)S(1)} %pad_maximum_fusion.3), channel_id=1, source_target_pairs={{0,384},{64,448},{128,0},{192,64},{256,128},{320,192},{384,256},{4... | collective-permute-start | bytes 101384 | tf_op jit(solution)/shard_map/ppermute | solution.py:33
  66.0 2.8 %collective-permute-start.10 = (f32[2,33,128]{2,1,0:T(8,128)S(1)}, f32[2,33,128]{2,1,0:T(8,128)S(1)}, u32[]{:S(2)}, u32[]{:S(2)}) collective-permute-start(f32[2,33,128]{2,1,0:T(8,128)S(1)} %pad_maximum_fusion.3), channel_id=1, source_target_pairs={{0,448},{64,0},{128,64},{192,128},{256,192},{320,256},{384,320},{4... | collective-permute-start | bytes 101384 | tf_op jit(solution)/shard_map/ppermute | solution.py:33
  69.1 2.3 %collective-permute-done.10 = f32[2,33,128]{2,1,0:T(8,128)S(1)} collective-permute-done((f32[2,33,128]{2,1,0:T(8,128)S(1)}, f32[2,33,128]{2,1,0:T(8,128)S(1)}, u32[]{:S(2)}, u32[]{:S(2)}) %collective-permute-start.10) | collective-permute-done | bytes 33824 | tf_op jit(solution)/shard_map/ppermute | solution.py:33
  71.5 3.4 %collective-permute-start.11 = (f32[2,32,128]{2,1,0:T(8,128)S(1)}, f32[2,32,128]{2,1,0:T(8,128)S(1)}, u32[]{:S(2)}, u32[]{:S(2)}) collective-permute-start(f32[2,32,128]{2,1,0:T(8,128)S(1)} %fusion.21), channel_id=1, source_target_pairs={{0,16},{16,32},{32,48},{48,0},{1,17},{17,33},{33,49},{49,1},{2,18}... | collective-permute-start | bytes 98312 | tf_op jit(solution)/shard_map/ppermute | solution.py:33
  74.9 4.3 %collective-permute-start.12 = (f32[2,32,128]{2,1,0:T(8,128)S(1)}, f32[2,32,128]{2,1,0:T(8,128)S(1)}, u32[]{:S(2)}, u32[]{:S(2)}) collective-permute-start(f32[2,32,128]{2,1,0:T(8,128)S(1)} %fusion.21), channel_id=1, source_target_pairs={{0,32},{16,48},{32,0},{48,16},{1,33},{17,49},{33,1},{49,17},{2,34}... | collective-permute-start | bytes 98312 | tf_op jit(solution)/shard_map/ppermute | solution.py:33
  79.2 1.9 %collective-permute-start.13 = (f32[2,32,128]{2,1,0:T(8,128)S(1)}, f32[2,32,128]{2,1,0:T(8,128)S(1)}, u32[]{:S(2)}, u32[]{:S(2)}) collective-permute-start(f32[2,32,128]{2,1,0:T(8,128)S(1)} %fusion.21), channel_id=1, source_target_pairs={{0,48},{16,0},{32,16},{48,32},{1,49},{17,1},{33,17},{49,33},{2,50}... | collective-permute-start | bytes 98312 | tf_op jit(solution)/shard_map/ppermute | solution.py:33
  81.2 2.2 %fusion.9 = f32[1024,1,128]{0,2,1:T(8,128)} fusion(f32[1024]{0:T(1024)S(1)} %bitcast.140, bf16[1024,4,128]{0,2,1:T(8,128)(2,1)S(1)} %bitcast.122, bf16[1024,4,128]{0,2,1:T(8,128)(2,1)S(1)} %bitcast.117, bf16[1024,4,128]{0,2,1:T(8,128)(2,1)S(1)} %bitcast.129), kind=kOutput, calls=%fused_computation.19 | convolution fusion | flops 543162368 | bytes 1318912 | tf_op jit(solution)/shard_map/dot_general | solution.py:101
  84.1 6.7 %collective-permute-start.14 = (f32[2,128,128]{2,1,0:T(8,128)S(1)}, f32[2,128,128]{2,1,0:T(8,128)S(1)}, u32[]{:S(2)}, u32[]{:S(2)}) collective-permute-start(f32[2,128,128]{2,1,0:T(8,128)S(1)} %fusion.18), channel_id=1, source_target_pairs={{0,8},{8,0},{1,9},{9,1},{2,10},{10,2},{3,11},{11,3},{4,12},{12,4},... | collective-permute-start | bytes 393224 | tf_op jit(solution)/shard_map/ppermute | solution.py:87
  92.9 4.2 %multiply_reduce_fusion = (f32[1024]{0:T(1024)S(1)}, f32[1024,4,128]{0,2,1:T(8,128)}) fusion(bf16[1024,4,128]{0,2,1:T(8,128)(2,1)S(1)} %bitcast.130, f32[4,128,128]{2,1,0:T(8,128)} %copy-done.4, f32[2,128,128]{2,1,0:T(8,128)S(1)} %fusion.18, f32[2,128,128]{2,1,0:T(8,128)S(1)} %collective-permute-done.14, f32[4]{0:T(128)S(1)} %copy-done.9, pred[]{:T(512)S(6)} %eq.7, ...), kind=kOutput, calls=%fused_computation.9 | convolution fusion | flops 810417152 | bytes 5787665 | tf_op jit(solution)/shard_map/thd,hde->the/dot_general | solution.py:122
  97.1 2.0 %copy.145 = f32[1024,512]{1,0:T(8,128)S(1)} copy(f32[1024,512]{0,1:T(8,128)} %bitcast.125) | data formatting | bytes 4194304 | tf_op jit(solution)/shard_map/convert_element_type | solution.py:126
  99.2 1.3 broadcast_select_fusion.1
  102.1 40.5 %all_to_all.5 = bf16[8,129,512]{2,1,0:T(8,128)(2,1)S(1)} all-to-all(bf16[8,129,512]{2,1,0:T(8,128)(2,1)S(1)} %pad_maximum_fusion), channel_id=1, replica_groups=mesh['cy'=8,'cx'=4,'cc'=2,'head'=8] {'head'}, dimensions={0} | all-to-all | bytes 2113536 | tf_op jit(solution)/shard_map/all_to_all | solution.py:137
  143.6 1.3 copy.147
  (81 shorter events, 14.5 us)
Async XLA Ops:
  0.0 4.1 %copy-start = (bf16[1024,512]{1,0:T(8,128)(2,1)S(1)}, bf16[1024,512]{1,0:T(8,128)(2,1)}, u32[]{:S(2)}) copy-start(bf16[1024,512]{1,0:T(8,128)(2,1)} %param.12) | copy-start | bytes 3145732
  4.7 11.4 %copy-start.1 = (bf16[1024,512]{1,0:T(8,128)(2,1)S(1)}, bf16[1024,512]{1,0:T(8,128)(2,1)}, u32[]{:S(2)}) copy-start(bf16[1024,512]{1,0:T(8,128)(2,1)} %param.10) | copy-start | bytes 3145732
  6.7 14.0 %collective-permute-start = (f32[4,129,128]{2,1,0:T(8,128)}, f32[4,129,128]{2,1,0:T(8,128)}, u32[]{:S(2)}, u32[]{:S(2)}) collective-permute-start(f32[4,129,128]{2,1,0:T(8,128)} %pad_maximum_fusion.1), channel_id=1, source_target_pairs={{0,8},{8,0},{1,9},{9,1},{2,10},{10,2},{3,11},{11,3},{4,12},{12,4},... | collective-permute-start | bytes 792584 | tf_op jit(solution)/shard_map/ppermute | solution.py:59
  17.4 15.5 %copy-start.2 = (bf16[1024,512]{0,1:T(8,128)(2,1)S(1)}, bf16[1024,512]{0,1:T(8,128)(2,1)}, u32[]{:S(2)}) copy-start(bf16[1024,512]{0,1:T(8,128)(2,1)} %copy.125) | copy-start | bytes 3145732
  22.7 10.2 %copy-start.7 = (f32[2]{0:T(128)}, f32[2]{0:T(128)S(1)}, u32[]{:S(2)}) copy-start(f32[2]{0:T(128)S(1)} %get-tuple-element.45) | copy-start | bytes 28
  23.7 0.7 copy-start.4
  24.5 11.5 %collective-permute-start.1 = (f32[2,129,128]{2,1,0:T(8,128)S(1)}, f32[2,129,128]{2,1,0:T(8,128)}, u32[]{:S(2)}, u32[]{:S(2)}) collective-permute-start(f32[2,129,128]{2,1,0:T(8,128)S(1)} %pad_maximum_fusion.2), channel_id=1, source_target_pairs={{0,16},{16,32},{32,48},{48,0},{1,17},{17,33},{33,49},{49,1},{2,18}... | collective-permute-start | bytes 396296 | tf_op jit(solution)/shard_map/ppermute | solution.py:33
  26.4 9.6 %collective-permute-start.2 = (f32[2,129,128]{2,1,0:T(8,128)S(1)}, f32[2,129,128]{2,1,0:T(8,128)}, u32[]{:S(2)}, u32[]{:S(2)}) collective-permute-start(f32[2,129,128]{2,1,0:T(8,128)S(1)} %pad_maximum_fusion.2), channel_id=1, source_target_pairs={{0,32},{16,48},{32,0},{48,16},{1,33},{17,49},{33,1},{49,17},{2,34}... | collective-permute-start | bytes 396296 | tf_op jit(solution)/shard_map/ppermute | solution.py:33
  28.4 9.8 %collective-permute-start.3 = (f32[2,129,128]{2,1,0:T(8,128)S(1)}, f32[2,129,128]{2,1,0:T(8,128)}, u32[]{:S(2)}, u32[]{:S(2)}) collective-permute-start(f32[2,129,128]{2,1,0:T(8,128)S(1)} %pad_maximum_fusion.2), channel_id=1, source_target_pairs={{0,48},{16,0},{32,16},{48,32},{1,49},{17,1},{33,17},{49,33},{2,50}... | collective-permute-start | bytes 396296 | tf_op jit(solution)/shard_map/ppermute | solution.py:33
  33.0 7.4 %copy-start.8 = (f32[2]{0:T(128)S(1)}, f32[2]{0:T(128)}, u32[]{:S(2)}) copy-start(f32[2]{0:T(128)} %copy-done.7) | copy-start | bytes 28
  42.3 18.6 %collective-permute-start.4 = (f32[2,33,128]{2,1,0:T(8,128)S(1)}, f32[2,33,128]{2,1,0:T(8,128)S(1)}, u32[]{:S(2)}, u32[]{:S(2)}) collective-permute-start(f32[2,33,128]{2,1,0:T(8,128)S(1)} %pad_maximum_fusion.3), channel_id=1, source_target_pairs={{0,64},{64,128},{128,192},{192,256},{256,320},{320,384},{384,448},... | collective-permute-start | bytes 101384 | tf_op jit(solution)/shard_map/ppermute | solution.py:33
  44.2 21.8 %collective-permute-start.5 = (f32[2,33,128]{2,1,0:T(8,128)S(1)}, f32[2,33,128]{2,1,0:T(8,128)S(1)}, u32[]{:S(2)}, u32[]{:S(2)}) collective-permute-start(f32[2,33,128]{2,1,0:T(8,128)S(1)} %pad_maximum_fusion.3), channel_id=1, source_target_pairs={{0,128},{64,192},{128,256},{192,320},{256,384},{320,448},{384,0},{... | collective-permute-start | bytes 101384 | tf_op jit(solution)/shard_map/ppermute | solution.py:33
  46.2 22.7 %collective-permute-start.6 = (f32[2,33,128]{2,1,0:T(8,128)S(1)}, f32[2,33,128]{2,1,0:T(8,128)S(1)}, u32[]{:S(2)}, u32[]{:S(2)}) collective-permute-start(f32[2,33,128]{2,1,0:T(8,128)S(1)} %pad_maximum_fusion.3), channel_id=1, source_target_pairs={{0,192},{64,256},{128,320},{192,384},{256,448},{320,0},{384,64},{4... | collective-permute-start | bytes 101384 | tf_op jit(solution)/shard_map/ppermute | solution.py:33
  49.5 31.6 %copy-start.5 = (f32[1024,1]{0,1:T(1,128)S(1)}, f32[1024,1]{0,1:T(1,128)}, u32[]{:S(2)}) copy-start(f32[1024,1]{0,1:T(1,128)} %get-tuple-element.70) | copy-start | bytes 12292
  52.5 16.5 %collective-permute-start.7 = (f32[2,33,128]{2,1,0:T(8,128)S(1)}, f32[2,33,128]{2,1,0:T(8,128)S(1)}, u32[]{:S(2)}, u32[]{:S(2)}) collective-permute-start(f32[2,33,128]{2,1,0:T(8,128)S(1)} %pad_maximum_fusion.3), channel_id=1, source_target_pairs={{0,256},{64,320},{128,384},{192,448},{256,0},{320,64},{384,128},{4... | collective-permute-start | bytes 101384 | tf_op jit(solution)/shard_map/ppermute | solution.py:33
  58.6 10.4 %collective-permute-start.8 = (f32[2,33,128]{2,1,0:T(8,128)S(1)}, f32[2,33,128]{2,1,0:T(8,128)S(1)}, u32[]{:S(2)}, u32[]{:S(2)}) collective-permute-start(f32[2,33,128]{2,1,0:T(8,128)S(1)} %pad_maximum_fusion.3), channel_id=1, source_target_pairs={{0,320},{64,384},{128,448},{192,0},{256,64},{320,128},{384,192},{4... | collective-permute-start | bytes 101384 | tf_op jit(solution)/shard_map/ppermute | solution.py:33
  60.9 8.1 %collective-permute-start.9 = (f32[2,33,128]{2,1,0:T(8,128)S(1)}, f32[2,33,128]{2,1,0:T(8,128)S(1)}, u32[]{:S(2)}, u32[]{:S(2)}) collective-permute-start(f32[2,33,128]{2,1,0:T(8,128)S(1)} %pad_maximum_fusion.3), channel_id=1, source_target_pairs={{0,384},{64,448},{128,0},{192,64},{256,128},{320,192},{384,256},{4... | collective-permute-start | bytes 101384 | tf_op jit(solution)/shard_map/ppermute | solution.py:33
  66.0 5.4 %collective-permute-start.10 = (f32[2,33,128]{2,1,0:T(8,128)S(1)}, f32[2,33,128]{2,1,0:T(8,128)S(1)}, u32[]{:S(2)}, u32[]{:S(2)}) collective-permute-start(f32[2,33,128]{2,1,0:T(8,128)S(1)} %pad_maximum_fusion.3), channel_id=1, source_target_pairs={{0,448},{64,0},{128,64},{192,128},{256,192},{320,256},{384,320},{4... | collective-permute-start | bytes 101384 | tf_op jit(solution)/shard_map/ppermute | solution.py:33
  71.5 11.9 %collective-permute-start.11 = (f32[2,32,128]{2,1,0:T(8,128)S(1)}, f32[2,32,128]{2,1,0:T(8,128)S(1)}, u32[]{:S(2)}, u32[]{:S(2)}) collective-permute-start(f32[2,32,128]{2,1,0:T(8,128)S(1)} %fusion.21), channel_id=1, source_target_pairs={{0,16},{16,32},{32,48},{48,0},{1,17},{17,33},{33,49},{49,1},{2,18}... | collective-permute-start | bytes 98312 | tf_op jit(solution)/shard_map/ppermute | solution.py:33
  74.9 8.5 %collective-permute-start.12 = (f32[2,32,128]{2,1,0:T(8,128)S(1)}, f32[2,32,128]{2,1,0:T(8,128)S(1)}, u32[]{:S(2)}, u32[]{:S(2)}) collective-permute-start(f32[2,32,128]{2,1,0:T(8,128)S(1)} %fusion.21), channel_id=1, source_target_pairs={{0,32},{16,48},{32,0},{48,16},{1,33},{17,49},{33,1},{49,17},{2,34}... | collective-permute-start | bytes 98312 | tf_op jit(solution)/shard_map/ppermute | solution.py:33
  79.2 4.8 %collective-permute-start.13 = (f32[2,32,128]{2,1,0:T(8,128)S(1)}, f32[2,32,128]{2,1,0:T(8,128)S(1)}, u32[]{:S(2)}, u32[]{:S(2)}) collective-permute-start(f32[2,32,128]{2,1,0:T(8,128)S(1)} %fusion.21), channel_id=1, source_target_pairs={{0,48},{16,0},{32,16},{48,32},{1,49},{17,1},{33,17},{49,33},{2,50}... | collective-permute-start | bytes 98312 | tf_op jit(solution)/shard_map/ppermute | solution.py:33
  81.1 2.8 %copy-start.6 = (f32[2]{0:T(128)S(1)}, f32[2]{0:T(128)}, u32[]{:S(2)}) copy-start(f32[2]{0:T(128)} %get-tuple-element.76) | copy-start | bytes 28
  81.2 11.0 %copy-start.10 = (s32[3]{0:T(128)S(1)}, s32[3]{0:T(128)}, u32[]{:S(2)}) copy-start(s32[3]{0:T(128)} %constant.134.clone.1) | copy-start | bytes 40
  81.2 11.7 %copy-start.9 = (f32[4]{0:T(128)S(1)}, f32[4]{0:T(128)}, u32[]{:S(2)}) copy-start(f32[4]{0:T(128)} %get-tuple-element.29) | copy-start | bytes 52
  84.1 8.8 %collective-permute-start.14 = (f32[2,128,128]{2,1,0:T(8,128)S(1)}, f32[2,128,128]{2,1,0:T(8,128)S(1)}, u32[]{:S(2)}, u32[]{:S(2)}) collective-permute-start(f32[2,128,128]{2,1,0:T(8,128)S(1)} %fusion.18), channel_id=1, source_target_pairs={{0,8},{8,0},{1,9},{9,1},{2,10},{10,2},{3,11},{11,3},{4,12},{12,4},... | collective-permute-start | bytes 393224 | tf_op jit(solution)/shard_map/ppermute | solution.py:87
  97.1 4.3 %copy-start.3 = (bf16[1024,512]{1,0:T(8,128)(2,1)S(1)}, bf16[1024,512]{1,0:T(8,128)(2,1)}, u32[]{:S(2)}) copy-start(bf16[1024,512]{1,0:T(8,128)(2,1)} %param.14) | copy-start | bytes 3145732

commit v3 on v2

--- a/solution.py
+++ b/solution.py
@@ -50,6 +50,20 @@
     return log_before, before, log_after, after
 
 
+def exclusive_scan(log, state, axis, n):
+    def shift(packed, d):
+        return lax.ppermute(packed, axis, [(j, j + d) for j in range(n - d)])
+
+    cur_log, cur = unpack(shift(pack(log, state), 1))
+    d = 1
+    while d < n:
+        got_log, got = unpack(shift(pack(cur_log, cur), d))
+        cur = jnp.exp(cur_log)[:, None, None] * got + cur
+        cur_log = cur_log + got_log
+        d *= 2
+    return cur_log, cur
+
+
 def carried_state(L, S):
     rows, cols, cores = lax.axis_size("cy"), lax.axis_size("cx"), lax.axis_size("cc")
     y, x, c = lax.axis_index("cy"), lax.axis_index("cx"), lax.axis_index("cc")
@@ -75,8 +89,7 @@
 
     part = size // cols
     q_state = lax.dynamic_slice_in_dim(row_state, x * part, part, 1)
-    col_pieces = [unpack(p) for p in shifted(pack(row_log, q_state), "cy", rows)]
-    y_log, y_state, _, _ = scan_pieces([p[0] for p in col_pieces], [p[1] for p in col_pieces], y, rows)
+    y_log, y_state = exclusive_scan(row_log, q_state, "cy", rows)
 
     parts = shifted(y_state, "cx", cols)
     ordered = [lax.select_n((x - q) % cols, *parts) for q in range(cols)]

time: 146 us -> 143 us (0.979)
  starting transfers between devices: 57 us -> 49.7 us
  other arithmetic: 12.1 us -> 16.4 us
    ppermute x13 -> x6, starting transfers between devices: 41.6 us -> 18.3 us  [shifted(): out.append(lax.ppermute(x, axis, [(j, (j + s) % n) for j in range(n)]))]
    ppermute x0 -> x4, starting transfers between devices: none -> 13.9 us  [shift(): return lax.ppermute(packed, axis, [(j, j + d) for j in range(n - d)])]
    ppermute x1, starting transfers between devices: 6.68 us -> 8.74 us  [carried_state(): other = lax.ppermute(chip_before, 'cc', [(0, 1), (1, 0)])]
    ppermute x1, waiting for transfers between devices: 0.01 us -> 1.5 us  [carried_state(): pair = unpack(lax.ppermute(pack(L, S), 'cc', [(0, 1), (1, 0)]))]
    ppermute x13 -> x6, waiting for transfers between devices: 5.08 us -> 4.84 us  [shifted(): out.append(lax.ppermute(x, axis, [(j, (j + s) % n) for j in range(n)]))]
    unnamed x29 -> x23, local copies, waits for them, and re-layouts: 5.46 us -> 5.43 us
  transfers between devices with their start and end apart: 15 -> 12, of which waited for: 4 -> 3; matrix products, arithmetic and copies ran while one was open for 11% -> 11% of each run, Pallas kernels for 0% -> 0%
where the time goes in v3:
time: 143 us; the launch traced here: 142 us
  starting transfers between devices  49.7 us (35%)
  blocking collectives  40.5 us (28%)
  other arithmetic  16.4 us (11%)
  matrix products  15.9 us (11%)
  local copies, waits for them, and re-layouts  13.4 us (9%)
  waiting for transfers between devices  6.35 us (4%)
    all_to_all x1, blocking collectives, body(): lax.all_to_all(payload, 'head', split_axis=0, concat_axis=0, tiled=True)  40.5 us
    ppermute x6, starting transfers between devices, shifted(): out.append(lax.ppermute(x, axis, [(j, (j + s) % n) for j in range(n)]))  18.3 us
    ppermute x4, starting transfers between devices, shift(): return lax.ppermute(packed, axis, [(j, j + d) for j in range(n - d)])  13.9 us
    dot_general x4, matrix products, inner_head(): return jnp.dot(weights, vh, preferred_element_type=F32)  10.5 us
    ppermute x1, starting transfers between devices, carried_state(): pair = unpack(lax.ppermute(pack(L, S), 'cc', [(0, 1), (1, 0)]))  8.78 us
    ppermute x1, starting transfers between devices, carried_state(): other = lax.ppermute(chip_before, 'cc', [(0, 1), (1, 0)])  8.74 us
    unnamed x23, local copies, waits for them, and re-layouts  5.43 us
    ppermute x6, waiting for transfers between devices, shifted(): out.append(lax.ppermute(x, axis, [(j, (j + s) % n) for j in range(n)]))  4.84 us
  transfers between devices with their start and end apart: 12, of which 3 were waited for; matrix products, arithmetic and copies ran while one was open for 11% of the time, Pallas kernels for 0%

profile of v3, /device:TPU:1, one launch (start us, length us, event | category | flops | bytes accessed | tf_op | source)
XLA Modules:
  0.0 142.5 jit_solution(4782176501312779890)
XLA Ops:
  0.8 1.1 reduce-window.6
  3.2 1.5 %copy.127 = bf16[1024,512]{0,1:T(8,128)(2,1)S(1)} copy(bf16[1024,512]{1,0:T(8,128)(2,1)} %param.11) | data formatting | bytes 2097152 | tf_op args[1]
  5.2 1.2 fusion.1
  7.3 8.8 %collective-permute-start = (f32[4,129,128]{2,1,0:T(8,128)}, f32[4,129,128]{2,1,0:T(8,128)}, u32[]{:S(2)}, u32[]{:S(2)}) collective-permute-start(f32[4,129,128]{2,1,0:T(8,128)} %pad_maximum_fusion.1), channel_id=1, source_target_pairs={{0,8},{8,0},{1,9},{9,1},{2,10},{10,2},{3,11},{11,3},{4,12},{12,4},... | collective-permute-start | bytes 792584 | tf_op jit(solution)/shard_map/ppermute | solution.py:73
  16.1 1.5 %collective-permute-done = f32[4,129,128]{2,1,0:T(8,128)} collective-permute-done((f32[4,129,128]{2,1,0:T(8,128)}, f32[4,129,128]{2,1,0:T(8,128)}, u32[]{:S(2)}, u32[]{:S(2)}) %collective-permute-start) | collective-permute-done | bytes 264224 | tf_op jit(solution)/shard_map/ppermute | solution.py:73
  17.6 1.3 fusion.31
  21.3 1.9 %collective-permute-start.1 = (f32[2,129,128]{2,1,0:T(8,128)S(1)}, f32[2,129,128]{2,1,0:T(8,128)}, u32[]{:S(2)}, u32[]{:S(2)}) collective-permute-start(f32[2,129,128]{2,1,0:T(8,128)S(1)} %pad_maximum_fusion.2), channel_id=1, source_target_pairs={{0,16},{16,32},{32,48},{48,0},{1,17},{17,33},{33,49},{49,1},{2,18}... | collective-permute-start | bytes 396296 | tf_op jit(solution)/shard_map/ppermute | solution.py:33
  23.3 1.9 %collective-permute-start.2 = (f32[2,129,128]{2,1,0:T(8,128)S(1)}, f32[2,129,128]{2,1,0:T(8,128)}, u32[]{:S(2)}, u32[]{:S(2)}) collective-permute-start(f32[2,129,128]{2,1,0:T(8,128)S(1)} %pad_maximum_fusion.2), channel_id=1, source_target_pairs={{0,32},{16,48},{32,0},{48,16},{1,33},{17,49},{33,1},{49,17},{2,34}... | collective-permute-start | bytes 396296 | tf_op jit(solution)/shard_map/ppermute | solution.py:33
  25.2 4.6 %collective-permute-start.3 = (f32[2,129,128]{2,1,0:T(8,128)S(1)}, f32[2,129,128]{2,1,0:T(8,128)}, u32[]{:S(2)}, u32[]{:S(2)}) collective-permute-start(f32[2,129,128]{2,1,0:T(8,128)S(1)} %pad_maximum_fusion.2), channel_id=1, source_target_pairs={{0,48},{16,0},{32,16},{48,32},{1,49},{17,1},{33,17},{49,33},{2,50}... | collective-permute-start | bytes 396296 | tf_op jit(solution)/shard_map/ppermute | solution.py:33
  29.8 1.9 %collective-permute-done.2 = f32[2,129,128]{2,1,0:T(8,128)} collective-permute-done((f32[2,129,128]{2,1,0:T(8,128)S(1)}, f32[2,129,128]{2,1,0:T(8,128)}, u32[]{:S(2)}, u32[]{:S(2)}) %collective-permute-start.2) | collective-permute-done | bytes 132128 | tf_op jit(solution)/shard_map/ppermute | solution.py:33
  31.7 2.9 %collective-permute-done.3 = f32[2,129,128]{2,1,0:T(8,128)} collective-permute-done((f32[2,129,128]{2,1,0:T(8,128)S(1)}, f32[2,129,128]{2,1,0:T(8,128)}, u32[]{:S(2)}, u32[]{:S(2)}) %collective-permute-start.3) | collective-permute-done | bytes 132128 | tf_op jit(solution)/shard_map/ppermute | solution.py:33
  35.6 1.4 exponential_reduce_fusion.3
  37.6 1.1 fusion.54
  39.5 1.3 collective-permute-start.4
  41.4 1.3 copy.125
  42.9 2.8 %collective-permute-start.5 = (f32[2,33,128]{2,1,0:T(8,128)S(1)}, f32[2,33,128]{2,1,0:T(8,128)S(1)}, u32[]{:S(2)}, u32[]{:S(2)}) collective-permute-start(f32[2,33,128]{2,1,0:T(8,128)S(1)} %pad_maximum_fusion.4), channel_id=1, source_target_pairs={{0,64},{64,128},{128,192},{192,256},{256,320},{320,384},{384,448},... | collective-permute-start | bytes 101384 | tf_op jit(solution)/shard_map/ppermute | solution.py:55
  45.8 3.2 %fusion.10 = f32[1024,1,128]{0,2,1:T(8,128)} fusion(f32[1024]{0:T(1024)S(1)} %bitcast.143, bf16[1024,4,128]{0,2,1:T(8,128)(2,1)S(1)} %bitcast.119, bf16[1024,4,128]{0,2,1:T(8,128)(2,1)S(1)} %bitcast.114, bf16[1024,4,128]{0,2,1:T(8,128)(2,1)} %bitcast.126), kind=kOutput, calls=%fused_computation.20 | convolution fusion | flops 543162368 | bytes 1318912 | tf_op jit(solution)/shard_map/dot_general | solution.py:114
  49.3 2.8 %collective-permute-start.6 = (f32[2,33,128]{2,1,0:T(8,128)S(1)}, f32[2,33,128]{2,1,0:T(8,128)S(1)}, u32[]{:S(2)}, u32[]{:S(2)}) collective-permute-start(f32[2,33,128]{2,1,0:T(8,128)S(1)} %pad_maximum_fusion.5), channel_id=1, source_target_pairs={{0,128},{64,192},{128,256},{192,320},{256,384},{320,448},{1,129},{... | collective-permute-start | bytes 101384 | tf_op jit(solution)/shard_map/ppermute | solution.py:55
  52.0 2.2 %fusion.11 = f32[1024,1,128]{0,2,1:T(8,128)} fusion(f32[1024]{0:T(1024)S(1)} %bitcast.142, bf16[1024,4,128]{0,2,1:T(8,128)(2,1)S(1)} %bitcast.120, bf16[1024,4,128]{0,2,1:T(8,128)(2,1)S(1)} %bitcast.115, bf16[1024,4,128]{0,2,1:T(8,128)(2,1)S(1)} %bitcast.127), kind=kOutput, calls=%fused_computation.21 | convolution fusion | flops 543162368 | bytes 1318912 | tf_op jit(solution)/shard_map/dot_general | solution.py:114
  54.5 7.0 %collective-permute-start.7 = (f32[2,33,128]{2,1,0:T(8,128)S(1)}, f32[2,33,128]{2,1,0:T(8,128)S(1)}, u32[]{:S(2)}, u32[]{:S(2)}) collective-permute-start(f32[2,33,128]{2,1,0:T(8,128)S(1)} %pad_maximum_fusion.6), channel_id=1, source_target_pairs={{0,256},{64,320},{128,384},{192,448},{1,257},{65,321},{129,385},{1... | collective-permute-start | bytes 101384 | tf_op jit(solution)/shard_map/ppermute | solution.py:55
  61.5 2.2 %fusion.12 = f32[1024,1,128]{0,2,1:T(8,128)} fusion(f32[1024]{0:T(1024)S(1)} %bitcast.141, bf16[1024,4,128]{0,2,1:T(8,128)(2,1)S(1)} %bitcast.121, bf16[1024,4,128]{0,2,1:T(8,128)(2,1)S(1)} %bitcast.116, bf16[1024,4,128]{0,2,1:T(8,128)(2,1)S(1)} %bitcast.128), kind=kOutput, calls=%fused_computation.22 | convolution fusion | flops 543162368 | bytes 1318912 | tf_op jit(solution)/shard_map/dot_general | solution.py:114
  64.4 4.3 %collective-permute-start.10 = (f32[2,32,128]{2,1,0:T(8,128)}, f32[2,32,128]{2,1,0:T(8,128)}, u32[]{:S(2)}, u32[]{:S(2)}) collective-permute-start(f32[2,32,128]{2,1,0:T(8,128)} %fusion.21), channel_id=1, source_target_pairs={{0,48},{16,0},{32,16},{48,32},{1,49},{17,1},{33,17},{49,33},{2,50}... | collective-permute-start | bytes 98312 | tf_op jit(solution)/shard_map/ppermute | solution.py:33
  68.6 1.9 %collective-permute-start.8 = (f32[2,32,128]{2,1,0:T(8,128)}, f32[2,32,128]{2,1,0:T(8,128)}, u32[]{:S(2)}, u32[]{:S(2)}) collective-permute-start(f32[2,32,128]{2,1,0:T(8,128)} %fusion.21), channel_id=1, source_target_pairs={{0,16},{16,32},{32,48},{48,0},{1,17},{17,33},{33,49},{49,1},{2,18}... | collective-permute-start | bytes 98312 | tf_op jit(solution)/shard_map/ppermute | solution.py:33
  70.6 3.7 %collective-permute-start.9 = (f32[2,32,128]{2,1,0:T(8,128)}, f32[2,32,128]{2,1,0:T(8,128)}, u32[]{:S(2)}, u32[]{:S(2)}) collective-permute-start(f32[2,32,128]{2,1,0:T(8,128)} %fusion.21), channel_id=1, source_target_pairs={{0,32},{16,48},{32,0},{48,16},{1,33},{17,49},{33,1},{49,17},{2,34}... | collective-permute-start | bytes 98312 | tf_op jit(solution)/shard_map/ppermute | solution.py:33
  74.3 2.9 %fusion.9 = f32[1024,1,128]{0,2,1:T(8,128)} fusion(f32[1024]{0:T(1024)} %bitcast.140, bf16[1024,4,128]{0,2,1:T(8,128)(2,1)S(1)} %bitcast.122, bf16[1024,4,128]{0,2,1:T(8,128)(2,1)S(1)} %bitcast.117, bf16[1024,4,128]{0,2,1:T(8,128)(2,1)S(1)} %bitcast.129), kind=kOutput, calls=%fused_computation.19 | convolution fusion | flops 543162368 | bytes 1318912 | tf_op jit(solution)/shard_map/dot_general | solution.py:114
  78.8 8.7 %collective-permute-start.11 = (f32[2,128,128]{2,1,0:T(8,128)S(1)}, f32[2,128,128]{2,1,0:T(8,128)S(1)}, u32[]{:S(2)}, u32[]{:S(2)}) collective-permute-start(f32[2,128,128]{2,1,0:T(8,128)S(1)} %fusion.18), channel_id=1, source_target_pairs={{0,8},{8,0},{1,9},{9,1},{2,10},{10,2},{3,11},{11,3},{4,12},{12,4},... | collective-permute-start | bytes 393224 | tf_op jit(solution)/shard_map/ppermute | solution.py:100
  89.0 1.4 %and_reduce_fusion = pred[]{:T(512)} fusion(s32[3]{0:T(128)} %constant.124.clone.1, s32[2]{0:T(128)S(1)} %iota_multiply_fusion, s32[1]{0:T(128)} %constant.123.clone.1), kind=kLoop, calls=%fused_computation.91 | loop fusion | flops 14 | bytes 25 | tf_op jit(solution)/shard_map/reduce.3
  90.4 4.2 %multiply_reduce_fusion = (f32[1024]{0:T(1024)S(1)}, f32[1024,4,128]{0,2,1:T(8,128)}) fusion(bf16[1024,4,128]{0,2,1:T(8,128)(2,1)S(1)} %bitcast.130, f32[4,128,128]{2,1,0:T(8,128)S(1)} %copy-done.5, f32[2,128,128]{2,1,0:T(8,128)S(1)} %fusion.18, f32[2,128,128]{2,1,0:T(8,128)S(1)} %collective-permute-done.11, f32[4]{0:T(128)} %get-tuple-element.29, ...), kind=kOutput, calls=%fused_computation.9 | convolution fusion | flops 810417152 | bytes 5787665 | tf_op jit(solution)/shard_map/thd,hde->the/dot_general | solution.py:135
  94.6 2.0 %copy.145 = f32[1024,512]{1,0:T(8,128)S(1)} copy(f32[1024,512]{0,1:T(8,128)} %bitcast.125) | data formatting | bytes 4194304 | tf_op jit(solution)/shard_map/convert_element_type | solution.py:139
  96.6 1.4 broadcast_select_fusion.1
  99.6 40.5 %all_to_all.5 = bf16[8,129,512]{2,1,0:T(8,128)(2,1)S(1)} all-to-all(bf16[8,129,512]{2,1,0:T(8,128)(2,1)S(1)} %pad_maximum_fusion), channel_id=1, replica_groups=mesh['cy'=8,'cx'=4,'cc'=2,'head'=8] {'head'}, dimensions={0} | all-to-all | bytes 2113536 | tf_op jit(solution)/shard_map/all_to_all | solution.py:150
  141.2 1.3 copy.147
  (79 shorter events, 15.8 us)
Async XLA Ops:
  0.0 4.7 %copy-start = (bf16[1024,512]{1,0:T(8,128)(2,1)S(1)}, bf16[1024,512]{1,0:T(8,128)(2,1)}, u32[]{:S(2)}) copy-start(bf16[1024,512]{1,0:T(8,128)(2,1)} %param.12) | copy-start | bytes 3145732
  6.5 35.0 %copy-start.1 = (bf16[1024,512]{1,0:T(8,128)(2,1)S(1)}, bf16[1024,512]{1,0:T(8,128)(2,1)}, u32[]{:S(2)}) copy-start(bf16[1024,512]{1,0:T(8,128)(2,1)} %param.10) | copy-start | bytes 3145732
  7.3 10.3 %collective-permute-start = (f32[4,129,128]{2,1,0:T(8,128)}, f32[4,129,128]{2,1,0:T(8,128)}, u32[]{:S(2)}, u32[]{:S(2)}) collective-permute-start(f32[4,129,128]{2,1,0:T(8,128)} %pad_maximum_fusion.1), channel_id=1, source_target_pairs={{0,8},{8,0},{1,9},{9,1},{2,10},{10,2},{3,11},{11,3},{4,12},{12,4},... | collective-permute-start | bytes 792584 | tf_op jit(solution)/shard_map/ppermute | solution.py:73
  19.6 3.7 %copy-start.7 = (f32[2]{0:T(128)}, f32[2]{0:T(128)S(1)}, u32[]{:S(2)}) copy-start(f32[2]{0:T(128)S(1)} %get-tuple-element.46) | copy-start | bytes 28
  20.6 0.7 copy-start.4
  21.3 8.5 %collective-permute-start.1 = (f32[2,129,128]{2,1,0:T(8,128)S(1)}, f32[2,129,128]{2,1,0:T(8,128)}, u32[]{:S(2)}, u32[]{:S(2)}) collective-permute-start(f32[2,129,128]{2,1,0:T(8,128)S(1)} %pad_maximum_fusion.2), channel_id=1, source_target_pairs={{0,16},{16,32},{32,48},{48,0},{1,17},{17,33},{33,49},{49,1},{2,18}... | collective-permute-start | bytes 396296 | tf_op jit(solution)/shard_map/ppermute | solution.py:33
  23.3 8.4 %collective-permute-start.2 = (f32[2,129,128]{2,1,0:T(8,128)S(1)}, f32[2,129,128]{2,1,0:T(8,128)}, u32[]{:S(2)}, u32[]{:S(2)}) collective-permute-start(f32[2,129,128]{2,1,0:T(8,128)S(1)} %pad_maximum_fusion.2), channel_id=1, source_target_pairs={{0,32},{16,48},{32,0},{48,16},{1,33},{17,49},{33,1},{49,17},{2,34}... | collective-permute-start | bytes 396296 | tf_op jit(solution)/shard_map/ppermute | solution.py:33
  25.2 9.4 %collective-permute-start.3 = (f32[2,129,128]{2,1,0:T(8,128)S(1)}, f32[2,129,128]{2,1,0:T(8,128)}, u32[]{:S(2)}, u32[]{:S(2)}) collective-permute-start(f32[2,129,128]{2,1,0:T(8,128)S(1)} %pad_maximum_fusion.2), channel_id=1, source_target_pairs={{0,48},{16,0},{32,16},{48,32},{1,49},{17,1},{33,17},{49,33},{2,50}... | collective-permute-start | bytes 396296 | tf_op jit(solution)/shard_map/ppermute | solution.py:33
  39.5 3.2 %collective-permute-start.4 = (f32[2,33,128]{2,1,0:T(8,128)S(1)}, f32[2,33,128]{2,1,0:T(8,128)S(1)}, u32[]{:S(2)}, u32[]{:S(2)}) collective-permute-start(f32[2,33,128]{2,1,0:T(8,128)S(1)} %pad_maximum_fusion.3), channel_id=1, source_target_pairs={{0,64},{64,128},{128,192},{192,256},{256,320},{320,384},{384,448},... | collective-permute-start | bytes 101384 | tf_op jit(solution)/shard_map/ppermute | solution.py:55
  42.9 6.1 %collective-permute-start.5 = (f32[2,33,128]{2,1,0:T(8,128)S(1)}, f32[2,33,128]{2,1,0:T(8,128)S(1)}, u32[]{:S(2)}, u32[]{:S(2)}) collective-permute-start(f32[2,33,128]{2,1,0:T(8,128)S(1)} %pad_maximum_fusion.4), channel_id=1, source_target_pairs={{0,64},{64,128},{128,192},{192,256},{256,320},{320,384},{384,448},... | collective-permute-start | bytes 101384 | tf_op jit(solution)/shard_map/ppermute | solution.py:55
  45.8 6.3 %copy-start.2 = (bf16[1024,512]{0,1:T(8,128)(2,1)S(1)}, bf16[1024,512]{0,1:T(8,128)(2,1)}, u32[]{:S(2)}) copy-start(bf16[1024,512]{0,1:T(8,128)(2,1)} %copy.125) | copy-start | bytes 3145732
  49.3 5.0 %collective-permute-start.6 = (f32[2,33,128]{2,1,0:T(8,128)S(1)}, f32[2,33,128]{2,1,0:T(8,128)S(1)}, u32[]{:S(2)}, u32[]{:S(2)}) collective-permute-start(f32[2,33,128]{2,1,0:T(8,128)S(1)} %pad_maximum_fusion.5), channel_id=1, source_target_pairs={{0,128},{64,192},{128,256},{192,320},{256,384},{320,448},{1,129},{... | collective-permute-start | bytes 101384 | tf_op jit(solution)/shard_map/ppermute | solution.py:55
  54.5 9.2 %collective-permute-start.7 = (f32[2,33,128]{2,1,0:T(8,128)S(1)}, f32[2,33,128]{2,1,0:T(8,128)S(1)}, u32[]{:S(2)}, u32[]{:S(2)}) collective-permute-start(f32[2,33,128]{2,1,0:T(8,128)S(1)} %pad_maximum_fusion.6), channel_id=1, source_target_pairs={{0,256},{64,320},{128,384},{192,448},{1,257},{65,321},{129,385},{1... | collective-permute-start | bytes 101384 | tf_op jit(solution)/shard_map/ppermute | solution.py:55
  64.4 12.8 %collective-permute-start.10 = (f32[2,32,128]{2,1,0:T(8,128)}, f32[2,32,128]{2,1,0:T(8,128)}, u32[]{:S(2)}, u32[]{:S(2)}) collective-permute-start(f32[2,32,128]{2,1,0:T(8,128)} %fusion.21), channel_id=1, source_target_pairs={{0,48},{16,0},{32,16},{48,32},{1,49},{17,1},{33,17},{49,33},{2,50}... | collective-permute-start | bytes 98312 | tf_op jit(solution)/shard_map/ppermute | solution.py:33
  68.6 8.6 %collective-permute-start.8 = (f32[2,32,128]{2,1,0:T(8,128)}, f32[2,32,128]{2,1,0:T(8,128)}, u32[]{:S(2)}, u32[]{:S(2)}) collective-permute-start(f32[2,32,128]{2,1,0:T(8,128)} %fusion.21), channel_id=1, source_target_pairs={{0,16},{16,32},{32,48},{48,0},{1,17},{17,33},{33,49},{49,1},{2,18}... | collective-permute-start | bytes 98312 | tf_op jit(solution)/shard_map/ppermute | solution.py:33
  70.6 6.6 %collective-permute-start.9 = (f32[2,32,128]{2,1,0:T(8,128)}, f32[2,32,128]{2,1,0:T(8,128)}, u32[]{:S(2)}, u32[]{:S(2)}) collective-permute-start(f32[2,32,128]{2,1,0:T(8,128)} %fusion.21), channel_id=1, source_target_pairs={{0,32},{16,48},{32,0},{48,16},{1,33},{17,49},{33,1},{49,17},{2,34}... | collective-permute-start | bytes 98312 | tf_op jit(solution)/shard_map/ppermute | solution.py:33
  74.3 16.1 %copy-start.5 = (f32[4,128,128]{2,1,0:T(8,128)S(1)}, f32[4,128,128]{2,1,0:T(8,128)}, u32[]{:S(2)}) copy-start(f32[4,128,128]{2,1,0:T(8,128)} %copy-done.4) | copy-start | bytes 786436
  74.3 16.1 %copy-start.6 = (f32[1024,4]{0,1:T(4,128)S(1)}, f32[1024,4]{0,1:T(4,128)}, u32[]{:S(2)}) copy-start(f32[1024,4]{0,1:T(4,128)} %get-tuple-element.68) | copy-start | bytes 49156
  78.8 11.6 %collective-permute-start.11 = (f32[2,128,128]{2,1,0:T(8,128)S(1)}, f32[2,128,128]{2,1,0:T(8,128)S(1)}, u32[]{:S(2)}, u32[]{:S(2)}) collective-permute-start(f32[2,128,128]{2,1,0:T(8,128)S(1)} %fusion.18), channel_id=1, source_target_pairs={{0,8},{8,0},{1,9},{9,1},{2,10},{10,2},{3,11},{11,3},{4,12},{12,4},... | collective-permute-start | bytes 393224 | tf_op jit(solution)/shard_map/ppermute | solution.py:100
  94.6 4.4 %copy-start.3 = (bf16[1024,512]{1,0:T(8,128)(2,1)S(1)}, bf16[1024,512]{1,0:T(8,128)(2,1)}, u32[]{:S(2)}) copy-start(bf16[1024,512]{1,0:T(8,128)(2,1)} %param.14) | copy-start | bytes 3145732

commit v4 on v3

--- a/solution.py
+++ b/solution.py
@@ -121,19 +121,29 @@
     cum = jnp.cumsum(log_decay, axis=0)
     last = cum[-1]
 
-    k3 = keys.reshape(count, heads, size)
-    v3 = values.reshape(count, heads, size)
-    q3 = queries.reshape(count, heads, size)
-    keyed = k3.astype(F32) * jnp.exp(last[None, :] - cum)[:, :, None]
-    state = jnp.einsum("thd,the->hde", keyed, v3.astype(F32), precision=HI)
+    def cols(array, h):
+        return array[:, h * size : (h + 1) * size]
+
+    state = jnp.stack(
+        [
+            jnp.dot(
+                (cols(keys, h).astype(F32) * jnp.exp(last[h] - cum[:, h])[:, None]).T,
+                cols(values, h).astype(F32),
+                precision=HI,
+            )
+            for h in range(heads)
+        ]
+    )
 
     carried = carried_state(last, state)
 
-    inner = jnp.stack(
-        [inner_head(q3[:, h], k3[:, h], v3[:, h], cum[:, h]) for h in range(heads)], axis=1
-    )
-    across = jnp.einsum("thd,hde->the", q3.astype(F32), carried, precision=HI)
-    attended = (inner + jnp.exp(cum)[:, :, None] * across).reshape(count, width).astype(jnp.bfloat16)
+    joined = []
+    for h in range(heads):
+        qh = cols(queries, h)
+        inner = inner_head(qh, cols(keys, h), cols(values, h), cum[:, h])
+        across = jnp.dot(qh.astype(F32), carried[h], precision=HI)
+        joined.append(inner + jnp.exp(cum[:, h])[:, None] * across)
+    attended = jnp.concatenate(joined, axis=1).astype(jnp.bfloat16)
 
     groups = lax.axis_size("head")
     shade = attended.astype(F32)
@@ -143,9 +153,14 @@
     chunk = count // groups
     high = sums.astype(jnp.bfloat16)
     low = (sums - high.astype(F32)).astype(jnp.bfloat16)
-    extra = jnp.zeros((groups, 1, width), jnp.bfloat16)
-    extra = extra.at[:, 0, :chunk].set(high.reshape(groups, chunk))
-    extra = extra.at[:, 0, chunk : 2 * chunk].set(low.reshape(groups, chunk))
+    extra = jnp.concatenate(
+        [
+            high.reshape(groups, 1, chunk),
+            low.reshape(groups, 1, chunk),
+            jnp.zeros((groups, 1, width - 2 * chunk), jnp.bfloat16),
+        ],
+        axis=2,
+    )
     payload = jnp.concatenate([shaped.reshape(groups, chunk, width), extra], axis=1)
     got = lax.all_to_all(payload, "head", split_axis=0, concat_axis=0, tiled=True)
     parts = got[:, -1, :].astype(F32)

time: 143 us -> 140 us (0.979)
  other arithmetic: 16.4 us -> 9.58 us
  local copies, waits for them, and re-layouts: 13.4 us -> 6.74 us
  matrix products: 15.9 us -> 22.1 us
  waiting for transfers between devices: 6.35 us -> 9.67 us
    ppermute x4, starting transfers between devices: 13.9 us -> 18.3 us  [shift(): return lax.ppermute(packed, axis, [(j, j + d) for j in range(n - d)])]
    dot_general x2 -> x8, matrix products: 5.38 us -> 9.4 us  [the longest x4 6.99 us: body(): jnp.dot((cols(keys, h).astype(F32) * jnp.exp(last[h] - cum[:, h])[:, None...]
    ppermute x6, starting transfers between devices: 18.3 us -> 14.5 us  [shifted(): out.append(lax.ppermute(x, axis, [(j, (j + s) % n) for j in range(n)]))]
    unnamed x23 -> x20, local copies, waits for them, and re-layouts: 5.43 us -> 2.2 us
    another operation x5 -> x2, other arithmetic: 4.16 us -> 1.31 us
    exp x1, other arithmetic: 0.63 us -> 3.16 us  [body(): joined.append(inner + jnp.exp(cum[:, h])[:, None] * across)]
    dot_general x4, matrix products: 10.5 us -> 12.7 us  [inner_head(): return jnp.dot(weights, vh, preferred_element_type=F32)]
    ppermute x4, waiting for transfers between devices: 0.01 us -> 2.17 us  [shift(): return lax.ppermute(packed, axis, [(j, j + d) for j in range(n - d)])]
  transfers between devices with their start and end apart: 12 -> 12, of which waited for: 3 -> 6; matrix products, arithmetic and copies ran while one was open for 11% -> 10% of each run, Pallas kernels for 0% -> 0%
where the time goes in v4:
time: 140 us; the launch traced here: 139 us
  starting transfers between devices  50 us (36%)
  blocking collectives  40.5 us (29%)
  matrix products  22.1 us (16%)
  waiting for transfers between devices  9.67 us (7%)
  other arithmetic  9.58 us (7%)
  local copies, waits for them, and re-layouts  6.74 us (5%)
    all_to_all x1, blocking collectives, body(): lax.all_to_all(payload, 'head', split_axis=0, concat_axis=0, tiled=True)  40.5 us
    ppermute x4, starting transfers between devices, shift(): return lax.ppermute(packed, axis, [(j, j + d) for j in range(n - d)])  18.3 us
    ppermute x6, starting transfers between devices, shifted(): out.append(lax.ppermute(x, axis, [(j, (j + s) % n) for j in range(n)]))  14.5 us
    dot_general x4, matrix products, inner_head(): return jnp.dot(weights, vh, preferred_element_type=F32)  12.7 us
    ppermute x1, starting transfers between devices, carried_state(): pair = unpack(lax.ppermute(pack(L, S), 'cc', [(0, 1), (1, 0)]))  8.79 us
    ppermute x1, starting transfers between devices, carried_state(): other = lax.ppermute(chip_before, 'cc', [(0, 1), (1, 0)])  8.38 us
    dot_general x4, matrix products, body(): jnp.dot((cols(keys, h).astype(F32) * jnp.exp(last[h] - cum[:, h])[:, None...  6.99 us
    ppermute x6, waiting for transfers between devices, shifted(): out.append(lax.ppermute(x, axis, [(j, (j + s) % n) for j in range(n)]))  6.34 us
  transfers between devices with their start and end apart: 12, of which 6 were waited for; matrix products, arithmetic and copies ran while one was open for 10% of the time, Pallas kernels for 0%

profile of v4, /device:TPU:1, one launch (start us, length us, event | category | flops | bytes accessed | tf_op | source)
XLA Modules:
  0.0 139.0 jit_solution(13137893502072788323)
XLA Ops:
  0.8 1.1 reduce-window.6
  3.2 3.2 %slice_exponential_fusion.3 = (f32[1024,1]{0,1:T(1,128)S(1)}, f32[1024,1]{0,1:T(1,128)S(1)}, f32[1024,1]{0,1:T(1,128)S(1)}, f32[1024,1]{0,1:T(1,128)S(1)}, f32[1...) fusion(f32[1024,4]{0,1:T(4,128)S(1)} %bitcast.95, ...), kind=kLoop, calls=%fused_computation.174 | loop fusion | flops 4096 | bytes 65552 | tf_op jit(solution)/shard_map/exp | solution.py:145
  6.4 1.8 %convolution_bitcast_fusion.3 = f32[1,128,128]{2,1,0:T(8,128)S(1)} fusion(f32[1024]{0:T(1024)S(1)} %bitcast.111, bf16[1024,512]{1,0:T(8,128)(2,1)} %param.8, bf16[1024,512]{1,0:T(8,128)(2,1)} %param.7), kind=kOutput, calls=%fused_computation.34 | convolution fusion | flops 201588736 | bytes 593920 | tf_op jit(solution)/shard_map/dot_general | solution.py:129
  8.2 1.8 %convolution_bitcast_fusion.2 = f32[1,128,128]{2,1,0:T(8,128)S(1)} fusion(f32[1024]{0:T(1024)S(1)} %bitcast.110, bf16[1024,512]{1,0:T(8,128)(2,1)} %param.8, bf16[1024,512]{1,0:T(8,128)(2,1)} %param.7), kind=kOutput, calls=%fused_computation.33 | convolution fusion | flops 201588736 | bytes 593920 | tf_op jit(solution)/shard_map/dot_general | solution.py:129
  10.0 1.7 %convolution_bitcast_fusion.1 = f32[1,128,128]{2,1,0:T(8,128)S(1)} fusion(f32[1024]{0:T(1024)S(1)} %bitcast.109, bf16[1024,512]{1,0:T(8,128)(2,1)S(1)} %copy-done.7, bf16[1024,512]{1,0:T(8,128)(2,1)} %param.7), kind=kOutput, calls=%fused_computation.32 | convolution fusion | flops 201588736 | bytes 593920 | tf_op jit(solution)/shard_map/dot_general | solution.py:129
  11.7 1.7 %convolution_bitcast_fusion = f32[1,128,128]{2,1,0:T(8,128)S(1)} fusion(f32[1024]{0:T(1024)S(1)} %bitcast.108, bf16[1024,512]{1,0:T(8,128)(2,1)S(1)} %copy-done.7, bf16[1024,512]{1,0:T(8,128)(2,1)} %param.7), kind=kOutput, calls=%fused_computation.31 | convolution fusion | flops 201588736 | bytes 593920 | tf_op jit(solution)/shard_map/dot_general | solution.py:129
  13.5 8.8 %collective-permute-start = (f32[4,129,128]{2,1,0:T(8,128)S(1)}, f32[4,129,128]{2,1,0:T(8,128)S(1)}, u32[]{:S(2)}, u32[]{:S(2)}) collective-permute-start(f32[4,129,128]{2,1,0:T(8,128)S(1)} %pad_maximum_fusion.1), channel_id=1, source_target_pairs={{0,8},{8,0},{1,9},{9,1},{2,10},{10,2},{3,11},{11,3},{4,12},{12,4},... | collective-permute-start | bytes 792584 | tf_op jit(solution)/shard_map/ppermute | solution.py:73
  22.3 1.2 collective-permute-done
  24.6 2.1 %collective-permute-start.3 = (f32[2,129,128]{2,1,0:T(8,128)S(1)}, f32[2,129,128]{2,1,0:T(8,128)S(1)}, u32[]{:S(2)}, u32[]{:S(2)}) collective-permute-start(f32[2,129,128]{2,1,0:T(8,128)S(1)} %pad_maximum_fusion.3), channel_id=1, source_target_pairs={{0,48},{16,0},{32,16},{48,32},{1,49},{17,1},{33,17},{49,33},{2,50}... | collective-permute-start | bytes 396296 | tf_op jit(solution)/shard_map/ppermute | solution.py:33
  26.6 1.9 %collective-permute-start.2 = (f32[2,129,128]{2,1,0:T(8,128)S(1)}, f32[2,129,128]{2,1,0:T(8,128)S(1)}, u32[]{:S(2)}, u32[]{:S(2)}) collective-permute-start(f32[2,129,128]{2,1,0:T(8,128)S(1)} %pad_maximum_fusion.3), channel_id=1, source_target_pairs={{0,32},{16,48},{32,0},{48,16},{1,33},{17,49},{33,1},{49,17},{2,34}... | collective-permute-start | bytes 396296 | tf_op jit(solution)/shard_map/ppermute | solution.py:33
  28.6 3.4 %collective-permute-start.1 = (f32[2,129,128]{2,1,0:T(8,128)S(1)}, f32[2,129,128]{2,1,0:T(8,128)S(1)}, u32[]{:S(2)}, u32[]{:S(2)}) collective-permute-start(f32[2,129,128]{2,1,0:T(8,128)S(1)} %pad_maximum_fusion.3), channel_id=1, source_target_pairs={{0,16},{16,32},{32,48},{48,0},{1,17},{17,33},{33,49},{49,1},{2,18}... | collective-permute-start | bytes 396296 | tf_op jit(solution)/shard_map/ppermute | solution.py:33
  32.0 3.0 %collective-permute-done.2 = f32[2,129,128]{2,1,0:T(8,128)S(1)} collective-permute-done((f32[2,129,128]{2,1,0:T(8,128)S(1)}, f32[2,129,128]{2,1,0:T(8,128)S(1)}, u32[]{:S(2)}, u32[]{:S(2)}) %collective-permute-start.2) | collective-permute-done | bytes 132128 | tf_op jit(solution)/shard_map/ppermute | solution.py:33
  34.9 2.8 %collective-permute-done.1 = f32[2,129,128]{2,1,0:T(8,128)S(1)} collective-permute-done((f32[2,129,128]{2,1,0:T(8,128)S(1)}, f32[2,129,128]{2,1,0:T(8,128)S(1)}, u32[]{:S(2)}, u32[]{:S(2)}) %collective-permute-start.1) | collective-permute-done | bytes 132128 | tf_op jit(solution)/shard_map/ppermute | solution.py:33
  38.4 1.3 collective-permute-start.4
  39.7 1.1 collective-permute-done.4
  40.9 3.6 %collective-permute-start.5 = (f32[2,33,128]{2,1,0:T(8,128)S(1)}, f32[2,33,128]{2,1,0:T(8,128)S(1)}, u32[]{:S(2)}, u32[]{:S(2)}) collective-permute-start(f32[2,33,128]{2,1,0:T(8,128)S(1)} %pad_maximum_fusion.5), channel_id=1, source_target_pairs={{0,64},{64,128},{128,192},{192,256},{256,320},{320,384},{384,448},... | collective-permute-start | bytes 101384 | tf_op jit(solution)/shard_map/ppermute | solution.py:55
  44.6 1.1 collective-permute-done.5
  45.9 4.3 %collective-permute-start.6 = (f32[2,33,128]{2,1,0:T(8,128)S(1)}, f32[2,33,128]{2,1,0:T(8,128)S(1)}, u32[]{:S(2)}, u32[]{:S(2)}) collective-permute-start(f32[2,33,128]{2,1,0:T(8,128)S(1)} %pad_maximum_fusion.6), channel_id=1, source_target_pairs={{0,128},{64,192},{128,256},{192,320},{256,384},{320,448},{1,129},{... | collective-permute-start | bytes 101384 | tf_op jit(solution)/shard_map/ppermute | solution.py:55
  50.2 3.1 %fusion.6 = f32[1024,128]{0,1:T(8,128)} fusion(f32[1024]{0:T(1024)S(1)} %bitcast.107, bf16[1024,512]{1,0:T(8,128)(2,1)S(1)} %copy-done, bf16[1024,512]{1,0:T(8,128)(2,1)S(1)} %copy-done.7, bf16[1024,512]{1,0:T(8,128)(2,1)} %param.7), kind=kOutput, calls=%fused_computation.14 | convolution fusion | flops 543162368 | bytes 1318912 | tf_op jit(solution)/shard_map/dot_general | solution.py:114
  53.6 9.0 %collective-permute-start.7 = (f32[2,33,128]{2,1,0:T(8,128)S(1)}, f32[2,33,128]{2,1,0:T(8,128)S(1)}, u32[]{:S(2)}, u32[]{:S(2)}) collective-permute-start(f32[2,33,128]{2,1,0:T(8,128)S(1)} %pad_maximum_fusion.7), channel_id=1, source_target_pairs={{0,256},{64,320},{128,384},{192,448},{1,257},{65,321},{129,385},{1... | collective-permute-start | bytes 101384 | tf_op jit(solution)/shard_map/ppermute | solution.py:55
  62.7 3.2 %fusion.5 = f32[1024,128]{0,1:T(8,128)} fusion(f32[1024]{0:T(1024)S(1)} %bitcast.106, bf16[1024,512]{1,0:T(8,128)(2,1)S(1)} %copy-done, bf16[1024,512]{1,0:T(8,128)(2,1)S(1)} %copy-done.7, bf16[1024,512]{1,0:T(8,128)(2,1)} %param.7), kind=kOutput, calls=%fused_computation.13 | convolution fusion | flops 543162368 | bytes 1318912 | tf_op jit(solution)/shard_map/dot_general | solution.py:114
  65.9 1.9 %collective-permute-start.10 = (f32[2,32,128]{2,1,0:T(8,128)S(1)}, f32[2,32,128]{2,1,0:T(8,128)S(1)}, u32[]{:S(2)}, u32[]{:S(2)}) collective-permute-start(f32[2,32,128]{2,1,0:T(8,128)S(1)} %fusion.65), channel_id=1, source_target_pairs={{0,48},{16,0},{32,16},{48,32},{1,49},{17,1},{33,17},{49,33},{2,50}... | collective-permute-start | bytes 98312 | tf_op jit(solution)/shard_map/ppermute | solution.py:33
  67.8 2.3 %collective-permute-start.9 = (f32[2,32,128]{2,1,0:T(8,128)S(1)}, f32[2,32,128]{2,1,0:T(8,128)S(1)}, u32[]{:S(2)}, u32[]{:S(2)}) collective-permute-start(f32[2,32,128]{2,1,0:T(8,128)S(1)} %fusion.65), channel_id=1, source_target_pairs={{0,32},{16,48},{32,0},{48,16},{1,33},{17,49},{33,1},{49,17},{2,34}... | collective-permute-start | bytes 98312 | tf_op jit(solution)/shard_map/ppermute | solution.py:33
  70.2 2.9 %collective-permute-start.8 = (f32[2,32,128]{2,1,0:T(8,128)S(1)}, f32[2,32,128]{2,1,0:T(8,128)S(1)}, u32[]{:S(2)}, u32[]{:S(2)}) collective-permute-start(f32[2,32,128]{2,1,0:T(8,128)S(1)} %fusion.65), channel_id=1, source_target_pairs={{0,16},{16,32},{32,48},{48,0},{1,17},{17,33},{33,49},{49,1},{2,18}... | collective-permute-start | bytes 98312 | tf_op jit(solution)/shard_map/ppermute | solution.py:33
  73.1 3.1 %fusion.4 = f32[1024,128]{0,1:T(8,128)} fusion(f32[1024]{0:T(1024)S(1)} %bitcast.105, bf16[1024,512]{1,0:T(8,128)(2,1)S(1)} %copy-done, bf16[1024,512]{1,0:T(8,128)(2,1)S(1)} %copy-done.7, bf16[1024,512]{1,0:T(8,128)(2,1)} %param.7), kind=kOutput, calls=%fused_computation.12 | convolution fusion | flops 543162368 | bytes 1318912 | tf_op jit(solution)/shard_map/dot_general | solution.py:114
  77.6 8.4 %collective-permute-start.11 = (f32[2,128,128]{2,1,0:T(8,128)}, f32[2,128,128]{2,1,0:T(8,128)}, u32[]{:S(2)}, u32[]{:S(2)}) collective-permute-start(f32[2,128,128]{2,1,0:T(8,128)} %fusion.64), channel_id=1, source_target_pairs={{0,8},{8,0},{1,9},{9,1},{2,10},{10,2},{3,11},{11,3},{4,12},{12,4},... | collective-permute-start | bytes 393224 | tf_op jit(solution)/shard_map/ppermute | solution.py:100
  86.0 3.3 %fusion.3 = f32[1024,128]{0,1:T(8,128)} fusion(f32[1024]{0:T(1024)S(1)} %bitcast.104, bf16[1024,512]{1,0:T(8,128)(2,1)} %param.8, bf16[1024,512]{1,0:T(8,128)(2,1)} %param.7, bf16[1024,512]{1,0:T(8,128)(2,1)S(1)} %copy-done), kind=kOutput, calls=%fused_computation.11 | convolution fusion | flops 543162368 | bytes 1318912 | tf_op jit(solution)/shard_map/dot_general | solution.py:114
  89.8 0.8 dynamic_slice.15
  90.7 1.2 add_select_fusion
  91.9 1.2 fusion.18
  96.1 40.5 %all_to_all.5 = bf16[8,129,512]{2,1,0:T(8,128)(2,1)S(1)} all-to-all(bf16[8,129,512]{2,1,0:T(8,128)(2,1)S(1)} %maximum_maximum_fusion), channel_id=1, replica_groups=mesh['cy'=8,'cx'=4,'cc'=2,'head'=8] {'head'}, dimensions={0} | all-to-all | bytes 2113536 | tf_op jit(solution)/shard_map/all_to_all | solution.py:165
  137.7 1.3 copy.35
  (82 shorter events, 10.5 us)
Async XLA Ops:
  0.0 10.0 %copy-start.7 = (bf16[1024,512]{1,0:T(8,128)(2,1)S(1)}, bf16[1024,512]{1,0:T(8,128)(2,1)}, u32[]{:S(2)}) copy-start(bf16[1024,512]{1,0:T(8,128)(2,1)} %param.8) | copy-start | bytes 3145732
  13.5 10.0 %collective-permute-start = (f32[4,129,128]{2,1,0:T(8,128)S(1)}, f32[4,129,128]{2,1,0:T(8,128)S(1)}, u32[]{:S(2)}, u32[]{:S(2)}) collective-permute-start(f32[4,129,128]{2,1,0:T(8,128)S(1)} %pad_maximum_fusion.1), channel_id=1, source_target_pairs={{0,8},{8,0},{1,9},{9,1},{2,10},{10,2},{3,11},{11,3},{4,12},{12,4},... | collective-permute-start | bytes 792584 | tf_op jit(solution)/shard_map/ppermute | solution.py:73
  24.4 25.8 %copy-start = (bf16[1024,512]{1,0:T(8,128)(2,1)S(1)}, bf16[1024,512]{1,0:T(8,128)(2,1)}, u32[]{:S(2)}) copy-start(bf16[1024,512]{1,0:T(8,128)(2,1)} %param.6) | copy-start | bytes 3145732
  24.6 7.4 %collective-permute-start.3 = (f32[2,129,128]{2,1,0:T(8,128)S(1)}, f32[2,129,128]{2,1,0:T(8,128)S(1)}, u32[]{:S(2)}, u32[]{:S(2)}) collective-permute-start(f32[2,129,128]{2,1,0:T(8,128)S(1)} %pad_maximum_fusion.3), channel_id=1, source_target_pairs={{0,48},{16,0},{32,16},{48,32},{1,49},{17,1},{33,17},{49,33},{2,50}... | collective-permute-start | bytes 396296 | tf_op jit(solution)/shard_map/ppermute | solution.py:33
  26.6 8.3 %collective-permute-start.2 = (f32[2,129,128]{2,1,0:T(8,128)S(1)}, f32[2,129,128]{2,1,0:T(8,128)S(1)}, u32[]{:S(2)}, u32[]{:S(2)}) collective-permute-start(f32[2,129,128]{2,1,0:T(8,128)S(1)} %pad_maximum_fusion.3), channel_id=1, source_target_pairs={{0,32},{16,48},{32,0},{48,16},{1,33},{17,49},{33,1},{49,17},{2,34}... | collective-permute-start | bytes 396296 | tf_op jit(solution)/shard_map/ppermute | solution.py:33
  28.6 9.2 %collective-permute-start.1 = (f32[2,129,128]{2,1,0:T(8,128)S(1)}, f32[2,129,128]{2,1,0:T(8,128)S(1)}, u32[]{:S(2)}, u32[]{:S(2)}) collective-permute-start(f32[2,129,128]{2,1,0:T(8,128)S(1)} %pad_maximum_fusion.3), channel_id=1, source_target_pairs={{0,16},{16,32},{32,48},{48,0},{1,17},{17,33},{33,49},{49,1},{2,18}... | collective-permute-start | bytes 396296 | tf_op jit(solution)/shard_map/ppermute | solution.py:33
  38.4 2.4 %collective-permute-start.4 = (f32[2,33,128]{2,1,0:T(8,128)S(1)}, f32[2,33,128]{2,1,0:T(8,128)S(1)}, u32[]{:S(2)}, u32[]{:S(2)}) collective-permute-start(f32[2,33,128]{2,1,0:T(8,128)S(1)} %pad_maximum_fusion.4), channel_id=1, source_target_pairs={{0,64},{64,128},{128,192},{192,256},{256,320},{320,384},{384,448},... | collective-permute-start | bytes 101384 | tf_op jit(solution)/shard_map/ppermute | solution.py:55
  40.9 4.7 %collective-permute-start.5 = (f32[2,33,128]{2,1,0:T(8,128)S(1)}, f32[2,33,128]{2,1,0:T(8,128)S(1)}, u32[]{:S(2)}, u32[]{:S(2)}) collective-permute-start(f32[2,33,128]{2,1,0:T(8,128)S(1)} %pad_maximum_fusion.5), channel_id=1, source_target_pairs={{0,64},{64,128},{128,192},{192,256},{256,320},{320,384},{384,448},... | collective-permute-start | bytes 101384 | tf_op jit(solution)/shard_map/ppermute | solution.py:55
  45.9 7.4 %collective-permute-start.6 = (f32[2,33,128]{2,1,0:T(8,128)S(1)}, f32[2,33,128]{2,1,0:T(8,128)S(1)}, u32[]{:S(2)}, u32[]{:S(2)}) collective-permute-start(f32[2,33,128]{2,1,0:T(8,128)S(1)} %pad_maximum_fusion.6), channel_id=1, source_target_pairs={{0,128},{64,192},{128,256},{192,320},{256,384},{320,448},{1,129},{... | collective-permute-start | bytes 101384 | tf_op jit(solution)/shard_map/ppermute | solution.py:55
  53.6 12.2 %collective-permute-start.7 = (f32[2,33,128]{2,1,0:T(8,128)S(1)}, f32[2,33,128]{2,1,0:T(8,128)S(1)}, u32[]{:S(2)}, u32[]{:S(2)}) collective-permute-start(f32[2,33,128]{2,1,0:T(8,128)S(1)} %pad_maximum_fusion.7), channel_id=1, source_target_pairs={{0,256},{64,320},{128,384},{192,448},{1,257},{65,321},{129,385},{1... | collective-permute-start | bytes 101384 | tf_op jit(solution)/shard_map/ppermute | solution.py:55
  65.9 10.3 %collective-permute-start.10 = (f32[2,32,128]{2,1,0:T(8,128)S(1)}, f32[2,32,128]{2,1,0:T(8,128)S(1)}, u32[]{:S(2)}, u32[]{:S(2)}) collective-permute-start(f32[2,32,128]{2,1,0:T(8,128)S(1)} %fusion.65), channel_id=1, source_target_pairs={{0,48},{16,0},{32,16},{48,32},{1,49},{17,1},{33,17},{49,33},{2,50}... | collective-permute-start | bytes 98312 | tf_op jit(solution)/shard_map/ppermute | solution.py:33
  67.8 8.4 %collective-permute-start.9 = (f32[2,32,128]{2,1,0:T(8,128)S(1)}, f32[2,32,128]{2,1,0:T(8,128)S(1)}, u32[]{:S(2)}, u32[]{:S(2)}) collective-permute-start(f32[2,32,128]{2,1,0:T(8,128)S(1)} %fusion.65), channel_id=1, source_target_pairs={{0,32},{16,48},{32,0},{48,16},{1,33},{17,49},{33,1},{49,17},{2,34}... | collective-permute-start | bytes 98312 | tf_op jit(solution)/shard_map/ppermute | solution.py:33
  70.2 6.6 %collective-permute-start.8 = (f32[2,32,128]{2,1,0:T(8,128)S(1)}, f32[2,32,128]{2,1,0:T(8,128)S(1)}, u32[]{:S(2)}, u32[]{:S(2)}) collective-permute-start(f32[2,32,128]{2,1,0:T(8,128)S(1)} %fusion.65), channel_id=1, source_target_pairs={{0,16},{16,32},{32,48},{48,0},{1,17},{17,33},{33,49},{49,1},{2,18}... | collective-permute-start | bytes 98312 | tf_op jit(solution)/shard_map/ppermute | solution.py:33
  77.6 13.2 %collective-permute-start.11 = (f32[2,128,128]{2,1,0:T(8,128)}, f32[2,128,128]{2,1,0:T(8,128)}, u32[]{:S(2)}, u32[]{:S(2)}) collective-permute-start(f32[2,128,128]{2,1,0:T(8,128)} %fusion.64), channel_id=1, source_target_pairs={{0,8},{8,0},{1,9},{9,1},{2,10},{10,2},{3,11},{11,3},{4,12},{12,4},... | collective-permute-start | bytes 393224 | tf_op jit(solution)/shard_map/ppermute | solution.py:100
  85.9 3.3 %copy-start.1 = (bf16[1024,512]{1,0:T(8,128)(2,1)S(1)}, bf16[1024,512]{1,0:T(8,128)(2,1)}, u32[]{:S(2)}) copy-start(bf16[1024,512]{1,0:T(8,128)(2,1)} %param.10) | copy-start | bytes 3145732
  89.8 2.1 %copy-start.2 = (f32[1024,128]{0,1:T(8,128)S(1)}, f32[1024,128]{0,1:T(8,128)}, u32[]{:S(2)}) copy-start(f32[1024,128]{0,1:T(8,128)} %fusion.6) | copy-start | bytes 1572868
  89.8 3.3 %copy-start.3 = (f32[1024,128]{0,1:T(8,128)S(1)}, f32[1024,128]{0,1:T(8,128)}, u32[]{:S(2)}) copy-start(f32[1024,128]{0,1:T(8,128)} %fusion.5) | copy-start | bytes 1572868
  89.8 3.3 %copy-start.6 = (f32[1024,1]{0,1:T(1,128)S(1)}, f32[1024,1]{0,1:T(1,128)}, u32[]{:S(2)}) copy-start(f32[1024,1]{0,1:T(1,128)} %get-tuple-element.51) | copy-start | bytes 12292
  91.9 1.6 %copy-start.4 = (f32[1024,128]{0,1:T(8,128)S(1)}, f32[1024,128]{0,1:T(8,128)}, u32[]{:S(2)}) copy-start(f32[1024,128]{0,1:T(8,128)} %fusion.4) | copy-start | bytes 1572868
  93.1 1.0 copy-start.5

commit v5 on v4

--- a/solution.py
+++ b/solution.py
@@ -124,16 +124,9 @@
     def cols(array, h):
         return array[:, h * size : (h + 1) * size]
 
-    state = jnp.stack(
-        [
-            jnp.dot(
-                (cols(keys, h).astype(F32) * jnp.exp(last[h] - cum[:, h])[:, None]).T,
-                cols(values, h).astype(F32),
-                precision=HI,
-            )
-            for h in range(heads)
-        ]
-    )
+    k3 = keys.reshape(count, heads, size).astype(F32)
+    keyed = k3 * jnp.exp(last[None, :] - cum)[:, :, None]
+    state = jnp.einsum("thd,the->hde", keyed, values.reshape(count, heads, size).astype(F32), precision=HI)
 
     carried = carried_state(last, state)
 

time: 140 us -> 144 us (1.029)
  other arithmetic: 9.58 us -> 16 us
  matrix products: 22.1 us -> 16 us
  local copies, waits for them, and re-layouts: 6.74 us -> 8.96 us
  starting transfers between devices: 50 us -> 52 us
    dot_general x4 -> x1, matrix products: 6.99 us -> 2.42 us  [body(): jnp.einsum('thd,the->hde', keyed, values.reshape(count, heads, size).asty...]
    exp x1, other arithmetic: 3.16 us -> 0.09 us  [body(): keyed = k3 * jnp.exp(last[None, :] - cum)[:, :, None]]
    add x3, other arithmetic: 0.22 us -> 3 us  [exclusive_scan(): cur = jnp.exp(cur_log)[:, None, None] * got + cur]
    dot_general x4, matrix products: 12.7 us -> 10.5 us  [inner_head(): return jnp.dot(weights, vh, preferred_element_type=F32)]
    concatenate x6, other arithmetic: 0.06 us -> 2.05 us  [pack(): return jnp.concatenate([state, row], axis=1)]
    ppermute x6, starting transfers between devices: 14.5 us -> 16.4 us  [shifted(): out.append(lax.ppermute(x, axis, [(j, (j + s) % n) for j in range(n)]))]
    convert_element_type x0 -> x1, local copies, waits for them, and re-layouts: none -> 1.49 us  [body(): k3 = keys.reshape(count, heads, size).astype(F32)]
    unnamed x20 -> x24, local copies, waits for them, and re-layouts: 2.2 us -> 3 us
  transfers between devices with their start and end apart: 12 -> 12, of which waited for: 6 -> 6; matrix products, arithmetic and copies ran while one was open for 10% -> 9% of each run, Pallas kernels for 0% -> 0%
where the time goes in v5:
time: 144 us; the launch traced here: 143 us
  starting transfers between devices  52 us (36%)
  blocking collectives  40.5 us (28%)
  other arithmetic  16 us (11%)
  matrix products  16 us (11%)
  waiting for transfers between devices  9.58 us (7%)
  local copies, waits for them, and re-layouts  8.96 us (6%)
    all_to_all x1, blocking collectives, body(): lax.all_to_all(payload, 'head', split_axis=0, concat_axis=0, tiled=True)  40.5 us
    ppermute x4, starting transfers between devices, shift(): return lax.ppermute(packed, axis, [(j, j + d) for j in range(n - d)])  17.8 us
    ppermute x6, starting transfers between devices, shifted(): out.append(lax.ppermute(x, axis, [(j, (j + s) % n) for j in range(n)]))  16.4 us
    dot_general x4, matrix products, inner_head(): return jnp.dot(weights, vh, preferred_element_type=F32)  10.5 us
    ppermute x1, starting transfers between devices, carried_state(): pair = unpack(lax.ppermute(pack(L, S), 'cc', [(0, 1), (1, 0)]))  8.92 us
    ppermute x1, starting transfers between devices, carried_state(): other = lax.ppermute(chip_before, 'cc', [(0, 1), (1, 0)])  8.9 us
    ppermute x6, waiting for transfers between devices, shifted(): out.append(lax.ppermute(x, axis, [(j, (j + s) % n) for j in range(n)]))  6.88 us
    dot_general x4, matrix products, body(): across = jnp.dot(qh.astype(F32), carried[h], precision=HI)  3.05 us
  transfers between devices with their start and end apart: 12, of which 6 were waited for; matrix products, arithmetic and copies ran while one was open for 9% of the time, Pallas kernels for 0%

profile of v5, /device:TPU:1, one launch (start us, length us, event | category | flops | bytes accessed | tf_op | source)
XLA Modules:
  0.0 143.3 jit_solution(6076015858392851521)
XLA Ops:
  0.7 1.1 reduce-window.6
  2.6 1.5 %copy.47 = f32[1024,512]{0,1:T(8,128)S(1)} copy(bf16[1024,512]{1,0:T(8,128)(2,1)} %param.7) | data formatting | bytes 3145728 | tf_op jit(solution)/shard_map/convert_element_type | solution.py:127
  4.0 2.4 %fusion.3 = f32[4,128,128]{2,1,0:T(8,128)S(1)} fusion(f32[1024,4,128]{0,2,1:T(8,128)S(1)} %bitcast.87, f32[1024,4]{0,1:T(4,128)S(1)} %subtract_exponential_fusion, bf16[1024,512]{1,0:T(8,128)(2,1)} %param.8), kind=kOutput, calls=%fused_computation.11 | convolution fusion | flops 805830656 | bytes 3424256 | tf_op jit(solution)/shard_map/thd,the->hde/dot_general | solution.py:129
  6.6 8.9 %collective-permute-start = (f32[4,129,128]{2,1,0:T(8,128)S(1)}, f32[4,129,128]{2,1,0:T(8,128)S(1)}, u32[]{:S(2)}, u32[]{:S(2)}) collective-permute-start(f32[4,129,128]{2,1,0:T(8,128)S(1)} %pad_maximum_fusion.1), channel_id=1, source_target_pairs={{0,8},{8,0},{1,9},{9,1},{2,10},{10,2},{3,11},{11,3},{4,12},{12,4},... | collective-permute-start | bytes 792584 | tf_op jit(solution)/shard_map/ppermute | solution.py:73
  15.5 1.2 collective-permute-done
  17.8 1.9 %collective-permute-start.3 = (f32[2,129,128]{2,1,0:T(8,128)S(1)}, f32[2,129,128]{2,1,0:T(8,128)S(1)}, u32[]{:S(2)}, u32[]{:S(2)}) collective-permute-start(f32[2,129,128]{2,1,0:T(8,128)S(1)} %pad_maximum_fusion.2), channel_id=1, source_target_pairs={{0,48},{16,0},{32,16},{48,32},{1,49},{17,1},{33,17},{49,33},{2,50}... | collective-permute-start | bytes 396296 | tf_op jit(solution)/shard_map/ppermute | solution.py:33
  19.7 3.4 %collective-permute-start.1 = (f32[2,129,128]{2,1,0:T(8,128)S(1)}, f32[2,129,128]{2,1,0:T(8,128)S(1)}, u32[]{:S(2)}, u32[]{:S(2)}) collective-permute-start(f32[2,129,128]{2,1,0:T(8,128)S(1)} %pad_maximum_fusion.2), channel_id=1, source_target_pairs={{0,16},{16,32},{32,48},{48,0},{1,17},{17,33},{33,49},{49,1},{2,18}... | collective-permute-start | bytes 396296 | tf_op jit(solution)/shard_map/ppermute | solution.py:33
  23.1 1.9 %collective-permute-start.2 = (f32[2,129,128]{2,1,0:T(8,128)S(1)}, f32[2,129,128]{2,1,0:T(8,128)S(1)}, u32[]{:S(2)}, u32[]{:S(2)}) collective-permute-start(f32[2,129,128]{2,1,0:T(8,128)S(1)} %pad_maximum_fusion.2), channel_id=1, source_target_pairs={{0,32},{16,48},{32,0},{48,16},{1,33},{17,49},{33,1},{49,17},{2,34}... | collective-permute-start | bytes 396296 | tf_op jit(solution)/shard_map/ppermute | solution.py:33
  25.0 2.7 %collective-permute-done.1 = f32[2,129,128]{2,1,0:T(8,128)S(1)} collective-permute-done((f32[2,129,128]{2,1,0:T(8,128)S(1)}, f32[2,129,128]{2,1,0:T(8,128)S(1)}, u32[]{:S(2)}, u32[]{:S(2)}) %collective-permute-start.1) | collective-permute-done | bytes 132128 | tf_op jit(solution)/shard_map/ppermute | solution.py:33
  27.7 3.0 %collective-permute-done.2 = f32[2,129,128]{2,1,0:T(8,128)S(1)} collective-permute-done((f32[2,129,128]{2,1,0:T(8,128)S(1)}, f32[2,129,128]{2,1,0:T(8,128)S(1)}, u32[]{:S(2)}, u32[]{:S(2)}) %collective-permute-start.2) | collective-permute-done | bytes 132128 | tf_op jit(solution)/shard_map/ppermute | solution.py:33
  32.8 1.3 collective-permute-start.4
  35.4 3.6 %collective-permute-start.5 = (f32[2,33,128]{2,1,0:T(8,128)S(1)}, f32[2,33,128]{2,1,0:T(8,128)S(1)}, u32[]{:S(2)}, u32[]{:S(2)}) collective-permute-start(f32[2,33,128]{2,1,0:T(8,128)S(1)} %pad_maximum_fusion.4), channel_id=1, source_target_pairs={{0,64},{64,128},{128,192},{192,256},{256,320},{320,384},{384,448},... | collective-permute-start | bytes 101384 | tf_op jit(solution)/shard_map/ppermute | solution.py:55
  41.5 4.0 %collective-permute-start.6 = (f32[2,33,128]{2,1,0:T(8,128)}, f32[2,33,128]{2,1,0:T(8,128)}, u32[]{:S(2)}, u32[]{:S(2)}) collective-permute-start(f32[2,33,128]{2,1,0:T(8,128)} %pad_maximum_fusion.5), channel_id=1, source_target_pairs={{0,128},{64,192},{128,256},{192,320},{256,384},{320,448},{1,129},{... | collective-permute-start | bytes 101384 | tf_op jit(solution)/shard_map/ppermute | solution.py:55
  45.5 3.2 %fusion.5 = f32[1024,128]{0,1:T(8,128)} fusion(f32[1024]{0:T(1024)} %bitcast.103, bf16[1024,512]{1,0:T(8,128)(2,1)} %param.8, bf16[1024,512]{1,0:T(8,128)(2,1)S(1)} %copy-done, bf16[1024,512]{1,0:T(8,128)(2,1)S(1)} %copy-done.1), kind=kOutput, calls=%fused_computation.13 | convolution fusion | flops 543162368 | bytes 1318912 | tf_op jit(solution)/shard_map/dot_general | solution.py:114
  48.7 1.4 exponential_reduce_fusion.1
  50.1 1.5 %fusion.51 = f32[2,32,128]{2,1,0:T(8,128)} fusion(f32[2,32,128]{2,1,0:T(8,128)} %copy-done.7, f32[2,33,128]{2,1,0:T(8,128)} %collective-permute-done.6, f32[2]{0:T(128)S(1)} %get-tuple-element.16), kind=kLoop, calls=%fused_computation.76 | loop fusion | flops 16384 | bytes 98312 | tf_op jit(solution)/shard_map/add | solution.py:61
  51.6 1.4 pad_maximum_fusion.6
  53.0 8.9 %collective-permute-start.7 = (f32[2,33,128]{2,1,0:T(8,128)}, f32[2,33,128]{2,1,0:T(8,128)}, u32[]{:S(2)}, u32[]{:S(2)}) collective-permute-start(f32[2,33,128]{2,1,0:T(8,128)} %pad_maximum_fusion.6), channel_id=1, source_target_pairs={{0,256},{64,320},{128,384},{192,448},{1,257},{65,321},{129,385},{1... | collective-permute-start | bytes 101384 | tf_op jit(solution)/shard_map/ppermute | solution.py:55
  61.9 2.9 %fusion.6 = f32[1024,128]{0,1:T(8,128)} fusion(f32[1024]{0:T(1024)} %bitcast.102, bf16[1024,512]{1,0:T(8,128)(2,1)S(1)} %copy-done.2, bf16[1024,512]{1,0:T(8,128)(2,1)S(1)} %copy-done, bf16[1024,512]{1,0:T(8,128)(2,1)S(1)} %copy-done.1), kind=kOutput, calls=%fused_computation.14 | convolution fusion | flops 543162368 | bytes 1318912 | tf_op jit(solution)/shard_map/dot_general | solution.py:114
  64.8 1.5 %fusion.50 = f32[2,32,128]{2,1,0:T(8,128)} fusion(f32[2,32,128]{2,1,0:T(8,128)} %fusion.51, f32[2,33,128]{2,1,0:T(8,128)} %collective-permute-done.7, f32[2]{0:T(128)} %get-tuple-element.10), kind=kLoop, calls=%fused_computation.74 | loop fusion | flops 16384 | bytes 98312 | tf_op jit(solution)/shard_map/add | solution.py:61
  66.3 4.1 %collective-permute-start.10 = (f32[2,32,128]{2,1,0:T(8,128)}, f32[2,32,128]{2,1,0:T(8,128)}, u32[]{:S(2)}, u32[]{:S(2)}) collective-permute-start(f32[2,32,128]{2,1,0:T(8,128)} %fusion.50), channel_id=1, source_target_pairs={{0,48},{16,0},{32,16},{48,32},{1,49},{17,1},{33,17},{49,33},{2,50}... | collective-permute-start | bytes 98312 | tf_op jit(solution)/shard_map/ppermute | solution.py:33
  70.4 1.9 %collective-permute-start.8 = (f32[2,32,128]{2,1,0:T(8,128)}, f32[2,32,128]{2,1,0:T(8,128)}, u32[]{:S(2)}, u32[]{:S(2)}) collective-permute-start(f32[2,32,128]{2,1,0:T(8,128)} %fusion.50), channel_id=1, source_target_pairs={{0,16},{16,32},{32,48},{48,0},{1,17},{17,33},{33,49},{49,1},{2,18}... | collective-permute-start | bytes 98312 | tf_op jit(solution)/shard_map/ppermute | solution.py:33
  72.3 3.1 %collective-permute-start.9 = (f32[2,32,128]{2,1,0:T(8,128)}, f32[2,32,128]{2,1,0:T(8,128)}, u32[]{:S(2)}, u32[]{:S(2)}) collective-permute-start(f32[2,32,128]{2,1,0:T(8,128)} %fusion.50), channel_id=1, source_target_pairs={{0,32},{16,48},{32,0},{48,16},{1,33},{17,49},{33,1},{49,17},{2,34}... | collective-permute-start | bytes 98312 | tf_op jit(solution)/shard_map/ppermute | solution.py:33
  75.4 2.2 %fusion.7 = f32[1024,128]{0,1:T(8,128)} fusion(f32[1024]{0:T(1024)S(1)} %bitcast.101, bf16[1024,512]{1,0:T(8,128)(2,1)S(1)} %copy-done.2, bf16[1024,512]{1,0:T(8,128)(2,1)S(1)} %copy-done, bf16[1024,512]{1,0:T(8,128)(2,1)S(1)} %copy-done.1), kind=kOutput, calls=%fused_computation.15 | convolution fusion | flops 543162368 | bytes 1318912 | tf_op jit(solution)/shard_map/dot_general | solution.py:114
  77.6 1.2 collective-permute-done.9
  79.7 1.4 fusion.49
  81.0 8.9 %collective-permute-start.11 = (f32[2,128,128]{2,1,0:T(8,128)}, f32[2,128,128]{2,1,0:T(8,128)}, u32[]{:S(2)}, u32[]{:S(2)}) collective-permute-start(f32[2,128,128]{2,1,0:T(8,128)} %fusion.49), channel_id=1, source_target_pairs={{0,8},{8,0},{1,9},{9,1},{2,10},{10,2},{3,11},{11,3},{4,12},{12,4},... | collective-permute-start | bytes 393224 | tf_op jit(solution)/shard_map/ppermute | solution.py:100
  89.9 2.2 %fusion.8 = f32[1024,128]{0,1:T(8,128)} fusion(f32[1024]{0:T(1024)S(1)} %bitcast.100, bf16[1024,512]{1,0:T(8,128)(2,1)S(1)} %copy-done.2, bf16[1024,512]{1,0:T(8,128)(2,1)S(1)} %copy-done, bf16[1024,512]{1,0:T(8,128)(2,1)S(1)} %copy-done.1), kind=kOutput, calls=%fused_computation.16 | convolution fusion | flops 543162368 | bytes 1318912 | tf_op jit(solution)/shard_map/dot_general | solution.py:114
  92.1 1.6 %copy.40 = bf16[1024,512]{0,1:T(8,128)(2,1)S(1)} copy(bf16[1024,512]{1,0:T(8,128)(2,1)} %param.10) | data formatting | bytes 2097152 | tf_op args[4]
  94.5 1.3 add_select_fusion
  100.5 40.5 %all_to_all.5 = bf16[8,129,512]{2,1,0:T(8,128)(2,1)S(1)} all-to-all(bf16[8,129,512]{2,1,0:T(8,128)(2,1)S(1)} %maximum_maximum_fusion), channel_id=1, replica_groups=mesh['cy'=8,'cx'=4,'cc'=2,'head'=8] {'head'}, dimensions={0} | all-to-all | bytes 2113536 | tf_op jit(solution)/shard_map/all_to_all | solution.py:158
  142.0 1.3 copy.46
  (84 shorter events, 15.8 us)
Async XLA Ops:
  6.5 39.0 %copy-start = (bf16[1024,512]{1,0:T(8,128)(2,1)S(1)}, bf16[1024,512]{1,0:T(8,128)(2,1)}, u32[]{:S(2)}) copy-start(bf16[1024,512]{1,0:T(8,128)(2,1)} %param.7) | copy-start | bytes 3145732
  6.5 39.0 %copy-start.1 = (bf16[1024,512]{1,0:T(8,128)(2,1)S(1)}, bf16[1024,512]{1,0:T(8,128)(2,1)}, u32[]{:S(2)}) copy-start(bf16[1024,512]{1,0:T(8,128)(2,1)} %param.6) | copy-start | bytes 3145732
  6.6 10.1 %collective-permute-start = (f32[4,129,128]{2,1,0:T(8,128)S(1)}, f32[4,129,128]{2,1,0:T(8,128)S(1)}, u32[]{:S(2)}, u32[]{:S(2)}) collective-permute-start(f32[4,129,128]{2,1,0:T(8,128)S(1)} %pad_maximum_fusion.1), channel_id=1, source_target_pairs={{0,8},{8,0},{1,9},{9,1},{2,10},{10,2},{3,11},{11,3},{4,12},{12,4},... | collective-permute-start | bytes 792584 | tf_op jit(solution)/shard_map/ppermute | solution.py:73
  17.8 7.2 %collective-permute-start.3 = (f32[2,129,128]{2,1,0:T(8,128)S(1)}, f32[2,129,128]{2,1,0:T(8,128)S(1)}, u32[]{:S(2)}, u32[]{:S(2)}) collective-permute-start(f32[2,129,128]{2,1,0:T(8,128)S(1)} %pad_maximum_fusion.2), channel_id=1, source_target_pairs={{0,48},{16,0},{32,16},{48,32},{1,49},{17,1},{33,17},{49,33},{2,50}... | collective-permute-start | bytes 396296 | tf_op jit(solution)/shard_map/ppermute | solution.py:33
  19.7 8.0 %collective-permute-start.1 = (f32[2,129,128]{2,1,0:T(8,128)S(1)}, f32[2,129,128]{2,1,0:T(8,128)S(1)}, u32[]{:S(2)}, u32[]{:S(2)}) collective-permute-start(f32[2,129,128]{2,1,0:T(8,128)S(1)} %pad_maximum_fusion.2), channel_id=1, source_target_pairs={{0,16},{16,32},{32,48},{48,0},{1,17},{17,33},{33,49},{49,1},{2,18}... | collective-permute-start | bytes 396296 | tf_op jit(solution)/shard_map/ppermute | solution.py:33
  23.1 7.6 %collective-permute-start.2 = (f32[2,129,128]{2,1,0:T(8,128)S(1)}, f32[2,129,128]{2,1,0:T(8,128)S(1)}, u32[]{:S(2)}, u32[]{:S(2)}) collective-permute-start(f32[2,129,128]{2,1,0:T(8,128)S(1)} %pad_maximum_fusion.2), channel_id=1, source_target_pairs={{0,32},{16,48},{32,0},{48,16},{1,33},{17,49},{33,1},{49,17},{2,34}... | collective-permute-start | bytes 396296 | tf_op jit(solution)/shard_map/ppermute | solution.py:33
  27.7 3.9 %copy-start.8 = (f32[2,129,128]{2,1,0:T(8,128)}, f32[2,129,128]{2,1,0:T(8,128)S(1)}, u32[]{:S(2)}) copy-start(f32[2,129,128]{2,1,0:T(8,128)S(1)} %collective-permute-done.1) | copy-start | bytes 396292
  30.7 0.9 copy-start.9
  32.8 2.4 %collective-permute-start.4 = (f32[2,33,128]{2,1,0:T(8,128)S(1)}, f32[2,33,128]{2,1,0:T(8,128)S(1)}, u32[]{:S(2)}, u32[]{:S(2)}) collective-permute-start(f32[2,33,128]{2,1,0:T(8,128)S(1)} %pad_maximum_fusion.3), channel_id=1, source_target_pairs={{0,64},{64,128},{128,192},{192,256},{256,320},{320,384},{384,448},... | collective-permute-start | bytes 101384 | tf_op jit(solution)/shard_map/ppermute | solution.py:55
  35.4 4.7 %collective-permute-start.5 = (f32[2,33,128]{2,1,0:T(8,128)S(1)}, f32[2,33,128]{2,1,0:T(8,128)S(1)}, u32[]{:S(2)}, u32[]{:S(2)}) collective-permute-start(f32[2,33,128]{2,1,0:T(8,128)S(1)} %pad_maximum_fusion.4), channel_id=1, source_target_pairs={{0,64},{64,128},{128,192},{192,256},{256,320},{320,384},{384,448},... | collective-permute-start | bytes 101384 | tf_op jit(solution)/shard_map/ppermute | solution.py:55
  40.8 4.7 %copy-start.7 = (f32[2,32,128]{2,1,0:T(8,128)}, f32[2,32,128]{2,1,0:T(8,128)S(1)}, u32[]{:S(2)}) copy-start(f32[2,32,128]{2,1,0:T(8,128)S(1)} %fusion.52) | copy-start | bytes 98308
  41.5 7.2 %collective-permute-start.6 = (f32[2,33,128]{2,1,0:T(8,128)}, f32[2,33,128]{2,1,0:T(8,128)}, u32[]{:S(2)}, u32[]{:S(2)}) collective-permute-start(f32[2,33,128]{2,1,0:T(8,128)} %pad_maximum_fusion.5), channel_id=1, source_target_pairs={{0,128},{64,192},{128,256},{192,320},{256,384},{320,448},{1,129},{... | collective-permute-start | bytes 101384 | tf_op jit(solution)/shard_map/ppermute | solution.py:55
  45.5 16.4 %copy-start.2 = (bf16[1024,512]{1,0:T(8,128)(2,1)S(1)}, bf16[1024,512]{1,0:T(8,128)(2,1)}, u32[]{:S(2)}) copy-start(bf16[1024,512]{1,0:T(8,128)(2,1)} %param.8) | copy-start | bytes 3145732
  53.0 11.8 %collective-permute-start.7 = (f32[2,33,128]{2,1,0:T(8,128)}, f32[2,33,128]{2,1,0:T(8,128)}, u32[]{:S(2)}, u32[]{:S(2)}) collective-permute-start(f32[2,33,128]{2,1,0:T(8,128)} %pad_maximum_fusion.6), channel_id=1, source_target_pairs={{0,256},{64,320},{128,384},{192,448},{1,257},{65,321},{129,385},{1... | collective-permute-start | bytes 101384 | tf_op jit(solution)/shard_map/ppermute | solution.py:55
  66.3 11.4 %collective-permute-start.10 = (f32[2,32,128]{2,1,0:T(8,128)}, f32[2,32,128]{2,1,0:T(8,128)}, u32[]{:S(2)}, u32[]{:S(2)}) collective-permute-start(f32[2,32,128]{2,1,0:T(8,128)} %fusion.50), channel_id=1, source_target_pairs={{0,48},{16,0},{32,16},{48,32},{1,49},{17,1},{33,17},{49,33},{2,50}... | collective-permute-start | bytes 98312 | tf_op jit(solution)/shard_map/ppermute | solution.py:33
  70.4 7.2 %collective-permute-start.8 = (f32[2,32,128]{2,1,0:T(8,128)}, f32[2,32,128]{2,1,0:T(8,128)}, u32[]{:S(2)}, u32[]{:S(2)}) collective-permute-start(f32[2,32,128]{2,1,0:T(8,128)} %fusion.50), channel_id=1, source_target_pairs={{0,16},{16,32},{32,48},{48,0},{1,17},{17,33},{33,49},{49,1},{2,18}... | collective-permute-start | bytes 98312 | tf_op jit(solution)/shard_map/ppermute | solution.py:33
  72.3 6.5 %collective-permute-start.9 = (f32[2,32,128]{2,1,0:T(8,128)}, f32[2,32,128]{2,1,0:T(8,128)}, u32[]{:S(2)}, u32[]{:S(2)}) collective-permute-start(f32[2,32,128]{2,1,0:T(8,128)} %fusion.50), channel_id=1, source_target_pairs={{0,32},{16,48},{32,0},{48,16},{1,33},{17,49},{33,1},{49,17},{2,34}... | collective-permute-start | bytes 98312 | tf_op jit(solution)/shard_map/ppermute | solution.py:33
  81.0 13.5 %collective-permute-start.11 = (f32[2,128,128]{2,1,0:T(8,128)}, f32[2,128,128]{2,1,0:T(8,128)}, u32[]{:S(2)}, u32[]{:S(2)}) collective-permute-start(f32[2,128,128]{2,1,0:T(8,128)} %fusion.49), channel_id=1, source_target_pairs={{0,8},{8,0},{1,9},{9,1},{2,10},{10,2},{3,11},{11,3},{4,12},{12,4},... | collective-permute-start | bytes 393224 | tf_op jit(solution)/shard_map/ppermute | solution.py:100
  92.1 3.7 %copy-start.3 = (f32[1024,128]{0,1:T(8,128)S(1)}, f32[1024,128]{0,1:T(8,128)}, u32[]{:S(2)}) copy-start(f32[1024,128]{0,1:T(8,128)} %fusion.5) | copy-start | bytes 1572868
  92.1 4.8 %copy-start.4 = (f32[1024,128]{0,1:T(8,128)S(1)}, f32[1024,128]{0,1:T(8,128)}, u32[]{:S(2)}) copy-start(f32[1024,128]{0,1:T(8,128)} %fusion.6) | copy-start | bytes 1572868
  93.7 4.4 %copy-start.5 = (f32[1024,128]{0,1:T(8,128)S(1)}, f32[1024,128]{0,1:T(8,128)}, u32[]{:S(2)}) copy-start(f32[1024,128]{0,1:T(8,128)} %fusion.7) | copy-start | bytes 1572868
  94.5 4.0 %copy-start.6 = (f32[1024,128]{0,1:T(8,128)S(1)}, f32[1024,128]{0,1:T(8,128)}, u32[]{:S(2)}) copy-start(f32[1024,128]{0,1:T(8,128)} %fusion.8) | copy-start | bytes 1572868

commit v6 on v4

--- a/solution.py
+++ b/solution.py
@@ -54,8 +54,12 @@
     def shift(packed, d):
         return lax.ppermute(packed, axis, [(j, j + d) for j in range(n - d)])
 
-    cur_log, cur = unpack(shift(pack(log, state), 1))
-    d = 1
+    packed = pack(log, state)
+    one_log, one = unpack(shift(packed, 1))
+    two_log, two = unpack(shift(packed, 2))
+    cur = jnp.exp(one_log)[:, None, None] * two + one
+    cur_log = one_log + two_log
+    d = 2
     while d < n:
         got_log, got = unpack(shift(pack(cur_log, cur), d))
         cur = jnp.exp(cur_log)[:, None, None] * got + cur

time: 140 us -> 135 us (0.964)
  starting transfers between devices: 50 us -> 46.7 us
    ppermute x4, starting transfers between devices: 18.3 us -> 16.3 us  [shift(): return lax.ppermute(packed, axis, [(j, j + d) for j in range(n - d)])]
  transfers between devices with their start and end apart: 12 -> 12, of which waited for: 6 -> 5; matrix products, arithmetic and copies ran while one was open for 10% -> 11% of each run, Pallas kernels for 0% -> 0%
where the time goes in v6:
time: 135 us; the launch traced here: 134 us
  starting transfers between devices  46.7 us (35%)
  blocking collectives  40.5 us (30%)
  matrix products  22.1 us (16%)
  other arithmetic  9.62 us (7%)
  waiting for transfers between devices  8.58 us (6%)
  local copies, waits for them, and re-layouts  6.54 us (5%)
    all_to_all x1, blocking collectives, body(): lax.all_to_all(payload, 'head', split_axis=0, concat_axis=0, tiled=True)  40.5 us
    ppermute x4, starting transfers between devices, shift(): return lax.ppermute(packed, axis, [(j, j + d) for j in range(n - d)])  16.3 us
    ppermute x6, starting transfers between devices, shifted(): out.append(lax.ppermute(x, axis, [(j, (j + s) % n) for j in range(n)]))  14.5 us
    dot_general x4, matrix products, inner_head(): return jnp.dot(weights, vh, preferred_element_type=F32)  12.7 us
    ppermute x1, starting transfers between devices, carried_state(): pair = unpack(lax.ppermute(pack(L, S), 'cc', [(0, 1), (1, 0)]))  8.79 us
    ppermute x1, starting transfers between devices, carried_state(): other = lax.ppermute(chip_before, 'cc', [(0, 1), (1, 0)])  7.08 us
    dot_general x4, matrix products, body(): jnp.dot((cols(keys, h).astype(F32) * jnp.exp(last[h] - cum[:, h])[:, None...  6.97 us
    ppermute x6, waiting for transfers between devices, shifted(): out.append(lax.ppermute(x, axis, [(j, (j + s) % n) for j in range(n)]))  6.34 us
  transfers between devices with their start and end apart: 12, of which 5 were waited for; matrix products, arithmetic and copies ran while one was open for 11% of the time, Pallas kernels for 0%

profile of v6, /device:TPU:1, one launch (start us, length us, event | category | flops | bytes accessed | tf_op | source)
XLA Modules:
  0.0 134.4 jit_solution(14382593386045042674)
XLA Ops:
  0.0 0.8 copy.47
  0.8 1.1 reduce-window.6
  3.2 3.2 %slice_exponential_fusion.3 = (f32[1024,1]{0,1:T(1,128)S(1)}, f32[1024,1]{0,1:T(1,128)S(1)}, f32[1024,1]{0,1:T(1,128)S(1)}, f32[1024,1]{0,1:T(1,128)S(1)}, f32[1...) fusion(f32[1024,4]{0,1:T(4,128)S(1)} %bitcast.95, ...), kind=kLoop, calls=%fused_computation.172 | loop fusion | flops 4096 | bytes 65552 | tf_op jit(solution)/shard_map/exp | solution.py:149
  6.4 1.8 %convolution_bitcast_fusion.3 = f32[1,128,128]{2,1,0:T(8,128)S(1)} fusion(f32[1024]{0:T(1024)S(1)} %bitcast.111, bf16[1024,512]{1,0:T(8,128)(2,1)} %param.8, bf16[1024,512]{1,0:T(8,128)(2,1)} %param.7), kind=kOutput, calls=%fused_computation.34 | convolution fusion | flops 201588736 | bytes 593920 | tf_op jit(solution)/shard_map/dot_general | solution.py:133
  8.2 1.8 %convolution_bitcast_fusion.2 = f32[1,128,128]{2,1,0:T(8,128)S(1)} fusion(f32[1024]{0:T(1024)S(1)} %bitcast.110, bf16[1024,512]{1,0:T(8,128)(2,1)} %param.8, bf16[1024,512]{1,0:T(8,128)(2,1)} %param.7), kind=kOutput, calls=%fused_computation.33 | convolution fusion | flops 201588736 | bytes 593920 | tf_op jit(solution)/shard_map/dot_general | solution.py:133
  10.0 1.7 %convolution_bitcast_fusion.1 = f32[1,128,128]{2,1,0:T(8,128)S(1)} fusion(f32[1024]{0:T(1024)S(1)} %bitcast.109, bf16[1024,512]{1,0:T(8,128)(2,1)S(1)} %copy-done.7, bf16[1024,512]{1,0:T(8,128)(2,1)} %param.7), kind=kOutput, calls=%fused_computation.32 | convolution fusion | flops 201588736 | bytes 593920 | tf_op jit(solution)/shard_map/dot_general | solution.py:133
  11.7 1.7 %convolution_bitcast_fusion = f32[1,128,128]{2,1,0:T(8,128)S(1)} fusion(f32[1024]{0:T(1024)S(1)} %bitcast.108, bf16[1024,512]{1,0:T(8,128)(2,1)S(1)} %copy-done.7, bf16[1024,512]{1,0:T(8,128)(2,1)} %param.7), kind=kOutput, calls=%fused_computation.31 | convolution fusion | flops 201588736 | bytes 593920 | tf_op jit(solution)/shard_map/dot_general | solution.py:133
  13.5 8.8 %collective-permute-start = (f32[4,129,128]{2,1,0:T(8,128)S(1)}, f32[4,129,128]{2,1,0:T(8,128)S(1)}, u32[]{:S(2)}, u32[]{:S(2)}) collective-permute-start(f32[4,129,128]{2,1,0:T(8,128)S(1)} %pad_maximum_fusion.1), channel_id=1, source_target_pairs={{0,8},{8,0},{1,9},{9,1},{2,10},{10,2},{3,11},{11,3},{4,12},{12,4},... | collective-permute-start | bytes 792584 | tf_op jit(solution)/shard_map/ppermute | solution.py:77
  22.3 1.2 collective-permute-done
  24.6 2.1 %collective-permute-start.3 = (f32[2,129,128]{2,1,0:T(8,128)S(1)}, f32[2,129,128]{2,1,0:T(8,128)S(1)}, u32[]{:S(2)}, u32[]{:S(2)}) collective-permute-start(f32[2,129,128]{2,1,0:T(8,128)S(1)} %pad_maximum_fusion.3), channel_id=1, source_target_pairs={{0,48},{16,0},{32,16},{48,32},{1,49},{17,1},{33,17},{49,33},{2,50}... | collective-permute-start | bytes 396296 | tf_op jit(solution)/shard_map/ppermute | solution.py:33
  26.6 1.9 %collective-permute-start.2 = (f32[2,129,128]{2,1,0:T(8,128)S(1)}, f32[2,129,128]{2,1,0:T(8,128)S(1)}, u32[]{:S(2)}, u32[]{:S(2)}) collective-permute-start(f32[2,129,128]{2,1,0:T(8,128)S(1)} %pad_maximum_fusion.3), channel_id=1, source_target_pairs={{0,32},{16,48},{32,0},{48,16},{1,33},{17,49},{33,1},{49,17},{2,34}... | collective-permute-start | bytes 396296 | tf_op jit(solution)/shard_map/ppermute | solution.py:33
  28.6 3.4 %collective-permute-start.1 = (f32[2,129,128]{2,1,0:T(8,128)S(1)}, f32[2,129,128]{2,1,0:T(8,128)S(1)}, u32[]{:S(2)}, u32[]{:S(2)}) collective-permute-start(f32[2,129,128]{2,1,0:T(8,128)S(1)} %pad_maximum_fusion.3), channel_id=1, source_target_pairs={{0,16},{16,32},{32,48},{48,0},{1,17},{17,33},{33,49},{49,1},{2,18}... | collective-permute-start | bytes 396296 | tf_op jit(solution)/shard_map/ppermute | solution.py:33
  31.9 3.0 %collective-permute-done.2 = f32[2,129,128]{2,1,0:T(8,128)S(1)} collective-permute-done((f32[2,129,128]{2,1,0:T(8,128)S(1)}, f32[2,129,128]{2,1,0:T(8,128)S(1)}, u32[]{:S(2)}, u32[]{:S(2)}) %collective-permute-start.2) | collective-permute-done | bytes 132128 | tf_op jit(solution)/shard_map/ppermute | solution.py:33
  34.9 2.8 %collective-permute-done.1 = f32[2,129,128]{2,1,0:T(8,128)S(1)} collective-permute-done((f32[2,129,128]{2,1,0:T(8,128)S(1)}, f32[2,129,128]{2,1,0:T(8,128)S(1)}, u32[]{:S(2)}, u32[]{:S(2)}) %collective-permute-start.1) | collective-permute-done | bytes 132128 | tf_op jit(solution)/shard_map/ppermute | solution.py:33
  38.4 1.6 %collective-permute-start.5 = (f32[2,33,128]{2,1,0:T(8,128)S(1)}, f32[2,33,128]{2,1,0:T(8,128)S(1)}, u32[]{:S(2)}, u32[]{:S(2)}) collective-permute-start(f32[2,33,128]{2,1,0:T(8,128)S(1)} %pad_maximum_fusion.4), channel_id=1, source_target_pairs={{0,128},{64,192},{128,256},{192,320},{256,384},{320,448},{1,129},{... | collective-permute-start | bytes 101384 | tf_op jit(solution)/shard_map/ppermute | solution.py:55
  40.0 3.2 %collective-permute-start.4 = (f32[2,33,128]{2,1,0:T(8,128)S(1)}, f32[2,33,128]{2,1,0:T(8,128)S(1)}, u32[]{:S(2)}, u32[]{:S(2)}) collective-permute-start(f32[2,33,128]{2,1,0:T(8,128)S(1)} %pad_maximum_fusion.4), channel_id=1, source_target_pairs={{0,64},{64,128},{128,192},{192,256},{256,320},{320,384},{384,448},... | collective-permute-start | bytes 101384 | tf_op jit(solution)/shard_map/ppermute | solution.py:55
  43.2 1.1 collective-permute-done.4
  44.5 5.9 %collective-permute-start.6 = (f32[2,33,128]{2,1,0:T(8,128)S(1)}, f32[2,33,128]{2,1,0:T(8,128)S(1)}, u32[]{:S(2)}, u32[]{:S(2)}) collective-permute-start(f32[2,33,128]{2,1,0:T(8,128)S(1)} %pad_maximum_fusion.5), channel_id=1, source_target_pairs={{0,128},{64,192},{128,256},{192,320},{256,384},{320,448},{1,129},{... | collective-permute-start | bytes 101384 | tf_op jit(solution)/shard_map/ppermute | solution.py:55
  50.4 3.1 %fusion.6 = f32[1024,128]{0,1:T(8,128)} fusion(f32[1024]{0:T(1024)S(1)} %bitcast.107, bf16[1024,512]{1,0:T(8,128)(2,1)S(1)} %copy-done, bf16[1024,512]{1,0:T(8,128)(2,1)S(1)} %copy-done.7, bf16[1024,512]{1,0:T(8,128)(2,1)} %param.7), kind=kOutput, calls=%fused_computation.14 | convolution fusion | flops 543162368 | bytes 1318912 | tf_op jit(solution)/shard_map/dot_general | solution.py:118
  53.8 5.6 %collective-permute-start.7 = (f32[2,33,128]{2,1,0:T(8,128)S(1)}, f32[2,33,128]{2,1,0:T(8,128)S(1)}, u32[]{:S(2)}, u32[]{:S(2)}) collective-permute-start(f32[2,33,128]{2,1,0:T(8,128)S(1)} %pad_maximum_fusion.6), channel_id=1, source_target_pairs={{0,256},{64,320},{128,384},{192,448},{1,257},{65,321},{129,385},{1... | collective-permute-start | bytes 101384 | tf_op jit(solution)/shard_map/ppermute | solution.py:55
  59.4 3.1 %fusion.5 = f32[1024,128]{0,1:T(8,128)} fusion(f32[1024]{0:T(1024)S(1)} %bitcast.106, bf16[1024,512]{1,0:T(8,128)(2,1)S(1)} %copy-done, bf16[1024,512]{1,0:T(8,128)(2,1)S(1)} %copy-done.7, bf16[1024,512]{1,0:T(8,128)(2,1)} %param.7), kind=kOutput, calls=%fused_computation.13 | convolution fusion | flops 543162368 | bytes 1318912 | tf_op jit(solution)/shard_map/dot_general | solution.py:118
  62.6 1.9 %collective-permute-start.10 = (f32[2,32,128]{2,1,0:T(8,128)S(1)}, f32[2,32,128]{2,1,0:T(8,128)S(1)}, u32[]{:S(2)}, u32[]{:S(2)}) collective-permute-start(f32[2,32,128]{2,1,0:T(8,128)S(1)} %fusion.65), channel_id=1, source_target_pairs={{0,48},{16,0},{32,16},{48,32},{1,49},{17,1},{33,17},{49,33},{2,50}... | collective-permute-start | bytes 98312 | tf_op jit(solution)/shard_map/ppermute | solution.py:33
  64.6 2.5 %collective-permute-start.9 = (f32[2,32,128]{2,1,0:T(8,128)S(1)}, f32[2,32,128]{2,1,0:T(8,128)S(1)}, u32[]{:S(2)}, u32[]{:S(2)}) collective-permute-start(f32[2,32,128]{2,1,0:T(8,128)S(1)} %fusion.65), channel_id=1, source_target_pairs={{0,32},{16,48},{32,0},{48,16},{1,33},{17,49},{33,1},{49,17},{2,34}... | collective-permute-start | bytes 98312 | tf_op jit(solution)/shard_map/ppermute | solution.py:33
  67.1 2.8 %collective-permute-start.8 = (f32[2,32,128]{2,1,0:T(8,128)S(1)}, f32[2,32,128]{2,1,0:T(8,128)S(1)}, u32[]{:S(2)}, u32[]{:S(2)}) collective-permute-start(f32[2,32,128]{2,1,0:T(8,128)S(1)} %fusion.65), channel_id=1, source_target_pairs={{0,16},{16,32},{32,48},{48,0},{1,17},{17,33},{33,49},{49,1},{2,18}... | collective-permute-start | bytes 98312 | tf_op jit(solution)/shard_map/ppermute | solution.py:33
  69.9 3.1 %fusion.4 = f32[1024,128]{0,1:T(8,128)} fusion(f32[1024]{0:T(1024)S(1)} %bitcast.105, bf16[1024,512]{1,0:T(8,128)(2,1)S(1)} %copy-done, bf16[1024,512]{1,0:T(8,128)(2,1)S(1)} %copy-done.7, bf16[1024,512]{1,0:T(8,128)(2,1)} %param.7), kind=kOutput, calls=%fused_computation.12 | convolution fusion | flops 543162368 | bytes 1318912 | tf_op jit(solution)/shard_map/dot_general | solution.py:118
  74.3 7.1 %collective-permute-start.11 = (f32[2,128,128]{2,1,0:T(8,128)}, f32[2,128,128]{2,1,0:T(8,128)}, u32[]{:S(2)}, u32[]{:S(2)}) collective-permute-start(f32[2,128,128]{2,1,0:T(8,128)} %fusion.64), channel_id=1, source_target_pairs={{0,8},{8,0},{1,9},{9,1},{2,10},{10,2},{3,11},{11,3},{4,12},{12,4},... | collective-permute-start | bytes 393224 | tf_op jit(solution)/shard_map/ppermute | solution.py:104
  81.4 3.3 %fusion.3 = f32[1024,128]{0,1:T(8,128)} fusion(f32[1024]{0:T(1024)S(1)} %bitcast.104, bf16[1024,512]{1,0:T(8,128)(2,1)} %param.8, bf16[1024,512]{1,0:T(8,128)(2,1)} %param.7, bf16[1024,512]{1,0:T(8,128)(2,1)S(1)} %copy-done), kind=kOutput, calls=%fused_computation.11 | convolution fusion | flops 543162368 | bytes 1318912 | tf_op jit(solution)/shard_map/dot_general | solution.py:118
  85.3 0.8 dynamic_slice.15
  86.2 1.2 add_select_fusion
  87.4 1.2 fusion.18
  91.6 40.5 %all_to_all.5 = bf16[8,129,512]{2,1,0:T(8,128)(2,1)S(1)} all-to-all(bf16[8,129,512]{2,1,0:T(8,128)(2,1)S(1)} %maximum_maximum_fusion), channel_id=1, replica_groups=mesh['cy'=8,'cx'=4,'cc'=2,'head'=8] {'head'}, dimensions={0} | all-to-all | bytes 2113536 | tf_op jit(solution)/shard_map/all_to_all | solution.py:169
  133.1 1.3 copy.35
  (78 shorter events, 9.5 us)
Async XLA Ops:
  0.0 10.0 %copy-start.7 = (bf16[1024,512]{1,0:T(8,128)(2,1)S(1)}, bf16[1024,512]{1,0:T(8,128)(2,1)}, u32[]{:S(2)}) copy-start(bf16[1024,512]{1,0:T(8,128)(2,1)} %param.8) | copy-start | bytes 3145732
  13.5 10.0 %collective-permute-start = (f32[4,129,128]{2,1,0:T(8,128)S(1)}, f32[4,129,128]{2,1,0:T(8,128)S(1)}, u32[]{:S(2)}, u32[]{:S(2)}) collective-permute-start(f32[4,129,128]{2,1,0:T(8,128)S(1)} %pad_maximum_fusion.1), channel_id=1, source_target_pairs={{0,8},{8,0},{1,9},{9,1},{2,10},{10,2},{3,11},{11,3},{4,12},{12,4},... | collective-permute-start | bytes 792584 | tf_op jit(solution)/shard_map/ppermute | solution.py:77
  24.4 26.1 %copy-start = (bf16[1024,512]{1,0:T(8,128)(2,1)S(1)}, bf16[1024,512]{1,0:T(8,128)(2,1)}, u32[]{:S(2)}) copy-start(bf16[1024,512]{1,0:T(8,128)(2,1)} %param.6) | copy-start | bytes 3145732
  24.6 7.4 %collective-permute-start.3 = (f32[2,129,128]{2,1,0:T(8,128)S(1)}, f32[2,129,128]{2,1,0:T(8,128)S(1)}, u32[]{:S(2)}, u32[]{:S(2)}) collective-permute-start(f32[2,129,128]{2,1,0:T(8,128)S(1)} %pad_maximum_fusion.3), channel_id=1, source_target_pairs={{0,48},{16,0},{32,16},{48,32},{1,49},{17,1},{33,17},{49,33},{2,50}... | collective-permute-start | bytes 396296 | tf_op jit(solution)/shard_map/ppermute | solution.py:33
  26.6 8.3 %collective-permute-start.2 = (f32[2,129,128]{2,1,0:T(8,128)S(1)}, f32[2,129,128]{2,1,0:T(8,128)S(1)}, u32[]{:S(2)}, u32[]{:S(2)}) collective-permute-start(f32[2,129,128]{2,1,0:T(8,128)S(1)} %pad_maximum_fusion.3), channel_id=1, source_target_pairs={{0,32},{16,48},{32,0},{48,16},{1,33},{17,49},{33,1},{49,17},{2,34}... | collective-permute-start | bytes 396296 | tf_op jit(solution)/shard_map/ppermute | solution.py:33
  28.6 9.2 %collective-permute-start.1 = (f32[2,129,128]{2,1,0:T(8,128)S(1)}, f32[2,129,128]{2,1,0:T(8,128)S(1)}, u32[]{:S(2)}, u32[]{:S(2)}) collective-permute-start(f32[2,129,128]{2,1,0:T(8,128)S(1)} %pad_maximum_fusion.3), channel_id=1, source_target_pairs={{0,16},{16,32},{32,48},{48,0},{1,17},{17,33},{33,49},{49,1},{2,18}... | collective-permute-start | bytes 396296 | tf_op jit(solution)/shard_map/ppermute | solution.py:33
  38.4 4.8 %collective-permute-start.5 = (f32[2,33,128]{2,1,0:T(8,128)S(1)}, f32[2,33,128]{2,1,0:T(8,128)S(1)}, u32[]{:S(2)}, u32[]{:S(2)}) collective-permute-start(f32[2,33,128]{2,1,0:T(8,128)S(1)} %pad_maximum_fusion.4), channel_id=1, source_target_pairs={{0,128},{64,192},{128,256},{192,320},{256,384},{320,448},{1,129},{... | collective-permute-start | bytes 101384 | tf_op jit(solution)/shard_map/ppermute | solution.py:55
  40.0 4.3 %collective-permute-start.4 = (f32[2,33,128]{2,1,0:T(8,128)S(1)}, f32[2,33,128]{2,1,0:T(8,128)S(1)}, u32[]{:S(2)}, u32[]{:S(2)}) collective-permute-start(f32[2,33,128]{2,1,0:T(8,128)S(1)} %pad_maximum_fusion.4), channel_id=1, source_target_pairs={{0,64},{64,128},{128,192},{192,256},{256,320},{320,384},{384,448},... | collective-permute-start | bytes 101384 | tf_op jit(solution)/shard_map/ppermute | solution.py:55
  44.5 9.0 %collective-permute-start.6 = (f32[2,33,128]{2,1,0:T(8,128)S(1)}, f32[2,33,128]{2,1,0:T(8,128)S(1)}, u32[]{:S(2)}, u32[]{:S(2)}) collective-permute-start(f32[2,33,128]{2,1,0:T(8,128)S(1)} %pad_maximum_fusion.5), channel_id=1, source_target_pairs={{0,128},{64,192},{128,256},{192,320},{256,384},{320,448},{1,129},{... | collective-permute-start | bytes 101384 | tf_op jit(solution)/shard_map/ppermute | solution.py:55
  53.8 8.7 %collective-permute-start.7 = (f32[2,33,128]{2,1,0:T(8,128)S(1)}, f32[2,33,128]{2,1,0:T(8,128)S(1)}, u32[]{:S(2)}, u32[]{:S(2)}) collective-permute-start(f32[2,33,128]{2,1,0:T(8,128)S(1)} %pad_maximum_fusion.6), channel_id=1, source_target_pairs={{0,256},{64,320},{128,384},{192,448},{1,257},{65,321},{129,385},{1... | collective-permute-start | bytes 101384 | tf_op jit(solution)/shard_map/ppermute | solution.py:55
  62.6 10.3 %collective-permute-start.10 = (f32[2,32,128]{2,1,0:T(8,128)S(1)}, f32[2,32,128]{2,1,0:T(8,128)S(1)}, u32[]{:S(2)}, u32[]{:S(2)}) collective-permute-start(f32[2,32,128]{2,1,0:T(8,128)S(1)} %fusion.65), channel_id=1, source_target_pairs={{0,48},{16,0},{32,16},{48,32},{1,49},{17,1},{33,17},{49,33},{2,50}... | collective-permute-start | bytes 98312 | tf_op jit(solution)/shard_map/ppermute | solution.py:33
  64.6 8.4 %collective-permute-start.9 = (f32[2,32,128]{2,1,0:T(8,128)S(1)}, f32[2,32,128]{2,1,0:T(8,128)S(1)}, u32[]{:S(2)}, u32[]{:S(2)}) collective-permute-start(f32[2,32,128]{2,1,0:T(8,128)S(1)} %fusion.65), channel_id=1, source_target_pairs={{0,32},{16,48},{32,0},{48,16},{1,33},{17,49},{33,1},{49,17},{2,34}... | collective-permute-start | bytes 98312 | tf_op jit(solution)/shard_map/ppermute | solution.py:33
  67.1 6.4 %collective-permute-start.8 = (f32[2,32,128]{2,1,0:T(8,128)S(1)}, f32[2,32,128]{2,1,0:T(8,128)S(1)}, u32[]{:S(2)}, u32[]{:S(2)}) collective-permute-start(f32[2,32,128]{2,1,0:T(8,128)S(1)} %fusion.65), channel_id=1, source_target_pairs={{0,16},{16,32},{32,48},{48,0},{1,17},{17,33},{33,49},{49,1},{2,18}... | collective-permute-start | bytes 98312 | tf_op jit(solution)/shard_map/ppermute | solution.py:33
  74.3 11.9 %collective-permute-start.11 = (f32[2,128,128]{2,1,0:T(8,128)}, f32[2,128,128]{2,1,0:T(8,128)}, u32[]{:S(2)}, u32[]{:S(2)}) collective-permute-start(f32[2,128,128]{2,1,0:T(8,128)} %fusion.64), channel_id=1, source_target_pairs={{0,8},{8,0},{1,9},{9,1},{2,10},{10,2},{3,11},{11,3},{4,12},{12,4},... | collective-permute-start | bytes 393224 | tf_op jit(solution)/shard_map/ppermute | solution.py:104
  81.4 3.3 %copy-start.1 = (bf16[1024,512]{1,0:T(8,128)(2,1)S(1)}, bf16[1024,512]{1,0:T(8,128)(2,1)}, u32[]{:S(2)}) copy-start(bf16[1024,512]{1,0:T(8,128)(2,1)} %param.10) | copy-start | bytes 3145732
  85.2 2.1 %copy-start.2 = (f32[1024,128]{0,1:T(8,128)S(1)}, f32[1024,128]{0,1:T(8,128)}, u32[]{:S(2)}) copy-start(f32[1024,128]{0,1:T(8,128)} %fusion.6) | copy-start | bytes 1572868
  85.2 3.3 %copy-start.3 = (f32[1024,128]{0,1:T(8,128)S(1)}, f32[1024,128]{0,1:T(8,128)}, u32[]{:S(2)}) copy-start(f32[1024,128]{0,1:T(8,128)} %fusion.5) | copy-start | bytes 1572868
  85.3 3.3 %copy-start.6 = (f32[1024,1]{0,1:T(1,128)S(1)}, f32[1024,1]{0,1:T(1,128)}, u32[]{:S(2)}) copy-start(f32[1024,1]{0,1:T(1,128)} %get-tuple-element.50) | copy-start | bytes 12292
  87.4 1.6 %copy-start.4 = (f32[1024,128]{0,1:T(8,128)S(1)}, f32[1024,128]{0,1:T(8,128)}, u32[]{:S(2)}) copy-start(f32[1024,128]{0,1:T(8,128)} %fusion.4) | copy-start | bytes 1572868
  88.6 1.0 copy-start.5

commit v7 on v6

--- a/solution.py
+++ b/solution.py
@@ -72,7 +72,6 @@
     rows, cols, cores = lax.axis_size("cy"), lax.axis_size("cx"), lax.axis_size("cc")
     y, x, c = lax.axis_index("cy"), lax.axis_index("cx"), lax.axis_index("cc")
     heads, size = S.shape[0], S.shape[1]
-    group = heads // cores
 
     pair = unpack(lax.ppermute(pack(L, S), "cc", [(0, 1), (1, 0)]))
     L0 = jnp.where(c == 0, L, pair[0])
@@ -81,15 +80,12 @@
     S1 = jnp.where(c == 0, pair[1], S)
     chip_log = L0 + L1
     chip_state = jnp.exp(L1)[:, None, None] * S0 + S1
-    g_log = lax.dynamic_slice_in_dim(chip_log, c * group, group, 0)
-    g_state = lax.dynamic_slice_in_dim(chip_state, c * group, group, 0)
-
-    row_pieces = [unpack(p) for p in shifted(pack(g_log, g_state), "cx", cols)]
+    row_pieces = [unpack(p) for p in shifted(pack(chip_log, chip_state), "cx", cols)]
     e_log, e_state, f_log, f_state = scan_pieces(
         [p[0] for p in row_pieces], [p[1] for p in row_pieces], x, cols
     )
-    row_log = e_log + g_log + f_log
-    row_state = jnp.exp(f_log)[:, None, None] * (jnp.exp(g_log)[:, None, None] * e_state + g_state) + f_state
+    row_log = e_log + chip_log + f_log
+    row_state = jnp.exp(f_log)[:, None, None] * (jnp.exp(chip_log)[:, None, None] * e_state + chip_state) + f_state
 
     part = size // cols
     q_state = lax.dynamic_slice_in_dim(row_state, x * part, part, 1)
@@ -100,12 +96,7 @@
     y_full = jnp.concatenate(ordered, axis=1)
 
     chip_before = jnp.exp(e_log)[:, None, None] * y_full + e_state
-
-    other = lax.ppermute(chip_before, "cc", [(0, 1), (1, 0)])
-    full0 = jnp.concatenate([chip_before, other], axis=0)
-    full1 = jnp.concatenate([other, chip_before], axis=0)
-    chip_full = jnp.where(c == 0, full0, full1)
-    return jnp.where(c == 0, chip_full, jnp.exp(L0)[:, None, None] * chip_full + S0)
+    return jnp.where(c == 0, chip_before, jnp.exp(L0)[:, None, None] * chip_before + S0)
 
 
 def inner_head(qh, kh, vh, ch):

time: 135 us -> 136 us (level)
  the two profiles are of different devices: /device:TPU:1 before, /device:TPU:4 now
where the time goes in v7:
time: 136 us
  starting transfers between devices  46.7 us (34%)
  blocking collectives  37.8 us (28%)
  matrix products  21.6 us (16%)
  other arithmetic  12.7 us (9%)
  waiting for transfers between devices  9.89 us (7%)
  local copies, waits for them, and re-layouts  6.44 us (5%)
    all_to_all x1, blocking collectives, body(): lax.all_to_all(payload, 'head', split_axis=0, concat_axis=0, tiled=True)  37.8 us
    ppermute x6, starting transfers between devices, shifted(): out.append(lax.ppermute(x, axis, [(j, (j + s) % n) for j in range(n)]))  25.5 us
    ppermute x4, starting transfers between devices, shift(): return lax.ppermute(packed, axis, [(j, j + d) for j in range(n - d)])  19.2 us
    dot_general x4, matrix products, inner_head(): return jnp.dot(weights, vh, preferred_element_type=F32)  13 us
    ppermute x6, waiting for transfers between devices, shifted(): out.append(lax.ppermute(x, axis, [(j, (j + s) % n) for j in range(n)]))  8.36 us
    dot_general x4, matrix products, body(): jnp.dot((cols(keys, h).astype(F32) * jnp.exp(last[h] - cum[:, h])[:, None...  6.97 us
    exp x1, other arithmetic, body(): joined.append(inner + jnp.exp(cum[:, h])[:, None] * across)  3.12 us
  transfers between devices with their start and end apart: 11, of which 3 were waited for; matrix products, arithmetic and copies ran while one was open for 11% of the time, Pallas kernels for 0%

profile of v7, /device:TPU:4, one launch (start us, length us, event | category | flops | bytes accessed | tf_op | source)
XLA Modules:
  0.0 135.6 jit_solution(9044564086378736844)
XLA Ops:
  0.0 0.8 copy.47
  0.8 1.1 reduce-window.6
  3.2 3.1 %slice_exponential_fusion.3 = (f32[1024,1]{0,1:T(1,128)S(1)}, f32[1024,1]{0,1:T(1,128)S(1)}, f32[1024,1]{0,1:T(1,128)S(1)}, f32[1024,1]{0,1:T(1,128)S(1)}, f32[1...) fusion(f32[1024,4]{0,1:T(4,128)S(1)} %bitcast.95, ...), kind=kLoop, calls=%fused_computation.165 | loop fusion | flops 4096 | bytes 65552 | tf_op jit(solution)/shard_map/exp | solution.py:140
  6.3 1.8 %convolution_bitcast_fusion.3 = f32[1,128,128]{2,1,0:T(8,128)S(1)} fusion(f32[1024]{0:T(1024)S(1)} %bitcast.111, bf16[1024,512]{1,0:T(8,128)(2,1)} %param.8, bf16[1024,512]{1,0:T(8,128)(2,1)} %param.7), kind=kOutput, calls=%fused_computation.34 | convolution fusion | flops 201588736 | bytes 593920 | tf_op jit(solution)/shard_map/dot_general | solution.py:124
  8.1 1.8 %convolution_bitcast_fusion.2 = f32[1,128,128]{2,1,0:T(8,128)S(1)} fusion(f32[1024]{0:T(1024)S(1)} %bitcast.110, bf16[1024,512]{1,0:T(8,128)(2,1)} %param.8, bf16[1024,512]{1,0:T(8,128)(2,1)} %param.7), kind=kOutput, calls=%fused_computation.33 | convolution fusion | flops 201588736 | bytes 593920 | tf_op jit(solution)/shard_map/dot_general | solution.py:124
  9.9 1.7 %convolution_bitcast_fusion.1 = f32[1,128,128]{2,1,0:T(8,128)S(1)} fusion(f32[1024]{0:T(1024)S(1)} %bitcast.109, bf16[1024,512]{1,0:T(8,128)(2,1)S(1)} %copy-done.11, bf16[1024,512]{1,0:T(8,128)(2,1)} %param.7), kind=kOutput, calls=%fused_computation.32 | convolution fusion | flops 201588736 | bytes 593920 | tf_op jit(solution)/shard_map/dot_general | solution.py:124
  11.6 1.7 %convolution_bitcast_fusion = f32[1,128,128]{2,1,0:T(8,128)S(1)} fusion(f32[1024]{0:T(1024)S(1)} %bitcast.108, bf16[1024,512]{1,0:T(8,128)(2,1)S(1)} %copy-done.11, bf16[1024,512]{1,0:T(8,128)(2,1)} %param.7), kind=kOutput, calls=%fused_computation.31 | convolution fusion | flops 201588736 | bytes 593920 | tf_op jit(solution)/shard_map/dot_general | solution.py:124
  13.5 1.9 %collective-permute-start = (f32[4,129,128]{2,1,0:T(8,128)S(1)}, f32[4,129,128]{2,1,0:T(8,128)S(1)}, u32[]{:S(2)}, u32[]{:S(2)}) collective-permute-start(f32[4,129,128]{2,1,0:T(8,128)S(1)} %pad_maximum_fusion.1), channel_id=1, source_target_pairs={{0,8},{8,0},{1,9},{9,1},{2,10},{10,2},{3,11},{11,3},{4,12},{12,4},... | collective-permute-start | bytes 792584 | tf_op jit(solution)/shard_map/ppermute | solution.py:76
  15.4 1.5 %collective-permute-done = f32[4,129,128]{2,1,0:T(8,128)S(1)} collective-permute-done((f32[4,129,128]{2,1,0:T(8,128)S(1)}, f32[4,129,128]{2,1,0:T(8,128)S(1)}, u32[]{:S(2)}, u32[]{:S(2)}) %collective-permute-start) | collective-permute-done | bytes 264224 | tf_op jit(solution)/shard_map/ppermute | solution.py:76
  17.8 2.4 %collective-permute-start.3 = (f32[4,129,128]{2,1,0:T(8,128)S(1)}, f32[4,129,128]{2,1,0:T(8,128)S(1)}, u32[]{:S(2)}, u32[]{:S(2)}) collective-permute-start(f32[4,129,128]{2,1,0:T(8,128)S(1)} %pad_maximum_fusion.2), channel_id=1, source_target_pairs={{0,48},{16,0},{32,16},{48,32},{1,49},{17,1},{33,17},{49,33},{2,50}... | collective-permute-start | bytes 792584 | tf_op jit(solution)/shard_map/ppermute | solution.py:33
  20.3 7.3 %collective-permute-start.2 = (f32[4,129,128]{2,1,0:T(8,128)S(1)}, f32[4,129,128]{2,1,0:T(8,128)}, u32[]{:S(2)}, u32[]{:S(2)}) collective-permute-start(f32[4,129,128]{2,1,0:T(8,128)S(1)} %pad_maximum_fusion.2), channel_id=1, source_target_pairs={{0,32},{16,48},{32,0},{48,16},{1,33},{17,49},{33,1},{49,17},{2,34}... | collective-permute-start | bytes 792584 | tf_op jit(solution)/shard_map/ppermute | solution.py:33
  27.5 4.5 %collective-permute-start.1 = (f32[4,129,128]{2,1,0:T(8,128)S(1)}, f32[4,129,128]{2,1,0:T(8,128)S(1)}, u32[]{:S(2)}, u32[]{:S(2)}) collective-permute-start(f32[4,129,128]{2,1,0:T(8,128)S(1)} %pad_maximum_fusion.2), channel_id=1, source_target_pairs={{0,16},{16,32},{32,48},{48,0},{1,17},{17,33},{33,49},{49,1},{2,18}... | collective-permute-start | bytes 792584 | tf_op jit(solution)/shard_map/ppermute | solution.py:33
  32.1 3.0 %collective-permute-done.2 = f32[4,129,128]{2,1,0:T(8,128)} collective-permute-done((f32[4,129,128]{2,1,0:T(8,128)S(1)}, f32[4,129,128]{2,1,0:T(8,128)}, u32[]{:S(2)}, u32[]{:S(2)}) %collective-permute-start.2) | collective-permute-done | bytes 264224 | tf_op jit(solution)/shard_map/ppermute | solution.py:33
  35.1 5.3 %collective-permute-done.1 = f32[4,129,128]{2,1,0:T(8,128)S(1)} collective-permute-done((f32[4,129,128]{2,1,0:T(8,128)S(1)}, f32[4,129,128]{2,1,0:T(8,128)S(1)}, u32[]{:S(2)}, u32[]{:S(2)}) %collective-permute-start.1) | collective-permute-done | bytes 264224 | tf_op jit(solution)/shard_map/ppermute | solution.py:33
  40.4 0.8 fusion.80
  42.0 1.3 fusion.92
  43.4 2.1 %collective-permute-start.5 = (f32[4,33,128]{2,1,0:T(8,128)S(1)}, f32[4,33,128]{2,1,0:T(8,128)S(1)}, u32[]{:S(2)}, u32[]{:S(2)}) collective-permute-start(f32[4,33,128]{2,1,0:T(8,128)S(1)} %pad_maximum_fusion.4), channel_id=1, source_target_pairs={{0,128},{64,192},{128,256},{192,320},{256,384},{320,448},{1,129},{... | collective-permute-start | bytes 202760 | tf_op jit(solution)/shard_map/ppermute | solution.py:55
  45.5 3.5 %collective-permute-start.4 = (f32[4,33,128]{2,1,0:T(8,128)S(1)}, f32[4,33,128]{2,1,0:T(8,128)S(1)}, u32[]{:S(2)}, u32[]{:S(2)}) collective-permute-start(f32[4,33,128]{2,1,0:T(8,128)S(1)} %pad_maximum_fusion.4), channel_id=1, source_target_pairs={{0,64},{64,128},{128,192},{192,256},{256,320},{320,384},{384,448},... | collective-permute-start | bytes 202760 | tf_op jit(solution)/shard_map/ppermute | solution.py:55
  49.0 3.2 %fusion.6 = f32[1024,128]{0,1:T(8,128)} fusion(f32[1024]{0:T(1024)S(1)} %bitcast.107, bf16[1024,512]{1,0:T(8,128)(2,1)S(1)} %copy-done, bf16[1024,512]{1,0:T(8,128)(2,1)} %param.8, bf16[1024,512]{1,0:T(8,128)(2,1)} %param.7), kind=kOutput, calls=%fused_computation.14 | convolution fusion | flops 543162368 | bytes 1318912 | tf_op jit(solution)/shard_map/dot_general | solution.py:109
  52.6 5.3 %collective-permute-start.6 = (f32[4,33,128]{2,1,0:T(8,128)S(1)}, f32[4,33,128]{2,1,0:T(8,128)S(1)}, u32[]{:S(2)}, u32[]{:S(2)}) collective-permute-start(f32[4,33,128]{2,1,0:T(8,128)S(1)} %pad_maximum_fusion.5), channel_id=1, source_target_pairs={{0,128},{64,192},{128,256},{192,320},{256,384},{320,448},{1,129},{... | collective-permute-start | bytes 202760 | tf_op jit(solution)/shard_map/ppermute | solution.py:55
  57.9 3.2 %fusion.5 = f32[1024,128]{0,1:T(8,128)} fusion(f32[1024]{0:T(1024)S(1)} %bitcast.106, bf16[1024,512]{1,0:T(8,128)(2,1)S(1)} %copy-done, bf16[1024,512]{1,0:T(8,128)(2,1)} %param.8, bf16[1024,512]{1,0:T(8,128)(2,1)} %param.7), kind=kOutput, calls=%fused_computation.13 | convolution fusion | flops 543162368 | bytes 1318912 | tf_op jit(solution)/shard_map/dot_general | solution.py:109
  61.4 8.3 %collective-permute-start.7 = (f32[4,33,128]{2,1,0:T(8,128)S(1)}, f32[4,33,128]{2,1,0:T(8,128)S(1)}, u32[]{:S(2)}, u32[]{:S(2)}) collective-permute-start(f32[4,33,128]{2,1,0:T(8,128)S(1)} %pad_maximum_fusion.6), channel_id=1, source_target_pairs={{0,256},{64,320},{128,384},{192,448},{1,257},{65,321},{129,385},{1... | collective-permute-start | bytes 202760 | tf_op jit(solution)/shard_map/ppermute | solution.py:55
  69.7 3.2 %fusion.4 = f32[1024,128]{0,1:T(8,128)} fusion(f32[1024]{0:T(1024)S(1)} %bitcast.105, bf16[1024,512]{1,0:T(8,128)(2,1)S(1)} %copy-done, bf16[1024,512]{1,0:T(8,128)(2,1)} %param.8, bf16[1024,512]{1,0:T(8,128)(2,1)} %param.7), kind=kOutput, calls=%fused_computation.12 | convolution fusion | flops 543162368 | bytes 1318912 | tf_op jit(solution)/shard_map/dot_general | solution.py:109
  73.6 1.9 %collective-permute-start.10 = (f32[4,32,128]{2,1,0:T(8,128)}, f32[4,32,128]{2,1,0:T(8,128)}, u32[]{:S(2)}, u32[]{:S(2)}) collective-permute-start(f32[4,32,128]{2,1,0:T(8,128)} %fusion.64), channel_id=1, source_target_pairs={{0,48},{16,0},{32,16},{48,32},{1,49},{17,1},{33,17},{49,33},{2,50}... | collective-permute-start | bytes 196616 | tf_op jit(solution)/shard_map/ppermute | solution.py:33
  75.6 4.7 %collective-permute-start.9 = (f32[4,32,128]{2,1,0:T(8,128)}, f32[4,32,128]{2,1,0:T(8,128)}, u32[]{:S(2)}, u32[]{:S(2)}) collective-permute-start(f32[4,32,128]{2,1,0:T(8,128)} %fusion.64), channel_id=1, source_target_pairs={{0,32},{16,48},{32,0},{48,16},{1,33},{17,49},{33,1},{49,17},{2,34}... | collective-permute-start | bytes 196616 | tf_op jit(solution)/shard_map/ppermute | solution.py:33
  80.2 4.7 %collective-permute-start.8 = (f32[4,32,128]{2,1,0:T(8,128)}, f32[4,32,128]{2,1,0:T(8,128)}, u32[]{:S(2)}, u32[]{:S(2)}) collective-permute-start(f32[4,32,128]{2,1,0:T(8,128)} %fusion.64), channel_id=1, source_target_pairs={{0,16},{16,32},{32,48},{48,0},{1,17},{17,33},{33,49},{49,1},{2,18}... | collective-permute-start | bytes 196616 | tf_op jit(solution)/shard_map/ppermute | solution.py:33
  85.0 3.3 %fusion.3 = f32[1024,128]{0,1:T(8,128)} fusion(f32[1024]{0:T(1024)S(1)} %bitcast.104, bf16[1024,512]{1,0:T(8,128)(2,1)} %param.8, bf16[1024,512]{1,0:T(8,128)(2,1)} %param.7, bf16[1024,512]{1,0:T(8,128)(2,1)S(1)} %copy-done), kind=kOutput, calls=%fused_computation.11 | convolution fusion | flops 543162368 | bytes 1318912 | tf_op jit(solution)/shard_map/dot_general | solution.py:109
  88.8 0.8 dynamic_slice.7
  89.7 1.0 select_select_fusion.3
  90.7 1.1 add_select_fusion
  95.4 37.8 %all_to_all.5 = bf16[8,129,512]{2,1,0:T(8,128)(2,1)S(1)} all-to-all(bf16[8,129,512]{2,1,0:T(8,128)(2,1)S(1)} %maximum_maximum_fusion), channel_id=1, replica_groups=mesh['cy'=8,'cx'=4,'cc'=2,'head'=8] {'head'}, dimensions={0} | all-to-all | bytes 2113536 | tf_op jit(solution)/shard_map/all_to_all | solution.py:160
  134.3 1.3 copy.35
  (77 shorter events, 9.4 us)
Async XLA Ops:
  0.0 9.9 %copy-start.11 = (bf16[1024,512]{1,0:T(8,128)(2,1)S(1)}, bf16[1024,512]{1,0:T(8,128)(2,1)}, u32[]{:S(2)}) copy-start(bf16[1024,512]{1,0:T(8,128)(2,1)} %param.8) | copy-start | bytes 3145732
  11.6 40.6 %copy-start.3 = (f32[1,128,128]{2,1,0:T(8,128)}, f32[1,128,128]{2,1,0:T(8,128)S(1)}, u32[]{:S(2)}) copy-start(f32[1,128,128]{2,1,0:T(8,128)S(1)} %convolution_bitcast_fusion.1) | copy-start | bytes 196612
  13.4 38.9 %copy-start.4 = (f32[1,128,128]{2,1,0:T(8,128)}, f32[1,128,128]{2,1,0:T(8,128)S(1)}, u32[]{:S(2)}) copy-start(f32[1,128,128]{2,1,0:T(8,128)S(1)} %convolution_bitcast_fusion) | copy-start | bytes 196612
  13.5 3.5 %collective-permute-start = (f32[4,129,128]{2,1,0:T(8,128)S(1)}, f32[4,129,128]{2,1,0:T(8,128)S(1)}, u32[]{:S(2)}, u32[]{:S(2)}) collective-permute-start(f32[4,129,128]{2,1,0:T(8,128)S(1)} %pad_maximum_fusion.1), channel_id=1, source_target_pairs={{0,8},{8,0},{1,9},{9,1},{2,10},{10,2},{3,11},{11,3},{4,12},{12,4},... | collective-permute-start | bytes 792584 | tf_op jit(solution)/shard_map/ppermute | solution.py:76
  16.9 35.3 %copy-start.2 = (f32[4,129,128]{2,1,0:T(8,128)}, f32[4,129,128]{2,1,0:T(8,128)S(1)}, u32[]{:S(2)}) copy-start(f32[4,129,128]{2,1,0:T(8,128)S(1)} %collective-permute-done) | copy-start | bytes 792580
  17.8 14.3 %collective-permute-start.3 = (f32[4,129,128]{2,1,0:T(8,128)S(1)}, f32[4,129,128]{2,1,0:T(8,128)S(1)}, u32[]{:S(2)}, u32[]{:S(2)}) collective-permute-start(f32[4,129,128]{2,1,0:T(8,128)S(1)} %pad_maximum_fusion.2), channel_id=1, source_target_pairs={{0,48},{16,0},{32,16},{48,32},{1,49},{17,1},{33,17},{49,33},{2,50}... | collective-permute-start | bytes 792584 | tf_op jit(solution)/shard_map/ppermute | solution.py:33
  20.3 14.8 %collective-permute-start.2 = (f32[4,129,128]{2,1,0:T(8,128)S(1)}, f32[4,129,128]{2,1,0:T(8,128)}, u32[]{:S(2)}, u32[]{:S(2)}) collective-permute-start(f32[4,129,128]{2,1,0:T(8,128)S(1)} %pad_maximum_fusion.2), channel_id=1, source_target_pairs={{0,32},{16,48},{32,0},{48,16},{1,33},{17,49},{33,1},{49,17},{2,34}... | collective-permute-start | bytes 792584 | tf_op jit(solution)/shard_map/ppermute | solution.py:33
  27.5 12.9 %collective-permute-start.1 = (f32[4,129,128]{2,1,0:T(8,128)S(1)}, f32[4,129,128]{2,1,0:T(8,128)S(1)}, u32[]{:S(2)}, u32[]{:S(2)}) collective-permute-start(f32[4,129,128]{2,1,0:T(8,128)S(1)} %pad_maximum_fusion.2), channel_id=1, source_target_pairs={{0,16},{16,32},{32,48},{48,0},{1,17},{17,33},{33,49},{49,1},{2,18}... | collective-permute-start | bytes 792584 | tf_op jit(solution)/shard_map/ppermute | solution.py:33
  40.4 1.5 %copy-start.9 = (f32[4,129,128]{2,1,0:T(8,128)}, f32[4,129,128]{2,1,0:T(8,128)S(1)}, u32[]{:S(2)}) copy-start(f32[4,129,128]{2,1,0:T(8,128)S(1)} %collective-permute-done.1) | copy-start | bytes 792580
  42.0 7.0 %copy-start = (bf16[1024,512]{1,0:T(8,128)(2,1)S(1)}, bf16[1024,512]{1,0:T(8,128)(2,1)}, u32[]{:S(2)}) copy-start(bf16[1024,512]{1,0:T(8,128)(2,1)} %param.6) | copy-start | bytes 3145732
  43.4 8.8 %collective-permute-start.5 = (f32[4,33,128]{2,1,0:T(8,128)S(1)}, f32[4,33,128]{2,1,0:T(8,128)S(1)}, u32[]{:S(2)}, u32[]{:S(2)}) collective-permute-start(f32[4,33,128]{2,1,0:T(8,128)S(1)} %pad_maximum_fusion.4), channel_id=1, source_target_pairs={{0,128},{64,192},{128,256},{192,320},{256,384},{320,448},{1,129},{... | collective-permute-start | bytes 202760 | tf_op jit(solution)/shard_map/ppermute | solution.py:55
  45.5 6.7 %collective-permute-start.4 = (f32[4,33,128]{2,1,0:T(8,128)S(1)}, f32[4,33,128]{2,1,0:T(8,128)S(1)}, u32[]{:S(2)}, u32[]{:S(2)}) collective-permute-start(f32[4,33,128]{2,1,0:T(8,128)S(1)} %pad_maximum_fusion.4), channel_id=1, source_target_pairs={{0,64},{64,128},{128,192},{192,256},{256,320},{320,384},{384,448},... | collective-permute-start | bytes 202760 | tf_op jit(solution)/shard_map/ppermute | solution.py:55
  52.6 8.5 %collective-permute-start.6 = (f32[4,33,128]{2,1,0:T(8,128)S(1)}, f32[4,33,128]{2,1,0:T(8,128)S(1)}, u32[]{:S(2)}, u32[]{:S(2)}) collective-permute-start(f32[4,33,128]{2,1,0:T(8,128)S(1)} %pad_maximum_fusion.5), channel_id=1, source_target_pairs={{0,128},{64,192},{128,256},{192,320},{256,384},{320,448},{1,129},{... | collective-permute-start | bytes 202760 | tf_op jit(solution)/shard_map/ppermute | solution.py:55
  61.4 11.6 %collective-permute-start.7 = (f32[4,33,128]{2,1,0:T(8,128)S(1)}, f32[4,33,128]{2,1,0:T(8,128)S(1)}, u32[]{:S(2)}, u32[]{:S(2)}) collective-permute-start(f32[4,33,128]{2,1,0:T(8,128)S(1)} %pad_maximum_fusion.6), channel_id=1, source_target_pairs={{0,256},{64,320},{128,384},{192,448},{1,257},{65,321},{129,385},{1... | collective-permute-start | bytes 202760 | tf_op jit(solution)/shard_map/ppermute | solution.py:55
  69.7 15.2 %copy-start.10 = (f32[1024,1]{0,1:T(1,128)S(1)}, f32[1024,1]{0,1:T(1,128)}, u32[]{:S(2)}) copy-start(f32[1024,1]{0,1:T(1,128)} %get-tuple-element.54) | copy-start | bytes 12292
  73.6 16.0 %collective-permute-start.10 = (f32[4,32,128]{2,1,0:T(8,128)}, f32[4,32,128]{2,1,0:T(8,128)}, u32[]{:S(2)}, u32[]{:S(2)}) collective-permute-start(f32[4,32,128]{2,1,0:T(8,128)} %fusion.64), channel_id=1, source_target_pairs={{0,48},{16,0},{32,16},{48,32},{1,49},{17,1},{33,17},{49,33},{2,50}... | collective-permute-start | bytes 196616 | tf_op jit(solution)/shard_map/ppermute | solution.py:33
  75.6 14.1 %collective-permute-start.9 = (f32[4,32,128]{2,1,0:T(8,128)}, f32[4,32,128]{2,1,0:T(8,128)}, u32[]{:S(2)}, u32[]{:S(2)}) collective-permute-start(f32[4,32,128]{2,1,0:T(8,128)} %fusion.64), channel_id=1, source_target_pairs={{0,32},{16,48},{32,0},{48,16},{1,33},{17,49},{33,1},{49,17},{2,34}... | collective-permute-start | bytes 196616 | tf_op jit(solution)/shard_map/ppermute | solution.py:33
  80.2 9.5 %collective-permute-start.8 = (f32[4,32,128]{2,1,0:T(8,128)}, f32[4,32,128]{2,1,0:T(8,128)}, u32[]{:S(2)}, u32[]{:S(2)}) collective-permute-start(f32[4,32,128]{2,1,0:T(8,128)} %fusion.64), channel_id=1, source_target_pairs={{0,16},{16,32},{32,48},{48,0},{1,17},{17,33},{33,49},{49,1},{2,18}... | collective-permute-start | bytes 196616 | tf_op jit(solution)/shard_map/ppermute | solution.py:33
  85.0 3.3 %copy-start.1 = (bf16[1024,512]{1,0:T(8,128)(2,1)S(1)}, bf16[1024,512]{1,0:T(8,128)(2,1)}, u32[]{:S(2)}) copy-start(bf16[1024,512]{1,0:T(8,128)(2,1)} %param.10) | copy-start | bytes 3145732
  88.8 3.0 %copy-start.5 = (f32[1024,128]{0,1:T(8,128)S(1)}, f32[1024,128]{0,1:T(8,128)}, u32[]{:S(2)}) copy-start(f32[1024,128]{0,1:T(8,128)} %fusion.6) | copy-start | bytes 1572868
  90.7 1.6 %copy-start.6 = (f32[1024,128]{0,1:T(8,128)S(1)}, f32[1024,128]{0,1:T(8,128)}, u32[]{:S(2)}) copy-start(f32[1024,128]{0,1:T(8,128)} %fusion.5) | copy-start | bytes 1572868
  91.9 1.0 copy-start.7
  92.3 1.1 copy-start.8

commit v8 on v4

--- a/solution.py
+++ b/solution.py
@@ -54,8 +54,15 @@
     def shift(packed, d):
         return lax.ppermute(packed, axis, [(j, j + d) for j in range(n - d)])
 
-    cur_log, cur = unpack(shift(pack(log, state), 1))
-    d = 1
+    packed = pack(log, state)
+    first = min(4, n - 1)
+    cur_log = jnp.zeros_like(log)
+    cur = jnp.zeros_like(state)
+    for d in range(1, first + 1):
+        got_log, got = unpack(shift(packed, d))
+        cur = cur + jnp.exp(cur_log)[:, None, None] * got
+        cur_log = cur_log + got_log
+    d = first
     while d < n:
         got_log, got = unpack(shift(pack(cur_log, cur), d))
         cur = jnp.exp(cur_log)[:, None, None] * got + cur

time: 140 us -> 131 us (0.936)
  starting transfers between devices: 50 us -> 43.8 us
  waiting for transfers between devices: 9.67 us -> 7.51 us
    ppermute x1, starting transfers between devices: 8.38 us -> 4.44 us  [carried_state(): other = lax.ppermute(chip_before, 'cc', [(0, 1), (1, 0)])]
    ppermute x4 -> x5, starting transfers between devices: 18.3 us -> 16.1 us  [shift(): return lax.ppermute(packed, axis, [(j, j + d) for j in range(n - d)])]
    ppermute x4 -> x5, waiting for transfers between devices: 2.17 us -> 0.01 us  [shift(): return lax.ppermute(packed, axis, [(j, j + d) for j in range(n - d)])]
  transfers between devices with their start and end apart: 12 -> 13, of which waited for: 6 -> 4; matrix products, arithmetic and copies ran while one was open for 10% -> 11% of each run, Pallas kernels for 0% -> 0%
where the time goes in v8:
time: 131 us; the launch traced here: 130 us
  starting transfers between devices  43.8 us (33%)
  blocking collectives  40.5 us (31%)
  matrix products  22.1 us (17%)
  other arithmetic  9.53 us (7%)
  waiting for transfers between devices  7.51 us (6%)
  local copies, waits for them, and re-layouts  6.58 us (5%)
    all_to_all x1, blocking collectives, body(): lax.all_to_all(payload, 'head', split_axis=0, concat_axis=0, tiled=True)  40.5 us
    ppermute x5, starting transfers between devices, shift(): return lax.ppermute(packed, axis, [(j, j + d) for j in range(n - d)])  16.1 us
    ppermute x6, starting transfers between devices, shifted(): out.append(lax.ppermute(x, axis, [(j, (j + s) % n) for j in range(n)]))  14.5 us
    dot_general x4, matrix products, inner_head(): return jnp.dot(weights, vh, preferred_element_type=F32)  12.7 us
    ppermute x1, starting transfers between devices, carried_state(): pair = unpack(lax.ppermute(pack(L, S), 'cc', [(0, 1), (1, 0)]))  8.79 us
    dot_general x4, matrix products, body(): jnp.dot((cols(keys, h).astype(F32) * jnp.exp(last[h] - cum[:, h])[:, None...  6.97 us
    ppermute x6, waiting for transfers between devices, shifted(): out.append(lax.ppermute(x, axis, [(j, (j + s) % n) for j in range(n)]))  6.34 us
    ppermute x1, starting transfers between devices, carried_state(): other = lax.ppermute(chip_before, 'cc', [(0, 1), (1, 0)])  4.44 us
  transfers between devices with their start and end apart: 13, of which 4 were waited for; matrix products, arithmetic and copies ran while one was open for 11% of the time, Pallas kernels for 0%

profile of v8, /device:TPU:1, one launch (start us, length us, event | category | flops | bytes accessed | tf_op | source)
XLA Modules:
  0.0 130.5 jit_solution(10278914075771401753)
XLA Ops:
  0.0 0.8 copy.47
  0.8 1.1 reduce-window.6
  3.2 3.2 %slice_exponential_fusion.3 = (f32[1024,1]{0,1:T(1,128)S(1)}, f32[1024,1]{0,1:T(1,128)S(1)}, f32[1024,1]{0,1:T(1,128)S(1)}, f32[1024,1]{0,1:T(1,128)S(1)}, f32[1...) fusion(f32[1024,4]{0,1:T(4,128)S(1)} %bitcast.95, ...), kind=kLoop, calls=%fused_computation.174 | loop fusion | flops 4096 | bytes 65552 | tf_op jit(solution)/shard_map/exp | solution.py:152
  6.4 1.8 %convolution_bitcast_fusion.3 = f32[1,128,128]{2,1,0:T(8,128)S(1)} fusion(f32[1024]{0:T(1024)S(1)} %bitcast.111, bf16[1024,512]{1,0:T(8,128)(2,1)} %param.8, bf16[1024,512]{1,0:T(8,128)(2,1)} %param.7), kind=kOutput, calls=%fused_computation.34 | convolution fusion | flops 201588736 | bytes 593920 | tf_op jit(solution)/shard_map/dot_general | solution.py:136
  8.2 1.8 %convolution_bitcast_fusion.2 = f32[1,128,128]{2,1,0:T(8,128)S(1)} fusion(f32[1024]{0:T(1024)S(1)} %bitcast.110, bf16[1024,512]{1,0:T(8,128)(2,1)} %param.8, bf16[1024,512]{1,0:T(8,128)(2,1)} %param.7), kind=kOutput, calls=%fused_computation.33 | convolution fusion | flops 201588736 | bytes 593920 | tf_op jit(solution)/shard_map/dot_general | solution.py:136
  10.0 1.7 %convolution_bitcast_fusion.1 = f32[1,128,128]{2,1,0:T(8,128)S(1)} fusion(f32[1024]{0:T(1024)S(1)} %bitcast.109, bf16[1024,512]{1,0:T(8,128)(2,1)S(1)} %copy-done.7, bf16[1024,512]{1,0:T(8,128)(2,1)} %param.7), kind=kOutput, calls=%fused_computation.32 | convolution fusion | flops 201588736 | bytes 593920 | tf_op jit(solution)/shard_map/dot_general | solution.py:136
  11.7 1.7 %convolution_bitcast_fusion = f32[1,128,128]{2,1,0:T(8,128)S(1)} fusion(f32[1024]{0:T(1024)S(1)} %bitcast.108, bf16[1024,512]{1,0:T(8,128)(2,1)S(1)} %copy-done.7, bf16[1024,512]{1,0:T(8,128)(2,1)} %param.7), kind=kOutput, calls=%fused_computation.31 | convolution fusion | flops 201588736 | bytes 593920 | tf_op jit(solution)/shard_map/dot_general | solution.py:136
  13.5 8.8 %collective-permute-start = (f32[4,129,128]{2,1,0:T(8,128)S(1)}, f32[4,129,128]{2,1,0:T(8,128)S(1)}, u32[]{:S(2)}, u32[]{:S(2)}) collective-permute-start(f32[4,129,128]{2,1,0:T(8,128)S(1)} %pad_maximum_fusion.1), channel_id=1, source_target_pairs={{0,8},{8,0},{1,9},{9,1},{2,10},{10,2},{3,11},{11,3},{4,12},{12,4},... | collective-permute-start | bytes 792584 | tf_op jit(solution)/shard_map/ppermute | solution.py:80
  22.3 1.2 collective-permute-done
  24.6 2.1 %collective-permute-start.3 = (f32[2,129,128]{2,1,0:T(8,128)S(1)}, f32[2,129,128]{2,1,0:T(8,128)S(1)}, u32[]{:S(2)}, u32[]{:S(2)}) collective-permute-start(f32[2,129,128]{2,1,0:T(8,128)S(1)} %pad_maximum_fusion.3), channel_id=1, source_target_pairs={{0,48},{16,0},{32,16},{48,32},{1,49},{17,1},{33,17},{49,33},{2,50}... | collective-permute-start | bytes 396296 | tf_op jit(solution)/shard_map/ppermute | solution.py:33
  26.6 1.9 %collective-permute-start.2 = (f32[2,129,128]{2,1,0:T(8,128)S(1)}, f32[2,129,128]{2,1,0:T(8,128)S(1)}, u32[]{:S(2)}, u32[]{:S(2)}) collective-permute-start(f32[2,129,128]{2,1,0:T(8,128)S(1)} %pad_maximum_fusion.3), channel_id=1, source_target_pairs={{0,32},{16,48},{32,0},{48,16},{1,33},{17,49},{33,1},{49,17},{2,34}... | collective-permute-start | bytes 396296 | tf_op jit(solution)/shard_map/ppermute | solution.py:33
  28.6 3.4 %collective-permute-start.1 = (f32[2,129,128]{2,1,0:T(8,128)S(1)}, f32[2,129,128]{2,1,0:T(8,128)S(1)}, u32[]{:S(2)}, u32[]{:S(2)}) collective-permute-start(f32[2,129,128]{2,1,0:T(8,128)S(1)} %pad_maximum_fusion.3), channel_id=1, source_target_pairs={{0,16},{16,32},{32,48},{48,0},{1,17},{17,33},{33,49},{49,1},{2,18}... | collective-permute-start | bytes 396296 | tf_op jit(solution)/shard_map/ppermute | solution.py:33
  31.9 3.0 %collective-permute-done.2 = f32[2,129,128]{2,1,0:T(8,128)S(1)} collective-permute-done((f32[2,129,128]{2,1,0:T(8,128)S(1)}, f32[2,129,128]{2,1,0:T(8,128)S(1)}, u32[]{:S(2)}, u32[]{:S(2)}) %collective-permute-start.2) | collective-permute-done | bytes 132128 | tf_op jit(solution)/shard_map/ppermute | solution.py:33
  34.9 2.8 %collective-permute-done.1 = f32[2,129,128]{2,1,0:T(8,128)S(1)} collective-permute-done((f32[2,129,128]{2,1,0:T(8,128)S(1)}, f32[2,129,128]{2,1,0:T(8,128)S(1)}, u32[]{:S(2)}, u32[]{:S(2)}) %collective-permute-start.1) | collective-permute-done | bytes 132128 | tf_op jit(solution)/shard_map/ppermute | solution.py:33
  38.4 4.9 %collective-permute-start.7 = (f32[2,33,128]{2,1,0:T(8,128)S(1)}, f32[2,33,128]{2,1,0:T(8,128)S(1)}, u32[]{:S(2)}, u32[]{:S(2)}) collective-permute-start(f32[2,33,128]{2,1,0:T(8,128)S(1)} %pad_maximum_fusion.4), channel_id=1, source_target_pairs={{0,256},{64,320},{128,384},{192,448},{1,257},{65,321},{129,385},{1... | collective-permute-start | bytes 101384 | tf_op jit(solution)/shard_map/ppermute | solution.py:55
  43.2 2.5 %collective-permute-start.6 = (f32[2,33,128]{2,1,0:T(8,128)S(1)}, f32[2,33,128]{2,1,0:T(8,128)S(1)}, u32[]{:S(2)}, u32[]{:S(2)}) collective-permute-start(f32[2,33,128]{2,1,0:T(8,128)S(1)} %pad_maximum_fusion.4), channel_id=1, source_target_pairs={{0,192},{64,256},{128,320},{192,384},{256,448},{1,193},{65,257},{1... | collective-permute-start | bytes 101384 | tf_op jit(solution)/shard_map/ppermute | solution.py:55
  45.8 1.3 collective-permute-start.5
  47.1 2.8 %collective-permute-start.4 = (f32[2,33,128]{2,1,0:T(8,128)S(1)}, f32[2,33,128]{2,1,0:T(8,128)S(1)}, u32[]{:S(2)}, u32[]{:S(2)}) collective-permute-start(f32[2,33,128]{2,1,0:T(8,128)S(1)} %pad_maximum_fusion.4), channel_id=1, source_target_pairs={{0,64},{64,128},{128,192},{192,256},{256,320},{320,384},{384,448},... | collective-permute-start | bytes 101384 | tf_op jit(solution)/shard_map/ppermute | solution.py:55
  49.9 3.1 %fusion.6 = f32[1024,128]{0,1:T(8,128)} fusion(f32[1024]{0:T(1024)S(1)} %bitcast.107, bf16[1024,512]{1,0:T(8,128)(2,1)S(1)} %copy-done, bf16[1024,512]{1,0:T(8,128)(2,1)S(1)} %copy-done.7, bf16[1024,512]{1,0:T(8,128)(2,1)} %param.7), kind=kOutput, calls=%fused_computation.14 | convolution fusion | flops 543162368 | bytes 1318912 | tf_op jit(solution)/shard_map/dot_general | solution.py:121
  53.5 4.6 %collective-permute-start.8 = (f32[2,33,128]{2,1,0:T(8,128)S(1)}, f32[2,33,128]{2,1,0:T(8,128)S(1)}, u32[]{:S(2)}, u32[]{:S(2)}) collective-permute-start(f32[2,33,128]{2,1,0:T(8,128)S(1)} %pad_maximum_fusion.5), channel_id=1, source_target_pairs={{0,256},{64,320},{128,384},{192,448},{1,257},{65,321},{129,385},{1... | collective-permute-start | bytes 101384 | tf_op jit(solution)/shard_map/ppermute | solution.py:55
  58.1 3.1 %fusion.5 = f32[1024,128]{0,1:T(8,128)} fusion(f32[1024]{0:T(1024)S(1)} %bitcast.106, bf16[1024,512]{1,0:T(8,128)(2,1)S(1)} %copy-done, bf16[1024,512]{1,0:T(8,128)(2,1)S(1)} %copy-done.7, bf16[1024,512]{1,0:T(8,128)(2,1)} %param.7), kind=kOutput, calls=%fused_computation.13 | convolution fusion | flops 543162368 | bytes 1318912 | tf_op jit(solution)/shard_map/dot_general | solution.py:121
  61.3 1.9 %collective-permute-start.11 = (f32[2,32,128]{2,1,0:T(8,128)S(1)}, f32[2,32,128]{2,1,0:T(8,128)S(1)}, u32[]{:S(2)}, u32[]{:S(2)}) collective-permute-start(f32[2,32,128]{2,1,0:T(8,128)S(1)} %fusion.65), channel_id=1, source_target_pairs={{0,48},{16,0},{32,16},{48,32},{1,49},{17,1},{33,17},{49,33},{2,50}... | collective-permute-start | bytes 98312 | tf_op jit(solution)/shard_map/ppermute | solution.py:33
  63.3 2.3 %collective-permute-start.10 = (f32[2,32,128]{2,1,0:T(8,128)S(1)}, f32[2,32,128]{2,1,0:T(8,128)S(1)}, u32[]{:S(2)}, u32[]{:S(2)}) collective-permute-start(f32[2,32,128]{2,1,0:T(8,128)S(1)} %fusion.65), channel_id=1, source_target_pairs={{0,32},{16,48},{32,0},{48,16},{1,33},{17,49},{33,1},{49,17},{2,34}... | collective-permute-start | bytes 98312 | tf_op jit(solution)/shard_map/ppermute | solution.py:33
  65.6 2.9 %collective-permute-start.9 = (f32[2,32,128]{2,1,0:T(8,128)S(1)}, f32[2,32,128]{2,1,0:T(8,128)S(1)}, u32[]{:S(2)}, u32[]{:S(2)}) collective-permute-start(f32[2,32,128]{2,1,0:T(8,128)S(1)} %fusion.65), channel_id=1, source_target_pairs={{0,16},{16,32},{32,48},{48,0},{1,17},{17,33},{33,49},{49,1},{2,18}... | collective-permute-start | bytes 98312 | tf_op jit(solution)/shard_map/ppermute | solution.py:33
  68.6 3.1 %fusion.4 = f32[1024,128]{0,1:T(8,128)} fusion(f32[1024]{0:T(1024)S(1)} %bitcast.105, bf16[1024,512]{1,0:T(8,128)(2,1)S(1)} %copy-done, bf16[1024,512]{1,0:T(8,128)(2,1)S(1)} %copy-done.7, bf16[1024,512]{1,0:T(8,128)(2,1)} %param.7), kind=kOutput, calls=%fused_computation.12 | convolution fusion | flops 543162368 | bytes 1318912 | tf_op jit(solution)/shard_map/dot_general | solution.py:121
  73.0 4.4 %collective-permute-start.12 = (f32[2,128,128]{2,1,0:T(8,128)}, f32[2,128,128]{2,1,0:T(8,128)}, u32[]{:S(2)}, u32[]{:S(2)}) collective-permute-start(f32[2,128,128]{2,1,0:T(8,128)} %fusion.64), channel_id=1, source_target_pairs={{0,8},{8,0},{1,9},{9,1},{2,10},{10,2},{3,11},{11,3},{4,12},{12,4},... | collective-permute-start | bytes 393224 | tf_op jit(solution)/shard_map/ppermute | solution.py:107
  77.4 3.3 %fusion.3 = f32[1024,128]{0,1:T(8,128)} fusion(f32[1024]{0:T(1024)S(1)} %bitcast.104, bf16[1024,512]{1,0:T(8,128)(2,1)} %param.8, bf16[1024,512]{1,0:T(8,128)(2,1)} %param.7, bf16[1024,512]{1,0:T(8,128)(2,1)S(1)} %copy-done), kind=kOutput, calls=%fused_computation.11 | convolution fusion | flops 543162368 | bytes 1318912 | tf_op jit(solution)/shard_map/dot_general | solution.py:121
  81.3 0.8 dynamic_slice.15
  82.2 1.2 add_select_fusion
  83.4 1.2 fusion.18
  87.6 40.5 %all_to_all.5 = bf16[8,129,512]{2,1,0:T(8,128)(2,1)S(1)} all-to-all(bf16[8,129,512]{2,1,0:T(8,128)(2,1)S(1)} %maximum_maximum_fusion), channel_id=1, replica_groups=mesh['cy'=8,'cx'=4,'cc'=2,'head'=8] {'head'}, dimensions={0} | all-to-all | bytes 2113536 | tf_op jit(solution)/shard_map/all_to_all | solution.py:172
  129.2 1.3 %copy.35 = bf16[128,4096]{1,0:T(8,128)(2,1)} copy(bf16[128,4096]{0,1:T(8,128)(2,1)S(1)} %bitcast.91) | data formatting | bytes 2097152 | tf_op jit(solution)/shard_map/convert_element_type | solution.py:177
  (78 shorter events, 9.5 us)
Async XLA Ops:
  0.0 10.0 %copy-start.7 = (bf16[1024,512]{1,0:T(8,128)(2,1)S(1)}, bf16[1024,512]{1,0:T(8,128)(2,1)}, u32[]{:S(2)}) copy-start(bf16[1024,512]{1,0:T(8,128)(2,1)} %param.8) | copy-start | bytes 3145732
  13.5 10.0 %collective-permute-start = (f32[4,129,128]{2,1,0:T(8,128)S(1)}, f32[4,129,128]{2,1,0:T(8,128)S(1)}, u32[]{:S(2)}, u32[]{:S(2)}) collective-permute-start(f32[4,129,128]{2,1,0:T(8,128)S(1)} %pad_maximum_fusion.1), channel_id=1, source_target_pairs={{0,8},{8,0},{1,9},{9,1},{2,10},{10,2},{3,11},{11,3},{4,12},{12,4},... | collective-permute-start | bytes 792584 | tf_op jit(solution)/shard_map/ppermute | solution.py:80
  24.4 25.5 %copy-start = (bf16[1024,512]{1,0:T(8,128)(2,1)S(1)}, bf16[1024,512]{1,0:T(8,128)(2,1)}, u32[]{:S(2)}) copy-start(bf16[1024,512]{1,0:T(8,128)(2,1)} %param.6) | copy-start | bytes 3145732
  24.6 7.4 %collective-permute-start.3 = (f32[2,129,128]{2,1,0:T(8,128)S(1)}, f32[2,129,128]{2,1,0:T(8,128)S(1)}, u32[]{:S(2)}, u32[]{:S(2)}) collective-permute-start(f32[2,129,128]{2,1,0:T(8,128)S(1)} %pad_maximum_fusion.3), channel_id=1, source_target_pairs={{0,48},{16,0},{32,16},{48,32},{1,49},{17,1},{33,17},{49,33},{2,50}... | collective-permute-start | bytes 396296 | tf_op jit(solution)/shard_map/ppermute | solution.py:33
  26.6 8.3 %collective-permute-start.2 = (f32[2,129,128]{2,1,0:T(8,128)S(1)}, f32[2,129,128]{2,1,0:T(8,128)S(1)}, u32[]{:S(2)}, u32[]{:S(2)}) collective-permute-start(f32[2,129,128]{2,1,0:T(8,128)S(1)} %pad_maximum_fusion.3), channel_id=1, source_target_pairs={{0,32},{16,48},{32,0},{48,16},{1,33},{17,49},{33,1},{49,17},{2,34}... | collective-permute-start | bytes 396296 | tf_op jit(solution)/shard_map/ppermute | solution.py:33
  28.6 9.2 %collective-permute-start.1 = (f32[2,129,128]{2,1,0:T(8,128)S(1)}, f32[2,129,128]{2,1,0:T(8,128)S(1)}, u32[]{:S(2)}, u32[]{:S(2)}) collective-permute-start(f32[2,129,128]{2,1,0:T(8,128)S(1)} %pad_maximum_fusion.3), channel_id=1, source_target_pairs={{0,16},{16,32},{32,48},{48,0},{1,17},{17,33},{33,49},{49,1},{2,18}... | collective-permute-start | bytes 396296 | tf_op jit(solution)/shard_map/ppermute | solution.py:33
  38.4 14.7 %collective-permute-start.7 = (f32[2,33,128]{2,1,0:T(8,128)S(1)}, f32[2,33,128]{2,1,0:T(8,128)S(1)}, u32[]{:S(2)}, u32[]{:S(2)}) collective-permute-start(f32[2,33,128]{2,1,0:T(8,128)S(1)} %pad_maximum_fusion.4), channel_id=1, source_target_pairs={{0,256},{64,320},{128,384},{192,448},{1,257},{65,321},{129,385},{1... | collective-permute-start | bytes 101384 | tf_op jit(solution)/shard_map/ppermute | solution.py:55
  43.2 9.8 %collective-permute-start.6 = (f32[2,33,128]{2,1,0:T(8,128)S(1)}, f32[2,33,128]{2,1,0:T(8,128)S(1)}, u32[]{:S(2)}, u32[]{:S(2)}) collective-permute-start(f32[2,33,128]{2,1,0:T(8,128)S(1)} %pad_maximum_fusion.4), channel_id=1, source_target_pairs={{0,192},{64,256},{128,320},{192,384},{256,448},{1,193},{65,257},{1... | collective-permute-start | bytes 101384 | tf_op jit(solution)/shard_map/ppermute | solution.py:55
  45.8 7.3 %collective-permute-start.5 = (f32[2,33,128]{2,1,0:T(8,128)S(1)}, f32[2,33,128]{2,1,0:T(8,128)S(1)}, u32[]{:S(2)}, u32[]{:S(2)}) collective-permute-start(f32[2,33,128]{2,1,0:T(8,128)S(1)} %pad_maximum_fusion.4), channel_id=1, source_target_pairs={{0,128},{64,192},{128,256},{192,320},{256,384},{320,448},{1,129},{... | collective-permute-start | bytes 101384 | tf_op jit(solution)/shard_map/ppermute | solution.py:55
  47.1 6.0 %collective-permute-start.4 = (f32[2,33,128]{2,1,0:T(8,128)S(1)}, f32[2,33,128]{2,1,0:T(8,128)S(1)}, u32[]{:S(2)}, u32[]{:S(2)}) collective-permute-start(f32[2,33,128]{2,1,0:T(8,128)S(1)} %pad_maximum_fusion.4), channel_id=1, source_target_pairs={{0,64},{64,128},{128,192},{192,256},{256,320},{320,384},{384,448},... | collective-permute-start | bytes 101384 | tf_op jit(solution)/shard_map/ppermute | solution.py:55
  53.5 7.7 %collective-permute-start.8 = (f32[2,33,128]{2,1,0:T(8,128)S(1)}, f32[2,33,128]{2,1,0:T(8,128)S(1)}, u32[]{:S(2)}, u32[]{:S(2)}) collective-permute-start(f32[2,33,128]{2,1,0:T(8,128)S(1)} %pad_maximum_fusion.5), channel_id=1, source_target_pairs={{0,256},{64,320},{128,384},{192,448},{1,257},{65,321},{129,385},{1... | collective-permute-start | bytes 101384 | tf_op jit(solution)/shard_map/ppermute | solution.py:55
  61.3 10.4 %collective-permute-start.11 = (f32[2,32,128]{2,1,0:T(8,128)S(1)}, f32[2,32,128]{2,1,0:T(8,128)S(1)}, u32[]{:S(2)}, u32[]{:S(2)}) collective-permute-start(f32[2,32,128]{2,1,0:T(8,128)S(1)} %fusion.65), channel_id=1, source_target_pairs={{0,48},{16,0},{32,16},{48,32},{1,49},{17,1},{33,17},{49,33},{2,50}... | collective-permute-start | bytes 98312 | tf_op jit(solution)/shard_map/ppermute | solution.py:33
  63.3 8.4 %collective-permute-start.10 = (f32[2,32,128]{2,1,0:T(8,128)S(1)}, f32[2,32,128]{2,1,0:T(8,128)S(1)}, u32[]{:S(2)}, u32[]{:S(2)}) collective-permute-start(f32[2,32,128]{2,1,0:T(8,128)S(1)} %fusion.65), channel_id=1, source_target_pairs={{0,32},{16,48},{32,0},{48,16},{1,33},{17,49},{33,1},{49,17},{2,34}... | collective-permute-start | bytes 98312 | tf_op jit(solution)/shard_map/ppermute | solution.py:33
  65.6 6.6 %collective-permute-start.9 = (f32[2,32,128]{2,1,0:T(8,128)S(1)}, f32[2,32,128]{2,1,0:T(8,128)S(1)}, u32[]{:S(2)}, u32[]{:S(2)}) collective-permute-start(f32[2,32,128]{2,1,0:T(8,128)S(1)} %fusion.65), channel_id=1, source_target_pairs={{0,16},{16,32},{32,48},{48,0},{1,17},{17,33},{33,49},{49,1},{2,18}... | collective-permute-start | bytes 98312 | tf_op jit(solution)/shard_map/ppermute | solution.py:33
  73.0 9.2 %collective-permute-start.12 = (f32[2,128,128]{2,1,0:T(8,128)}, f32[2,128,128]{2,1,0:T(8,128)}, u32[]{:S(2)}, u32[]{:S(2)}) collective-permute-start(f32[2,128,128]{2,1,0:T(8,128)} %fusion.64), channel_id=1, source_target_pairs={{0,8},{8,0},{1,9},{9,1},{2,10},{10,2},{3,11},{11,3},{4,12},{12,4},... | collective-permute-start | bytes 393224 | tf_op jit(solution)/shard_map/ppermute | solution.py:107
  77.4 3.3 %copy-start.1 = (bf16[1024,512]{1,0:T(8,128)(2,1)S(1)}, bf16[1024,512]{1,0:T(8,128)(2,1)}, u32[]{:S(2)}) copy-start(bf16[1024,512]{1,0:T(8,128)(2,1)} %param.10) | copy-start | bytes 3145732
  81.3 2.1 %copy-start.2 = (f32[1024,128]{0,1:T(8,128)S(1)}, f32[1024,128]{0,1:T(8,128)}, u32[]{:S(2)}) copy-start(f32[1024,128]{0,1:T(8,128)} %fusion.6) | copy-start | bytes 1572868
  81.3 3.3 %copy-start.3 = (f32[1024,128]{0,1:T(8,128)S(1)}, f32[1024,128]{0,1:T(8,128)}, u32[]{:S(2)}) copy-start(f32[1024,128]{0,1:T(8,128)} %fusion.5) | copy-start | bytes 1572868
  81.3 3.3 %copy-start.6 = (f32[1024,1]{0,1:T(1,128)S(1)}, f32[1024,1]{0,1:T(1,128)}, u32[]{:S(2)}) copy-start(f32[1024,1]{0,1:T(1,128)} %get-tuple-element.51) | copy-start | bytes 12292
  83.4 1.6 %copy-start.4 = (f32[1024,128]{0,1:T(8,128)S(1)}, f32[1024,128]{0,1:T(8,128)}, u32[]{:S(2)}) copy-start(f32[1024,128]{0,1:T(8,128)} %fusion.4) | copy-start | bytes 1572868
  84.6 1.0 copy-start.5

commit v9 on v8

--- a/solution.py
+++ b/solution.py
@@ -131,16 +131,8 @@
     def cols(array, h):
         return array[:, h * size : (h + 1) * size]
 
-    state = jnp.stack(
-        [
-            jnp.dot(
-                (cols(keys, h).astype(F32) * jnp.exp(last[h] - cum[:, h])[:, None]).T,
-                cols(values, h).astype(F32),
-                precision=HI,
-            )
-            for h in range(heads)
-        ]
-    )
+    keyed = keys.reshape(count, heads, size).astype(F32) * jnp.exp(last[None, :] - cum)[:, :, None]
+    state = jnp.einsum("thd,the->hde", keyed, values.reshape(count, heads, size).astype(F32), precision=HI)
 
     carried = carried_state(last, state)
 

time: 131 us -> 138 us (1.053)
  matrix products: 22.1 us -> 16 us
  other arithmetic: 9.53 us -> 14.7 us
  starting transfers between devices: 43.8 us -> 48.4 us
  local copies, waits for them, and re-layouts: 6.58 us -> 9.38 us
    dot_general x4 -> x1, matrix products: 6.97 us -> 2.42 us  [body(): jnp.einsum('thd,the->hde', keyed, values.reshape(count, heads, size).asty...]
    exp x1, other arithmetic: 3.16 us -> 0.09 us  [body(): jnp.exp(last[None, :] - cum)[:, :, None]]
    ppermute x1, starting transfers between devices: 4.44 us -> 7.21 us  [carried_state(): other = lax.ppermute(chip_before, 'cc', [(0, 1), (1, 0)])]
    dot_general x4, matrix products: 12.7 us -> 10.5 us  [inner_head(): return jnp.dot(weights, vh, preferred_element_type=F32)]
    concatenate x4, other arithmetic: 0.05 us -> 2.04 us  [pack(): return jnp.concatenate([state, row], axis=1)]
    convert_element_type x0 -> x1, local copies, waits for them, and re-layouts: none -> 1.49 us  [body(): keys.reshape(count, heads, size).astype(F32)]
    add x1, other arithmetic: 0.08 us -> 1.51 us  [exclusive_scan(): cur = cur + jnp.exp(cur_log)[:, None, None] * got]
    add x1, other arithmetic: 0.07 us -> 1.46 us  [exclusive_scan(): cur = jnp.exp(cur_log)[:, None, None] * got + cur]
  transfers between devices with their start and end apart: 13 -> 13, of which waited for: 4 -> 4; matrix products, arithmetic and copies ran while one was open for 11% -> 10% of each run, Pallas kernels for 0% -> 0%
where the time goes in v9:
time: 138 us; the launch traced here: 137 us
  starting transfers between devices  48.4 us (35%)
  blocking collectives  40.4 us (29%)
  matrix products  16 us (12%)
  other arithmetic  14.7 us (11%)
  local copies, waits for them, and re-layouts  9.38 us (7%)
  waiting for transfers between devices  7.94 us (6%)
    all_to_all x1, blocking collectives, body(): lax.all_to_all(payload, 'head', split_axis=0, concat_axis=0, tiled=True)  40.4 us
    ppermute x5, starting transfers between devices, shift(): return lax.ppermute(packed, axis, [(j, j + d) for j in range(n - d)])  16.5 us
    ppermute x6, starting transfers between devices, shifted(): out.append(lax.ppermute(x, axis, [(j, (j + s) % n) for j in range(n)]))  15.8 us
    dot_general x4, matrix products, inner_head(): return jnp.dot(weights, vh, preferred_element_type=F32)  10.5 us
    ppermute x1, starting transfers between devices, carried_state(): pair = unpack(lax.ppermute(pack(L, S), 'cc', [(0, 1), (1, 0)]))  8.92 us
    ppermute x1, starting transfers between devices, carried_state(): other = lax.ppermute(chip_before, 'cc', [(0, 1), (1, 0)])  7.21 us
    ppermute x6, waiting for transfers between devices, shifted(): out.append(lax.ppermute(x, axis, [(j, (j + s) % n) for j in range(n)]))  6.78 us
    dot_general x4, matrix products, body(): across = jnp.dot(qh.astype(F32), carried[h], precision=HI)  3.05 us
  transfers between devices with their start and end apart: 13, of which 4 were waited for; matrix products, arithmetic and copies ran while one was open for 10% of the time, Pallas kernels for 0%

profile of v9, /device:TPU:1, one launch (start us, length us, event | category | flops | bytes accessed | tf_op | source)
XLA Modules:
  0.0 137.2 jit_solution(3383645484106066554)
XLA Ops:
  0.7 1.1 reduce-window.6
  2.6 1.5 %copy.47 = f32[1024,512]{0,1:T(8,128)S(1)} copy(bf16[1024,512]{1,0:T(8,128)(2,1)} %param.7) | data formatting | bytes 3145728 | tf_op jit(solution)/shard_map/convert_element_type | solution.py:134
  4.0 2.4 %fusion.3 = f32[4,128,128]{2,1,0:T(8,128)S(1)} fusion(f32[1024,4,128]{0,2,1:T(8,128)S(1)} %bitcast.87, f32[1024,4]{0,1:T(4,128)S(1)} %subtract_exponential_fusion, bf16[1024,512]{1,0:T(8,128)(2,1)} %param.8), kind=kOutput, calls=%fused_computation.11 | convolution fusion | flops 805830656 | bytes 3424256 | tf_op jit(solution)/shard_map/thd,the->hde/dot_general | solution.py:135
  6.6 8.9 %collective-permute-start = (f32[4,129,128]{2,1,0:T(8,128)S(1)}, f32[4,129,128]{2,1,0:T(8,128)S(1)}, u32[]{:S(2)}, u32[]{:S(2)}) collective-permute-start(f32[4,129,128]{2,1,0:T(8,128)S(1)} %pad_maximum_fusion.1), channel_id=1, source_target_pairs={{0,8},{8,0},{1,9},{9,1},{2,10},{10,2},{3,11},{11,3},{4,12},{12,4},... | collective-permute-start | bytes 792584 | tf_op jit(solution)/shard_map/ppermute | solution.py:80
  15.5 1.1 collective-permute-done
  17.8 1.9 %collective-permute-start.3 = (f32[2,129,128]{2,1,0:T(8,128)S(1)}, f32[2,129,128]{2,1,0:T(8,128)S(1)}, u32[]{:S(2)}, u32[]{:S(2)}) collective-permute-start(f32[2,129,128]{2,1,0:T(8,128)S(1)} %pad_maximum_fusion.2), channel_id=1, source_target_pairs={{0,48},{16,0},{32,16},{48,32},{1,49},{17,1},{33,17},{49,33},{2,50}... | collective-permute-start | bytes 396296 | tf_op jit(solution)/shard_map/ppermute | solution.py:33
  19.7 3.4 %collective-permute-start.1 = (f32[2,129,128]{2,1,0:T(8,128)S(1)}, f32[2,129,128]{2,1,0:T(8,128)S(1)}, u32[]{:S(2)}, u32[]{:S(2)}) collective-permute-start(f32[2,129,128]{2,1,0:T(8,128)S(1)} %pad_maximum_fusion.2), channel_id=1, source_target_pairs={{0,16},{16,32},{32,48},{48,0},{1,17},{17,33},{33,49},{49,1},{2,18}... | collective-permute-start | bytes 396296 | tf_op jit(solution)/shard_map/ppermute | solution.py:33
  23.1 1.9 %collective-permute-start.2 = (f32[2,129,128]{2,1,0:T(8,128)S(1)}, f32[2,129,128]{2,1,0:T(8,128)S(1)}, u32[]{:S(2)}, u32[]{:S(2)}) collective-permute-start(f32[2,129,128]{2,1,0:T(8,128)S(1)} %pad_maximum_fusion.2), channel_id=1, source_target_pairs={{0,32},{16,48},{32,0},{48,16},{1,33},{17,49},{33,1},{49,17},{2,34}... | collective-permute-start | bytes 396296 | tf_op jit(solution)/shard_map/ppermute | solution.py:33
  25.6 2.1 %collective-permute-done.1 = f32[2,129,128]{2,1,0:T(8,128)S(1)} collective-permute-done((f32[2,129,128]{2,1,0:T(8,128)S(1)}, f32[2,129,128]{2,1,0:T(8,128)S(1)}, u32[]{:S(2)}, u32[]{:S(2)}) %collective-permute-start.1) | collective-permute-done | bytes 132128 | tf_op jit(solution)/shard_map/ppermute | solution.py:33
  27.7 3.0 %collective-permute-done.2 = f32[2,129,128]{2,1,0:T(8,128)S(1)} collective-permute-done((f32[2,129,128]{2,1,0:T(8,128)S(1)}, f32[2,129,128]{2,1,0:T(8,128)S(1)}, u32[]{:S(2)}, u32[]{:S(2)}) %collective-permute-start.2) | collective-permute-done | bytes 132128 | tf_op jit(solution)/shard_map/ppermute | solution.py:33
  32.5 1.9 %collective-permute-start.4 = (f32[2,33,128]{2,1,0:T(8,128)}, f32[2,33,128]{2,1,0:T(8,128)}, u32[]{:S(2)}, u32[]{:S(2)}) collective-permute-start(f32[2,33,128]{2,1,0:T(8,128)} %pad_maximum_fusion.3), channel_id=1, source_target_pairs={{0,64},{64,128},{128,192},{192,256},{256,320},{320,384},{384,448},... | collective-permute-start | bytes 101384 | tf_op jit(solution)/shard_map/ppermute | solution.py:55
  34.4 2.2 %collective-permute-start.5 = (f32[2,33,128]{2,1,0:T(8,128)}, f32[2,33,128]{2,1,0:T(8,128)}, u32[]{:S(2)}, u32[]{:S(2)}) collective-permute-start(f32[2,33,128]{2,1,0:T(8,128)} %pad_maximum_fusion.3), channel_id=1, source_target_pairs={{0,128},{64,192},{128,256},{192,320},{256,384},{320,448},{1,129},{... | collective-permute-start | bytes 101384 | tf_op jit(solution)/shard_map/ppermute | solution.py:55
  36.6 4.7 %collective-permute-start.6 = (f32[2,33,128]{2,1,0:T(8,128)}, f32[2,33,128]{2,1,0:T(8,128)}, u32[]{:S(2)}, u32[]{:S(2)}) collective-permute-start(f32[2,33,128]{2,1,0:T(8,128)} %pad_maximum_fusion.3), channel_id=1, source_target_pairs={{0,192},{64,256},{128,320},{192,384},{256,448},{1,193},{65,257},{1... | collective-permute-start | bytes 101384 | tf_op jit(solution)/shard_map/ppermute | solution.py:55
  41.2 2.0 %collective-permute-start.7 = (f32[2,33,128]{2,1,0:T(8,128)}, f32[2,33,128]{2,1,0:T(8,128)}, u32[]{:S(2)}, u32[]{:S(2)}) collective-permute-start(f32[2,33,128]{2,1,0:T(8,128)} %pad_maximum_fusion.3), channel_id=1, source_target_pairs={{0,256},{64,320},{128,384},{192,448},{1,257},{65,321},{129,385},{1... | collective-permute-start | bytes 101384 | tf_op jit(solution)/shard_map/ppermute | solution.py:55
  43.3 3.2 %fusion.5 = f32[1024,128]{0,1:T(8,128)} fusion(f32[1024]{0:T(1024)} %bitcast.103, bf16[1024,512]{1,0:T(8,128)(2,1)} %param.8, bf16[1024,512]{1,0:T(8,128)(2,1)S(1)} %copy-done, bf16[1024,512]{1,0:T(8,128)(2,1)S(1)} %copy-done.1), kind=kOutput, calls=%fused_computation.13 | convolution fusion | flops 543162368 | bytes 1318912 | tf_op jit(solution)/shard_map/dot_general | solution.py:121
  48.8 1.5 %fusion.51 = f32[2,32,128]{2,1,0:T(8,128)} fusion(f32[2,33,128]{2,1,0:T(8,128)} %collective-permute-done.7, f32[2,33,128]{2,1,0:T(8,128)} %collective-permute-done.6, f32[2,33,128]{2,1,0:T(8,128)} %collective-permute-done.5, f32[2,33,128]{2,1,0:T(8,128)} %collective-permute-done.4, f32[2]{0:T(128)S(1)} %get-tuple-element.15, f32[2]{0:T(128)S(1)} %get-tuple-element.14, ...), kind=kLoop, calls=%fused_computation.74 | loop fusion | flops 49152 | bytes 163864 | tf_op jit(solution)/shard_map/add | solution.py:63
  50.4 1.4 %pad_maximum_fusion.4 = f32[2,33,128]{2,1,0:T(8,128)} fusion(f32[2,1,128]{2,1,0:T(1,128)S(1)} %broadcast_in_dim.45, f32[2,32,128]{2,1,0:T(8,128)} %fusion.51), kind=kLoop, calls=%fused_computation.70 | loop fusion | flops 8448 | bytes 67584 | tf_op jit(solution)/shard_map/concatenate | solution.py:23
  51.8 5.7 %collective-permute-start.8 = (f32[2,33,128]{2,1,0:T(8,128)}, f32[2,33,128]{2,1,0:T(8,128)}, u32[]{:S(2)}, u32[]{:S(2)}) collective-permute-start(f32[2,33,128]{2,1,0:T(8,128)} %pad_maximum_fusion.4), channel_id=1, source_target_pairs={{0,256},{64,320},{128,384},{192,448},{1,257},{65,321},{129,385},{1... | collective-permute-start | bytes 101384 | tf_op jit(solution)/shard_map/ppermute | solution.py:55
  57.5 2.9 %fusion.6 = f32[1024,128]{0,1:T(8,128)} fusion(f32[1024]{0:T(1024)} %bitcast.102, bf16[1024,512]{1,0:T(8,128)(2,1)S(1)} %copy-done.2, bf16[1024,512]{1,0:T(8,128)(2,1)S(1)} %copy-done, bf16[1024,512]{1,0:T(8,128)(2,1)S(1)} %copy-done.1), kind=kOutput, calls=%fused_computation.14 | convolution fusion | flops 543162368 | bytes 1318912 | tf_op jit(solution)/shard_map/dot_general | solution.py:121
  60.5 1.5 %fusion.50 = f32[2,32,128]{2,1,0:T(8,128)} fusion(f32[2,32,128]{2,1,0:T(8,128)} %fusion.51, f32[2,33,128]{2,1,0:T(8,128)} %collective-permute-done.8, f32[2]{0:T(128)} %get-tuple-element.12), kind=kLoop, calls=%fused_computation.72 | loop fusion | flops 16384 | bytes 98312 | tf_op jit(solution)/shard_map/add | solution.py:68
  61.9 3.2 %collective-permute-start.10 = (f32[2,32,128]{2,1,0:T(8,128)}, f32[2,32,128]{2,1,0:T(8,128)}, u32[]{:S(2)}, u32[]{:S(2)}) collective-permute-start(f32[2,32,128]{2,1,0:T(8,128)} %fusion.50), channel_id=1, source_target_pairs={{0,32},{16,48},{32,0},{48,16},{1,33},{17,49},{33,1},{49,17},{2,34}... | collective-permute-start | bytes 98312 | tf_op jit(solution)/shard_map/ppermute | solution.py:33
  65.2 3.1 %collective-permute-start.11 = (f32[2,32,128]{2,1,0:T(8,128)}, f32[2,32,128]{2,1,0:T(8,128)}, u32[]{:S(2)}, u32[]{:S(2)}) collective-permute-start(f32[2,32,128]{2,1,0:T(8,128)} %fusion.50), channel_id=1, source_target_pairs={{0,48},{16,0},{32,16},{48,32},{1,49},{17,1},{33,17},{49,33},{2,50}... | collective-permute-start | bytes 98312 | tf_op jit(solution)/shard_map/ppermute | solution.py:33
  68.2 2.3 %collective-permute-start.9 = (f32[2,32,128]{2,1,0:T(8,128)}, f32[2,32,128]{2,1,0:T(8,128)}, u32[]{:S(2)}, u32[]{:S(2)}) collective-permute-start(f32[2,32,128]{2,1,0:T(8,128)} %fusion.50), channel_id=1, source_target_pairs={{0,16},{16,32},{32,48},{48,0},{1,17},{17,33},{33,49},{49,1},{2,18}... | collective-permute-start | bytes 98312 | tf_op jit(solution)/shard_map/ppermute | solution.py:33
  70.5 2.2 %fusion.7 = f32[1024,128]{0,1:T(8,128)} fusion(f32[1024]{0:T(1024)S(1)} %bitcast.101, bf16[1024,512]{1,0:T(8,128)(2,1)S(1)} %copy-done.2, bf16[1024,512]{1,0:T(8,128)(2,1)S(1)} %copy-done, bf16[1024,512]{1,0:T(8,128)(2,1)S(1)} %copy-done.1), kind=kOutput, calls=%fused_computation.15 | convolution fusion | flops 543162368 | bytes 1318912 | tf_op jit(solution)/shard_map/dot_general | solution.py:121
  72.7 1.7 %collective-permute-done.9 = f32[2,32,128]{2,1,0:T(8,128)} collective-permute-done((f32[2,32,128]{2,1,0:T(8,128)}, f32[2,32,128]{2,1,0:T(8,128)}, u32[]{:S(2)}, u32[]{:S(2)}) %collective-permute-start.9) | collective-permute-done | bytes 32800 | tf_op jit(solution)/shard_map/ppermute | solution.py:33
  75.3 1.4 fusion.49
  76.6 7.2 %collective-permute-start.12 = (f32[2,128,128]{2,1,0:T(8,128)}, f32[2,128,128]{2,1,0:T(8,128)}, u32[]{:S(2)}, u32[]{:S(2)}) collective-permute-start(f32[2,128,128]{2,1,0:T(8,128)} %fusion.49), channel_id=1, source_target_pairs={{0,8},{8,0},{1,9},{9,1},{2,10},{10,2},{3,11},{11,3},{4,12},{12,4},... | collective-permute-start | bytes 393224 | tf_op jit(solution)/shard_map/ppermute | solution.py:107
  83.8 2.2 %fusion.8 = f32[1024,128]{0,1:T(8,128)} fusion(f32[1024]{0:T(1024)S(1)} %bitcast.100, bf16[1024,512]{1,0:T(8,128)(2,1)S(1)} %copy-done.2, bf16[1024,512]{1,0:T(8,128)(2,1)S(1)} %copy-done, bf16[1024,512]{1,0:T(8,128)(2,1)S(1)} %copy-done.1), kind=kOutput, calls=%fused_computation.16 | convolution fusion | flops 543162368 | bytes 1318912 | tf_op jit(solution)/shard_map/dot_general | solution.py:121
  86.0 1.6 %copy.40 = bf16[1024,512]{0,1:T(8,128)(2,1)S(1)} copy(bf16[1024,512]{1,0:T(8,128)(2,1)} %param.10) | data formatting | bytes 2097152 | tf_op args[4]
  88.5 1.3 add_select_fusion
  94.4 40.4 %all_to_all.5 = bf16[8,129,512]{2,1,0:T(8,128)(2,1)S(1)} all-to-all(bf16[8,129,512]{2,1,0:T(8,128)(2,1)S(1)} %maximum_maximum_fusion), channel_id=1, replica_groups=mesh['cy'=8,'cx'=4,'cc'=2,'head'=8] {'head'}, dimensions={0} | all-to-all | bytes 2113536 | tf_op jit(solution)/shard_map/all_to_all | solution.py:164
  135.9 1.3 copy.46
  (74 shorter events, 14.7 us)
Async XLA Ops:
  6.5 36.8 %copy-start = (bf16[1024,512]{1,0:T(8,128)(2,1)S(1)}, bf16[1024,512]{1,0:T(8,128)(2,1)}, u32[]{:S(2)}) copy-start(bf16[1024,512]{1,0:T(8,128)(2,1)} %param.7) | copy-start | bytes 3145732
  6.5 36.8 %copy-start.1 = (bf16[1024,512]{1,0:T(8,128)(2,1)S(1)}, bf16[1024,512]{1,0:T(8,128)(2,1)}, u32[]{:S(2)}) copy-start(bf16[1024,512]{1,0:T(8,128)(2,1)} %param.6) | copy-start | bytes 3145732
  6.6 10.1 %collective-permute-start = (f32[4,129,128]{2,1,0:T(8,128)S(1)}, f32[4,129,128]{2,1,0:T(8,128)S(1)}, u32[]{:S(2)}, u32[]{:S(2)}) collective-permute-start(f32[4,129,128]{2,1,0:T(8,128)S(1)} %pad_maximum_fusion.1), channel_id=1, source_target_pairs={{0,8},{8,0},{1,9},{9,1},{2,10},{10,2},{3,11},{11,3},{4,12},{12,4},... | collective-permute-start | bytes 792584 | tf_op jit(solution)/shard_map/ppermute | solution.py:80
  17.8 7.9 %collective-permute-start.3 = (f32[2,129,128]{2,1,0:T(8,128)S(1)}, f32[2,129,128]{2,1,0:T(8,128)S(1)}, u32[]{:S(2)}, u32[]{:S(2)}) collective-permute-start(f32[2,129,128]{2,1,0:T(8,128)S(1)} %pad_maximum_fusion.2), channel_id=1, source_target_pairs={{0,48},{16,0},{32,16},{48,32},{1,49},{17,1},{33,17},{49,33},{2,50}... | collective-permute-start | bytes 396296 | tf_op jit(solution)/shard_map/ppermute | solution.py:33
  19.7 8.0 %collective-permute-start.1 = (f32[2,129,128]{2,1,0:T(8,128)S(1)}, f32[2,129,128]{2,1,0:T(8,128)S(1)}, u32[]{:S(2)}, u32[]{:S(2)}) collective-permute-start(f32[2,129,128]{2,1,0:T(8,128)S(1)} %pad_maximum_fusion.2), channel_id=1, source_target_pairs={{0,16},{16,32},{32,48},{48,0},{1,17},{17,33},{33,49},{49,1},{2,18}... | collective-permute-start | bytes 396296 | tf_op jit(solution)/shard_map/ppermute | solution.py:33
  23.1 7.6 %collective-permute-start.2 = (f32[2,129,128]{2,1,0:T(8,128)S(1)}, f32[2,129,128]{2,1,0:T(8,128)S(1)}, u32[]{:S(2)}, u32[]{:S(2)}) collective-permute-start(f32[2,129,128]{2,1,0:T(8,128)S(1)} %pad_maximum_fusion.2), channel_id=1, source_target_pairs={{0,32},{16,48},{32,0},{48,16},{1,33},{17,49},{33,1},{49,17},{2,34}... | collective-permute-start | bytes 396296 | tf_op jit(solution)/shard_map/ppermute | solution.py:33
  32.5 14.0 %collective-permute-start.4 = (f32[2,33,128]{2,1,0:T(8,128)}, f32[2,33,128]{2,1,0:T(8,128)}, u32[]{:S(2)}, u32[]{:S(2)}) collective-permute-start(f32[2,33,128]{2,1,0:T(8,128)} %pad_maximum_fusion.3), channel_id=1, source_target_pairs={{0,64},{64,128},{128,192},{192,256},{256,320},{320,384},{384,448},... | collective-permute-start | bytes 101384 | tf_op jit(solution)/shard_map/ppermute | solution.py:55
  34.4 12.1 %collective-permute-start.5 = (f32[2,33,128]{2,1,0:T(8,128)}, f32[2,33,128]{2,1,0:T(8,128)}, u32[]{:S(2)}, u32[]{:S(2)}) collective-permute-start(f32[2,33,128]{2,1,0:T(8,128)} %pad_maximum_fusion.3), channel_id=1, source_target_pairs={{0,128},{64,192},{128,256},{192,320},{256,384},{320,448},{1,129},{... | collective-permute-start | bytes 101384 | tf_op jit(solution)/shard_map/ppermute | solution.py:55
  36.6 9.9 %collective-permute-start.6 = (f32[2,33,128]{2,1,0:T(8,128)}, f32[2,33,128]{2,1,0:T(8,128)}, u32[]{:S(2)}, u32[]{:S(2)}) collective-permute-start(f32[2,33,128]{2,1,0:T(8,128)} %pad_maximum_fusion.3), channel_id=1, source_target_pairs={{0,192},{64,256},{128,320},{192,384},{256,448},{1,193},{65,257},{1... | collective-permute-start | bytes 101384 | tf_op jit(solution)/shard_map/ppermute | solution.py:55
  41.2 5.3 %collective-permute-start.7 = (f32[2,33,128]{2,1,0:T(8,128)}, f32[2,33,128]{2,1,0:T(8,128)}, u32[]{:S(2)}, u32[]{:S(2)}) collective-permute-start(f32[2,33,128]{2,1,0:T(8,128)} %pad_maximum_fusion.3), channel_id=1, source_target_pairs={{0,256},{64,320},{128,384},{192,448},{1,257},{65,321},{129,385},{1... | collective-permute-start | bytes 101384 | tf_op jit(solution)/shard_map/ppermute | solution.py:55
  43.3 14.2 %copy-start.2 = (bf16[1024,512]{1,0:T(8,128)(2,1)S(1)}, bf16[1024,512]{1,0:T(8,128)(2,1)}, u32[]{:S(2)}) copy-start(bf16[1024,512]{1,0:T(8,128)(2,1)} %param.8) | copy-start | bytes 3145732
  51.8 8.7 %collective-permute-start.8 = (f32[2,33,128]{2,1,0:T(8,128)}, f32[2,33,128]{2,1,0:T(8,128)}, u32[]{:S(2)}, u32[]{:S(2)}) collective-permute-start(f32[2,33,128]{2,1,0:T(8,128)} %pad_maximum_fusion.4), channel_id=1, source_target_pairs={{0,256},{64,320},{128,384},{192,448},{1,257},{65,321},{129,385},{1... | collective-permute-start | bytes 101384 | tf_op jit(solution)/shard_map/ppermute | solution.py:55
  61.9 10.8 %collective-permute-start.10 = (f32[2,32,128]{2,1,0:T(8,128)}, f32[2,32,128]{2,1,0:T(8,128)}, u32[]{:S(2)}, u32[]{:S(2)}) collective-permute-start(f32[2,32,128]{2,1,0:T(8,128)} %fusion.50), channel_id=1, source_target_pairs={{0,32},{16,48},{32,0},{48,16},{1,33},{17,49},{33,1},{49,17},{2,34}... | collective-permute-start | bytes 98312 | tf_op jit(solution)/shard_map/ppermute | solution.py:33
  65.2 7.6 %collective-permute-start.11 = (f32[2,32,128]{2,1,0:T(8,128)}, f32[2,32,128]{2,1,0:T(8,128)}, u32[]{:S(2)}, u32[]{:S(2)}) collective-permute-start(f32[2,32,128]{2,1,0:T(8,128)} %fusion.50), channel_id=1, source_target_pairs={{0,48},{16,0},{32,16},{48,32},{1,49},{17,1},{33,17},{49,33},{2,50}... | collective-permute-start | bytes 98312 | tf_op jit(solution)/shard_map/ppermute | solution.py:33
  68.2 6.2 %collective-permute-start.9 = (f32[2,32,128]{2,1,0:T(8,128)}, f32[2,32,128]{2,1,0:T(8,128)}, u32[]{:S(2)}, u32[]{:S(2)}) collective-permute-start(f32[2,32,128]{2,1,0:T(8,128)} %fusion.50), channel_id=1, source_target_pairs={{0,16},{16,32},{32,48},{48,0},{1,17},{17,33},{33,49},{49,1},{2,18}... | collective-permute-start | bytes 98312 | tf_op jit(solution)/shard_map/ppermute | solution.py:33
  76.6 11.8 %collective-permute-start.12 = (f32[2,128,128]{2,1,0:T(8,128)}, f32[2,128,128]{2,1,0:T(8,128)}, u32[]{:S(2)}, u32[]{:S(2)}) collective-permute-start(f32[2,128,128]{2,1,0:T(8,128)} %fusion.49), channel_id=1, source_target_pairs={{0,8},{8,0},{1,9},{9,1},{2,10},{10,2},{3,11},{11,3},{4,12},{12,4},... | collective-permute-start | bytes 393224 | tf_op jit(solution)/shard_map/ppermute | solution.py:107
  86.0 3.7 %copy-start.3 = (f32[1024,128]{0,1:T(8,128)S(1)}, f32[1024,128]{0,1:T(8,128)}, u32[]{:S(2)}) copy-start(f32[1024,128]{0,1:T(8,128)} %fusion.5) | copy-start | bytes 1572868
  86.0 4.8 %copy-start.4 = (f32[1024,128]{0,1:T(8,128)S(1)}, f32[1024,128]{0,1:T(8,128)}, u32[]{:S(2)}) copy-start(f32[1024,128]{0,1:T(8,128)} %fusion.6) | copy-start | bytes 1572868
  87.6 4.4 %copy-start.5 = (f32[1024,128]{0,1:T(8,128)S(1)}, f32[1024,128]{0,1:T(8,128)}, u32[]{:S(2)}) copy-start(f32[1024,128]{0,1:T(8,128)} %fusion.7) | copy-start | bytes 1572868
  88.4 4.0 %copy-start.6 = (f32[1024,128]{0,1:T(8,128)S(1)}, f32[1024,128]{0,1:T(8,128)}, u32[]{:S(2)}) copy-start(f32[1024,128]{0,1:T(8,128)} %fusion.8) | copy-start | bytes 1572868

commit v10 on v9

--- a/solution.py
+++ b/solution.py
@@ -111,6 +111,19 @@
     return jnp.where(c == 0, chip_full, jnp.exp(L0)[:, None, None] * chip_full + S0)
 
 
+def split3(x):
+    hi = lax.reduce_precision(x, exponent_bits=8, mantissa_bits=7)
+    rest = x - hi
+    mid = lax.reduce_precision(rest, exponent_bits=8, mantissa_bits=7)
+    lo = rest - mid
+    return hi.astype(jnp.bfloat16), mid.astype(jnp.bfloat16), lo.astype(jnp.bfloat16)
+
+
+def sum3(product, axis):
+    a, b, c = jnp.split(product, 3, axis=axis)
+    return (a + b) + c
+
+
 def inner_head(qh, kh, vh, ch):
     count = qh.shape[0]
     target_index = jnp.arange(count)
@@ -131,8 +144,13 @@
     def cols(array, h):
         return array[:, h * size : (h + 1) * size]
 
-    keyed = keys.reshape(count, heads, size).astype(F32) * jnp.exp(last[None, :] - cum)[:, :, None]
-    state = jnp.einsum("thd,the->hde", keyed, values.reshape(count, heads, size).astype(F32), precision=HI)
+    def block_state(h):
+        keyed = cols(keys, h).astype(F32) * jnp.exp(last[h] - cum[:, h])[:, None]
+        pieces = jnp.concatenate(split3(keyed), axis=1)
+        product = lax.dot_general(pieces, cols(values, h), (((0,), (0,)), ((), ())), preferred_element_type=F32)
+        return sum3(product, 0)
+
+    state = jnp.stack([block_state(h) for h in range(heads)])
 
     carried = carried_state(last, state)
 
@@ -140,7 +158,7 @@
     for h in range(heads):
         qh = cols(queries, h)
         inner = inner_head(qh, cols(keys, h), cols(values, h), cum[:, h])
-        across = jnp.dot(qh.astype(F32), carried[h], precision=HI)
+        across = sum3(jnp.dot(qh, jnp.concatenate(split3(carried[h]), axis=1), preferred_element_type=F32), 1)
         joined.append(inner + jnp.exp(cum[:, h])[:, None] * across)
     attended = jnp.concatenate(joined, axis=1).astype(jnp.bfloat16)
 

time: 138 us -> 140 us (1.014)
  waiting for transfers between devices: 7.94 us -> 11.9 us
  other arithmetic: 14.7 us -> 11 us
  local copies, waits for them, and re-layouts: 9.38 us -> 6.25 us
  starting transfers between devices: 48.4 us -> 51.5 us
  matrix products: 16 us -> 17.8 us
    ppermute x6, starting transfers between devices: 15.8 us -> 19.1 us  [shifted(): out.append(lax.ppermute(x, axis, [(j, (j + s) % n) for j in range(n)]))]
    exp x1, other arithmetic: 0.09 us -> 3.14 us  [body(): joined.append(inner + jnp.exp(cum[:, h])[:, None] * across)]
    convert_element_type x0 -> x2, other arithmetic: none -> 2.81 us  [split3(): hi.astype(jnp.bfloat16)]
    ppermute x5, waiting for transfers between devices: 0.01 us -> 2.14 us  [shift(): return lax.ppermute(packed, axis, [(j, j + d) for j in range(n - d)])]
    concatenate x4, other arithmetic: 2.04 us -> 0.05 us  [pack(): return jnp.concatenate([state, row], axis=1)]
    ppermute x6, waiting for transfers between devices: 6.78 us -> 8.58 us  [shifted(): out.append(lax.ppermute(x, axis, [(j, (j + s) % n) for j in range(n)]))]
    dot_general x5 -> x8, matrix products: 5.47 us -> 7.07 us  [the longest x4 5.43 us: body(): jnp.dot(qh, jnp.concatenate(split3(carried[h]), axis=1), preferred_elemen...]
    convert_element_type x1 -> x0, local copies, waits for them, and re-layouts: 1.49 us -> none  [body(): keys.reshape(count, heads, size).astype(F32)]
  transfers between devices with their start and end apart: 13 -> 13, of which waited for: 4 -> 6; matrix products, arithmetic and copies ran while one was open for 10% -> 1% of each run, Pallas kernels for 0% -> 0%
where the time goes in v10:
time: 140 us; the launch traced here: 139 us
  starting transfers between devices  51.5 us (37%)
  blocking collectives  40.5 us (29%)
  matrix products  17.8 us (13%)
  waiting for transfers between devices  11.9 us (8%)
  other arithmetic  11 us (8%)
  local copies, waits for them, and re-layouts  6.25 us (4%)
    all_to_all x1, blocking collectives, body(): lax.all_to_all(payload, 'head', split_axis=0, concat_axis=0, tiled=True)  40.5 us
    ppermute x6, starting transfers between devices, shifted(): out.append(lax.ppermute(x, axis, [(j, (j + s) % n) for j in range(n)]))  19.1 us
    ppermute x5, starting transfers between devices, shift(): return lax.ppermute(packed, axis, [(j, j + d) for j in range(n - d)])  16.9 us
    dot_general x4, matrix products, inner_head(): return jnp.dot(weights, vh, preferred_element_type=F32)  10.7 us
    ppermute x1, starting transfers between devices, carried_state(): pair = unpack(lax.ppermute(pack(L, S), 'cc', [(0, 1), (1, 0)]))  8.79 us
    ppermute x6, waiting for transfers between devices, shifted(): out.append(lax.ppermute(x, axis, [(j, (j + s) % n) for j in range(n)]))  8.58 us
    ppermute x1, starting transfers between devices, carried_state(): other = lax.ppermute(chip_before, 'cc', [(0, 1), (1, 0)])  6.76 us
    dot_general x4, matrix products, body(): jnp.dot(qh, jnp.concatenate(split3(carried[h]), axis=1), preferred_elemen...  5.43 us
  transfers between devices with their start and end apart: 13, of which 6 were waited for; matrix products, arithmetic and copies ran while one was open for 1% of the time, Pallas kernels for 0%

profile of v10, /device:TPU:1, one launch (start us, length us, event | category | flops | bytes accessed | tf_op | source)
XLA Modules:
  0.0 139.4 jit_solution(7970984400979180683)
XLA Ops:
  0.7 1.1 reduce-window.6
  3.1 3.1 %slice_exponential_fusion.3 = (f32[1024,1]{0,1:T(1,128)S(1)}, f32[1024,1]{0,1:T(1,128)S(1)}, f32[1024,1]{0,1:T(1,128)S(1)}, f32[1024,1]{0,1:T(1,128)S(1)}, f32[1...) fusion(f32[1024,4]{0,1:T(4,128)S(1)} %bitcast.107, ...), kind=kLoop, calls=%fused_computation.270 | loop fusion | flops 4096 | bytes 65552 | tf_op jit(solution)/shard_map/exp | solution.py:162
  6.3 2.1 %reduce-precision_convert_fusion.7 = (bf16[1024,128]{1,0:T(8,128)(2,1)S(1)}, bf16[1024,128]{1,0:T(8,128)(2,1)S(1)}, bf16[1024,128]{1,0:T(8,128)(2,1)S(1)}, bf16[...) fusion(f32[1024]{0:T(1024)S(1)} %bitcast.110, ...), kind=kLoop, calls=%fused_computation.68 | loop fusion | flops 4718592 | bytes 4210688 | tf_op jit(solution)/shard_map/convert_element_type | solution.py:119
  10.3 8.8 %collective-permute-start = (f32[4,129,128]{2,1,0:T(8,128)S(1)}, f32[4,129,128]{2,1,0:T(8,128)S(1)}, u32[]{:S(2)}, u32[]{:S(2)}) collective-permute-start(f32[4,129,128]{2,1,0:T(8,128)S(1)} %pad_maximum_fusion.1), channel_id=1, source_target_pairs={{0,8},{8,0},{1,9},{9,1},{2,10},{10,2},{3,11},{11,3},{4,12},{12,4},... | collective-permute-start | bytes 792584 | tf_op jit(solution)/shard_map/ppermute | solution.py:80
  19.1 1.2 collective-permute-done
  20.8 2.1 %collective-permute-start.1 = (f32[2,129,128]{2,1,0:T(8,128)S(1)}, f32[2,129,128]{2,1,0:T(8,128)S(1)}, u32[]{:S(2)}, u32[]{:S(2)}) collective-permute-start(f32[2,129,128]{2,1,0:T(8,128)S(1)} %pad_maximum_fusion.3), channel_id=1, source_target_pairs={{0,16},{16,32},{32,48},{48,0},{1,17},{17,33},{33,49},{49,1},{2,18}... | collective-permute-start | bytes 396296 | tf_op jit(solution)/shard_map/ppermute | solution.py:33
  22.8 1.9 %collective-permute-start.2 = (f32[2,129,128]{2,1,0:T(8,128)S(1)}, f32[2,129,128]{2,1,0:T(8,128)S(1)}, u32[]{:S(2)}, u32[]{:S(2)}) collective-permute-start(f32[2,129,128]{2,1,0:T(8,128)S(1)} %pad_maximum_fusion.3), channel_id=1, source_target_pairs={{0,32},{16,48},{32,0},{48,16},{1,33},{17,49},{33,1},{49,17},{2,34}... | collective-permute-start | bytes 396296 | tf_op jit(solution)/shard_map/ppermute | solution.py:33
  24.8 4.6 %collective-permute-start.3 = (f32[2,129,128]{2,1,0:T(8,128)S(1)}, f32[2,129,128]{2,1,0:T(8,128)S(1)}, u32[]{:S(2)}, u32[]{:S(2)}) collective-permute-start(f32[2,129,128]{2,1,0:T(8,128)S(1)} %pad_maximum_fusion.3), channel_id=1, source_target_pairs={{0,48},{16,0},{32,16},{48,32},{1,49},{17,1},{33,17},{49,33},{2,50}... | collective-permute-start | bytes 396296 | tf_op jit(solution)/shard_map/ppermute | solution.py:33
  29.4 1.8 %collective-permute-done.2 = f32[2,129,128]{2,1,0:T(8,128)S(1)} collective-permute-done((f32[2,129,128]{2,1,0:T(8,128)S(1)}, f32[2,129,128]{2,1,0:T(8,128)S(1)}, u32[]{:S(2)}, u32[]{:S(2)}) %collective-permute-start.2) | collective-permute-done | bytes 132128 | tf_op jit(solution)/shard_map/ppermute | solution.py:33
  31.2 2.9 %collective-permute-done.3 = f32[2,129,128]{2,1,0:T(8,128)S(1)} collective-permute-done((f32[2,129,128]{2,1,0:T(8,128)S(1)}, f32[2,129,128]{2,1,0:T(8,128)S(1)}, u32[]{:S(2)}, u32[]{:S(2)}) %collective-permute-start.3) | collective-permute-done | bytes 132128 | tf_op jit(solution)/shard_map/ppermute | solution.py:33
  34.7 1.3 collective-permute-start.4
  36.0 1.3 collective-permute-start.5
  37.3 4.5 %collective-permute-start.6 = (f32[2,33,128]{2,1,0:T(8,128)S(1)}, f32[2,33,128]{2,1,0:T(8,128)S(1)}, u32[]{:S(2)}, u32[]{:S(2)}) collective-permute-start(f32[2,33,128]{2,1,0:T(8,128)S(1)} %pad_maximum_fusion.4), channel_id=1, source_target_pairs={{0,192},{64,256},{128,320},{192,384},{256,448},{1,193},{65,257},{1... | collective-permute-start | bytes 101384 | tf_op jit(solution)/shard_map/ppermute | solution.py:55
  41.9 2.0 %collective-permute-start.7 = (f32[2,33,128]{2,1,0:T(8,128)S(1)}, f32[2,33,128]{2,1,0:T(8,128)S(1)}, u32[]{:S(2)}, u32[]{:S(2)}) collective-permute-start(f32[2,33,128]{2,1,0:T(8,128)S(1)} %pad_maximum_fusion.4), channel_id=1, source_target_pairs={{0,256},{64,320},{128,384},{192,448},{1,257},{65,321},{129,385},{1... | collective-permute-start | bytes 101384 | tf_op jit(solution)/shard_map/ppermute | solution.py:55
  45.5 7.7 %collective-permute-start.8 = (f32[2,33,128]{2,1,0:T(8,128)S(1)}, f32[2,33,128]{2,1,0:T(8,128)S(1)}, u32[]{:S(2)}, u32[]{:S(2)}) collective-permute-start(f32[2,33,128]{2,1,0:T(8,128)S(1)} %pad_maximum_fusion.5), channel_id=1, source_target_pairs={{0,256},{64,320},{128,384},{192,448},{1,257},{65,321},{129,385},{1... | collective-permute-start | bytes 101384 | tf_op jit(solution)/shard_map/ppermute | solution.py:55
  53.2 1.1 collective-permute-done.8
  54.3 4.3 %collective-permute-start.10 = (f32[2,32,128]{2,1,0:T(8,128)S(1)}, f32[2,32,128]{2,1,0:T(8,128)S(1)}, u32[]{:S(2)}, u32[]{:S(2)}) collective-permute-start(f32[2,32,128]{2,1,0:T(8,128)S(1)} %fusion.105), channel_id=1, source_target_pairs={{0,32},{16,48},{32,0},{48,16},{1,33},{17,49},{33,1},{49,17},{2,34}... | collective-permute-start | bytes 98312 | tf_op jit(solution)/shard_map/ppermute | solution.py:33
  58.6 4.4 %collective-permute-start.11 = (f32[2,32,128]{2,1,0:T(8,128)S(1)}, f32[2,32,128]{2,1,0:T(8,128)S(1)}, u32[]{:S(2)}, u32[]{:S(2)}) collective-permute-start(f32[2,32,128]{2,1,0:T(8,128)S(1)} %fusion.105), channel_id=1, source_target_pairs={{0,48},{16,0},{32,16},{48,32},{1,49},{17,1},{33,17},{49,33},{2,50}... | collective-permute-start | bytes 98312 | tf_op jit(solution)/shard_map/ppermute | solution.py:33
  63.0 1.9 %collective-permute-start.9 = (f32[2,32,128]{2,1,0:T(8,128)S(1)}, f32[2,32,128]{2,1,0:T(8,128)S(1)}, u32[]{:S(2)}, u32[]{:S(2)}) collective-permute-start(f32[2,32,128]{2,1,0:T(8,128)S(1)} %fusion.105), channel_id=1, source_target_pairs={{0,16},{16,32},{32,48},{48,0},{1,17},{17,33},{33,49},{49,1},{2,18}... | collective-permute-start | bytes 98312 | tf_op jit(solution)/shard_map/ppermute | solution.py:33
  65.0 3.8 %collective-permute-done.9 = f32[2,32,128]{2,1,0:T(8,128)S(1)} collective-permute-done((f32[2,32,128]{2,1,0:T(8,128)S(1)}, f32[2,32,128]{2,1,0:T(8,128)S(1)}, u32[]{:S(2)}, u32[]{:S(2)}) %collective-permute-start.9) | collective-permute-done | bytes 32800 | tf_op jit(solution)/shard_map/ppermute | solution.py:33
  69.0 6.8 %collective-permute-start.12 = (f32[2,128,128]{2,1,0:T(8,128)S(1)}, f32[2,128,128]{2,1,0:T(8,128)S(1)}, u32[]{:S(2)}, u32[]{:S(2)}) collective-permute-start(f32[2,128,128]{2,1,0:T(8,128)S(1)} %fusion.76), channel_id=1, source_target_pairs={{0,8},{8,0},{1,9},{9,1},{2,10},{10,2},{3,11},{11,3},{4,12},{12,4},... | collective-permute-start | bytes 393224 | tf_op jit(solution)/shard_map/ppermute | solution.py:107
  77.9 1.3 convolution_bitcast_fusion.3
  79.2 2.5 %fusion.11 = bf16[1024,128]{0,1:T(8,128)(2,1)S(1)} fusion(f32[1024]{0:T(1024)S(1)} %bitcast.123, f32[1024,384]{0,1:T(8,128)S(1)} %convolution_bitcast_fusion.3, f32[1024]{0:T(1024)S(1)} %bitcast.122, bf16[1024,512]{1,0:T(8,128)(2,1)} %param.8, bf16[1024,512]{1,0:T(8,128)(2,1)} %param.6, bf16[1024,512]{1,0:T(8,128)(2,1)} %param.7), kind=kOutput, calls=%fused_computation.23 | convolution fusion | flops 543817728 | bytes 2633728 | tf_op jit(solution)/shard_map/dot_general | solution.py:134
  81.7 1.3 convolution_bitcast_fusion.2
  83.1 2.5 %fusion.12 = bf16[1024,128]{0,1:T(8,128)(2,1)S(1)} fusion(f32[1024]{0:T(1024)S(1)} %bitcast.121, f32[1024,384]{0,1:T(8,128)S(1)} %convolution_bitcast_fusion.2, f32[1024]{0:T(1024)S(1)} %bitcast.120, bf16[1024,512]{1,0:T(8,128)(2,1)} %param.6, bf16[1024,512]{1,0:T(8,128)(2,1)} %param.8, bf16[1024,512]{1,0:T(8,128)(2,1)} %param.7), kind=kOutput, calls=%fused_computation.24 | convolution fusion | flops 543817728 | bytes 2633728 | tf_op jit(solution)/shard_map/dot_general | solution.py:134
  85.6 1.3 convolution_bitcast_fusion.1
  86.9 2.5 %fusion.13 = bf16[1024,128]{0,1:T(8,128)(2,1)S(1)} fusion(f32[1024]{0:T(1024)} %bitcast.119, f32[1024,384]{0,1:T(8,128)S(1)} %convolution_bitcast_fusion.1, f32[1024]{0:T(1024)} %bitcast.118, bf16[1024,512]{1,0:T(8,128)(2,1)} %param.6, bf16[1024,512]{1,0:T(8,128)(2,1)} %param.8, bf16[1024,512]{1,0:T(8,128)(2,1)} %param.7), kind=kOutput, calls=%fused_computation.25 | convolution fusion | flops 543817728 | bytes 2633728 | tf_op jit(solution)/shard_map/dot_general | solution.py:134
  89.5 1.4 %convolution_bitcast_fusion = f32[1024,384]{0,1:T(8,128)S(1)} fusion(bf16[1024,512]{1,0:T(8,128)(2,1)} %param.6, bf16[128,128]{1,0:T(8,128)(2,1)} %get-tuple-element.57, bf16[128,128]{1,0:T(8,128)(2,1)} %get-tuple-element.61, bf16[128,128]{1,0:T(8,128)(2,1)} %get-tuple-element.65), kind=kOutput, calls=%fused_computation.11 | convolution fusion | flops 100958208 | bytes 1933312 | tf_op jit(solution)/shard_map/dot_general | solution.py:161
  90.9 3.2 %fusion.14 = bf16[1024,128]{0,1:T(8,128)(2,1)} fusion(f32[1024]{0:T(1024)} %bitcast.117, f32[1024,384]{0,1:T(8,128)S(1)} %convolution_bitcast_fusion, f32[1024]{0:T(1024)S(1)} %bitcast.116, bf16[1024,512]{1,0:T(8,128)(2,1)} %param.6, bf16[1024,512]{1,0:T(8,128)(2,1)} %param.8, bf16[1024,512]{1,0:T(8,128)(2,1)} %param.7), kind=kOutput, calls=%fused_computation.26 | convolution fusion | flops 543817728 | bytes 2633728 | tf_op jit(solution)/shard_map/dot_general | solution.py:134
  94.1 1.7 %fusion.1 = (bf16[1024,512]{0,1:T(8,128)(2,1)S(1)}, f32[1024]{0:T(1024)S(1)}) fusion(bf16[1024,512]{0,1:T(8,128)(2,1)S(1)} %copy.29, f32[512]{0:T(512)S(1)} %dynamic_slice.15, bf16[1024,128]{0,1:T(8,128)(2,1)} %fusion.14, bf16[1024,128]{0,1:T(8,128)(2,1)S(1)} %fusion.13, bf16[1024,128]{0,1:T(8,128)(2,1)S(1)} %fusion.12, bf16[1024,128]{0,1:T(8,128)(2,1)S(1)} %fusion.11), kind=kLoop, calls=%fused_computation.8 | loop fusion | flops 8911872 | bytes 3151872 | tf_op jit(solution)/shard_map/convert_element_type | solution.py:169
  96.6 40.5 %all_to_all.5 = bf16[8,129,512]{2,1,0:T(8,128)(2,1)S(1)} all-to-all(bf16[8,129,512]{2,1,0:T(8,128)(2,1)S(1)} %maximum_maximum_fusion), channel_id=1, replica_groups=mesh['cy'=8,'cx'=4,'cc'=2,'head'=8] {'head'}, dimensions={0} | all-to-all | bytes 2113536 | tf_op jit(solution)/shard_map/all_to_all | solution.py:182
  138.1 1.3 copy.35
  (72 shorter events, 10.5 us)
Async XLA Ops:
  6.3 2.1 %copy-start.1 = (bf16[1024,512]{1,0:T(8,128)(2,1)S(1)}, bf16[1024,512]{1,0:T(8,128)(2,1)}, u32[]{:S(2)}) copy-start(bf16[1024,512]{1,0:T(8,128)(2,1)} %param.8) | copy-start | bytes 3145732
  10.3 10.0 %collective-permute-start = (f32[4,129,128]{2,1,0:T(8,128)S(1)}, f32[4,129,128]{2,1,0:T(8,128)S(1)}, u32[]{:S(2)}, u32[]{:S(2)}) collective-permute-start(f32[4,129,128]{2,1,0:T(8,128)S(1)} %pad_maximum_fusion.1), channel_id=1, source_target_pairs={{0,8},{8,0},{1,9},{9,1},{2,10},{10,2},{3,11},{11,3},{4,12},{12,4},... | collective-permute-start | bytes 792584 | tf_op jit(solution)/shard_map/ppermute | solution.py:80
  20.6 55.2 %copy-start = (bf16[1024,512]{1,0:T(8,128)(2,1)S(1)}, bf16[1024,512]{1,0:T(8,128)(2,1)}, u32[]{:S(2)}) copy-start(bf16[1024,512]{1,0:T(8,128)(2,1)} %param.10) | copy-start | bytes 3145732
  20.8 8.6 %collective-permute-start.1 = (f32[2,129,128]{2,1,0:T(8,128)S(1)}, f32[2,129,128]{2,1,0:T(8,128)S(1)}, u32[]{:S(2)}, u32[]{:S(2)}) collective-permute-start(f32[2,129,128]{2,1,0:T(8,128)S(1)} %pad_maximum_fusion.3), channel_id=1, source_target_pairs={{0,16},{16,32},{32,48},{48,0},{1,17},{17,33},{33,49},{49,1},{2,18}... | collective-permute-start | bytes 396296 | tf_op jit(solution)/shard_map/ppermute | solution.py:33
  22.8 8.3 %collective-permute-start.2 = (f32[2,129,128]{2,1,0:T(8,128)S(1)}, f32[2,129,128]{2,1,0:T(8,128)S(1)}, u32[]{:S(2)}, u32[]{:S(2)}) collective-permute-start(f32[2,129,128]{2,1,0:T(8,128)S(1)} %pad_maximum_fusion.3), channel_id=1, source_target_pairs={{0,32},{16,48},{32,0},{48,16},{1,33},{17,49},{33,1},{49,17},{2,34}... | collective-permute-start | bytes 396296 | tf_op jit(solution)/shard_map/ppermute | solution.py:33
  24.8 9.3 %collective-permute-start.3 = (f32[2,129,128]{2,1,0:T(8,128)S(1)}, f32[2,129,128]{2,1,0:T(8,128)S(1)}, u32[]{:S(2)}, u32[]{:S(2)}) collective-permute-start(f32[2,129,128]{2,1,0:T(8,128)S(1)} %pad_maximum_fusion.3), channel_id=1, source_target_pairs={{0,48},{16,0},{32,16},{48,32},{1,49},{17,1},{33,17},{49,33},{2,50}... | collective-permute-start | bytes 396296 | tf_op jit(solution)/shard_map/ppermute | solution.py:33
  34.7 9.2 %collective-permute-start.4 = (f32[2,33,128]{2,1,0:T(8,128)S(1)}, f32[2,33,128]{2,1,0:T(8,128)S(1)}, u32[]{:S(2)}, u32[]{:S(2)}) collective-permute-start(f32[2,33,128]{2,1,0:T(8,128)S(1)} %pad_maximum_fusion.4), channel_id=1, source_target_pairs={{0,64},{64,128},{128,192},{192,256},{256,320},{320,384},{384,448},... | collective-permute-start | bytes 101384 | tf_op jit(solution)/shard_map/ppermute | solution.py:55
  36.0 7.9 %collective-permute-start.5 = (f32[2,33,128]{2,1,0:T(8,128)S(1)}, f32[2,33,128]{2,1,0:T(8,128)S(1)}, u32[]{:S(2)}, u32[]{:S(2)}) collective-permute-start(f32[2,33,128]{2,1,0:T(8,128)S(1)} %pad_maximum_fusion.4), channel_id=1, source_target_pairs={{0,128},{64,192},{128,256},{192,320},{256,384},{320,448},{1,129},{... | collective-permute-start | bytes 101384 | tf_op jit(solution)/shard_map/ppermute | solution.py:55
  37.3 6.6 %collective-permute-start.6 = (f32[2,33,128]{2,1,0:T(8,128)S(1)}, f32[2,33,128]{2,1,0:T(8,128)S(1)}, u32[]{:S(2)}, u32[]{:S(2)}) collective-permute-start(f32[2,33,128]{2,1,0:T(8,128)S(1)} %pad_maximum_fusion.4), channel_id=1, source_target_pairs={{0,192},{64,256},{128,320},{192,384},{256,448},{1,193},{65,257},{1... | collective-permute-start | bytes 101384 | tf_op jit(solution)/shard_map/ppermute | solution.py:55
  41.9 3.1 %collective-permute-start.7 = (f32[2,33,128]{2,1,0:T(8,128)S(1)}, f32[2,33,128]{2,1,0:T(8,128)S(1)}, u32[]{:S(2)}, u32[]{:S(2)}) collective-permute-start(f32[2,33,128]{2,1,0:T(8,128)S(1)} %pad_maximum_fusion.4), channel_id=1, source_target_pairs={{0,256},{64,320},{128,384},{192,448},{1,257},{65,321},{129,385},{1... | collective-permute-start | bytes 101384 | tf_op jit(solution)/shard_map/ppermute | solution.py:55
  45.5 8.8 %collective-permute-start.8 = (f32[2,33,128]{2,1,0:T(8,128)S(1)}, f32[2,33,128]{2,1,0:T(8,128)S(1)}, u32[]{:S(2)}, u32[]{:S(2)}) collective-permute-start(f32[2,33,128]{2,1,0:T(8,128)S(1)} %pad_maximum_fusion.5), channel_id=1, source_target_pairs={{0,256},{64,320},{128,384},{192,448},{1,257},{65,321},{129,385},{1... | collective-permute-start | bytes 101384 | tf_op jit(solution)/shard_map/ppermute | solution.py:55
  54.3 10.7 %collective-permute-start.10 = (f32[2,32,128]{2,1,0:T(8,128)S(1)}, f32[2,32,128]{2,1,0:T(8,128)S(1)}, u32[]{:S(2)}, u32[]{:S(2)}) collective-permute-start(f32[2,32,128]{2,1,0:T(8,128)S(1)} %fusion.105), channel_id=1, source_target_pairs={{0,32},{16,48},{32,0},{48,16},{1,33},{17,49},{33,1},{49,17},{2,34}... | collective-permute-start | bytes 98312 | tf_op jit(solution)/shard_map/ppermute | solution.py:33
  58.6 6.4 %collective-permute-start.11 = (f32[2,32,128]{2,1,0:T(8,128)S(1)}, f32[2,32,128]{2,1,0:T(8,128)S(1)}, u32[]{:S(2)}, u32[]{:S(2)}) collective-permute-start(f32[2,32,128]{2,1,0:T(8,128)S(1)} %fusion.105), channel_id=1, source_target_pairs={{0,48},{16,0},{32,16},{48,32},{1,49},{17,1},{33,17},{49,33},{2,50}... | collective-permute-start | bytes 98312 | tf_op jit(solution)/shard_map/ppermute | solution.py:33
  63.0 5.9 %collective-permute-start.9 = (f32[2,32,128]{2,1,0:T(8,128)S(1)}, f32[2,32,128]{2,1,0:T(8,128)S(1)}, u32[]{:S(2)}, u32[]{:S(2)}) collective-permute-start(f32[2,32,128]{2,1,0:T(8,128)S(1)} %fusion.105), channel_id=1, source_target_pairs={{0,16},{16,32},{32,48},{48,0},{1,17},{17,33},{33,49},{49,1},{2,18}... | collective-permute-start | bytes 98312 | tf_op jit(solution)/shard_map/ppermute | solution.py:33
  69.0 8.1 %collective-permute-start.12 = (f32[2,128,128]{2,1,0:T(8,128)S(1)}, f32[2,128,128]{2,1,0:T(8,128)S(1)}, u32[]{:S(2)}, u32[]{:S(2)}) collective-permute-start(f32[2,128,128]{2,1,0:T(8,128)S(1)} %fusion.76), channel_id=1, source_target_pairs={{0,8},{8,0},{1,9},{9,1},{2,10},{10,2},{3,11},{11,3},{4,12},{12,4},... | collective-permute-start | bytes 393224 | tf_op jit(solution)/shard_map/ppermute | solution.py:107

commit v11 on v8

--- a/solution.py
+++ b/solution.py
@@ -71,6 +71,25 @@
     return cur_log, cur
 
 
+def exclusive_scan_rounds(log, state, axis, n, widths):
+    def shift(packed, d):
+        return lax.ppermute(packed, axis, [(j, j + d) for j in range(n - d)])
+
+    cur_log, cur = jnp.zeros_like(log), jnp.zeros_like(state)
+    sent, window = pack(log, state), 1
+    for count in widths:
+        for j in range(1, count + 1) if window == 1 else range(1, count):
+            d = j * window
+            if d >= n:
+                break
+            got_log, got = unpack(shift(sent, d))
+            cur = cur + jnp.exp(cur_log)[:, None, None] * got
+            cur_log = cur_log + got_log
+        window = window * count
+        sent = pack(cur_log, cur)
+    return cur_log, cur
+
+
 def carried_state(L, S):
     rows, cols, cores = lax.axis_size("cy"), lax.axis_size("cx"), lax.axis_size("cc")
     y, x, c = lax.axis_index("cy"), lax.axis_index("cx"), lax.axis_index("cc")
@@ -87,22 +106,8 @@
     g_log = lax.dynamic_slice_in_dim(chip_log, c * group, group, 0)
     g_state = lax.dynamic_slice_in_dim(chip_state, c * group, group, 0)
 
-    row_pieces = [unpack(p) for p in shifted(pack(g_log, g_state), "cx", cols)]
-    e_log, e_state, f_log, f_state = scan_pieces(
-        [p[0] for p in row_pieces], [p[1] for p in row_pieces], x, cols
-    )
-    row_log = e_log + g_log + f_log
-    row_state = jnp.exp(f_log)[:, None, None] * (jnp.exp(g_log)[:, None, None] * e_state + g_state) + f_state
-
-    part = size // cols
-    q_state = lax.dynamic_slice_in_dim(row_state, x * part, part, 1)
-    y_log, y_state = exclusive_scan(row_log, q_state, "cy", rows)
-
-    parts = shifted(y_state, "cx", cols)
-    ordered = [lax.select_n((x - q) % cols, *parts) for q in range(cols)]
-    y_full = jnp.concatenate(ordered, axis=1)
-
-    chip_before = jnp.exp(e_log)[:, None, None] * y_full + e_state
+    chips = rows * cols
+    e_log, chip_before = exclusive_scan_rounds(g_log, g_state, ("cy", "cx"), chips, (4, 4, 2))
 
     other = lax.ppermute(chip_before, "cc", [(0, 1), (1, 0)])
     full0 = jnp.concatenate([chip_before, other], axis=0)

time: 131 us -> 132 us (level)
  the two profiles are of different devices: /device:TPU:1 before, /device:TPU:43 now
where the time goes in v11:
time: 132 us
  blocking collectives  40.5 us (31%)
  starting transfers between devices  27.3 us (21%)
  waiting for transfers between devices  25.6 us (19%)
  matrix products  22.1 us (17%)
  other arithmetic  9.25 us (7%)
  local copies, waits for them, and re-layouts  6.49 us (5%)
    all_to_all x1, blocking collectives, body(): lax.all_to_all(payload, 'head', split_axis=0, concat_axis=0, tiled=True)  40.5 us
    ppermute x8, waiting for transfers between devices, shift(): return lax.ppermute(packed, axis, [(j, j + d) for j in range(n - d)])  24.4 us
    ppermute x8, starting transfers between devices, shift(): return lax.ppermute(packed, axis, [(j, j + d) for j in range(n - d)])  18.9 us
    dot_general x4, matrix products, inner_head(): return jnp.dot(weights, vh, preferred_element_type=F32)  12.7 us
    dot_general x4, matrix products, body(): jnp.dot((cols(keys, h).astype(F32) * jnp.exp(last[h] - cum[:, h])[:, None...  6.95 us
    ppermute x1, starting transfers between devices, carried_state(): other = lax.ppermute(chip_before, 'cc', [(0, 1), (1, 0)])  5.67 us
    exp x1, other arithmetic, body(): joined.append(inner + jnp.exp(cum[:, h])[:, None] * across)  3.16 us
    ppermute x1, starting transfers between devices, carried_state(): pair = unpack(lax.ppermute(pack(L, S), 'cc', [(0, 1), (1, 0)]))  2.72 us
  transfers between devices with their start and end apart: 10, of which 5 were waited for; matrix products, arithmetic and copies ran while one was open for 11% of the time, Pallas kernels for 0%

profile of v11, /device:TPU:43, one launch (start us, length us, event | category | flops | bytes accessed | tf_op | source)
XLA Modules:
  0.0 131.5 jit_solution(7051029925272700260)
XLA Ops:
  0.0 0.8 copy.47
  0.8 1.1 reduce-window.6
  3.2 3.2 %slice_exponential_fusion.3 = (f32[1024,1]{0,1:T(1,128)S(1)}, f32[1024,1]{0,1:T(1,128)S(1)}, f32[1024,1]{0,1:T(1,128)S(1)}, f32[1024,1]{0,1:T(1,128)S(1)}, f32[1...) fusion(f32[1024,4]{0,1:T(4,128)S(1)} %bitcast.95, ...), kind=kLoop, calls=%fused_computation.150 | loop fusion | flops 4096 | bytes 65552 | tf_op jit(solution)/shard_map/exp | solution.py:157
  6.4 1.8 %convolution_bitcast_fusion.3 = f32[1,128,128]{2,1,0:T(8,128)S(1)} fusion(f32[1024]{0:T(1024)S(1)} %bitcast.111, bf16[1024,512]{1,0:T(8,128)(2,1)} %param.8, bf16[1024,512]{1,0:T(8,128)(2,1)} %param.7), kind=kOutput, calls=%fused_computation.34 | convolution fusion | flops 201588736 | bytes 593920 | tf_op jit(solution)/shard_map/dot_general | solution.py:141
  8.2 1.8 %convolution_bitcast_fusion.2 = f32[1,128,128]{2,1,0:T(8,128)S(1)} fusion(f32[1024]{0:T(1024)S(1)} %bitcast.110, bf16[1024,512]{1,0:T(8,128)(2,1)} %param.8, bf16[1024,512]{1,0:T(8,128)(2,1)} %param.7), kind=kOutput, calls=%fused_computation.33 | convolution fusion | flops 201588736 | bytes 593920 | tf_op jit(solution)/shard_map/dot_general | solution.py:141
  10.0 1.7 %convolution_bitcast_fusion.1 = f32[1,128,128]{2,1,0:T(8,128)S(1)} fusion(f32[1024]{0:T(1024)S(1)} %bitcast.109, bf16[1024,512]{1,0:T(8,128)(2,1)S(1)} %copy-done.7, bf16[1024,512]{1,0:T(8,128)(2,1)} %param.7), kind=kOutput, calls=%fused_computation.32 | convolution fusion | flops 201588736 | bytes 593920 | tf_op jit(solution)/shard_map/dot_general | solution.py:141
  11.7 1.7 %convolution_bitcast_fusion = f32[1,128,128]{2,1,0:T(8,128)S(1)} fusion(f32[1024]{0:T(1024)S(1)} %bitcast.108, bf16[1024,512]{1,0:T(8,128)(2,1)S(1)} %copy-done.7, bf16[1024,512]{1,0:T(8,128)(2,1)} %param.7), kind=kOutput, calls=%fused_computation.31 | convolution fusion | flops 201588736 | bytes 593920 | tf_op jit(solution)/shard_map/dot_general | solution.py:141
  13.5 2.7 %collective-permute-start = (f32[4,129,128]{2,1,0:T(8,128)S(1)}, f32[4,129,128]{2,1,0:T(8,128)S(1)}, u32[]{:S(2)}, u32[]{:S(2)}) collective-permute-start(f32[4,129,128]{2,1,0:T(8,128)S(1)} %pad_maximum_fusion.1), channel_id=1, source_target_pairs={{0,8},{8,0},{1,9},{9,1},{2,10},{10,2},{3,11},{11,3},{4,12},{12,4},... | collective-permute-start | bytes 792584 | tf_op jit(solution)/shard_map/ppermute | solution.py:99
  16.2 1.2 collective-permute-done
  18.5 2.3 %collective-permute-start.3 = (f32[2,129,128]{2,1,0:T(8,128)S(1)}, f32[2,129,128]{2,1,0:T(8,128)S(1)}, u32[]{:S(2)}, u32[]{:S(2)}) collective-permute-start(f32[2,129,128]{2,1,0:T(8,128)S(1)} %pad_maximum_fusion.3), channel_id=1, source_target_pairs={{0,48},{16,64},{32,80},{48,96},{64,112},{80,128},{96,144},{112,160... | collective-permute-start | bytes 396296 | tf_op jit(solution)/shard_map/ppermute | solution.py:76
  20.7 4.0 %collective-permute-start.2 = (f32[2,129,128]{2,1,0:T(8,128)S(1)}, f32[2,129,128]{2,1,0:T(8,128)S(1)}, u32[]{:S(2)}, u32[]{:S(2)}) collective-permute-start(f32[2,129,128]{2,1,0:T(8,128)S(1)} %pad_maximum_fusion.3), channel_id=1, source_target_pairs={{0,32},{16,48},{32,64},{48,80},{64,96},{80,112},{96,128},{112,144}... | collective-permute-start | bytes 396296 | tf_op jit(solution)/shard_map/ppermute | solution.py:76
  24.8 3.4 %collective-permute-start.1 = (f32[2,129,128]{2,1,0:T(8,128)S(1)}, f32[2,129,128]{2,1,0:T(8,128)S(1)}, u32[]{:S(2)}, u32[]{:S(2)}) collective-permute-start(f32[2,129,128]{2,1,0:T(8,128)S(1)} %pad_maximum_fusion.3), channel_id=1, source_target_pairs={{0,16},{16,32},{32,48},{48,64},{64,80},{80,96},{96,112},{112,128},... | collective-permute-start | bytes 396296 | tf_op jit(solution)/shard_map/ppermute | solution.py:76
  28.2 3.1 %fusion.6 = f32[1024,128]{0,1:T(8,128)} fusion(f32[1024]{0:T(1024)S(1)} %bitcast.107, bf16[1024,512]{1,0:T(8,128)(2,1)S(1)} %copy-done, bf16[1024,512]{1,0:T(8,128)(2,1)S(1)} %copy-done.7, bf16[1024,512]{1,0:T(8,128)(2,1)} %param.7), kind=kOutput, calls=%fused_computation.14 | convolution fusion | flops 543162368 | bytes 1318912 | tf_op jit(solution)/shard_map/dot_general | solution.py:126
  31.4 2.3 %collective-permute-start.4 = (f32[2,129,128]{2,1,0:T(8,128)S(1)}, f32[2,129,128]{2,1,0:T(8,128)S(1)}, u32[]{:S(2)}, u32[]{:S(2)}) collective-permute-start(f32[2,129,128]{2,1,0:T(8,128)S(1)} %pad_maximum_fusion.3), channel_id=1, source_target_pairs={{0,64},{16,80},{32,96},{48,112},{64,128},{80,144},{96,160},{112,17... | collective-permute-start | bytes 396296 | tf_op jit(solution)/shard_map/ppermute | solution.py:76
  33.8 3.4 %collective-permute-done.4 = f32[2,129,128]{2,1,0:T(8,128)S(1)} collective-permute-done((f32[2,129,128]{2,1,0:T(8,128)S(1)}, f32[2,129,128]{2,1,0:T(8,128)S(1)}, u32[]{:S(2)}, u32[]{:S(2)}) %collective-permute-start.4) | collective-permute-done | bytes 132128 | tf_op jit(solution)/shard_map/ppermute | solution.py:76
  37.5 2.4 %collective-permute-start.6 = (f32[2,129,128]{2,1,0:T(8,128)S(1)}, f32[2,129,128]{2,1,0:T(8,128)S(1)}, u32[]{:S(2)}, u32[]{:S(2)}) collective-permute-start(f32[2,129,128]{2,1,0:T(8,128)S(1)} %pad_maximum_fusion.4), channel_id=1, source_target_pairs={{0,128},{16,144},{32,160},{48,176},{64,192},{80,208},{96,224},{112... | collective-permute-start | bytes 396296 | tf_op jit(solution)/shard_map/ppermute | solution.py:76
  39.8 1.9 %collective-permute-start.5 = (f32[2,129,128]{2,1,0:T(8,128)S(1)}, f32[2,129,128]{2,1,0:T(8,128)S(1)}, u32[]{:S(2)}, u32[]{:S(2)}) collective-permute-start(f32[2,129,128]{2,1,0:T(8,128)S(1)} %pad_maximum_fusion.4), channel_id=1, source_target_pairs={{0,64},{16,80},{32,96},{48,112},{64,128},{80,144},{96,160},{112,17... | collective-permute-start | bytes 396296 | tf_op jit(solution)/shard_map/ppermute | solution.py:76
  41.8 3.1 %fusion.5 = f32[1024,128]{0,1:T(8,128)} fusion(f32[1024]{0:T(1024)S(1)} %bitcast.106, bf16[1024,512]{1,0:T(8,128)(2,1)S(1)} %copy-done, bf16[1024,512]{1,0:T(8,128)(2,1)S(1)} %copy-done.7, bf16[1024,512]{1,0:T(8,128)(2,1)} %param.7), kind=kOutput, calls=%fused_computation.13 | convolution fusion | flops 543162368 | bytes 1318912 | tf_op jit(solution)/shard_map/dot_general | solution.py:126
  44.9 1.3 collective-permute-start.7
  46.2 3.7 %collective-permute-done.5 = f32[2,129,128]{2,1,0:T(8,128)S(1)} collective-permute-done((f32[2,129,128]{2,1,0:T(8,128)S(1)}, f32[2,129,128]{2,1,0:T(8,128)S(1)}, u32[]{:S(2)}, u32[]{:S(2)}) %collective-permute-start.5) | collective-permute-done | bytes 132128 | tf_op jit(solution)/shard_map/ppermute | solution.py:76
  50.0 12.1 %collective-permute-done.7 = f32[2,129,128]{2,1,0:T(8,128)S(1)} collective-permute-done((f32[2,129,128]{2,1,0:T(8,128)S(1)}, f32[2,129,128]{2,1,0:T(8,128)S(1)}, u32[]{:S(2)}, u32[]{:S(2)}) %collective-permute-start.7) | collective-permute-done | bytes 132128 | tf_op jit(solution)/shard_map/ppermute | solution.py:76
  62.4 1.3 collective-permute-start.8
  63.7 3.1 %fusion.4 = f32[1024,128]{0,1:T(8,128)} fusion(f32[1024]{0:T(1024)S(1)} %bitcast.105, bf16[1024,512]{1,0:T(8,128)(2,1)S(1)} %copy-done, bf16[1024,512]{1,0:T(8,128)(2,1)S(1)} %copy-done.7, bf16[1024,512]{1,0:T(8,128)(2,1)} %param.7), kind=kOutput, calls=%fused_computation.12 | convolution fusion | flops 543162368 | bytes 1318912 | tf_op jit(solution)/shard_map/dot_general | solution.py:126
  66.8 5.3 %collective-permute-done.8 = f32[2,129,128]{2,1,0:T(8,128)S(1)} collective-permute-done((f32[2,129,128]{2,1,0:T(8,128)S(1)}, f32[2,129,128]{2,1,0:T(8,128)S(1)}, u32[]{:S(2)}, u32[]{:S(2)}) %collective-permute-start.8) | collective-permute-done | bytes 132128 | tf_op jit(solution)/shard_map/ppermute | solution.py:76
  72.8 5.7 %collective-permute-start.9 = (f32[2,128,128]{2,1,0:T(8,128)}, f32[2,128,128]{2,1,0:T(8,128)}, u32[]{:S(2)}, u32[]{:S(2)}) collective-permute-start(f32[2,128,128]{2,1,0:T(8,128)} %fusion.63), channel_id=1, source_target_pairs={{0,8},{8,0},{1,9},{9,1},{2,10},{10,2},{3,11},{11,3},{4,12},{12,4},... | collective-permute-start | bytes 393224 | tf_op jit(solution)/shard_map/ppermute | solution.py:112
  78.5 3.3 %fusion.3 = f32[1024,128]{0,1:T(8,128)} fusion(f32[1024]{0:T(1024)S(1)} %bitcast.104, bf16[1024,512]{1,0:T(8,128)(2,1)} %param.8, bf16[1024,512]{1,0:T(8,128)(2,1)} %param.7, bf16[1024,512]{1,0:T(8,128)(2,1)S(1)} %copy-done), kind=kOutput, calls=%fused_computation.11 | convolution fusion | flops 543162368 | bytes 1318912 | tf_op jit(solution)/shard_map/dot_general | solution.py:126
  82.4 0.8 dynamic_slice.11
  83.3 1.2 add_select_fusion
  84.5 1.2 fusion.18
  87.2 0.7 fusion.1
  88.7 40.5 %all_to_all.5 = bf16[8,129,512]{2,1,0:T(8,128)(2,1)S(1)} all-to-all(bf16[8,129,512]{2,1,0:T(8,128)(2,1)S(1)} %maximum_maximum_fusion), channel_id=1, replica_groups=mesh['cy'=8,'cx'=4,'cc'=2,'head'=8] {'head'}, dimensions={0} | all-to-all | bytes 2113536 | tf_op jit(solution)/shard_map/all_to_all | solution.py:177
  130.2 1.3 copy.35
  (66 shorter events, 7.8 us)
Async XLA Ops:
  0.0 10.0 %copy-start.7 = (bf16[1024,512]{1,0:T(8,128)(2,1)S(1)}, bf16[1024,512]{1,0:T(8,128)(2,1)}, u32[]{:S(2)}) copy-start(bf16[1024,512]{1,0:T(8,128)(2,1)} %param.8) | copy-start | bytes 3145732
  13.5 14.8 %copy-start = (bf16[1024,512]{1,0:T(8,128)(2,1)S(1)}, bf16[1024,512]{1,0:T(8,128)(2,1)}, u32[]{:S(2)}) copy-start(bf16[1024,512]{1,0:T(8,128)(2,1)} %param.6) | copy-start | bytes 3145732
  13.5 3.9 %collective-permute-start = (f32[4,129,128]{2,1,0:T(8,128)S(1)}, f32[4,129,128]{2,1,0:T(8,128)S(1)}, u32[]{:S(2)}, u32[]{:S(2)}) collective-permute-start(f32[4,129,128]{2,1,0:T(8,128)S(1)} %pad_maximum_fusion.1), channel_id=1, source_target_pairs={{0,8},{8,0},{1,9},{9,1},{2,10},{10,2},{3,11},{11,3},{4,12},{12,4},... | collective-permute-start | bytes 792584 | tf_op jit(solution)/shard_map/ppermute | solution.py:99
  18.5 15.2 %collective-permute-start.3 = (f32[2,129,128]{2,1,0:T(8,128)S(1)}, f32[2,129,128]{2,1,0:T(8,128)S(1)}, u32[]{:S(2)}, u32[]{:S(2)}) collective-permute-start(f32[2,129,128]{2,1,0:T(8,128)S(1)} %pad_maximum_fusion.3), channel_id=1, source_target_pairs={{0,48},{16,64},{32,80},{48,96},{64,112},{80,128},{96,144},{112,160... | collective-permute-start | bytes 396296 | tf_op jit(solution)/shard_map/ppermute | solution.py:76
  20.7 12.9 %collective-permute-start.2 = (f32[2,129,128]{2,1,0:T(8,128)S(1)}, f32[2,129,128]{2,1,0:T(8,128)S(1)}, u32[]{:S(2)}, u32[]{:S(2)}) collective-permute-start(f32[2,129,128]{2,1,0:T(8,128)S(1)} %pad_maximum_fusion.3), channel_id=1, source_target_pairs={{0,32},{16,48},{32,64},{48,80},{64,96},{80,112},{96,128},{112,144}... | collective-permute-start | bytes 396296 | tf_op jit(solution)/shard_map/ppermute | solution.py:76
  24.8 8.9 %collective-permute-start.1 = (f32[2,129,128]{2,1,0:T(8,128)S(1)}, f32[2,129,128]{2,1,0:T(8,128)S(1)}, u32[]{:S(2)}, u32[]{:S(2)}) collective-permute-start(f32[2,129,128]{2,1,0:T(8,128)S(1)} %pad_maximum_fusion.3), channel_id=1, source_target_pairs={{0,16},{16,32},{32,48},{48,64},{64,80},{80,96},{96,112},{112,128},... | collective-permute-start | bytes 396296 | tf_op jit(solution)/shard_map/ppermute | solution.py:76
  31.4 5.8 %collective-permute-start.4 = (f32[2,129,128]{2,1,0:T(8,128)S(1)}, f32[2,129,128]{2,1,0:T(8,128)S(1)}, u32[]{:S(2)}, u32[]{:S(2)}) collective-permute-start(f32[2,129,128]{2,1,0:T(8,128)S(1)} %pad_maximum_fusion.3), channel_id=1, source_target_pairs={{0,64},{16,80},{32,96},{48,112},{64,128},{80,144},{96,160},{112,17... | collective-permute-start | bytes 396296 | tf_op jit(solution)/shard_map/ppermute | solution.py:76
  37.5 8.7 %collective-permute-start.6 = (f32[2,129,128]{2,1,0:T(8,128)S(1)}, f32[2,129,128]{2,1,0:T(8,128)S(1)}, u32[]{:S(2)}, u32[]{:S(2)}) collective-permute-start(f32[2,129,128]{2,1,0:T(8,128)S(1)} %pad_maximum_fusion.4), channel_id=1, source_target_pairs={{0,128},{16,144},{32,160},{48,176},{64,192},{80,208},{96,224},{112... | collective-permute-start | bytes 396296 | tf_op jit(solution)/shard_map/ppermute | solution.py:76
  39.8 10.1 %collective-permute-start.5 = (f32[2,129,128]{2,1,0:T(8,128)S(1)}, f32[2,129,128]{2,1,0:T(8,128)S(1)}, u32[]{:S(2)}, u32[]{:S(2)}) collective-permute-start(f32[2,129,128]{2,1,0:T(8,128)S(1)} %pad_maximum_fusion.4), channel_id=1, source_target_pairs={{0,64},{16,80},{32,96},{48,112},{64,128},{80,144},{96,160},{112,17... | collective-permute-start | bytes 396296 | tf_op jit(solution)/shard_map/ppermute | solution.py:76
  44.9 17.2 %collective-permute-start.7 = (f32[2,129,128]{2,1,0:T(8,128)S(1)}, f32[2,129,128]{2,1,0:T(8,128)S(1)}, u32[]{:S(2)}, u32[]{:S(2)}) collective-permute-start(f32[2,129,128]{2,1,0:T(8,128)S(1)} %pad_maximum_fusion.4), channel_id=1, source_target_pairs={{0,192},{16,208},{32,224},{48,240},{64,256},{80,272},{96,288},{112... | collective-permute-start | bytes 396296 | tf_op jit(solution)/shard_map/ppermute | solution.py:76
  62.4 9.7 %collective-permute-start.8 = (f32[2,129,128]{2,1,0:T(8,128)S(1)}, f32[2,129,128]{2,1,0:T(8,128)S(1)}, u32[]{:S(2)}, u32[]{:S(2)}) collective-permute-start(f32[2,129,128]{2,1,0:T(8,128)S(1)} %pad_maximum_fusion.5), channel_id=1, source_target_pairs={{0,256},{16,272},{32,288},{48,304},{64,320},{80,336},{96,352},{112... | collective-permute-start | bytes 396296 | tf_op jit(solution)/shard_map/ppermute | solution.py:76
  72.8 10.5 %collective-permute-start.9 = (f32[2,128,128]{2,1,0:T(8,128)}, f32[2,128,128]{2,1,0:T(8,128)}, u32[]{:S(2)}, u32[]{:S(2)}) collective-permute-start(f32[2,128,128]{2,1,0:T(8,128)} %fusion.63), channel_id=1, source_target_pairs={{0,8},{8,0},{1,9},{9,1},{2,10},{10,2},{3,11},{11,3},{4,12},{12,4},... | collective-permute-start | bytes 393224 | tf_op jit(solution)/shard_map/ppermute | solution.py:112
  78.5 3.3 %copy-start.1 = (bf16[1024,512]{1,0:T(8,128)(2,1)S(1)}, bf16[1024,512]{1,0:T(8,128)(2,1)}, u32[]{:S(2)}) copy-start(bf16[1024,512]{1,0:T(8,128)(2,1)} %param.10) | copy-start | bytes 3145732
  82.4 2.1 %copy-start.2 = (f32[1024,128]{0,1:T(8,128)S(1)}, f32[1024,128]{0,1:T(8,128)}, u32[]{:S(2)}) copy-start(f32[1024,128]{0,1:T(8,128)} %fusion.6) | copy-start | bytes 1572868
  82.4 3.3 %copy-start.3 = (f32[1024,128]{0,1:T(8,128)S(1)}, f32[1024,128]{0,1:T(8,128)}, u32[]{:S(2)}) copy-start(f32[1024,128]{0,1:T(8,128)} %fusion.5) | copy-start | bytes 1572868
  82.4 3.3 %copy-start.6 = (f32[1024,1]{0,1:T(1,128)S(1)}, f32[1024,1]{0,1:T(1,128)}, u32[]{:S(2)}) copy-start(f32[1024,1]{0,1:T(1,128)} %get-tuple-element.32) | copy-start | bytes 12292
  84.5 1.6 %copy-start.4 = (f32[1024,128]{0,1:T(8,128)S(1)}, f32[1024,128]{0,1:T(8,128)}, u32[]{:S(2)}) copy-start(f32[1024,128]{0,1:T(8,128)} %fusion.4) | copy-start | bytes 1572868
  85.7 1.0 copy-start.5

commit v12 on v10

--- a/solution.py
+++ b/solution.py
@@ -158,7 +158,7 @@
     for h in range(heads):
         qh = cols(queries, h)
         inner = inner_head(qh, cols(keys, h), cols(values, h), cum[:, h])
-        across = sum3(jnp.dot(qh, jnp.concatenate(split3(carried[h]), axis=1), preferred_element_type=F32), 1)
+        across = jnp.dot(qh.astype(F32), carried[h], precision=HI)
         joined.append(inner + jnp.exp(cum[:, h])[:, None] * across)
     attended = jnp.concatenate(joined, axis=1).astype(jnp.bfloat16)
 

time: 140 us -> 132 us (0.943)
  waiting for transfers between devices: 11.9 us -> 6.72 us
  starting transfers between devices: 51.5 us -> 48.8 us
    ppermute x6, waiting for transfers between devices: 8.58 us -> 5.55 us  [shifted(): out.append(lax.ppermute(x, axis, [(j, (j + s) % n) for j in range(n)]))]
    dot_general x4, matrix products: 5.43 us -> 2.41 us  [body(): across = jnp.dot(qh.astype(F32), carried[h], precision=HI)]
    ppermute x5, waiting for transfers between devices: 2.14 us -> 0.01 us  [shift(): return lax.ppermute(packed, axis, [(j, j + d) for j in range(n - d)])]
    ppermute x5, starting transfers between devices: 16.9 us -> 14.7 us  [shift(): return lax.ppermute(packed, axis, [(j, j + d) for j in range(n - d)])]
    dot_general x4, matrix products: 10.7 us -> 12.6 us  [inner_head(): return jnp.dot(weights, vh, preferred_element_type=F32)]
    convert_element_type x2 -> x1, other arithmetic: 2.81 us -> 2.13 us  [split3(): hi.astype(jnp.bfloat16)]
  transfers between devices with their start and end apart: 13 -> 13, of which waited for: 6 -> 4; matrix products, arithmetic and copies ran while one was open for 1% -> 11% of each run, Pallas kernels for 0% -> 0%
where the time goes in v12:
time: 132 us; the launch traced here: 131 us
  starting transfers between devices  48.8 us (37%)
  blocking collectives  40.5 us (31%)
  matrix products  16.7 us (13%)
  other arithmetic  11.6 us (9%)
  waiting for transfers between devices  6.72 us (5%)
  local copies, waits for them, and re-layouts  6.51 us (5%)
    all_to_all x1, blocking collectives, body(): lax.all_to_all(payload, 'head', split_axis=0, concat_axis=0, tiled=True)  40.5 us
    ppermute x6, starting transfers between devices, shifted(): out.append(lax.ppermute(x, axis, [(j, (j + s) % n) for j in range(n)]))  19.1 us
    ppermute x5, starting transfers between devices, shift(): return lax.ppermute(packed, axis, [(j, j + d) for j in range(n - d)])  14.7 us
    dot_general x4, matrix products, inner_head(): return jnp.dot(weights, vh, preferred_element_type=F32)  12.6 us
    ppermute x1, starting transfers between devices, carried_state(): pair = unpack(lax.ppermute(pack(L, S), 'cc', [(0, 1), (1, 0)]))  8.78 us
    ppermute x1, starting transfers between devices, carried_state(): other = lax.ppermute(chip_before, 'cc', [(0, 1), (1, 0)])  6.18 us
    ppermute x6, waiting for transfers between devices, shifted(): out.append(lax.ppermute(x, axis, [(j, (j + s) % n) for j in range(n)]))  5.55 us
    exp x1, other arithmetic, body(): joined.append(inner + jnp.exp(cum[:, h])[:, None] * across)  3.16 us
  transfers between devices with their start and end apart: 13, of which 4 were waited for; matrix products, arithmetic and copies ran while one was open for 11% of the time, Pallas kernels for 0%

profile of v12, /device:TPU:1, one launch (start us, length us, event | category | flops | bytes accessed | tf_op | source)
XLA Modules:
  0.0 131.3 jit_solution(7972701664373152315)
XLA Ops:
  0.0 0.7 copy.47
  0.7 1.1 reduce-window.6
  3.1 3.2 %slice_exponential_fusion.3 = (f32[1024,1]{0,1:T(1,128)}, f32[1024,1]{0,1:T(1,128)S(1)}, f32[1024,1]{0,1:T(1,128)S(1)}, f32[1024,1]{0,1:T(1,128)}, f32[1024,1]{0...) fusion(f32[1024,4]{0,1:T(4,128)S(1)} %bitcast.95, ...), kind=kLoop, calls=%fused_computation.218 | loop fusion | flops 4096 | bytes 65552 | tf_op jit(solution)/shard_map/exp | solution.py:162
  6.3 2.1 %reduce-precision_convert_fusion.7 = (bf16[1024,128]{1,0:T(8,128)(2,1)S(1)}, bf16[1024,128]{1,0:T(8,128)(2,1)S(1)}, bf16[1024,128]{1,0:T(8,128)(2,1)S(1)}, bf16[...) fusion(f32[1024]{0:T(1024)S(1)} %bitcast.102, ...), kind=kLoop, calls=%fused_computation.72 | loop fusion | flops 4718592 | bytes 4210688 | tf_op jit(solution)/shard_map/convert_element_type | solution.py:119
  10.3 8.8 %collective-permute-start = (f32[4,129,128]{2,1,0:T(8,128)S(1)}, f32[4,129,128]{2,1,0:T(8,128)S(1)}, u32[]{:S(2)}, u32[]{:S(2)}) collective-permute-start(f32[4,129,128]{2,1,0:T(8,128)S(1)} %pad_maximum_fusion.1), channel_id=1, source_target_pairs={{0,8},{8,0},{1,9},{9,1},{2,10},{10,2},{3,11},{11,3},{4,12},{12,4},... | collective-permute-start | bytes 792584 | tf_op jit(solution)/shard_map/ppermute | solution.py:80
  19.1 1.2 collective-permute-done
  21.3 2.1 %collective-permute-start.1 = (f32[2,129,128]{2,1,0:T(8,128)S(1)}, f32[2,129,128]{2,1,0:T(8,128)S(1)}, u32[]{:S(2)}, u32[]{:S(2)}) collective-permute-start(f32[2,129,128]{2,1,0:T(8,128)S(1)} %pad_maximum_fusion.3), channel_id=1, source_target_pairs={{0,16},{16,32},{32,48},{48,0},{1,17},{17,33},{33,49},{49,1},{2,18}... | collective-permute-start | bytes 396296 | tf_op jit(solution)/shard_map/ppermute | solution.py:33
  23.4 1.9 %collective-permute-start.2 = (f32[2,129,128]{2,1,0:T(8,128)S(1)}, f32[2,129,128]{2,1,0:T(8,128)S(1)}, u32[]{:S(2)}, u32[]{:S(2)}) collective-permute-start(f32[2,129,128]{2,1,0:T(8,128)S(1)} %pad_maximum_fusion.3), channel_id=1, source_target_pairs={{0,32},{16,48},{32,0},{48,16},{1,33},{17,49},{33,1},{49,17},{2,34}... | collective-permute-start | bytes 396296 | tf_op jit(solution)/shard_map/ppermute | solution.py:33
  25.3 4.6 %collective-permute-start.3 = (f32[2,129,128]{2,1,0:T(8,128)S(1)}, f32[2,129,128]{2,1,0:T(8,128)S(1)}, u32[]{:S(2)}, u32[]{:S(2)}) collective-permute-start(f32[2,129,128]{2,1,0:T(8,128)S(1)} %pad_maximum_fusion.3), channel_id=1, source_target_pairs={{0,48},{16,0},{32,16},{48,32},{1,49},{17,1},{33,17},{49,33},{2,50}... | collective-permute-start | bytes 396296 | tf_op jit(solution)/shard_map/ppermute | solution.py:33
  29.9 1.8 %collective-permute-done.2 = f32[2,129,128]{2,1,0:T(8,128)S(1)} collective-permute-done((f32[2,129,128]{2,1,0:T(8,128)S(1)}, f32[2,129,128]{2,1,0:T(8,128)S(1)}, u32[]{:S(2)}, u32[]{:S(2)}) %collective-permute-start.2) | collective-permute-done | bytes 132128 | tf_op jit(solution)/shard_map/ppermute | solution.py:33
  31.7 2.9 %collective-permute-done.3 = f32[2,129,128]{2,1,0:T(8,128)S(1)} collective-permute-done((f32[2,129,128]{2,1,0:T(8,128)S(1)}, f32[2,129,128]{2,1,0:T(8,128)S(1)}, u32[]{:S(2)}, u32[]{:S(2)}) %collective-permute-start.3) | collective-permute-done | bytes 132128 | tf_op jit(solution)/shard_map/ppermute | solution.py:33
  35.3 1.3 collective-permute-start.4
  36.6 1.3 collective-permute-start.5
  37.9 4.5 %collective-permute-start.6 = (f32[2,33,128]{2,1,0:T(8,128)S(1)}, f32[2,33,128]{2,1,0:T(8,128)S(1)}, u32[]{:S(2)}, u32[]{:S(2)}) collective-permute-start(f32[2,33,128]{2,1,0:T(8,128)S(1)} %pad_maximum_fusion.4), channel_id=1, source_target_pairs={{0,192},{64,256},{128,320},{192,384},{256,448},{1,193},{65,257},{1... | collective-permute-start | bytes 101384 | tf_op jit(solution)/shard_map/ppermute | solution.py:55
  42.4 2.0 %collective-permute-start.7 = (f32[2,33,128]{2,1,0:T(8,128)S(1)}, f32[2,33,128]{2,1,0:T(8,128)S(1)}, u32[]{:S(2)}, u32[]{:S(2)}) collective-permute-start(f32[2,33,128]{2,1,0:T(8,128)S(1)} %pad_maximum_fusion.4), channel_id=1, source_target_pairs={{0,256},{64,320},{128,384},{192,448},{1,257},{65,321},{129,385},{1... | collective-permute-start | bytes 101384 | tf_op jit(solution)/shard_map/ppermute | solution.py:55
  44.5 3.1 %fusion.3 = f32[1024,128]{0,1:T(8,128)} fusion(f32[1024]{0:T(1024)S(1)} %bitcast.111, bf16[1024,512]{1,0:T(8,128)(2,1)} %param.8, bf16[1024,512]{1,0:T(8,128)(2,1)S(1)} %copy-done, bf16[1024,512]{1,0:T(8,128)(2,1)S(1)} %copy-done.2), kind=kOutput, calls=%fused_computation.11 | convolution fusion | flops 543162368 | bytes 1318912 | tf_op jit(solution)/shard_map/dot_general | solution.py:134
  48.1 5.6 %collective-permute-start.8 = (f32[2,33,128]{2,1,0:T(8,128)S(1)}, f32[2,33,128]{2,1,0:T(8,128)S(1)}, u32[]{:S(2)}, u32[]{:S(2)}) collective-permute-start(f32[2,33,128]{2,1,0:T(8,128)S(1)} %pad_maximum_fusion.5), channel_id=1, source_target_pairs={{0,256},{64,320},{128,384},{192,448},{1,257},{65,321},{129,385},{1... | collective-permute-start | bytes 101384 | tf_op jit(solution)/shard_map/ppermute | solution.py:55
  53.7 3.1 %fusion.4 = f32[1024,128]{0,1:T(8,128)} fusion(f32[1024]{0:T(1024)S(1)} %bitcast.110, bf16[1024,512]{1,0:T(8,128)(2,1)S(1)} %copy-done, bf16[1024,512]{1,0:T(8,128)(2,1)} %param.8, bf16[1024,512]{1,0:T(8,128)(2,1)S(1)} %copy-done.2), kind=kOutput, calls=%fused_computation.12 | convolution fusion | flops 543162368 | bytes 1318912 | tf_op jit(solution)/shard_map/dot_general | solution.py:134
  56.9 4.3 %collective-permute-start.10 = (f32[2,32,128]{2,1,0:T(8,128)S(1)}, f32[2,32,128]{2,1,0:T(8,128)S(1)}, u32[]{:S(2)}, u32[]{:S(2)}) collective-permute-start(f32[2,32,128]{2,1,0:T(8,128)S(1)} %fusion.81), channel_id=1, source_target_pairs={{0,32},{16,48},{32,0},{48,16},{1,33},{17,49},{33,1},{49,17},{2,34}... | collective-permute-start | bytes 98312 | tf_op jit(solution)/shard_map/ppermute | solution.py:33
  61.2 4.4 %collective-permute-start.11 = (f32[2,32,128]{2,1,0:T(8,128)S(1)}, f32[2,32,128]{2,1,0:T(8,128)S(1)}, u32[]{:S(2)}, u32[]{:S(2)}) collective-permute-start(f32[2,32,128]{2,1,0:T(8,128)S(1)} %fusion.81), channel_id=1, source_target_pairs={{0,48},{16,0},{32,16},{48,32},{1,49},{17,1},{33,17},{49,33},{2,50}... | collective-permute-start | bytes 98312 | tf_op jit(solution)/shard_map/ppermute | solution.py:33
  65.6 1.9 %collective-permute-start.9 = (f32[2,32,128]{2,1,0:T(8,128)S(1)}, f32[2,32,128]{2,1,0:T(8,128)S(1)}, u32[]{:S(2)}, u32[]{:S(2)}) collective-permute-start(f32[2,32,128]{2,1,0:T(8,128)S(1)} %fusion.81), channel_id=1, source_target_pairs={{0,16},{16,32},{32,48},{48,0},{1,17},{17,33},{33,49},{49,1},{2,18}... | collective-permute-start | bytes 98312 | tf_op jit(solution)/shard_map/ppermute | solution.py:33
  67.5 3.1 %fusion.5 = f32[1024,128]{0,1:T(8,128)} fusion(f32[1024]{0:T(1024)S(1)} %bitcast.109, bf16[1024,512]{1,0:T(8,128)(2,1)S(1)} %copy-done, bf16[1024,512]{1,0:T(8,128)(2,1)} %param.8, bf16[1024,512]{1,0:T(8,128)(2,1)S(1)} %copy-done.2), kind=kOutput, calls=%fused_computation.13 | convolution fusion | flops 543162368 | bytes 1318912 | tf_op jit(solution)/shard_map/dot_general | solution.py:134
  70.7 0.8 collective-permute-done.9
  71.5 0.7 fusion.76
  72.2 6.2 %collective-permute-start.12 = (f32[2,128,128]{2,1,0:T(8,128)}, f32[2,128,128]{2,1,0:T(8,128)}, u32[]{:S(2)}, u32[]{:S(2)}) collective-permute-start(f32[2,128,128]{2,1,0:T(8,128)} %fusion.76), channel_id=1, source_target_pairs={{0,8},{8,0},{1,9},{9,1},{2,10},{10,2},{3,11},{11,3},{4,12},{12,4},... | collective-permute-start | bytes 393224 | tf_op jit(solution)/shard_map/ppermute | solution.py:107
  78.4 3.2 %fusion.6 = f32[1024,128]{0,1:T(8,128)} fusion(f32[1024]{0:T(1024)} %bitcast.108, bf16[1024,512]{1,0:T(8,128)(2,1)S(1)} %copy-done, bf16[1024,512]{1,0:T(8,128)(2,1)} %param.8, bf16[1024,512]{1,0:T(8,128)(2,1)S(1)} %copy-done.2), kind=kOutput, calls=%fused_computation.14 | convolution fusion | flops 543162368 | bytes 1318912 | tf_op jit(solution)/shard_map/dot_general | solution.py:134
  82.2 0.8 dynamic_slice.15
  83.1 1.2 add_select_fusion
  84.3 1.1 fusion.15
  87.0 0.7 fusion.1
  88.5 40.5 %all_to_all.5 = bf16[8,129,512]{2,1,0:T(8,128)(2,1)S(1)} all-to-all(bf16[8,129,512]{2,1,0:T(8,128)(2,1)S(1)} %maximum_maximum_fusion), channel_id=1, replica_groups=mesh['cy'=8,'cx'=4,'cc'=2,'head'=8] {'head'}, dimensions={0} | all-to-all | bytes 2113536 | tf_op jit(solution)/shard_map/all_to_all | solution.py:182
  130.0 1.3 copy.35
  (85 shorter events, 9.1 us)
Async XLA Ops:
  6.3 2.1 %copy-start.8 = (bf16[1024,512]{1,0:T(8,128)(2,1)S(1)}, bf16[1024,512]{1,0:T(8,128)(2,1)}, u32[]{:S(2)}) copy-start(bf16[1024,512]{1,0:T(8,128)(2,1)} %param.8) | copy-start | bytes 3145732
  10.3 9.9 %collective-permute-start = (f32[4,129,128]{2,1,0:T(8,128)S(1)}, f32[4,129,128]{2,1,0:T(8,128)S(1)}, u32[]{:S(2)}, u32[]{:S(2)}) collective-permute-start(f32[4,129,128]{2,1,0:T(8,128)S(1)} %pad_maximum_fusion.1), channel_id=1, source_target_pairs={{0,8},{8,0},{1,9},{9,1},{2,10},{10,2},{3,11},{11,3},{4,12},{12,4},... | collective-permute-start | bytes 792584 | tf_op jit(solution)/shard_map/ppermute | solution.py:80
  21.1 23.4 %copy-start.2 = (bf16[1024,512]{1,0:T(8,128)(2,1)S(1)}, bf16[1024,512]{1,0:T(8,128)(2,1)}, u32[]{:S(2)}) copy-start(bf16[1024,512]{1,0:T(8,128)(2,1)} %param.7) | copy-start | bytes 3145732
  21.1 23.3 %copy-start = (bf16[1024,512]{1,0:T(8,128)(2,1)S(1)}, bf16[1024,512]{1,0:T(8,128)(2,1)}, u32[]{:S(2)}) copy-start(bf16[1024,512]{1,0:T(8,128)(2,1)} %param.6) | copy-start | bytes 3145732
  21.3 8.6 %collective-permute-start.1 = (f32[2,129,128]{2,1,0:T(8,128)S(1)}, f32[2,129,128]{2,1,0:T(8,128)S(1)}, u32[]{:S(2)}, u32[]{:S(2)}) collective-permute-start(f32[2,129,128]{2,1,0:T(8,128)S(1)} %pad_maximum_fusion.3), channel_id=1, source_target_pairs={{0,16},{16,32},{32,48},{48,0},{1,17},{17,33},{33,49},{49,1},{2,18}... | collective-permute-start | bytes 396296 | tf_op jit(solution)/shard_map/ppermute | solution.py:33
  23.4 8.3 %collective-permute-start.2 = (f32[2,129,128]{2,1,0:T(8,128)S(1)}, f32[2,129,128]{2,1,0:T(8,128)S(1)}, u32[]{:S(2)}, u32[]{:S(2)}) collective-permute-start(f32[2,129,128]{2,1,0:T(8,128)S(1)} %pad_maximum_fusion.3), channel_id=1, source_target_pairs={{0,32},{16,48},{32,0},{48,16},{1,33},{17,49},{33,1},{49,17},{2,34}... | collective-permute-start | bytes 396296 | tf_op jit(solution)/shard_map/ppermute | solution.py:33
  25.3 9.3 %collective-permute-start.3 = (f32[2,129,128]{2,1,0:T(8,128)S(1)}, f32[2,129,128]{2,1,0:T(8,128)S(1)}, u32[]{:S(2)}, u32[]{:S(2)}) collective-permute-start(f32[2,129,128]{2,1,0:T(8,128)S(1)} %pad_maximum_fusion.3), channel_id=1, source_target_pairs={{0,48},{16,0},{32,16},{48,32},{1,49},{17,1},{33,17},{49,33},{2,50}... | collective-permute-start | bytes 396296 | tf_op jit(solution)/shard_map/ppermute | solution.py:33
  35.3 12.4 %collective-permute-start.4 = (f32[2,33,128]{2,1,0:T(8,128)S(1)}, f32[2,33,128]{2,1,0:T(8,128)S(1)}, u32[]{:S(2)}, u32[]{:S(2)}) collective-permute-start(f32[2,33,128]{2,1,0:T(8,128)S(1)} %pad_maximum_fusion.4), channel_id=1, source_target_pairs={{0,64},{64,128},{128,192},{192,256},{256,320},{320,384},{384,448},... | collective-permute-start | bytes 101384 | tf_op jit(solution)/shard_map/ppermute | solution.py:55
  36.6 11.1 %collective-permute-start.5 = (f32[2,33,128]{2,1,0:T(8,128)S(1)}, f32[2,33,128]{2,1,0:T(8,128)S(1)}, u32[]{:S(2)}, u32[]{:S(2)}) collective-permute-start(f32[2,33,128]{2,1,0:T(8,128)S(1)} %pad_maximum_fusion.4), channel_id=1, source_target_pairs={{0,128},{64,192},{128,256},{192,320},{256,384},{320,448},{1,129},{... | collective-permute-start | bytes 101384 | tf_op jit(solution)/shard_map/ppermute | solution.py:55
  37.9 9.8 %collective-permute-start.6 = (f32[2,33,128]{2,1,0:T(8,128)S(1)}, f32[2,33,128]{2,1,0:T(8,128)S(1)}, u32[]{:S(2)}, u32[]{:S(2)}) collective-permute-start(f32[2,33,128]{2,1,0:T(8,128)S(1)} %pad_maximum_fusion.4), channel_id=1, source_target_pairs={{0,192},{64,256},{128,320},{192,384},{256,448},{1,193},{65,257},{1... | collective-permute-start | bytes 101384 | tf_op jit(solution)/shard_map/ppermute | solution.py:55
  42.4 5.2 %collective-permute-start.7 = (f32[2,33,128]{2,1,0:T(8,128)S(1)}, f32[2,33,128]{2,1,0:T(8,128)S(1)}, u32[]{:S(2)}, u32[]{:S(2)}) collective-permute-start(f32[2,33,128]{2,1,0:T(8,128)S(1)} %pad_maximum_fusion.4), channel_id=1, source_target_pairs={{0,256},{64,320},{128,384},{192,448},{1,257},{65,321},{129,385},{1... | collective-permute-start | bytes 101384 | tf_op jit(solution)/shard_map/ppermute | solution.py:55
  48.1 8.7 %collective-permute-start.8 = (f32[2,33,128]{2,1,0:T(8,128)S(1)}, f32[2,33,128]{2,1,0:T(8,128)S(1)}, u32[]{:S(2)}, u32[]{:S(2)}) collective-permute-start(f32[2,33,128]{2,1,0:T(8,128)S(1)} %pad_maximum_fusion.5), channel_id=1, source_target_pairs={{0,256},{64,320},{128,384},{192,448},{1,257},{65,321},{129,385},{1... | collective-permute-start | bytes 101384 | tf_op jit(solution)/shard_map/ppermute | solution.py:55
  56.9 13.7 %collective-permute-start.10 = (f32[2,32,128]{2,1,0:T(8,128)S(1)}, f32[2,32,128]{2,1,0:T(8,128)S(1)}, u32[]{:S(2)}, u32[]{:S(2)}) collective-permute-start(f32[2,32,128]{2,1,0:T(8,128)S(1)} %fusion.81), channel_id=1, source_target_pairs={{0,32},{16,48},{32,0},{48,16},{1,33},{17,49},{33,1},{49,17},{2,34}... | collective-permute-start | bytes 98312 | tf_op jit(solution)/shard_map/ppermute | solution.py:33
  61.2 9.5 %collective-permute-start.11 = (f32[2,32,128]{2,1,0:T(8,128)S(1)}, f32[2,32,128]{2,1,0:T(8,128)S(1)}, u32[]{:S(2)}, u32[]{:S(2)}) collective-permute-start(f32[2,32,128]{2,1,0:T(8,128)S(1)} %fusion.81), channel_id=1, source_target_pairs={{0,48},{16,0},{32,16},{48,32},{1,49},{17,1},{33,17},{49,33},{2,50}... | collective-permute-start | bytes 98312 | tf_op jit(solution)/shard_map/ppermute | solution.py:33
  65.6 5.9 %collective-permute-start.9 = (f32[2,32,128]{2,1,0:T(8,128)S(1)}, f32[2,32,128]{2,1,0:T(8,128)S(1)}, u32[]{:S(2)}, u32[]{:S(2)}) collective-permute-start(f32[2,32,128]{2,1,0:T(8,128)S(1)} %fusion.81), channel_id=1, source_target_pairs={{0,16},{16,32},{32,48},{48,0},{1,17},{17,33},{33,49},{49,1},{2,18}... | collective-permute-start | bytes 98312 | tf_op jit(solution)/shard_map/ppermute | solution.py:33
  72.2 10.9 %collective-permute-start.12 = (f32[2,128,128]{2,1,0:T(8,128)}, f32[2,128,128]{2,1,0:T(8,128)}, u32[]{:S(2)}, u32[]{:S(2)}) collective-permute-start(f32[2,128,128]{2,1,0:T(8,128)} %fusion.76), channel_id=1, source_target_pairs={{0,8},{8,0},{1,9},{9,1},{2,10},{10,2},{3,11},{11,3},{4,12},{12,4},... | collective-permute-start | bytes 393224 | tf_op jit(solution)/shard_map/ppermute | solution.py:107
  78.4 3.2 %copy-start.1 = (bf16[1024,512]{1,0:T(8,128)(2,1)S(1)}, bf16[1024,512]{1,0:T(8,128)(2,1)}, u32[]{:S(2)}) copy-start(bf16[1024,512]{1,0:T(8,128)(2,1)} %param.10) | copy-start | bytes 3145732
  82.2 2.1 %copy-start.3 = (f32[1024,128]{0,1:T(8,128)S(1)}, f32[1024,128]{0,1:T(8,128)}, u32[]{:S(2)}) copy-start(f32[1024,128]{0,1:T(8,128)} %fusion.3) | copy-start | bytes 1572868
  82.2 3.3 %copy-start.4 = (f32[1024,128]{0,1:T(8,128)S(1)}, f32[1024,128]{0,1:T(8,128)}, u32[]{:S(2)}) copy-start(f32[1024,128]{0,1:T(8,128)} %fusion.4) | copy-start | bytes 1572868
  82.2 3.3 %copy-start.7 = (f32[1024,1]{0,1:T(1,128)S(1)}, f32[1024,1]{0,1:T(1,128)}, u32[]{:S(2)}) copy-start(f32[1024,1]{0,1:T(1,128)} %get-tuple-element.70) | copy-start | bytes 12292
  84.3 1.6 %copy-start.5 = (f32[1024,128]{0,1:T(8,128)S(1)}, f32[1024,128]{0,1:T(8,128)}, u32[]{:S(2)}) copy-start(f32[1024,128]{0,1:T(8,128)} %fusion.5) | copy-start | bytes 1572868
  85.5 1.0 copy-start.6

commit v13 on v8

--- a/solution.py
+++ b/solution.py
@@ -77,22 +77,31 @@
     heads, size = S.shape[0], S.shape[1]
     group = heads // cores
 
-    pair = unpack(lax.ppermute(pack(L, S), "cc", [(0, 1), (1, 0)]))
-    L0 = jnp.where(c == 0, L, pair[0])
-    S0 = jnp.where(c == 0, S, pair[1])
-    L1 = jnp.where(c == 0, pair[0], L)
-    S1 = jnp.where(c == 0, pair[1], S)
-    chip_log = L0 + L1
-    chip_state = jnp.exp(L1)[:, None, None] * S0 + S1
-    g_log = lax.dynamic_slice_in_dim(chip_log, c * group, group, 0)
-    g_state = lax.dynamic_slice_in_dim(chip_state, c * group, group, 0)
+    line = cols * cores
+    i = x * cores + c
 
-    row_pieces = [unpack(p) for p in shifted(pack(g_log, g_state), "cx", cols)]
-    e_log, e_state, f_log, f_state = scan_pieces(
-        [p[0] for p in row_pieces], [p[1] for p in row_pieces], x, cols
-    )
-    row_log = e_log + g_log + f_log
-    row_state = jnp.exp(f_log)[:, None, None] * (jnp.exp(g_log)[:, None, None] * e_state + g_state) + f_state
+    def group_of(g):
+        return (
+            lax.dynamic_slice_in_dim(L, g * group, group, 0),
+            lax.dynamic_slice_in_dim(S, g * group, group, 0),
+        )
+
+    own_log, own = group_of(c)
+    logs, states = [own_log], [own]
+    for s in range(1, line):
+        sent = pack(*group_of((c + s) % cores))
+        got_log, got = unpack(lax.ppermute(sent, ("cx", "cc"), [(j, (j + s) % line) for j in range(line)]))
+        logs.append(got_log)
+        states.append(got)
+    e_log, e_state, f_log, f_state = scan_pieces(logs, states, i, line)
+    c_log = jnp.zeros_like(own_log)
+    c_state = jnp.zeros_like(own)
+    for s in range(1, line):
+        early = jnp.logical_and(s <= i, s > c)
+        c_state = c_state + jnp.where(early, jnp.exp(c_log), 0.0)[:, None, None] * states[s]
+        c_log = c_log + jnp.where(early, logs[s], 0.0)
+    row_log = e_log + own_log + f_log
+    row_state = jnp.exp(f_log)[:, None, None] * (jnp.exp(own_log)[:, None, None] * e_state + own) + f_state
 
     part = size // cols
     q_state = lax.dynamic_slice_in_dim(row_state, x * part, part, 1)
@@ -102,13 +111,14 @@
     ordered = [lax.select_n((x - q) % cols, *parts) for q in range(cols)]
     y_full = jnp.concatenate(ordered, axis=1)
 
-    chip_before = jnp.exp(e_log)[:, None, None] * y_full + e_state
-
-    other = lax.ppermute(chip_before, "cc", [(0, 1), (1, 0)])
-    full0 = jnp.concatenate([chip_before, other], axis=0)
-    full1 = jnp.concatenate([other, chip_before], axis=0)
-    chip_full = jnp.where(c == 0, full0, full1)
-    return jnp.where(c == 0, chip_full, jnp.exp(L0)[:, None, None] * chip_full + S0)
+    mine = jnp.exp(e_log)[:, None, None] * y_full + e_state
+    chip_before = jnp.exp(c_log)[:, None, None] * y_full + c_state
+    first_log, first = group_of(0)
+    sent = jnp.where(c == 0, jnp.exp(first_log)[:, None, None] * mine + first, chip_before)
+    other = lax.ppermute(sent, "cc", [(0, 1), (1, 0)])
+    full0 = jnp.concatenate([mine, other], axis=0)
+    full1 = jnp.concatenate([other, mine], axis=0)
+    return jnp.where(c == 0, full0, full1)
 
 
 def inner_head(qh, kh, vh, ch):

time: 131 us -> 142 us (1.084)
  starting transfers between devices: 43.8 us -> 51.4 us
  other arithmetic: 9.53 us -> 14.5 us
  local copies, waits for them, and re-layouts: 6.58 us -> 10.3 us
  waiting for transfers between devices: 7.51 us -> 4.22 us
  matrix products: 22.1 us -> 20.6 us
    ppermute x2 -> x8, starting transfers between devices: 13.2 us -> 26.8 us  [the longest x7 23.2 us: carried_state(): lax.ppermute(sent, ('cx', 'cc'), [(j, (j + s) % line) for j in range(line)])]
    ppermute x6 -> x3, waiting for transfers between devices: 6.34 us -> 0.01 us  [shifted(): out.append(lax.ppermute(x, axis, [(j, (j + s) % n) for j in range(n)]))]
    ppermute x6 -> x3, starting transfers between devices: 14.5 us -> 9.98 us  [shifted(): out.append(lax.ppermute(x, axis, [(j, (j + s) % n) for j in range(n)]))]
    ppermute x2 -> x8, waiting for transfers between devices: 1.16 us -> 4.2 us  [the longest x7 3.51 us: carried_state(): lax.ppermute(sent, ('cx', 'cc'), [(j, (j + s) % line) for j in range(line)])]
    exp x2, local copies, waits for them, and re-layouts: 0.18 us -> 2.64 us  [the longest x1 1.38 us: carried_state(): jnp.exp(first_log)[:, None, None] * mine + first]
    select_n x3 -> x4, other arithmetic: 1.41 us -> 3.41 us  [the longest x2 2.08 us: carried_state(): jnp.where(early, jnp.exp(c_log), 0.0)[:, None, None] * states[s]]
    ppermute x5, starting transfers between devices: 16.1 us -> 14.6 us  [shift(): return lax.ppermute(packed, axis, [(j, j + d) for j in range(n - d)])]
    unnamed x20 -> x32, local copies, waits for them, and re-layouts: 2.19 us -> 3.22 us
  transfers between devices with their start and end apart: 13 -> 16, of which waited for: 4 -> 3; matrix products, arithmetic and copies ran while one was open for 11% -> 14% of each run, Pallas kernels for 0% -> 0%
where the time goes in v13:
time: 142 us; the launch traced here: 141 us
  starting transfers between devices  51.4 us (36%)
  blocking collectives  39.5 us (28%)
  matrix products  20.6 us (15%)
  other arithmetic  14.5 us (10%)
  local copies, waits for them, and re-layouts  10.3 us (7%)
  waiting for transfers between devices  4.22 us (3%)
    all_to_all x1, blocking collectives, body(): lax.all_to_all(payload, 'head', split_axis=0, concat_axis=0, tiled=True)  39.5 us
    ppermute x7, starting transfers between devices, carried_state(): lax.ppermute(sent, ('cx', 'cc'), [(j, (j + s) % line) for j in range(line)])  23.2 us
    ppermute x5, starting transfers between devices, shift(): return lax.ppermute(packed, axis, [(j, j + d) for j in range(n - d)])  14.6 us
    dot_general x4, matrix products, inner_head(): return jnp.dot(weights, vh, preferred_element_type=F32)  12 us
    ppermute x3, starting transfers between devices, shifted(): out.append(lax.ppermute(x, axis, [(j, (j + s) % n) for j in range(n)]))  9.98 us
    dot_general x4, matrix products, body(): jnp.dot((cols(keys, h).astype(F32) * jnp.exp(last[h] - cum[:, h])[:, None...  6.88 us
    ppermute x1, starting transfers between devices, carried_state(): other = lax.ppermute(sent, 'cc', [(0, 1), (1, 0)])  3.62 us
    ppermute x7, waiting for transfers between devices, carried_state(): lax.ppermute(sent, ('cx', 'cc'), [(j, (j + s) % line) for j in range(line)])  3.51 us
  transfers between devices with their start and end apart: 16, of which 3 were waited for; matrix products, arithmetic and copies ran while one was open for 14% of the time, Pallas kernels for 0%

profile of v13, /device:TPU:1, one launch (start us, length us, event | category | flops | bytes accessed | tf_op | source)
XLA Modules:
  0.0 141.2 jit_solution(15122606929862044945)
XLA Ops:
  3.1 3.2 %slice_exponential_fusion.4 = (f32[1024,1]{0,1:T(1,128)}, f32[1024,1]{0,1:T(1,128)S(1)}, f32[1024,1]{0,1:T(1,128)S(1)}, f32[1024,1]{0,1:T(1,128)}, f32[1024,1]{0...) fusion(f32[1024,4]{0,1:T(4,128)S(1)} %bitcast.94, ...), kind=kLoop, calls=%fused_computation.255 | loop fusion | flops 4096 | bytes 65552 | tf_op jit(solution)/shard_map/exp | solution.py:162
  6.3 1.8 %convolution_bitcast_fusion.2 = f32[1,128,128]{2,1,0:T(8,128)S(1)} fusion(f32[1024]{0:T(1024)S(1)} %bitcast.110, bf16[1024,512]{1,0:T(8,128)(2,1)} %param.8, bf16[1024,512]{1,0:T(8,128)(2,1)} %param.7), kind=kOutput, calls=%fused_computation.33 | convolution fusion | flops 201588736 | bytes 593920 | tf_op jit(solution)/shard_map/dot_general | solution.py:146
  8.1 1.7 %convolution_bitcast_fusion.3 = f32[1,128,128]{2,1,0:T(8,128)S(1)} fusion(f32[1024]{0:T(1024)S(1)} %bitcast.109, bf16[1024,512]{1,0:T(8,128)(2,1)S(1)} %copy-done.13, bf16[1024,512]{1,0:T(8,128)(2,1)} %param.7), kind=kOutput, calls=%fused_computation.34 | convolution fusion | flops 201588736 | bytes 593920 | tf_op jit(solution)/shard_map/dot_general | solution.py:146
  9.8 1.7 %convolution_bitcast_fusion = f32[1,128,128]{2,1,0:T(8,128)S(1)} fusion(f32[1024]{0:T(1024)S(1)} %bitcast.108, bf16[1024,512]{1,0:T(8,128)(2,1)S(1)} %copy-done.13, bf16[1024,512]{1,0:T(8,128)(2,1)} %param.7), kind=kOutput, calls=%fused_computation.31 | convolution fusion | flops 201588736 | bytes 593920 | tf_op jit(solution)/shard_map/dot_general | solution.py:146
  11.5 1.7 %convolution_bitcast_fusion.1 = f32[1,128,128]{2,1,0:T(8,128)S(1)} fusion(f32[1024]{0:T(1024)S(1)} %bitcast.107, bf16[1024,512]{1,0:T(8,128)(2,1)S(1)} %copy-done.13, bf16[1024,512]{1,0:T(8,128)(2,1)} %param.7), kind=kOutput, calls=%fused_computation.32 | convolution fusion | flops 201588736 | bytes 593920 | tf_op jit(solution)/shard_map/dot_general | solution.py:146
  13.4 1.3 exponential_reduce_fusion.4
  14.7 2.6 %collective-permute-start = (f32[2,129,128]{2,1,0:T(8,128)S(1)}, f32[2,129,128]{2,1,0:T(8,128)S(1)}, u32[]{:S(2)}, u32[]{:S(2)}) collective-permute-start(f32[2,129,128]{2,1,0:T(8,128)S(1)} %pad_maximum_fusion.2), channel_id=1, source_target_pairs={{0,8},{8,16},{16,24},{24,32},{32,40},{40,48},{48,56},{56,0},{1,9},... | collective-permute-start | bytes 396296 | tf_op jit(solution)/shard_map/ppermute | solution.py:93
  17.4 3.1 %collective-permute-start.1 = (f32[2,129,128]{2,1,0:T(8,128)S(1)}, f32[2,129,128]{2,1,0:T(8,128)}, u32[]{:S(2)}, u32[]{:S(2)}) collective-permute-start(f32[2,129,128]{2,1,0:T(8,128)S(1)} %pad_maximum_fusion.3), channel_id=1, source_target_pairs={{0,16},{8,24},{16,32},{24,40},{32,48},{40,56},{48,0},{56,8},{1,17}... | collective-permute-start | bytes 396296 | tf_op jit(solution)/shard_map/ppermute | solution.py:93
  21.3 3.4 %collective-permute-start.2 = (f32[2,129,128]{2,1,0:T(8,128)}, f32[2,129,128]{2,1,0:T(8,128)S(1)}, u32[]{:S(2)}, u32[]{:S(2)}) collective-permute-start(f32[2,129,128]{2,1,0:T(8,128)} %pad_maximum_fusion.4), channel_id=1, source_target_pairs={{0,24},{8,32},{16,40},{24,48},{32,56},{40,0},{48,8},{56,16},{1,25}... | collective-permute-start | bytes 396296 | tf_op jit(solution)/shard_map/ppermute | solution.py:93
  25.5 7.2 %collective-permute-start.3 = (f32[2,129,128]{2,1,0:T(8,128)}, f32[2,129,128]{2,1,0:T(8,128)S(1)}, u32[]{:S(2)}, u32[]{:S(2)}) collective-permute-start(f32[2,129,128]{2,1,0:T(8,128)} %pad_maximum_fusion.5), channel_id=1, source_target_pairs={{0,32},{8,40},{16,48},{24,56},{32,0},{40,8},{48,16},{56,24},{1,33}... | collective-permute-start | bytes 396296 | tf_op jit(solution)/shard_map/ppermute | solution.py:93
  32.7 4.5 %collective-permute-start.4 = (f32[2,129,128]{2,1,0:T(8,128)S(1)}, f32[2,129,128]{2,1,0:T(8,128)S(1)}, u32[]{:S(2)}, u32[]{:S(2)}) collective-permute-start(f32[2,129,128]{2,1,0:T(8,128)S(1)} %pad_maximum_fusion.6), channel_id=1, source_target_pairs={{0,40},{8,48},{16,56},{24,0},{32,8},{40,16},{48,24},{56,32},{1,41}... | collective-permute-start | bytes 396296 | tf_op jit(solution)/shard_map/ppermute | solution.py:93
  37.3 3.2 %fusion.3 = f32[1024,128]{0,1:T(8,128)} fusion(f32[1024]{0:T(1024)S(1)} %bitcast.106, bf16[1024,512]{1,0:T(8,128)(2,1)} %param.8, bf16[1024,512]{1,0:T(8,128)(2,1)} %param.7, bf16[1024,512]{1,0:T(8,128)(2,1)S(1)} %copy-done), kind=kOutput, calls=%fused_computation.11 | convolution fusion | flops 543162368 | bytes 1318912 | tf_op jit(solution)/shard_map/dot_general | solution.py:131
  40.5 2.4 %fusion.4 = f32[1024,128]{0,1:T(8,128)S(1)} fusion(f32[1024]{0:T(1024)S(1)} %bitcast.105, bf16[1024,512]{1,0:T(8,128)(2,1)S(1)} %copy-done, bf16[1024,512]{1,0:T(8,128)(2,1)} %param.8, bf16[1024,512]{1,0:T(8,128)(2,1)} %param.7), kind=kOutput, calls=%fused_computation.12 | convolution fusion | flops 543162368 | bytes 1318912 | tf_op jit(solution)/shard_map/dot_general | solution.py:131
  43.1 1.9 %collective-permute-start.5 = (f32[2,129,128]{2,1,0:T(8,128)S(1)}, f32[2,129,128]{2,1,0:T(8,128)S(1)}, u32[]{:S(2)}, u32[]{:S(2)}) collective-permute-start(f32[2,129,128]{2,1,0:T(8,128)S(1)} %pad_maximum_fusion.7), channel_id=1, source_target_pairs={{0,48},{8,56},{16,0},{24,8},{32,16},{40,24},{48,32},{56,40},{1,49}... | collective-permute-start | bytes 396296 | tf_op jit(solution)/shard_map/ppermute | solution.py:93
  45.5 1.4 fusion.102
  47.6 2.8 %collective-permute-done.5 = f32[2,129,128]{2,1,0:T(8,128)S(1)} collective-permute-done((f32[2,129,128]{2,1,0:T(8,128)S(1)}, f32[2,129,128]{2,1,0:T(8,128)S(1)}, u32[]{:S(2)}, u32[]{:S(2)}) %collective-permute-start.5) | collective-permute-done | bytes 132128 | tf_op jit(solution)/shard_map/ppermute | solution.py:93
  53.9 2.9 %collective-permute-start.10 = (f32[2,33,128]{2,1,0:T(8,128)S(1)}, f32[2,33,128]{2,1,0:T(8,128)S(1)}, u32[]{:S(2)}, u32[]{:S(2)}) collective-permute-start(f32[2,33,128]{2,1,0:T(8,128)S(1)} %pad_maximum_fusion.10), channel_id=1, source_target_pairs={{0,256},{64,320},{128,384},{192,448},{1,257},{65,321},{129,385},{1... | collective-permute-start | bytes 101384 | tf_op jit(solution)/shard_map/ppermute | solution.py:55
  56.8 2.3 %collective-permute-start.7 = (f32[2,33,128]{2,1,0:T(8,128)S(1)}, f32[2,33,128]{2,1,0:T(8,128)S(1)}, u32[]{:S(2)}, u32[]{:S(2)}) collective-permute-start(f32[2,33,128]{2,1,0:T(8,128)S(1)} %pad_maximum_fusion.10), channel_id=1, source_target_pairs={{0,64},{64,128},{128,192},{192,256},{256,320},{320,384},{384,448},... | collective-permute-start | bytes 101384 | tf_op jit(solution)/shard_map/ppermute | solution.py:55
  59.1 2.4 %collective-permute-start.8 = (f32[2,33,128]{2,1,0:T(8,128)S(1)}, f32[2,33,128]{2,1,0:T(8,128)S(1)}, u32[]{:S(2)}, u32[]{:S(2)}) collective-permute-start(f32[2,33,128]{2,1,0:T(8,128)S(1)} %pad_maximum_fusion.10), channel_id=1, source_target_pairs={{0,128},{64,192},{128,256},{192,320},{256,384},{320,448},{1,129},{... | collective-permute-start | bytes 101384 | tf_op jit(solution)/shard_map/ppermute | solution.py:55
  61.6 1.6 %collective-permute-start.9 = (f32[2,33,128]{2,1,0:T(8,128)S(1)}, f32[2,33,128]{2,1,0:T(8,128)S(1)}, u32[]{:S(2)}, u32[]{:S(2)}) collective-permute-start(f32[2,33,128]{2,1,0:T(8,128)S(1)} %pad_maximum_fusion.10), channel_id=1, source_target_pairs={{0,192},{64,256},{128,320},{192,384},{256,448},{1,193},{65,257},{1... | collective-permute-start | bytes 101384 | tf_op jit(solution)/shard_map/ppermute | solution.py:55
  63.2 3.2 %fusion.5 = f32[1024,128]{0,1:T(8,128)} fusion(f32[1024]{0:T(1024)S(1)} %bitcast.104, bf16[1024,512]{1,0:T(8,128)(2,1)S(1)} %copy-done, bf16[1024,512]{1,0:T(8,128)(2,1)} %param.8, bf16[1024,512]{1,0:T(8,128)(2,1)} %param.7), kind=kOutput, calls=%fused_computation.13 | convolution fusion | flops 543162368 | bytes 1318912 | tf_op jit(solution)/shard_map/dot_general | solution.py:131
  66.9 5.3 %collective-permute-start.11 = (f32[2,33,128]{2,1,0:T(8,128)S(1)}, f32[2,33,128]{2,1,0:T(8,128)S(1)}, u32[]{:S(2)}, u32[]{:S(2)}) collective-permute-start(f32[2,33,128]{2,1,0:T(8,128)S(1)} %pad_maximum_fusion.11), channel_id=1, source_target_pairs={{0,256},{64,320},{128,384},{192,448},{1,257},{65,321},{129,385},{1... | collective-permute-start | bytes 101384 | tf_op jit(solution)/shard_map/ppermute | solution.py:55
  72.2 3.2 %fusion.6 = f32[1024,128]{0,1:T(8,128)} fusion(f32[1024]{0:T(1024)S(1)} %bitcast.103, bf16[1024,512]{1,0:T(8,128)(2,1)S(1)} %copy-done, bf16[1024,512]{1,0:T(8,128)(2,1)} %param.8, bf16[1024,512]{1,0:T(8,128)(2,1)} %param.7), kind=kOutput, calls=%fused_computation.14 | convolution fusion | flops 543162368 | bytes 1318912 | tf_op jit(solution)/shard_map/dot_general | solution.py:131
  75.4 2.5 %collective-permute-start.12 = (f32[2,32,128]{2,1,0:T(8,128)S(1)}, f32[2,32,128]{2,1,0:T(8,128)}, u32[]{:S(2)}, u32[]{:S(2)}) collective-permute-start(f32[2,32,128]{2,1,0:T(8,128)S(1)} %fusion.64), channel_id=1, source_target_pairs={{0,16},{16,32},{32,48},{48,0},{1,17},{17,33},{33,49},{49,1},{2,18}... | collective-permute-start | bytes 98312 | tf_op jit(solution)/shard_map/ppermute | solution.py:33
  78.0 5.5 %collective-permute-start.13 = (f32[2,32,128]{2,1,0:T(8,128)S(1)}, f32[2,32,128]{2,1,0:T(8,128)}, u32[]{:S(2)}, u32[]{:S(2)}) collective-permute-start(f32[2,32,128]{2,1,0:T(8,128)S(1)} %fusion.64), channel_id=1, source_target_pairs={{0,32},{16,48},{32,0},{48,16},{1,33},{17,49},{33,1},{49,17},{2,34}... | collective-permute-start | bytes 98312 | tf_op jit(solution)/shard_map/ppermute | solution.py:33
  83.5 1.9 %collective-permute-start.14 = (f32[2,32,128]{2,1,0:T(8,128)S(1)}, f32[2,32,128]{2,1,0:T(8,128)}, u32[]{:S(2)}, u32[]{:S(2)}) collective-permute-start(f32[2,32,128]{2,1,0:T(8,128)S(1)} %fusion.64), channel_id=1, source_target_pairs={{0,48},{16,0},{32,16},{48,32},{1,49},{17,1},{33,17},{49,33},{2,50}... | collective-permute-start | bytes 98312 | tf_op jit(solution)/shard_map/ppermute | solution.py:33
  85.5 1.4 fusion.121
  86.8 1.5 %copy.24 = bf16[1024,512]{0,1:T(8,128)(2,1)S(1)} copy(bf16[1024,512]{1,0:T(8,128)(2,1)} %param.10) | data formatting | bytes 2097152 | tf_op args[4]
  90.0 1.3 fusion.63
  91.3 3.6 %collective-permute-start.15 = (f32[2,128,128]{2,1,0:T(8,128)S(1)}, f32[2,128,128]{2,1,0:T(8,128)S(1)}, u32[]{:S(2)}, u32[]{:S(2)}) collective-permute-start(f32[2,128,128]{2,1,0:T(8,128)S(1)} %fusion.63), channel_id=1, source_target_pairs={{0,8},{8,0},{1,9},{9,1},{2,10},{10,2},{3,11},{11,3},{4,12},{12,4},... | collective-permute-start | bytes 393224 | tf_op jit(solution)/shard_map/ppermute | solution.py:118
  99.3 39.5 %all_to_all.5 = bf16[8,129,512]{2,1,0:T(8,128)(2,1)S(1)} all-to-all(bf16[8,129,512]{2,1,0:T(8,128)(2,1)S(1)} %maximum_maximum_fusion), channel_id=1, replica_groups=mesh['cy'=8,'cx'=4,'cc'=2,'head'=8] {'head'}, dimensions={0} | all-to-all | bytes 2113536 | tf_op jit(solution)/shard_map/all_to_all | solution.py:182
  139.8 1.3 copy.30
  (109 shorter events, 17.0 us)
Async XLA Ops:
  0.0 8.1 %copy-start.13 = (bf16[1024,512]{1,0:T(8,128)(2,1)S(1)}, bf16[1024,512]{1,0:T(8,128)(2,1)}, u32[]{:S(2)}) copy-start(bf16[1024,512]{1,0:T(8,128)(2,1)} %param.8) | copy-start | bytes 3145732
  2.4 3.9 %copy-start.7 = (f32[1,4,8,128]{3,1,2,0:T(4,128)}, f32[1,4,8,128]{3,1,2,0:T(4,128)S(1)}, u32[]{:S(2)}) copy-start(f32[1,4,8,128]{3,1,2,0:T(4,128)S(1)} %copy.41) | copy-start | bytes 49156
  9.8 3.5 %copy-start.6 = (f32[1,128,128]{2,1,0:T(8,128)}, f32[1,128,128]{2,1,0:T(8,128)S(1)}, u32[]{:S(2)}) copy-start(f32[1,128,128]{2,1,0:T(8,128)S(1)} %convolution_bitcast_fusion.3) | copy-start | bytes 196612
  13.4 23.9 %copy-start = (bf16[1024,512]{1,0:T(8,128)(2,1)S(1)}, bf16[1024,512]{1,0:T(8,128)(2,1)}, u32[]{:S(2)}) copy-start(bf16[1024,512]{1,0:T(8,128)(2,1)} %param.6) | copy-start | bytes 3145732
  14.7 28.4 %collective-permute-start = (f32[2,129,128]{2,1,0:T(8,128)S(1)}, f32[2,129,128]{2,1,0:T(8,128)S(1)}, u32[]{:S(2)}, u32[]{:S(2)}) collective-permute-start(f32[2,129,128]{2,1,0:T(8,128)S(1)} %pad_maximum_fusion.2), channel_id=1, source_target_pairs={{0,8},{8,16},{16,24},{24,32},{32,40},{40,48},{48,56},{56,0},{1,9},... | collective-permute-start | bytes 396296 | tf_op jit(solution)/shard_map/ppermute | solution.py:93
  17.4 27.7 %collective-permute-start.1 = (f32[2,129,128]{2,1,0:T(8,128)S(1)}, f32[2,129,128]{2,1,0:T(8,128)}, u32[]{:S(2)}, u32[]{:S(2)}) collective-permute-start(f32[2,129,128]{2,1,0:T(8,128)S(1)} %pad_maximum_fusion.3), channel_id=1, source_target_pairs={{0,16},{8,24},{16,32},{24,40},{32,48},{40,56},{48,0},{56,8},{1,17}... | collective-permute-start | bytes 396296 | tf_op jit(solution)/shard_map/ppermute | solution.py:93
  21.3 25.6 %collective-permute-start.2 = (f32[2,129,128]{2,1,0:T(8,128)}, f32[2,129,128]{2,1,0:T(8,128)S(1)}, u32[]{:S(2)}, u32[]{:S(2)}) collective-permute-start(f32[2,129,128]{2,1,0:T(8,128)} %pad_maximum_fusion.4), channel_id=1, source_target_pairs={{0,24},{8,32},{16,40},{24,48},{32,56},{40,0},{48,8},{56,16},{1,25}... | collective-permute-start | bytes 396296 | tf_op jit(solution)/shard_map/ppermute | solution.py:93
  25.5 21.4 %collective-permute-start.3 = (f32[2,129,128]{2,1,0:T(8,128)}, f32[2,129,128]{2,1,0:T(8,128)S(1)}, u32[]{:S(2)}, u32[]{:S(2)}) collective-permute-start(f32[2,129,128]{2,1,0:T(8,128)} %pad_maximum_fusion.5), channel_id=1, source_target_pairs={{0,32},{8,40},{16,48},{24,56},{32,0},{40,8},{48,16},{56,24},{1,33}... | collective-permute-start | bytes 396296 | tf_op jit(solution)/shard_map/ppermute | solution.py:93
  32.7 14.8 %collective-permute-start.4 = (f32[2,129,128]{2,1,0:T(8,128)S(1)}, f32[2,129,128]{2,1,0:T(8,128)S(1)}, u32[]{:S(2)}, u32[]{:S(2)}) collective-permute-start(f32[2,129,128]{2,1,0:T(8,128)S(1)} %pad_maximum_fusion.6), channel_id=1, source_target_pairs={{0,40},{8,48},{16,56},{24,0},{32,8},{40,16},{48,24},{56,32},{1,41}... | collective-permute-start | bytes 396296 | tf_op jit(solution)/shard_map/ppermute | solution.py:93
  40.5 11.3 %copy-start.11 = (f32[1,2]{0,1:T(2,128)S(1)}, f32[1,2]{0,1:T(2,128)}, u32[]{:S(2)}) copy-start(f32[1,2]{0,1:T(2,128)} %get-tuple-element.42) | copy-start | bytes 28
  43.1 9.4 %copy-start.5 = (f32[2,129,128]{2,1,0:T(8,128)}, f32[2,129,128]{2,1,0:T(8,128)S(1)}, u32[]{:S(2)}) copy-start(f32[2,129,128]{2,1,0:T(8,128)S(1)} %collective-permute-done) | copy-start | bytes 396292
  43.1 7.3 %collective-permute-start.5 = (f32[2,129,128]{2,1,0:T(8,128)S(1)}, f32[2,129,128]{2,1,0:T(8,128)S(1)}, u32[]{:S(2)}, u32[]{:S(2)}) collective-permute-start(f32[2,129,128]{2,1,0:T(8,128)S(1)} %pad_maximum_fusion.7), channel_id=1, source_target_pairs={{0,48},{8,56},{16,0},{24,8},{32,16},{40,24},{48,32},{56,40},{1,49}... | collective-permute-start | bytes 396296 | tf_op jit(solution)/shard_map/ppermute | solution.py:93
  45.1 6.0 %collective-permute-start.6 = (f32[2,129,128]{2,1,0:T(8,128)S(1)}, f32[2,129,128]{2,1,0:T(8,128)S(1)}, u32[]{:S(2)}, u32[]{:S(2)}) collective-permute-start(f32[2,129,128]{2,1,0:T(8,128)S(1)} %pad_maximum_fusion.8), channel_id=1, source_target_pairs={{0,56},{8,0},{16,8},{24,16},{32,24},{40,32},{48,40},{56,48},{1,57}... | collective-permute-start | bytes 396296 | tf_op jit(solution)/shard_map/ppermute | solution.py:93
  46.9 19.6 %copy-start.4 = (f32[2,129,128]{2,1,0:T(8,128)}, f32[2,129,128]{2,1,0:T(8,128)S(1)}, u32[]{:S(2)}) copy-start(f32[2,129,128]{2,1,0:T(8,128)S(1)} %collective-permute-done.3) | copy-start | bytes 396292
  52.5 1.3 copy-start.12
  53.9 12.6 %collective-permute-start.10 = (f32[2,33,128]{2,1,0:T(8,128)S(1)}, f32[2,33,128]{2,1,0:T(8,128)S(1)}, u32[]{:S(2)}, u32[]{:S(2)}) collective-permute-start(f32[2,33,128]{2,1,0:T(8,128)S(1)} %pad_maximum_fusion.10), channel_id=1, source_target_pairs={{0,256},{64,320},{128,384},{192,448},{1,257},{65,321},{129,385},{1... | collective-permute-start | bytes 101384 | tf_op jit(solution)/shard_map/ppermute | solution.py:55
  56.8 9.6 %collective-permute-start.7 = (f32[2,33,128]{2,1,0:T(8,128)S(1)}, f32[2,33,128]{2,1,0:T(8,128)S(1)}, u32[]{:S(2)}, u32[]{:S(2)}) collective-permute-start(f32[2,33,128]{2,1,0:T(8,128)S(1)} %pad_maximum_fusion.10), channel_id=1, source_target_pairs={{0,64},{64,128},{128,192},{192,256},{256,320},{320,384},{384,448},... | collective-permute-start | bytes 101384 | tf_op jit(solution)/shard_map/ppermute | solution.py:55
  59.1 7.3 %collective-permute-start.8 = (f32[2,33,128]{2,1,0:T(8,128)S(1)}, f32[2,33,128]{2,1,0:T(8,128)S(1)}, u32[]{:S(2)}, u32[]{:S(2)}) collective-permute-start(f32[2,33,128]{2,1,0:T(8,128)S(1)} %pad_maximum_fusion.10), channel_id=1, source_target_pairs={{0,128},{64,192},{128,256},{192,320},{256,384},{320,448},{1,129},{... | collective-permute-start | bytes 101384 | tf_op jit(solution)/shard_map/ppermute | solution.py:55
  61.6 4.9 %collective-permute-start.9 = (f32[2,33,128]{2,1,0:T(8,128)S(1)}, f32[2,33,128]{2,1,0:T(8,128)S(1)}, u32[]{:S(2)}, u32[]{:S(2)}) collective-permute-start(f32[2,33,128]{2,1,0:T(8,128)S(1)} %pad_maximum_fusion.10), channel_id=1, source_target_pairs={{0,192},{64,256},{128,320},{192,384},{256,448},{1,193},{65,257},{1... | collective-permute-start | bytes 101384 | tf_op jit(solution)/shard_map/ppermute | solution.py:55
  66.9 8.5 %collective-permute-start.11 = (f32[2,33,128]{2,1,0:T(8,128)S(1)}, f32[2,33,128]{2,1,0:T(8,128)S(1)}, u32[]{:S(2)}, u32[]{:S(2)}) collective-permute-start(f32[2,33,128]{2,1,0:T(8,128)S(1)} %pad_maximum_fusion.11), channel_id=1, source_target_pairs={{0,256},{64,320},{128,384},{192,448},{1,257},{65,321},{129,385},{1... | collective-permute-start | bytes 101384 | tf_op jit(solution)/shard_map/ppermute | solution.py:55
  75.4 13.7 %collective-permute-start.12 = (f32[2,32,128]{2,1,0:T(8,128)S(1)}, f32[2,32,128]{2,1,0:T(8,128)}, u32[]{:S(2)}, u32[]{:S(2)}) collective-permute-start(f32[2,32,128]{2,1,0:T(8,128)S(1)} %fusion.64), channel_id=1, source_target_pairs={{0,16},{16,32},{32,48},{48,0},{1,17},{17,33},{33,49},{49,1},{2,18}... | collective-permute-start | bytes 98312 | tf_op jit(solution)/shard_map/ppermute | solution.py:33
  78.0 11.2 %collective-permute-start.13 = (f32[2,32,128]{2,1,0:T(8,128)S(1)}, f32[2,32,128]{2,1,0:T(8,128)}, u32[]{:S(2)}, u32[]{:S(2)}) collective-permute-start(f32[2,32,128]{2,1,0:T(8,128)S(1)} %fusion.64), channel_id=1, source_target_pairs={{0,32},{16,48},{32,0},{48,16},{1,33},{17,49},{33,1},{49,17},{2,34}... | collective-permute-start | bytes 98312 | tf_op jit(solution)/shard_map/ppermute | solution.py:33
  83.5 5.6 %collective-permute-start.14 = (f32[2,32,128]{2,1,0:T(8,128)S(1)}, f32[2,32,128]{2,1,0:T(8,128)}, u32[]{:S(2)}, u32[]{:S(2)}) collective-permute-start(f32[2,32,128]{2,1,0:T(8,128)S(1)} %fusion.64), channel_id=1, source_target_pairs={{0,48},{16,0},{32,16},{48,32},{1,49},{17,1},{33,17},{49,33},{2,50}... | collective-permute-start | bytes 98312 | tf_op jit(solution)/shard_map/ppermute | solution.py:33
  88.3 6.6 %copy-start.10 = (f32[2]{0:T(128)S(1)}, f32[2]{0:T(128)}, u32[]{:S(2)}) copy-start(f32[2]{0:T(128)} %get-tuple-element.26) | copy-start | bytes 28
  90.0 5.8 %copy-start.1 = (f32[1024,128]{0,1:T(8,128)S(1)}, f32[1024,128]{0,1:T(8,128)}, u32[]{:S(2)}) copy-start(f32[1024,128]{0,1:T(8,128)} %fusion.3) | copy-start | bytes 1572868
  90.0 5.8 %copy-start.9 = (f32[1024,1]{0,1:T(1,128)S(1)}, f32[1024,1]{0,1:T(1,128)}, u32[]{:S(2)}) copy-start(f32[1024,1]{0,1:T(1,128)} %get-tuple-element.81) | copy-start | bytes 12292
  91.3 4.9 %copy-start.8 = (f32[1024,1]{0,1:T(1,128)S(1)}, f32[1024,1]{0,1:T(1,128)}, u32[]{:S(2)}) copy-start(f32[1024,1]{0,1:T(1,128)} %get-tuple-element.84) | copy-start | bytes 12292
  91.3 4.4 %collective-permute-start.15 = (f32[2,128,128]{2,1,0:T(8,128)S(1)}, f32[2,128,128]{2,1,0:T(8,128)S(1)}, u32[]{:S(2)}, u32[]{:S(2)}) collective-permute-start(f32[2,128,128]{2,1,0:T(8,128)S(1)} %fusion.63), channel_id=1, source_target_pairs={{0,8},{8,0},{1,9},{9,1},{2,10},{10,2},{3,11},{11,3},{4,12},{12,4},... | collective-permute-start | bytes 393224 | tf_op jit(solution)/shard_map/ppermute | solution.py:118
  95.8 1.0 copy-start.2
  96.2 1.1 copy-start.3

commit v14 on v8

--- a/solution.py
+++ b/solution.py
@@ -55,7 +55,7 @@
         return lax.ppermute(packed, axis, [(j, j + d) for j in range(n - d)])
 
     packed = pack(log, state)
-    first = min(4, n - 1)
+    first = n - 1
     cur_log = jnp.zeros_like(log)
     cur = jnp.zeros_like(state)
     for d in range(1, first + 1):
@@ -63,7 +63,7 @@
         cur = cur + jnp.exp(cur_log)[:, None, None] * got
         cur_log = cur_log + got_log
     d = first
-    while d < n:
+    while d < n - 1:
         got_log, got = unpack(shift(pack(cur_log, cur), d))
         cur = jnp.exp(cur_log)[:, None, None] * got + cur
         cur_log = cur_log + got_log

time: 131 us -> 130 us (level)
    ppermute x6, waiting for transfers between devices: 6.34 us -> 3.24 us  [shifted(): out.append(lax.ppermute(x, axis, [(j, (j + s) % n) for j in range(n)]))]
    ppermute x5 -> x7, waiting for transfers between devices: 0.01 us -> 2.98 us  [shift(): return lax.ppermute(packed, axis, [(j, j + d) for j in range(n - d)])]
    ppermute x5 -> x7, starting transfers between devices: 16.1 us -> 14.6 us  [shift(): return lax.ppermute(packed, axis, [(j, j + d) for j in range(n - d)])]
  transfers between devices with their start and end apart: 13 -> 15, of which waited for: 4 -> 4; matrix products, arithmetic and copies ran while one was open for 11% -> 11% of each run, Pallas kernels for 0% -> 0%
where the time goes in v14:
time: 130 us; the launch traced here: 129 us
  starting transfers between devices  42.7 us (33%)
  blocking collectives  40.5 us (31%)
  matrix products  22.1 us (17%)
  other arithmetic  9.43 us (7%)
  waiting for transfers between devices  7.38 us (6%)
  local copies, waits for them, and re-layouts  6.42 us (5%)
    all_to_all x1, blocking collectives, body(): lax.all_to_all(payload, 'head', split_axis=0, concat_axis=0, tiled=True)  40.5 us
    ppermute x7, starting transfers between devices, shift(): return lax.ppermute(packed, axis, [(j, j + d) for j in range(n - d)])  14.6 us
    ppermute x6, starting transfers between devices, shifted(): out.append(lax.ppermute(x, axis, [(j, (j + s) % n) for j in range(n)]))  14.4 us
    dot_general x4, matrix products, inner_head(): return jnp.dot(weights, vh, preferred_element_type=F32)  12.7 us
    ppermute x1, starting transfers between devices, carried_state(): pair = unpack(lax.ppermute(pack(L, S), 'cc', [(0, 1), (1, 0)]))  8.92 us
    dot_general x4, matrix products, body(): jnp.dot((cols(keys, h).astype(F32) * jnp.exp(last[h] - cum[:, h])[:, None...  6.95 us
    ppermute x1, starting transfers between devices, carried_state(): other = lax.ppermute(chip_before, 'cc', [(0, 1), (1, 0)])  4.75 us
    ppermute x6, waiting for transfers between devices, shifted(): out.append(lax.ppermute(x, axis, [(j, (j + s) % n) for j in range(n)]))  3.24 us
  transfers between devices with their start and end apart: 15, of which 4 were waited for; matrix products, arithmetic and copies ran while one was open for 11% of the time, Pallas kernels for 0%

profile of v14, /device:TPU:1, one launch (start us, length us, event | category | flops | bytes accessed | tf_op | source)
XLA Modules:
  0.0 128.9 jit_solution(17217702400458739674)
XLA Ops:
  0.8 1.1 reduce-window.6
  3.2 3.2 %slice_exponential_fusion.3 = (f32[1024,1]{0,1:T(1,128)S(1)}, f32[1024,1]{0,1:T(1,128)S(1)}, f32[1024,1]{0,1:T(1,128)S(1)}, f32[1024,1]{0,1:T(1,128)S(1)}, f32[1...) fusion(f32[1024,4]{0,1:T(4,128)S(1)} %bitcast.95, ...), kind=kLoop, calls=%fused_computation.182 | loop fusion | flops 4096 | bytes 65552 | tf_op jit(solution)/shard_map/exp | solution.py:152
  6.4 1.8 %convolution_bitcast_fusion.3 = f32[1,128,128]{2,1,0:T(8,128)S(1)} fusion(f32[1024]{0:T(1024)S(1)} %bitcast.111, bf16[1024,512]{1,0:T(8,128)(2,1)} %param.8, bf16[1024,512]{1,0:T(8,128)(2,1)} %param.7), kind=kOutput, calls=%fused_computation.34 | convolution fusion | flops 201588736 | bytes 593920 | tf_op jit(solution)/shard_map/dot_general | solution.py:136
  8.2 1.8 %convolution_bitcast_fusion.2 = f32[1,128,128]{2,1,0:T(8,128)S(1)} fusion(f32[1024]{0:T(1024)S(1)} %bitcast.110, bf16[1024,512]{1,0:T(8,128)(2,1)} %param.8, bf16[1024,512]{1,0:T(8,128)(2,1)} %param.7), kind=kOutput, calls=%fused_computation.33 | convolution fusion | flops 201588736 | bytes 593920 | tf_op jit(solution)/shard_map/dot_general | solution.py:136
  10.0 1.7 %convolution_bitcast_fusion.1 = f32[1,128,128]{2,1,0:T(8,128)S(1)} fusion(f32[1024]{0:T(1024)S(1)} %bitcast.109, bf16[1024,512]{1,0:T(8,128)(2,1)S(1)} %copy-done.7, bf16[1024,512]{1,0:T(8,128)(2,1)} %param.7), kind=kOutput, calls=%fused_computation.32 | convolution fusion | flops 201588736 | bytes 593920 | tf_op jit(solution)/shard_map/dot_general | solution.py:136
  11.7 1.7 %convolution_bitcast_fusion = f32[1,128,128]{2,1,0:T(8,128)S(1)} fusion(f32[1024]{0:T(1024)S(1)} %bitcast.108, bf16[1024,512]{1,0:T(8,128)(2,1)S(1)} %copy-done.7, bf16[1024,512]{1,0:T(8,128)(2,1)} %param.7), kind=kOutput, calls=%fused_computation.31 | convolution fusion | flops 201588736 | bytes 593920 | tf_op jit(solution)/shard_map/dot_general | solution.py:136
  13.5 8.9 %collective-permute-start = (f32[4,129,128]{2,1,0:T(8,128)S(1)}, f32[4,129,128]{2,1,0:T(8,128)S(1)}, u32[]{:S(2)}, u32[]{:S(2)}) collective-permute-start(f32[4,129,128]{2,1,0:T(8,128)S(1)} %pad_maximum_fusion.1), channel_id=1, source_target_pairs={{0,8},{8,0},{1,9},{9,1},{2,10},{10,2},{3,11},{11,3},{4,12},{12,4},... | collective-permute-start | bytes 792584 | tf_op jit(solution)/shard_map/ppermute | solution.py:80
  22.4 1.2 collective-permute-done
  24.7 1.9 %collective-permute-start.3 = (f32[2,129,128]{2,1,0:T(8,128)S(1)}, f32[2,129,128]{2,1,0:T(8,128)S(1)}, u32[]{:S(2)}, u32[]{:S(2)}) collective-permute-start(f32[2,129,128]{2,1,0:T(8,128)S(1)} %pad_maximum_fusion.3), channel_id=1, source_target_pairs={{0,48},{16,0},{32,16},{48,32},{1,49},{17,1},{33,17},{49,33},{2,50}... | collective-permute-start | bytes 396296 | tf_op jit(solution)/shard_map/ppermute | solution.py:33
  26.6 1.9 %collective-permute-start.2 = (f32[2,129,128]{2,1,0:T(8,128)S(1)}, f32[2,129,128]{2,1,0:T(8,128)S(1)}, u32[]{:S(2)}, u32[]{:S(2)}) collective-permute-start(f32[2,129,128]{2,1,0:T(8,128)S(1)} %pad_maximum_fusion.3), channel_id=1, source_target_pairs={{0,32},{16,48},{32,0},{48,16},{1,33},{17,49},{33,1},{49,17},{2,34}... | collective-permute-start | bytes 396296 | tf_op jit(solution)/shard_map/ppermute | solution.py:33
  28.5 3.4 %collective-permute-start.1 = (f32[2,129,128]{2,1,0:T(8,128)S(1)}, f32[2,129,128]{2,1,0:T(8,128)S(1)}, u32[]{:S(2)}, u32[]{:S(2)}) collective-permute-start(f32[2,129,128]{2,1,0:T(8,128)S(1)} %pad_maximum_fusion.3), channel_id=1, source_target_pairs={{0,16},{16,32},{32,48},{48,0},{1,17},{17,33},{33,49},{49,1},{2,18}... | collective-permute-start | bytes 396296 | tf_op jit(solution)/shard_map/ppermute | solution.py:33
  31.9 3.1 %fusion.6 = f32[1024,128]{0,1:T(8,128)} fusion(f32[1024]{0:T(1024)S(1)} %bitcast.107, bf16[1024,512]{1,0:T(8,128)(2,1)S(1)} %copy-done, bf16[1024,512]{1,0:T(8,128)(2,1)S(1)} %copy-done.7, bf16[1024,512]{1,0:T(8,128)(2,1)} %param.7), kind=kOutput, calls=%fused_computation.14 | convolution fusion | flops 543162368 | bytes 1318912 | tf_op jit(solution)/shard_map/dot_general | solution.py:121
  35.0 2.7 %collective-permute-done.1 = f32[2,129,128]{2,1,0:T(8,128)S(1)} collective-permute-done((f32[2,129,128]{2,1,0:T(8,128)S(1)}, f32[2,129,128]{2,1,0:T(8,128)S(1)}, u32[]{:S(2)}, u32[]{:S(2)}) %collective-permute-start.1) | collective-permute-done | bytes 132128 | tf_op jit(solution)/shard_map/ppermute | solution.py:33
  38.3 2.6 %collective-permute-start.6 = (f32[2,33,128]{2,1,0:T(8,128)S(1)}, f32[2,33,128]{2,1,0:T(8,128)S(1)}, u32[]{:S(2)}, u32[]{:S(2)}) collective-permute-start(f32[2,33,128]{2,1,0:T(8,128)S(1)} %pad_maximum_fusion.4), channel_id=1, source_target_pairs={{0,192},{64,256},{128,320},{192,384},{256,448},{1,193},{65,257},{1... | collective-permute-start | bytes 101384 | tf_op jit(solution)/shard_map/ppermute | solution.py:55
  41.0 4.5 %collective-permute-start.5 = (f32[2,33,128]{2,1,0:T(8,128)S(1)}, f32[2,33,128]{2,1,0:T(8,128)S(1)}, u32[]{:S(2)}, u32[]{:S(2)}) collective-permute-start(f32[2,33,128]{2,1,0:T(8,128)S(1)} %pad_maximum_fusion.4), channel_id=1, source_target_pairs={{0,128},{64,192},{128,256},{192,320},{256,384},{320,448},{1,129},{... | collective-permute-start | bytes 101384 | tf_op jit(solution)/shard_map/ppermute | solution.py:55
  45.5 2.3 %collective-permute-start.4 = (f32[2,33,128]{2,1,0:T(8,128)S(1)}, f32[2,33,128]{2,1,0:T(8,128)S(1)}, u32[]{:S(2)}, u32[]{:S(2)}) collective-permute-start(f32[2,33,128]{2,1,0:T(8,128)S(1)} %pad_maximum_fusion.4), channel_id=1, source_target_pairs={{0,64},{64,128},{128,192},{192,256},{256,320},{320,384},{384,448},... | collective-permute-start | bytes 101384 | tf_op jit(solution)/shard_map/ppermute | solution.py:55
  47.8 3.1 %fusion.5 = f32[1024,128]{0,1:T(8,128)} fusion(f32[1024]{0:T(1024)S(1)} %bitcast.106, bf16[1024,512]{1,0:T(8,128)(2,1)S(1)} %copy-done, bf16[1024,512]{1,0:T(8,128)(2,1)S(1)} %copy-done.7, bf16[1024,512]{1,0:T(8,128)(2,1)} %param.7), kind=kOutput, calls=%fused_computation.13 | convolution fusion | flops 543162368 | bytes 1318912 | tf_op jit(solution)/shard_map/dot_general | solution.py:121
  51.0 1.3 collective-permute-start.10
  52.2 1.3 %collective-permute-start.9 = (f32[2,33,128]{2,1,0:T(8,128)S(1)}, f32[2,33,128]{2,1,0:T(8,128)S(1)}, u32[]{:S(2)}, u32[]{:S(2)}) collective-permute-start(f32[2,33,128]{2,1,0:T(8,128)S(1)} %pad_maximum_fusion.4), channel_id=1, source_target_pairs={{0,384},{64,448},{1,385},{65,449},{2,386},{66,450},{3,387},{67,451... | collective-permute-start | bytes 101384 | tf_op jit(solution)/shard_map/ppermute | solution.py:55
  53.6 1.3 %collective-permute-start.8 = (f32[2,33,128]{2,1,0:T(8,128)S(1)}, f32[2,33,128]{2,1,0:T(8,128)S(1)}, u32[]{:S(2)}, u32[]{:S(2)}) collective-permute-start(f32[2,33,128]{2,1,0:T(8,128)S(1)} %pad_maximum_fusion.4), channel_id=1, source_target_pairs={{0,320},{64,384},{128,448},{1,321},{65,385},{129,449},{2,322},{66,... | collective-permute-start | bytes 101384 | tf_op jit(solution)/shard_map/ppermute | solution.py:55
  54.9 1.3 %collective-permute-start.7 = (f32[2,33,128]{2,1,0:T(8,128)S(1)}, f32[2,33,128]{2,1,0:T(8,128)S(1)}, u32[]{:S(2)}, u32[]{:S(2)}) collective-permute-start(f32[2,33,128]{2,1,0:T(8,128)S(1)} %pad_maximum_fusion.4), channel_id=1, source_target_pairs={{0,256},{64,320},{128,384},{192,448},{1,257},{65,321},{129,385},{1... | collective-permute-start | bytes 101384 | tf_op jit(solution)/shard_map/ppermute | solution.py:55
  56.3 3.0 %collective-permute-done.8 = f32[2,33,128]{2,1,0:T(8,128)S(1)} collective-permute-done((f32[2,33,128]{2,1,0:T(8,128)S(1)}, f32[2,33,128]{2,1,0:T(8,128)S(1)}, u32[]{:S(2)}, u32[]{:S(2)}) %collective-permute-start.8) | collective-permute-done | bytes 33824 | tf_op jit(solution)/shard_map/ppermute | solution.py:55
  59.5 1.9 %collective-permute-start.13 = (f32[2,32,128]{2,1,0:T(8,128)S(1)}, f32[2,32,128]{2,1,0:T(8,128)S(1)}, u32[]{:S(2)}, u32[]{:S(2)}) collective-permute-start(f32[2,32,128]{2,1,0:T(8,128)S(1)} %fusion.65), channel_id=1, source_target_pairs={{0,48},{16,0},{32,16},{48,32},{1,49},{17,1},{33,17},{49,33},{2,50}... | collective-permute-start | bytes 98312 | tf_op jit(solution)/shard_map/ppermute | solution.py:33
  61.4 1.9 %collective-permute-start.12 = (f32[2,32,128]{2,1,0:T(8,128)S(1)}, f32[2,32,128]{2,1,0:T(8,128)S(1)}, u32[]{:S(2)}, u32[]{:S(2)}) collective-permute-start(f32[2,32,128]{2,1,0:T(8,128)S(1)} %fusion.65), channel_id=1, source_target_pairs={{0,32},{16,48},{32,0},{48,16},{1,33},{17,49},{33,1},{49,17},{2,34}... | collective-permute-start | bytes 98312 | tf_op jit(solution)/shard_map/ppermute | solution.py:33
  63.3 3.4 %collective-permute-start.11 = (f32[2,32,128]{2,1,0:T(8,128)S(1)}, f32[2,32,128]{2,1,0:T(8,128)S(1)}, u32[]{:S(2)}, u32[]{:S(2)}) collective-permute-start(f32[2,32,128]{2,1,0:T(8,128)S(1)} %fusion.65), channel_id=1, source_target_pairs={{0,16},{16,32},{32,48},{48,0},{1,17},{17,33},{33,49},{49,1},{2,18}... | collective-permute-start | bytes 98312 | tf_op jit(solution)/shard_map/ppermute | solution.py:33
  66.7 3.1 %fusion.4 = f32[1024,128]{0,1:T(8,128)} fusion(f32[1024]{0:T(1024)S(1)} %bitcast.105, bf16[1024,512]{1,0:T(8,128)(2,1)S(1)} %copy-done, bf16[1024,512]{1,0:T(8,128)(2,1)S(1)} %copy-done.7, bf16[1024,512]{1,0:T(8,128)(2,1)} %param.7), kind=kOutput, calls=%fused_computation.12 | convolution fusion | flops 543162368 | bytes 1318912 | tf_op jit(solution)/shard_map/dot_general | solution.py:121
  71.1 4.7 %collective-permute-start.14 = (f32[2,128,128]{2,1,0:T(8,128)}, f32[2,128,128]{2,1,0:T(8,128)}, u32[]{:S(2)}, u32[]{:S(2)}) collective-permute-start(f32[2,128,128]{2,1,0:T(8,128)} %fusion.64), channel_id=1, source_target_pairs={{0,8},{8,0},{1,9},{9,1},{2,10},{10,2},{3,11},{11,3},{4,12},{12,4},... | collective-permute-start | bytes 393224 | tf_op jit(solution)/shard_map/ppermute | solution.py:107
  75.9 3.3 %fusion.3 = f32[1024,128]{0,1:T(8,128)} fusion(f32[1024]{0:T(1024)S(1)} %bitcast.104, bf16[1024,512]{1,0:T(8,128)(2,1)} %param.8, bf16[1024,512]{1,0:T(8,128)(2,1)} %param.7, bf16[1024,512]{1,0:T(8,128)(2,1)S(1)} %copy-done), kind=kOutput, calls=%fused_computation.11 | convolution fusion | flops 543162368 | bytes 1318912 | tf_op jit(solution)/shard_map/dot_general | solution.py:121
  80.7 1.2 add_select_fusion
  81.9 1.1 fusion.18
  86.1 40.5 %all_to_all.5 = bf16[8,129,512]{2,1,0:T(8,128)(2,1)S(1)} all-to-all(bf16[8,129,512]{2,1,0:T(8,128)(2,1)S(1)} %maximum_maximum_fusion), channel_id=1, replica_groups=mesh['cy'=8,'cx'=4,'cc'=2,'head'=8] {'head'}, dimensions={0} | all-to-all | bytes 2113536 | tf_op jit(solution)/shard_map/all_to_all | solution.py:172
  127.6 1.3 %copy.35 = bf16[128,4096]{1,0:T(8,128)(2,1)} copy(bf16[128,4096]{0,1:T(8,128)(2,1)S(1)} %bitcast.91) | data formatting | bytes 2097152 | tf_op jit(solution)/shard_map/convert_element_type | solution.py:177
  (78 shorter events, 10.9 us)
Async XLA Ops:
  0.0 10.0 %copy-start.7 = (bf16[1024,512]{1,0:T(8,128)(2,1)S(1)}, bf16[1024,512]{1,0:T(8,128)(2,1)}, u32[]{:S(2)}) copy-start(bf16[1024,512]{1,0:T(8,128)(2,1)} %param.8) | copy-start | bytes 3145732
  13.5 18.4 %copy-start = (bf16[1024,512]{1,0:T(8,128)(2,1)S(1)}, bf16[1024,512]{1,0:T(8,128)(2,1)}, u32[]{:S(2)}) copy-start(bf16[1024,512]{1,0:T(8,128)(2,1)} %param.6) | copy-start | bytes 3145732
  13.5 10.1 %collective-permute-start = (f32[4,129,128]{2,1,0:T(8,128)S(1)}, f32[4,129,128]{2,1,0:T(8,128)S(1)}, u32[]{:S(2)}, u32[]{:S(2)}) collective-permute-start(f32[4,129,128]{2,1,0:T(8,128)S(1)} %pad_maximum_fusion.1), channel_id=1, source_target_pairs={{0,8},{8,0},{1,9},{9,1},{2,10},{10,2},{3,11},{11,3},{4,12},{12,4},... | collective-permute-start | bytes 792584 | tf_op jit(solution)/shard_map/ppermute | solution.py:80
  24.7 10.4 %collective-permute-start.3 = (f32[2,129,128]{2,1,0:T(8,128)S(1)}, f32[2,129,128]{2,1,0:T(8,128)S(1)}, u32[]{:S(2)}, u32[]{:S(2)}) collective-permute-start(f32[2,129,128]{2,1,0:T(8,128)S(1)} %pad_maximum_fusion.3), channel_id=1, source_target_pairs={{0,48},{16,0},{32,16},{48,32},{1,49},{17,1},{33,17},{49,33},{2,50}... | collective-permute-start | bytes 396296 | tf_op jit(solution)/shard_map/ppermute | solution.py:33
  26.6 8.4 %collective-permute-start.2 = (f32[2,129,128]{2,1,0:T(8,128)S(1)}, f32[2,129,128]{2,1,0:T(8,128)S(1)}, u32[]{:S(2)}, u32[]{:S(2)}) collective-permute-start(f32[2,129,128]{2,1,0:T(8,128)S(1)} %pad_maximum_fusion.3), channel_id=1, source_target_pairs={{0,32},{16,48},{32,0},{48,16},{1,33},{17,49},{33,1},{49,17},{2,34}... | collective-permute-start | bytes 396296 | tf_op jit(solution)/shard_map/ppermute | solution.py:33
  28.5 9.2 %collective-permute-start.1 = (f32[2,129,128]{2,1,0:T(8,128)S(1)}, f32[2,129,128]{2,1,0:T(8,128)S(1)}, u32[]{:S(2)}, u32[]{:S(2)}) collective-permute-start(f32[2,129,128]{2,1,0:T(8,128)S(1)} %pad_maximum_fusion.3), channel_id=1, source_target_pairs={{0,16},{16,32},{32,48},{48,0},{1,17},{17,33},{33,49},{49,1},{2,18}... | collective-permute-start | bytes 396296 | tf_op jit(solution)/shard_map/ppermute | solution.py:33
  38.3 15.2 %collective-permute-start.6 = (f32[2,33,128]{2,1,0:T(8,128)S(1)}, f32[2,33,128]{2,1,0:T(8,128)S(1)}, u32[]{:S(2)}, u32[]{:S(2)}) collective-permute-start(f32[2,33,128]{2,1,0:T(8,128)S(1)} %pad_maximum_fusion.4), channel_id=1, source_target_pairs={{0,192},{64,256},{128,320},{192,384},{256,448},{1,193},{65,257},{1... | collective-permute-start | bytes 101384 | tf_op jit(solution)/shard_map/ppermute | solution.py:55
  41.0 13.9 %collective-permute-start.5 = (f32[2,33,128]{2,1,0:T(8,128)S(1)}, f32[2,33,128]{2,1,0:T(8,128)S(1)}, u32[]{:S(2)}, u32[]{:S(2)}) collective-permute-start(f32[2,33,128]{2,1,0:T(8,128)S(1)} %pad_maximum_fusion.4), channel_id=1, source_target_pairs={{0,128},{64,192},{128,256},{192,320},{256,384},{320,448},{1,129},{... | collective-permute-start | bytes 101384 | tf_op jit(solution)/shard_map/ppermute | solution.py:55
  45.5 10.7 %collective-permute-start.4 = (f32[2,33,128]{2,1,0:T(8,128)S(1)}, f32[2,33,128]{2,1,0:T(8,128)S(1)}, u32[]{:S(2)}, u32[]{:S(2)}) collective-permute-start(f32[2,33,128]{2,1,0:T(8,128)S(1)} %pad_maximum_fusion.4), channel_id=1, source_target_pairs={{0,64},{64,128},{128,192},{192,256},{256,320},{320,384},{384,448},... | collective-permute-start | bytes 101384 | tf_op jit(solution)/shard_map/ppermute | solution.py:55
  51.0 8.4 %collective-permute-start.10 = (f32[2,33,128]{2,1,0:T(8,128)S(1)}, f32[2,33,128]{2,1,0:T(8,128)S(1)}, u32[]{:S(2)}, u32[]{:S(2)}) collective-permute-start(f32[2,33,128]{2,1,0:T(8,128)S(1)} %pad_maximum_fusion.4), channel_id=1, source_target_pairs={{0,448},{1,449},{2,450},{3,451},{4,452},{5,453},{6,454},{7,455},{8... | collective-permute-start | bytes 101384 | tf_op jit(solution)/shard_map/ppermute | solution.py:55
  52.2 4.0 %collective-permute-start.9 = (f32[2,33,128]{2,1,0:T(8,128)S(1)}, f32[2,33,128]{2,1,0:T(8,128)S(1)}, u32[]{:S(2)}, u32[]{:S(2)}) collective-permute-start(f32[2,33,128]{2,1,0:T(8,128)S(1)} %pad_maximum_fusion.4), channel_id=1, source_target_pairs={{0,384},{64,448},{1,385},{65,449},{2,386},{66,450},{3,387},{67,451... | collective-permute-start | bytes 101384 | tf_op jit(solution)/shard_map/ppermute | solution.py:55
  53.6 5.7 %collective-permute-start.8 = (f32[2,33,128]{2,1,0:T(8,128)S(1)}, f32[2,33,128]{2,1,0:T(8,128)S(1)}, u32[]{:S(2)}, u32[]{:S(2)}) collective-permute-start(f32[2,33,128]{2,1,0:T(8,128)S(1)} %pad_maximum_fusion.4), channel_id=1, source_target_pairs={{0,320},{64,384},{128,448},{1,321},{65,385},{129,449},{2,322},{66,... | collective-permute-start | bytes 101384 | tf_op jit(solution)/shard_map/ppermute | solution.py:55
  54.9 4.4 %collective-permute-start.7 = (f32[2,33,128]{2,1,0:T(8,128)S(1)}, f32[2,33,128]{2,1,0:T(8,128)S(1)}, u32[]{:S(2)}, u32[]{:S(2)}) collective-permute-start(f32[2,33,128]{2,1,0:T(8,128)S(1)} %pad_maximum_fusion.4), channel_id=1, source_target_pairs={{0,256},{64,320},{128,384},{192,448},{1,257},{65,321},{129,385},{1... | collective-permute-start | bytes 101384 | tf_op jit(solution)/shard_map/ppermute | solution.py:55
  59.5 10.3 %collective-permute-start.13 = (f32[2,32,128]{2,1,0:T(8,128)S(1)}, f32[2,32,128]{2,1,0:T(8,128)S(1)}, u32[]{:S(2)}, u32[]{:S(2)}) collective-permute-start(f32[2,32,128]{2,1,0:T(8,128)S(1)} %fusion.65), channel_id=1, source_target_pairs={{0,48},{16,0},{32,16},{48,32},{1,49},{17,1},{33,17},{49,33},{2,50}... | collective-permute-start | bytes 98312 | tf_op jit(solution)/shard_map/ppermute | solution.py:33
  61.4 8.4 %collective-permute-start.12 = (f32[2,32,128]{2,1,0:T(8,128)S(1)}, f32[2,32,128]{2,1,0:T(8,128)S(1)}, u32[]{:S(2)}, u32[]{:S(2)}) collective-permute-start(f32[2,32,128]{2,1,0:T(8,128)S(1)} %fusion.65), channel_id=1, source_target_pairs={{0,32},{16,48},{32,0},{48,16},{1,33},{17,49},{33,1},{49,17},{2,34}... | collective-permute-start | bytes 98312 | tf_op jit(solution)/shard_map/ppermute | solution.py:33
  63.3 7.0 %collective-permute-start.11 = (f32[2,32,128]{2,1,0:T(8,128)S(1)}, f32[2,32,128]{2,1,0:T(8,128)S(1)}, u32[]{:S(2)}, u32[]{:S(2)}) collective-permute-start(f32[2,32,128]{2,1,0:T(8,128)S(1)} %fusion.65), channel_id=1, source_target_pairs={{0,16},{16,32},{32,48},{48,0},{1,17},{17,33},{33,49},{49,1},{2,18}... | collective-permute-start | bytes 98312 | tf_op jit(solution)/shard_map/ppermute | solution.py:33
  71.1 9.5 %collective-permute-start.14 = (f32[2,128,128]{2,1,0:T(8,128)}, f32[2,128,128]{2,1,0:T(8,128)}, u32[]{:S(2)}, u32[]{:S(2)}) collective-permute-start(f32[2,128,128]{2,1,0:T(8,128)} %fusion.64), channel_id=1, source_target_pairs={{0,8},{8,0},{1,9},{9,1},{2,10},{10,2},{3,11},{11,3},{4,12},{12,4},... | collective-permute-start | bytes 393224 | tf_op jit(solution)/shard_map/ppermute | solution.py:107
  75.9 3.3 %copy-start.1 = (bf16[1024,512]{1,0:T(8,128)(2,1)S(1)}, bf16[1024,512]{1,0:T(8,128)(2,1)}, u32[]{:S(2)}) copy-start(bf16[1024,512]{1,0:T(8,128)(2,1)} %param.10) | copy-start | bytes 3145732
  79.7 2.1 %copy-start.2 = (f32[1024,128]{0,1:T(8,128)S(1)}, f32[1024,128]{0,1:T(8,128)}, u32[]{:S(2)}) copy-start(f32[1024,128]{0,1:T(8,128)} %fusion.6) | copy-start | bytes 1572868
  79.8 3.3 %copy-start.3 = (f32[1024,128]{0,1:T(8,128)S(1)}, f32[1024,128]{0,1:T(8,128)}, u32[]{:S(2)}) copy-start(f32[1024,128]{0,1:T(8,128)} %fusion.5) | copy-start | bytes 1572868
  79.8 3.3 %copy-start.6 = (f32[1024,1]{0,1:T(1,128)S(1)}, f32[1024,1]{0,1:T(1,128)}, u32[]{:S(2)}) copy-start(f32[1024,1]{0,1:T(1,128)} %get-tuple-element.51) | copy-start | bytes 12292
  81.9 1.6 %copy-start.4 = (f32[1024,128]{0,1:T(8,128)S(1)}, f32[1024,128]{0,1:T(8,128)}, u32[]{:S(2)}) copy-start(f32[1024,128]{0,1:T(8,128)} %fusion.4) | copy-start | bytes 1572868
  83.1 1.0 copy-start.5
